TPU v7x, 32 devices: a whole 2x2x4 slice. The times are simulated.
32 devices in a mesh: space: 16 (over z, y, x), ray: 2 (over core).
Axes of the slice: x: 2, y: 2, z: 4, core: 2. Of those that a mesh axis runs over, the one named last changes fastest.
Arguments:
- positions: float32 [3, 512, 256], P(None, ('space', 'ray')), may hold values from -1 to 1
- spacing: float32 [512, 256], P(('space', 'ray')), may hold values from 0.003 to 0.03
- assign: int32 [512, 8, 1], P(('space', 'ray')), may hold values from 0 to 15; in each aligned block of 128 rows (0 to 127, 128 to 255, ..., all dimensions but the last counted through in order) at most 12 rows name the same one
- depth_rank: int32 [512, 8], P(('space', 'ray')), may hold values from 0 to 7, each once within a row
- pixel_grad: float32 [3, 512], P(None, ('space', 'ray')), may hold values from -96 to 96
- fourier: float32 [3, 128], replicated, may hold values from -4 to 4
- first_weight: bfloat16 [16, 256, 256], P('space'), may hold values from -0.375 to 0.375
- first_bias: float32 [16, 256], P('space'), may hold values from -3 to 3
- second_weight: bfloat16 [16, 256, 256], P('space'), may hold values from -0.375 to 0.375
- second_bias: float32 [16, 256], P('space'), may hold values from -3 to 3
- head_weight: bfloat16 [16, 4, 256], P('space'), may hold values from -0.375 to 0.375
- head_bias: float32 [16, 4], P('space'), may hold values from -3 to 3
Outputs:
- grad_first: float32 [16, 256, 256], P('space', 'ray')
- grad_second: float32 [16, 256, 256], P('space', 'ray')
- grad_head: float32 [16, 4, 256], P('space')
- grad_first_bias: float32 [16, 256], P('space')
- grad_second_bias: float32 [16, 256], P('space')
- grad_head_bias: float32 [16, 4], P('space')
Inputs may be any that keep to these rules, and one draw needn't show every extreme that they name: `assign`: within the segments of one device (aligned blocks of 128 rows in ray order), no partition is named more than 12 times. `depth_rank`: each ray's row names every place 0 to 7 once.
All inputs are finite; a program needn't handle non-finite values.
Results may differ from a plain program's by a relative error of at most 0.0053.
Values sent between devices are 32-bit elements; how exact they have to be, the bound alone decides.
No kernel may reach another device: no remote copies, remote signals or barrier semaphores. Data moves between devices by JAX's collectives and lax.ppermute only.
A program may use at most 64 MiB of HBM per device.

v0:
```python
import jax
import jax.numpy as jnp
from jax import lax
from jax.sharding import PartitionSpec as P

SEG_LEN = 32
SEGS = 8


two_pi = 6.283185307179586


def silu_slope(value):
    gate = jax.nn.sigmoid(value)
    return gate * (1.0 + value * (1.0 - gate))


def encode(samples, fourier):
    phases = two_pi * (
        samples[:, 0, :, None] * fourier[0]
        + samples[:, 1, :, None] * fourier[1]
        + samples[:, 2, :, None] * fourier[2]
    )
    joined = jnp.concatenate([jnp.sin(phases), jnp.cos(phases)], axis=-1)
    return joined.astype(jnp.bfloat16).reshape(-1, joined.shape[-1])


def network(samples, fourier, params):
    first_weight, first_bias, second_weight, second_bias, head_weight, head_bias = params
    seg_count, length = (samples.shape[0], samples.shape[2])
    encoded = encode(samples, fourier)
    pre_first = jnp.dot(encoded, first_weight, preferred_element_type=jnp.float32) + first_bias
    act_first = jax.nn.silu(pre_first).astype(jnp.bfloat16)
    pre_second = jnp.dot(act_first, second_weight, preferred_element_type=jnp.float32) + second_bias
    act_second = jax.nn.silu(pre_second).astype(jnp.bfloat16)
    head_raw = (
        lax.dot_general(
            act_second, head_weight, (((1,), (1,)), ((), ())), preferred_element_type=jnp.float32
        )
        + head_bias
    )
    head_raw = head_raw.reshape(seg_count, length, 4)
    density = jax.nn.softplus(head_raw[..., 0])
    colour = jax.nn.sigmoid(head_raw[..., 1:])
    optical = density * samples[:, 3, :]
    inclusive = jnp.cumsum(optical, axis=1)
    enter_light = jnp.exp(optical - inclusive)
    leave_light = jnp.exp(-inclusive)
    weight = enter_light - leave_light
    seg_colour = jnp.sum(weight[..., None] * colour, axis=1)
    seg_log = -inclusive[:, -1]
    saved = (
        encoded,
        pre_first,
        act_first,
        pre_second,
        act_second,
        head_raw,
        colour,
        weight,
        leave_light,
    )
    return (seg_colour, seg_log, saved)


def backward(samples, fourier, params, up_colour, up_log):
    first_weight, first_bias, second_weight, second_bias, head_weight, head_bias = params
    unused_colour, unused_log, saved = network(samples, fourier, params)
    encoded, pre_first, act_first, pre_second, act_second, head_raw, colour, weight, leave_light = (
        saved
    )
    energy = jnp.sum(colour * up_colour[:, None, :], axis=-1)
    spent = weight * energy
    remaining = jnp.sum(spent, axis=1, keepdims=True) - jnp.cumsum(spent, axis=1)
    grad_optical = leave_light * energy - remaining - up_log[:, None]
    grad_density = grad_optical * samples[:, 3, :] * jax.nn.sigmoid(head_raw[..., 0])
    grad_tint = weight[..., None] * up_colour[:, None, :] * colour * (1.0 - colour)
    grad_raw = (
        jnp.concatenate([grad_density[..., None], grad_tint], axis=-1)
        .reshape(-1, 4)
        .astype(jnp.bfloat16)
    )
    grad_head = lax.dot_general(
        grad_raw, act_second, (((0,), (0,)), ((), ())), preferred_element_type=jnp.float32
    )
    grad_head_bias = jnp.sum(grad_raw.astype(jnp.float32), axis=0)
    back_second = jnp.dot(grad_raw, head_weight, preferred_element_type=jnp.float32)
    delta_second = (back_second * silu_slope(pre_second)).astype(jnp.bfloat16)
    grad_second = lax.dot_general(
        act_first, delta_second, (((0,), (0,)), ((), ())), preferred_element_type=jnp.float32
    )
    grad_second_bias = jnp.sum(delta_second.astype(jnp.float32), axis=0)
    back_first = lax.dot_general(
        delta_second, second_weight, (((1,), (1,)), ((), ())), preferred_element_type=jnp.float32
    )
    delta_first = (back_first * silu_slope(pre_first)).astype(jnp.bfloat16)
    grad_first = lax.dot_general(
        encoded, delta_first, (((0,), (0,)), ((), ())), preferred_element_type=jnp.float32
    )
    grad_first_bias = jnp.sum(delta_first.astype(jnp.float32), axis=0)
    return (grad_first, grad_second, grad_head, grad_first_bias, grad_second_bias, grad_head_bias)


def composite(seg_colour, seg_log, depth_rank, pixel_rows):
    before = (depth_rank[:, None, :] < depth_rank[:, :, None]).astype(jnp.float32)
    prefix = jnp.exp(jnp.sum(before * seg_log[:, None, :], axis=2))
    up_colour = prefix[..., None] * pixel_rows[:, None, :]
    shaded = prefix * jnp.sum(seg_colour * pixel_rows[:, None, :], axis=2)
    up_log = jnp.sum(before * shaded[:, :, None], axis=1)
    return (up_colour, up_log)


def per_device(
    positions,
    spacing,
    assign,
    depth_rank,
    pixel_grad,
    fourier,
    first_weight,
    first_bias,
    second_weight,
    second_bias,
    head_weight,
    head_bias,
):
    groups = lax.axis_size("space")
    ray_count = positions.shape[1]
    total = ray_count * SEGS
    capacity = 3 * total // (2 * groups)
    slot_count = capacity * groups
    block_slots = 16
    blocks = slot_count // block_slots
    owner = assign.reshape(total)
    member = (owner[:, None] == jnp.arange(groups, dtype=jnp.int32)[None, :]).astype(jnp.int32)
    earlier = jnp.cumsum(member, axis=0) - member
    within = jnp.sum(earlier * member, axis=1)
    target = owner * capacity + within
    dispatch = (target[:, None] == jnp.arange(slot_count, dtype=jnp.int32)[None, :]).astype(
        jnp.float32
    )
    seg_pos = jnp.transpose(positions.reshape(3, total, SEG_LEN), (1, 0, 2))
    seg_gap = spacing.reshape(total, 1, SEG_LEN)
    segments = jnp.concatenate([seg_pos, seg_gap], axis=1).reshape(total, 4 * SEG_LEN)
    outgoing = lax.dot_general(
        dispatch,
        segments,
        (((0,), (0,)), ((), ())),
        precision=lax.Precision.HIGHEST,
        preferred_element_type=jnp.float32,
    )
    outgoing = outgoing.reshape(groups, capacity, 4 * SEG_LEN)
    arrived = lax.all_to_all(outgoing, "space", split_axis=0, concat_axis=0, tiled=True)
    stacked = arrived.reshape(blocks, block_slots, 4, SEG_LEN)
    params = tuple(
        (
            item[0]
            for item in (
                first_weight,
                first_bias,
                second_weight,
                second_bias,
                head_weight,
                head_bias,
            )
        )
    )

    def first_pass(piece):
        seg_colour, seg_log, unused = network(piece, fourier, params)
        return jnp.concatenate([seg_colour.T, seg_log[None, :]], axis=0)

    partial_rows = lax.map(first_pass, stacked)
    partials = jnp.transpose(partial_rows, (1, 0, 2)).reshape(4, groups, capacity)
    returned = lax.all_to_all(partials, "space", split_axis=1, concat_axis=1, tiled=True).reshape(
        4, slot_count
    )
    mine = lax.dot_general(
        dispatch,
        returned,
        (((1,), (1,)), ((), ())),
        precision=lax.Precision.HIGHEST,
        preferred_element_type=jnp.float32,
    )
    up_colour, up_log = composite(
        mine[:, :3].reshape(ray_count, SEGS, 3),
        mine[:, 3].reshape(ray_count, SEGS),
        depth_rank,
        pixel_grad.T,
    )
    upstream = jnp.concatenate([up_colour.reshape(total, 3), up_log.reshape(total, 1)], axis=1)
    sendback = lax.dot_general(
        upstream,
        dispatch,
        (((0,), (0,)), ((), ())),
        precision=lax.Precision.HIGHEST,
        preferred_element_type=jnp.float32,
    )
    sendback = sendback.reshape(4, groups, capacity)
    received = lax.all_to_all(sendback, "space", split_axis=1, concat_axis=1, tiled=True)
    received = jnp.transpose(received.reshape(4, blocks, block_slots), (1, 2, 0))
    start_sums = (
        jnp.zeros(first_weight.shape[1:], jnp.float32),
        jnp.zeros(second_weight.shape[1:], jnp.float32),
        jnp.zeros(head_weight.shape[1:], jnp.float32),
        jnp.zeros(first_bias.shape[1:], jnp.float32),
        jnp.zeros(second_bias.shape[1:], jnp.float32),
        jnp.zeros(head_bias.shape[1:], jnp.float32),
    )

    def second_pass(carry, inputs):
        piece, incoming = inputs
        result = backward(piece, fourier, params, incoming[:, :3], incoming[:, 3])
        return (jax.tree.map(jnp.add, carry, result), None)

    totals, unused_out = lax.scan(second_pass, start_sums, (stacked, received))
    grad_first, grad_second, grad_head, bias_first, bias_second, bias_head = totals
    small_sums = lax.psum((grad_head, bias_first, bias_second, bias_head), "ray")
    whole_first, whole_second = lax.psum((grad_first, grad_second), "ray")
    replicas = lax.axis_size("ray")
    position = lax.axis_index("ray")
    rows_first = whole_first.shape[0] // replicas
    rows_second = whole_second.shape[0] // replicas
    part_first = lax.dynamic_slice_in_dim(whole_first, position * rows_first, rows_first, 0)
    part_second = lax.dynamic_slice_in_dim(whole_second, position * rows_second, rows_second, 0)
    return (
        part_first[None],
        part_second[None],
        small_sums[0][None],
        small_sums[1][None],
        small_sums[2][None],
        small_sums[3][None],
    )


def solution(mesh):
    placed = (
        P(None, ("space", "ray"), None),
        P(("space", "ray"), None),
        P(("space", "ray"), None, None),
        P(("space", "ray"), None),
        P(None, ("space", "ray")),
        P(),
        P("space", None, None),
        P("space", None),
        P("space", None, None),
        P("space", None),
        P("space", None, None),
        P("space", None),
    )
    return jax.shard_map(
        per_device,
        mesh=mesh,
        in_specs=placed,
        out_specs=(
            P("space", "ray", None),
            P("space", "ray", None),
            P("space", None, None),
            P("space", None),
            P("space", None),
            P("space", None),
        ),
        check_vma=False,
    )
```

profile of v0, /device:TPU:0, one launch (start us, length us, event | category | flops | bytes accessed | tf_op | source)
XLA Modules:
  0.0 199.2 jit_solution(8023666779261984281)
XLA Ops:
  11.1 8.3 %all-to-all-start = ((f32[16,12,128]{2,1,0:T(8,128)}), f32[16,12,128]{2,1,0:T(8,128)S(1)}, u32[]{:S(2)}, u32[]{:S(2)}) async-start(f32[16,12,128]{2,1,0:T(8,128)} %fusion.50), calls=%async_computation | async-start | bytes 262144 | tf_op jit(solution)/shard_map/all_to_all | solution.py:153
  19.4 7.8 %all-to-all-done = f32[16,12,128]{2,1,0:T(8,128)S(1)} async-done(((f32[16,12,128]{2,1,0:T(8,128)}), f32[16,12,128]{2,1,0:T(8,128)S(1)}, u32[]{:S(2)}, u32[]{:S(2)}) %all-to-all-start) | async-done | bytes 98336 | tf_op jit(solution)/shard_map/all_to_all | solution.py:153
  28.4 34.9 %while.31 = (s32[]{:T(128)}, f32[12,4,16]{2,1,0:T(4,128)S(1)}, f32[12,16,4,32]{3,1,2,0:T(8,128)S(1)}, f32[3,128]{1,0:T(4,128)S(1)}, bf16[256,256]{1,0:T(8,128)(2...) while((s32[]{:T(128)}, f32[12,4,16]{2,1,0:T(4,128)S(1)}, ...), condition=%wide.region_5.6_spmd, body=%wide.region_2.5_spmd.sunk | while | flops 137922080 | bytes 1422801 | solution.py:173
  46.1 1.2 sine_convert_fusion.4
  64.0 3.5 %all-to-all-start.1 = ((f32[4,16,12]{2,0,1:T(4,128)}), f32[4,16,12]{2,0,1:T(4,128)S(1)}, u32[]{:S(2)}, u32[]{:S(2)}) async-start(f32[4,16,12]{2,0,1:T(4,128)} %copy.63), calls=%async_computation.1 | async-start | bytes 65536 | tf_op jit(solution)/shard_map/all_to_all | solution.py:175
  67.7 7.2 %all-to-all-done.1 = f32[4,16,12]{2,0,1:T(4,128)S(1)} async-done(((f32[4,16,12]{2,0,1:T(4,128)}), f32[4,16,12]{2,0,1:T(4,128)S(1)}, u32[]{:S(2)}, u32[]{:S(2)}) %all-to-all-start.1) | async-done | bytes 3104 | tf_op jit(solution)/shard_map/all_to_all | solution.py:175
  77.6 3.5 %all-to-all-start.2 = ((f32[4,16,12]{2,0,1:T(4,128)}), f32[4,16,12]{2,0,1:T(4,128)S(1)}, u32[]{:S(2)}, u32[]{:S(2)}) async-start(f32[4,16,12]{2,0,1:T(4,128)} %copy.69), calls=%async_computation.2 | async-start | bytes 65536 | tf_op jit(solution)/shard_map/all_to_all | solution.py:200
  81.2 7.3 %all-to-all-done.2 = f32[4,16,12]{2,0,1:T(4,128)S(1)} async-done(((f32[4,16,12]{2,0,1:T(4,128)}), f32[4,16,12]{2,0,1:T(4,128)S(1)}, u32[]{:S(2)}, u32[]{:S(2)}) %all-to-all-start.2) | async-done | bytes 3104 | tf_op jit(solution)/shard_map/all_to_all | solution.py:200
  88.5 85.9 %while.32 = (s32[]{:T(128)}, f32[256,256]{1,0:T(8,128)S(1)}, f32[256,256]{1,0:T(8,128)S(1)}, f32[4,256]{1,0:T(4,128)S(1)}, f32[256]{0:T(256)S(1)}, /*index=5*/f3...) while((s32[]{:T(128)}, f32[256,256]{1,0:T(8,128)S(1)}, ...), condition=%wide.region_17.18_spmd.clone, body=%wide.region_9.17_spmd.clone.sunk | while | flops 345741312 | bytes 7663575 | solution.py:216
  91.5 1.9 fusion.133
  98.7 1.9 fusion.133
  105.9 1.9 fusion.133
  113.0 1.9 fusion.133
  120.2 1.9 fusion.133
  127.3 1.9 fusion.133
  134.5 1.9 fusion.133
  141.7 1.9 fusion.133
  148.8 1.9 fusion.133
  156.0 1.9 fusion.133
  163.2 1.9 fusion.133
  170.3 1.9 fusion.133
  175.3 3.1 %all-reduce = (f32[1,4,256]{2,1,0:T(4,128)}, f32[1,256]{1,0:T(1,128)}, f32[1,256]{1,0:T(1,128)}, f32[1,4]{1,0:T(1,128)}) all-reduce(f32[1,4,256]{2,1,0:T(4,128)S(1)} %bitcast.270, f32[1,256]{1,0:T(1,128)S(1)} %bitcast.273, f32[1,256]{1,0:T(1,128)S(1)} %bitcast.274, f32[1,4]{1,0:T(1,128)S(1)} %bitcast.278), channel_id=1, replica_groups=mesh['space'=16,'ray'=2] {'ray'}, use_global_device_ids=true, to_apply=%region_20.21 | all-reduce | flops 1540 | bytes 12320 | tf_op jit(solution)/shard_map/psum | solution.py:218
  178.4 12.3 %all-reduce.4.cloned.1.call-done = (f32[256,256]{1,0:T(8,128)}, f32[256,256]{1,0:T(8,128)}) async-done(((f32[256,256]{1,0:T(8,128)}, f32[256,256]{1,0:T(8,128)}), (f32[256,256]{1,0:T(8,128)}, f32[256,256]{1,0:T(8,128)})) %all-reduce.4.cloned.1.call-update) | async-done | bytes 524304 | tf_op jit(solution)/shard_map/psum | solution.py:219
  190.7 1.7 dynamic-slice_bitcast_fusion.2
  (655 shorter events, 104.0 us)
Async XLA Ops:
  7.2 0.7 copy-start.8
  8.3 0.8 copy-start.5
  9.2 0.7 copy-start.7
  11.1 16.1 %all-to-all-start = ((f32[16,12,128]{2,1,0:T(8,128)}), f32[16,12,128]{2,1,0:T(8,128)S(1)}, u32[]{:S(2)}, u32[]{:S(2)}) async-start(f32[16,12,128]{2,1,0:T(8,128)} %fusion.50), calls=%async_computation | async-start | bytes 262144 | tf_op jit(solution)/shard_map/all_to_all | solution.py:153
  27.4 0.9 copy-start
  27.4 1.0 copy-start.10
  27.4 1.0 copy-start.11
  27.4 0.9 copy-start.12
  27.5 0.9 copy-start.3
  27.5 0.9 copy-start.6
  27.5 0.9 copy-start.13
  28.4 39.1 %copy-start.9 = (f32[3,16]{1,0:T(4,128)S(1)}, f32[3,16]{1,0:T(4,128)}, u32[]{:S(2)}) copy-start(f32[3,16]{1,0:T(4,128)} %param.20) | copy-start | bytes 580
  64.0 10.9 %all-to-all-start.1 = ((f32[4,16,12]{2,0,1:T(4,128)}), f32[4,16,12]{2,0,1:T(4,128)S(1)}, u32[]{:S(2)}, u32[]{:S(2)}) async-start(f32[4,16,12]{2,0,1:T(4,128)} %copy.63), calls=%async_computation.1 | async-start | bytes 65536 | tf_op jit(solution)/shard_map/all_to_all | solution.py:175
  75.5 0.7 copy-start.4
  77.6 10.9 %all-to-all-start.2 = ((f32[4,16,12]{2,0,1:T(4,128)}), f32[4,16,12]{2,0,1:T(4,128)S(1)}, u32[]{:S(2)}, u32[]{:S(2)}) async-start(f32[4,16,12]{2,0,1:T(4,128)} %copy.69), calls=%async_computation.2 | async-start | bytes 65536 | tf_op jit(solution)/shard_map/all_to_all | solution.py:200
  81.1 109.6 %all-reduce.4.cloned.1.call-start = ((), (), s32[]{:S(2)}) async-start(), calls=%async_computation.3 | async-start | bytes 1048576 | tf_op jit(solution)/shard_map/psum | solution.py:219
  174.5 0.7 copy-start.1
  174.5 0.8 copy-start.2
Sparse Core Ops, SparseCore 0:
  175.4 15.2 all-reduce.3
where the time goes:
time: 200 us; the launch traced here: 199 us
  other arithmetic  68.4 us (34%)
  matrix products  36.9 us (18%)
  waiting for transfers between devices  34.6 us (17%)
  local copies, waits for them, and re-layouts  24.2 us (12%)
  starting transfers between devices  15.3 us (8%)
  between operations  14.4 us (7%)
  blocking collectives  3.08 us (2%)
  loops' own time  2.37 us (1%)
    another operation x48, other arithmetic  31.5 us
    another operation x12, other arithmetic, backward(): jnp.cumsum(spent, axis=1)  22.6 us
    psum x1, waiting for transfers between devices, per_device(): whole_first, whole_second = lax.psum((grad_first, grad_second), 'ray')  12.3 us
    all_to_all x1, starting transfers between devices, per_device(): lax.all_to_all(outgoing, 'space', split_axis=0, concat_axis=0, tiled=True)  8.31 us
    all_to_all x1, waiting for transfers between devices, per_device(): lax.all_to_all(outgoing, 'space', split_axis=0, concat_axis=0, tiled=True)  7.79 us
    all_to_all x1, waiting for transfers between devices, per_device(): lax.all_to_all(sendback, 'space', split_axis=1, concat_axis=1, tiled=True)  7.26 us
    all_to_all x1, waiting for transfers between devices, per_device(): lax.all_to_all(partials, 'space', split_axis=1, concat_axis=1, tiled=True)  7.19 us
    dot_general x24, matrix products, network(): lax.dot_general(act_second, head_weight, (((1,), (1,)), ((), ())), prefer...  6.91 us
  transfers between devices with their start and end apart: 4, of which 4 were waited for; matrix products, arithmetic and copies ran while one was open for 0% of the time, Pallas kernels for 0%

commit v1 on v0

--- a/solution.py
+++ b/solution.py
@@ -63,9 +63,8 @@
     return (seg_colour, seg_log, saved)
 
 
-def backward(samples, fourier, params, up_colour, up_log):
+def backward(samples, params, saved, up_colour, up_log):
     first_weight, first_bias, second_weight, second_bias, head_weight, head_bias = params
-    unused_colour, unused_log, saved = network(samples, fourier, params)
     encoded, pre_first, act_first, pre_second, act_second, head_raw, colour, weight, leave_light = (
         saved
     )
@@ -129,8 +128,6 @@
     total = ray_count * SEGS
     capacity = 3 * total // (2 * groups)
     slot_count = capacity * groups
-    block_slots = 16
-    blocks = slot_count // block_slots
     owner = assign.reshape(total)
     member = (owner[:, None] == jnp.arange(groups, dtype=jnp.int32)[None, :]).astype(jnp.int32)
     earlier = jnp.cumsum(member, axis=0) - member
@@ -151,7 +148,7 @@
     )
     outgoing = outgoing.reshape(groups, capacity, 4 * SEG_LEN)
     arrived = lax.all_to_all(outgoing, "space", split_axis=0, concat_axis=0, tiled=True)
-    stacked = arrived.reshape(blocks, block_slots, 4, SEG_LEN)
+    samples = arrived.reshape(slot_count, 4, SEG_LEN)
     params = tuple(
         (
             item[0]
@@ -165,13 +162,10 @@
             )
         )
     )
-
-    def first_pass(piece):
-        seg_colour, seg_log, unused = network(piece, fourier, params)
-        return jnp.concatenate([seg_colour.T, seg_log[None, :]], axis=0)
-
-    partial_rows = lax.map(first_pass, stacked)
-    partials = jnp.transpose(partial_rows, (1, 0, 2)).reshape(4, groups, capacity)
+    seg_colour, seg_log, saved = network(samples, fourier, params)
+    partials = jnp.concatenate([seg_colour.T, seg_log[None, :]], axis=0).reshape(
+        4, groups, capacity
+    )
     returned = lax.all_to_all(partials, "space", split_axis=1, concat_axis=1, tiled=True).reshape(
         4, slot_count
     )
@@ -198,22 +192,8 @@
     )
     sendback = sendback.reshape(4, groups, capacity)
     received = lax.all_to_all(sendback, "space", split_axis=1, concat_axis=1, tiled=True)
-    received = jnp.transpose(received.reshape(4, blocks, block_slots), (1, 2, 0))
-    start_sums = (
-        jnp.zeros(first_weight.shape[1:], jnp.float32),
-        jnp.zeros(second_weight.shape[1:], jnp.float32),
-        jnp.zeros(head_weight.shape[1:], jnp.float32),
-        jnp.zeros(first_bias.shape[1:], jnp.float32),
-        jnp.zeros(second_bias.shape[1:], jnp.float32),
-        jnp.zeros(head_bias.shape[1:], jnp.float32),
-    )
-
-    def second_pass(carry, inputs):
-        piece, incoming = inputs
-        result = backward(piece, fourier, params, incoming[:, :3], incoming[:, 3])
-        return (jax.tree.map(jnp.add, carry, result), None)
-
-    totals, unused_out = lax.scan(second_pass, start_sums, (stacked, received))
+    received = received.reshape(4, slot_count).T
+    totals = backward(samples, params, saved, received[:, :3], received[:, 3])
     grad_first, grad_second, grad_head, bias_first, bias_second, bias_head = totals
     small_sums = lax.psum((grad_head, bias_first, bias_second, bias_head), "ray")
     whole_first, whole_second = lax.psum((grad_first, grad_second), "ray")

time: 200 us -> 124 us (0.62)
  other arithmetic: 68.4 us -> 17.4 us
  matrix products: 36.9 us -> 26.2 us
  waiting for transfers between devices: 34.6 us -> 24.5 us
  blocking collectives: 3.08 us -> 13 us
  local copies, waits for them, and re-layouts: 24.2 us -> 15.7 us
  starting transfers between devices: 15.3 us -> 11.9 us
  loops' own time: 2.37 us -> 0 us
    another operation x12 -> x1, other arithmetic: 22.6 us -> 0.06 us  [backward(): jnp.cumsum(spent, axis=1)]
    another operation x48 -> x2, other arithmetic: 31.5 us -> 12.7 us
    all_to_all x0 -> x1, blocking collectives: none -> 9.98 us  [per_device(): lax.all_to_all(sendback, 'space', split_axis=1, concat_axis=1, tiled=True)]
    all_to_all x1 -> x0, waiting for transfers between devices: 7.26 us -> none  [per_device(): lax.all_to_all(sendback, 'space', split_axis=1, concat_axis=1, tiled=True)]
    dot_general x24 -> x1, matrix products: 6.91 us -> 0.91 us  [network(): lax.dot_general(act_second, head_weight, (((1,), (1,)), ((), ())), prefer...]
    another operation x24 -> x1, other arithmetic: 4.45 us -> 0.06 us  [network(): inclusive = jnp.cumsum(optical, axis=1)]
    all_to_all x1 -> x0, starting transfers between devices: 3.5 us -> none  [per_device(): lax.all_to_all(sendback, 'space', split_axis=1, concat_axis=1, tiled=True)]
    unnamed x30 -> x31, local copies, waits for them, and re-layouts: 4.33 us -> 1 us
  transfers between devices with their start and end apart: 4 -> 3, of which waited for: 4 -> 3; matrix products, arithmetic and copies ran while one was open for 0% -> 2% of each run, Pallas kernels for 0% -> 0%
where the time goes in v1:
time: 124 us; the launch traced here: 123 us
  matrix products  26.2 us (21%)
  waiting for transfers between devices  24.5 us (20%)
  other arithmetic  17.4 us (14%)
  local copies, waits for them, and re-layouts  15.7 us (13%)
  between operations  14.4 us (12%)
  blocking collectives  13 us (10%)
  starting transfers between devices  11.9 us (10%)
    another operation x2, other arithmetic  12.7 us
    psum x1, waiting for transfers between devices, per_device(): whole_first, whole_second = lax.psum((grad_first, grad_second), 'ray')  11.7 us
    all_to_all x1, blocking collectives, per_device(): lax.all_to_all(sendback, 'space', split_axis=1, concat_axis=1, tiled=True)  9.98 us
    all_to_all x1, starting transfers between devices, per_device(): lax.all_to_all(outgoing, 'space', split_axis=0, concat_axis=0, tiled=True)  8.31 us
    all_to_all x1, waiting for transfers between devices, per_device(): lax.all_to_all(outgoing, 'space', split_axis=0, concat_axis=0, tiled=True)  7 us
    all_to_all x1, waiting for transfers between devices, per_device(): lax.all_to_all(partials, 'space', split_axis=1, concat_axis=1, tiled=True)  5.81 us
    dot_general x1, matrix products, backward(): jnp.dot(grad_raw, head_weight, preferred_element_type=jnp.float32)  4.84 us
    dot_general x1, matrix products, backward(): lax.dot_general(delta_second, second_weight, (((1,), (1,)), ((), ())), pr...  4.8 us
  transfers between devices with their start and end apart: 3, of which 3 were waited for; matrix products, arithmetic and copies ran while one was open for 2% of the time, Pallas kernels for 0%

profile of v1, /device:TPU:0, one launch (start us, length us, event | category | flops | bytes accessed | tf_op | source)
XLA Modules:
  0.0 123.1 jit_solution(9952207206459518545)
XLA Ops:
  8.5 0.9 reshape.231
  11.4 8.3 %all-to-all-start = ((f32[16,12,128]{2,1,0:T(8,128)}), f32[16,12,128]{2,1,0:T(8,128)S(1)}, u32[]{:S(2)}, u32[]{:S(2)}) async-start(f32[16,12,128]{2,1,0:T(8,128)} %fusion.11), calls=%async_computation | async-start | bytes 262144 | tf_op jit(solution)/shard_map/all_to_all | solution.py:150
  20.6 7.0 %all-to-all-done = f32[16,12,128]{2,1,0:T(8,128)S(1)} async-done(((f32[16,12,128]{2,1,0:T(8,128)}), f32[16,12,128]{2,1,0:T(8,128)S(1)}, u32[]{:S(2)}, u32[]{:S(2)}) %all-to-all-start) | async-done | bytes 98336 | tf_op jit(solution)/shard_map/all_to_all | solution.py:150
  27.8 0.9 slice_reduce_fusion.2
  29.0 12.6 %sine_convert_fusion = (bf16[6144,128]{1,0:T(8,128)(2,1)S(1)}, bf16[6144,128]{1,0:T(8,128)(2,1)S(1)}) fusion(f32[128]{0:T(128)S(1)} %get-tuple-element.23, f32[6144]{0:T(1024)S(1)} %mul.238, f32[128]{0:T(128)S(1)} %get-tuple-element.24, f32[6144]{0:T(1024)S(1)} %mul.233, f32[128]{0:T(128)S(1)} %get-tuple-element.22, f32[6144]{0:T(1024)S(1)} %mul.228), kind=kLoop, calls=%fused_computation.15 | loop fusion | flops 6291456 | bytes 3220992 | tf_op jit(solution)/shard_map/convert.4
  41.7 4.7 %multiply_convert_fusion.1 = (bf16[6144,256]{1,0:T(8,128)(2,1)S(1)}, f32[6144,256]{1,0:T(8,128)}) fusion(f32[256]{0:T(256)S(1)} %bitcast.131, bf16[1,256,256]{2,1,0:T(8,128)(2,1)} %param.18, bf16[6144,128]{1,0:T(8,128)(2,1)S(1)} %get-tuple-element.19, bf16[6144,128]{1,0:T(8,128)(2,1)S(1)} %get-tuple-element.18), kind=kOutput, calls=%fused_computation.11 | convolution fusion | flops 821035008 | bytes 12715008 | tf_op jit(solution)/shard_map/dot_general | solution.py:32
  46.4 4.4 %multiply_convert_fusion = (bf16[6144,256]{1,0:T(8,128)(2,1)S(1)}, f32[6144,256]{1,0:T(8,128)}) fusion(f32[256]{0:T(256)S(1)} %bitcast.132, bf16[6144,256]{1,0:T(8,128)(2,1)S(1)} %get-tuple-element.25, bf16[1,256,256]{2,1,0:T(8,128)(2,1)S(1)} %copy-done), kind=kOutput, calls=%fused_computation.9 | convolution fusion | flops 814743552 | bytes 12715008 | tf_op jit(solution)/shard_map/dot_general | solution.py:34
  50.8 0.9 convolution_add_fusion.2
  51.8 0.9 reshape.235
  52.7 0.9 slice.61
  54.0 1.2 multiply_reduce_fusion.1
  56.0 3.5 %all-to-all-start.1 = ((f32[4,16,12]{2,0,1:T(4,128)}), f32[4,16,12]{2,0,1:T(4,128)S(1)}, u32[]{:S(2)}, u32[]{:S(2)}) async-start(f32[4,16,12]{2,0,1:T(4,128)} %copy.61), calls=%async_computation.1 | async-start | bytes 65536 | tf_op jit(solution)/shard_map/all_to_all | solution.py:169
  61.0 5.8 %all-to-all-done.1 = f32[4,16,12]{2,0,1:T(4,128)S(1)} async-done(((f32[4,16,12]{2,0,1:T(4,128)}), f32[4,16,12]{2,0,1:T(4,128)S(1)}, u32[]{:S(2)}, u32[]{:S(2)}) %all-to-all-start.1) | async-done | bytes 3104 | tf_op jit(solution)/shard_map/all_to_all | solution.py:169
  71.0 10.0 %all_to_all.15 = f32[4,16,12]{2,0,1:T(4,128)S(1)} all-to-all(f32[4,16,12]{2,0,1:T(4,128)S(1)} %copy.67), channel_id=1, replica_groups=mesh['space'=16,'ray'=2] {'space'}, dimensions={1} | all-to-all | bytes 6144 | tf_op jit(solution)/shard_map/all_to_all | solution.py:194
  81.1 2.4 %multiply_reduce_fusion = (f32[192,32]{1,0:T(8,128)}, bf16[192,32,3]{1,0,2:T(8,128)(2,1)}) fusion(f32[192,3]{0,1:T(4,128)S(1)} %bitcast.122, f32[192,32,4]{1,0,2:T(8,128)} %reshape.235, f32[192,32]{1,0:T(8,128)S(1)} %copy.60), kind=kLoop, calls=%fused_computation.24 | loop fusion | flops 178176 | bytes 162048 | tf_op jit(solution)/shard_map/reduce_sum | solution.py:71
  83.5 1.0 copy.69
  84.9 1.1 concatenate.32
  86.0 4.8 %convert_reduce_fusion = (f32[256]{0:T(256)S(1)}, bf16[6144,256]{1,0:T(8,128)(2,1)S(1)}) fusion(f32[6144,256]{1,0:T(8,128)} %get-tuple-element.28, bf16[1,4,256]{2,1,0:T(4,128)(2,1)S(1)} %copy-done.6, bf16[6144,3]{0,1:T(4,128)(2,1)S(1)} %concatenate.32, bf16[6144,1]{0,1:T(2,128)(2,1)S(1)} %concatenate.31), kind=kOutput, calls=%fused_computation.7 | convolution fusion | flops 29982464 | bytes 9489408 | tf_op jit(solution)/shard_map/dot_general | solution.py:86
  90.8 1.7 %fusion.44 = f32[256,256]{1,0:T(8,128)} fusion(bf16[6144,256]{1,0:T(8,128)(2,1)S(1)} %copy-done.13, bf16[6144,256]{1,0:T(8,128)(2,1)S(1)} %get-tuple-element.32), kind=kOutput, calls=%fused_computation.97 | convolution fusion | flops 805306368 | bytes 6553600 | tf_op jit(solution)/shard_map/dot_general | solution.py:88
  92.6 4.8 %convert_reduce_fusion.1 = (f32[256]{0:T(256)S(1)}, bf16[6144,256]{1,0:T(8,128)(2,1)S(1)}) fusion(f32[6144,256]{1,0:T(8,128)} %get-tuple-element.26, bf16[6144,256]{1,0:T(8,128)(2,1)S(1)} %get-tuple-element.32, bf16[1,256,256]{2,1,0:T(8,128)(2,1)S(1)} %copy-done), kind=kOutput, calls=%fused_computation.8 | convolution fusion | flops 822607616 | bytes 12715008 | tf_op jit(solution)/shard_map/dot_general | solution.py:92
  97.4 1.7 %fusion.2 = f32[256,256]{1,0:T(8,128)} fusion(bf16[6144,256]{1,0:T(8,128)(2,1)S(1)} %get-tuple-element.30, bf16[6144,128]{1,0:T(8,128)(2,1)S(1)} %copy-done.4, bf16[6144,128]{1,0:T(8,128)(2,1)S(1)} %copy-done.2), kind=kOutput, calls=%fused_computation.17 | convolution fusion | flops 811597824 | bytes 6553600 | tf_op jit(solution)/shard_map/dot_general | solution.py:96
  99.8 3.1 %all-reduce = (f32[1,4,256]{2,1,0:T(4,128)}, f32[1,256]{1,0:T(1,128)}, f32[1,256]{1,0:T(1,128)}, f32[1,4]{1,0:T(1,128)}) all-reduce(f32[1,4,256]{2,1,0:T(4,128)S(1)} %convolution_bitcast_fusion, f32[1,256]{1,0:T(1,128)S(1)} %bitcast.130, f32[1,256]{1,0:T(1,128)S(1)} %bitcast.129, ...), channel_id=1, replica_groups=mesh['space'=16,'ray'=2] {'ray'}, use_global_device_ids=true, to_apply=%region_12.13 | all-reduce | flops 1540 | bytes 12320 | tf_op jit(solution)/shard_map/psum | solution.py:198
  102.9 11.7 %all-reduce.4.cloned.1.call-done = (f32[256,256]{1,0:T(8,128)}, f32[256,256]{1,0:T(8,128)}) async-done(((f32[256,256]{1,0:T(8,128)}, f32[256,256]{1,0:T(8,128)}), (f32[256,256]{1,0:T(8,128)}, f32[256,256]{1,0:T(8,128)})) %all-reduce.4.cloned.1.call-update) | async-done | bytes 524304 | tf_op jit(solution)/shard_map/psum | solution.py:199
  114.6 1.7 %dynamic-slice_bitcast_fusion = (f32[1,128,256]{2,1,0:T(8,128)}, f32[1,128,256]{2,1,0:T(8,128)}) fusion(f32[256,256]{1,0:T(8,128)} %get-tuple-element.14, s32[]{:T(128)S(6)} %select_n.14, f32[256,256]{1,0:T(8,128)} %get-tuple-element.13), kind=kLoop, calls=%fused_computation.29 | loop fusion | bytes 524292 | tf_op jit(solution)/shard_map/broadcast_in_dim | solution.py:208
  (92 shorter events, 12.6 us)
Async XLA Ops:
  7.2 39.2 %copy-start = (bf16[1,256,256]{2,1,0:T(8,128)(2,1)S(1)}, bf16[1,256,256]{2,1,0:T(8,128)(2,1)}, u32[]{:S(2)}) copy-start(bf16[1,256,256]{2,1,0:T(8,128)(2,1)} %param.20) | copy-start | bytes 393220
  8.3 33.3 %copy-start.10 = (f32[1,256]{1,0:T(1,128)S(1)}, f32[1,256]{1,0:T(1,128)}, u32[]{:S(2)}) copy-start(f32[1,256]{1,0:T(1,128)} %param.19) | copy-start | bytes 3076
  8.5 19.0 %copy-start.9 = (s32[128]{0:T(128)}, s32[128]{0:T(128)S(1)}, u32[]{:S(2)}) copy-start(s32[128]{0:T(128)S(1)} %multiply_add_fusion.1) | copy-start | bytes 1540
  11.4 16.1 %all-to-all-start = ((f32[16,12,128]{2,1,0:T(8,128)}), f32[16,12,128]{2,1,0:T(8,128)S(1)}, u32[]{:S(2)}, u32[]{:S(2)}) async-start(f32[16,12,128]{2,1,0:T(8,128)} %fusion.11), calls=%async_computation | async-start | bytes 262144 | tf_op jit(solution)/shard_map/all_to_all | solution.py:150
  41.6 4.8 %copy-start.1 = (bf16[6144,128]{1,0:T(8,128)(2,1)}, bf16[6144,128]{1,0:T(8,128)(2,1)S(1)}, u32[]{:S(2)}) copy-start(bf16[6144,128]{1,0:T(8,128)(2,1)S(1)} %get-tuple-element.18) | copy-start | bytes 4718596
  41.6 4.8 %copy-start.3 = (bf16[6144,128]{1,0:T(8,128)(2,1)}, bf16[6144,128]{1,0:T(8,128)(2,1)S(1)}, u32[]{:S(2)}) copy-start(bf16[6144,128]{1,0:T(8,128)(2,1)S(1)} %get-tuple-element.19) | copy-start | bytes 4718596
  41.7 4.8 %copy-start.11 = (f32[1,256]{1,0:T(1,128)S(1)}, f32[1,256]{1,0:T(1,128)}, u32[]{:S(2)}) copy-start(f32[1,256]{1,0:T(1,128)} %param.21) | copy-start | bytes 3076
  46.4 4.4 %copy-start.12 = (bf16[6144,256]{1,0:T(8,128)(2,1)}, bf16[6144,256]{1,0:T(8,128)(2,1)S(1)}, u32[]{:S(2)}) copy-start(bf16[6144,256]{1,0:T(8,128)(2,1)S(1)} %get-tuple-element.25) | copy-start | bytes 9437188
  46.4 4.4 %copy-start.6 = (bf16[1,4,256]{2,1,0:T(4,128)(2,1)S(1)}, bf16[1,4,256]{2,1,0:T(4,128)(2,1)}, u32[]{:S(2)}) copy-start(bf16[1,4,256]{2,1,0:T(4,128)(2,1)} %param.22) | copy-start | bytes 6148
  46.4 4.4 %copy-start.7 = (f32[1,4]{1,0:T(1,128)S(1)}, f32[1,4]{1,0:T(1,128)}, u32[]{:S(2)}) copy-start(f32[1,4]{1,0:T(1,128)} %param.23) | copy-start | bytes 52
  50.8 8.7 %copy-start.8 = (f32[3,16]{1,0:T(4,128)S(1)}, f32[3,16]{1,0:T(4,128)}, u32[]{:S(2)}) copy-start(f32[3,16]{1,0:T(4,128)} %param.16) | copy-start | bytes 580
  50.8 18.8 %copy-start.5 = (s32[16,8]{0,1:T(8,128)S(1)}, s32[16,8]{0,1:T(8,128)}, u32[]{:S(2)}) copy-start(s32[16,8]{0,1:T(8,128)} %param.15) | copy-start | bytes 1540
  56.0 10.9 %all-to-all-start.1 = ((f32[4,16,12]{2,0,1:T(4,128)}), f32[4,16,12]{2,0,1:T(4,128)S(1)}, u32[]{:S(2)}, u32[]{:S(2)}) async-start(f32[4,16,12]{2,0,1:T(4,128)} %copy.61), calls=%async_computation.1 | async-start | bytes 65536 | tf_op jit(solution)/shard_map/all_to_all | solution.py:169
  59.5 55.1 %all-reduce.4.cloned.1.call-start = ((), (), s32[]{:S(2)}) async-start(), calls=%async_computation.3 | async-start | bytes 1048576 | tf_op jit(solution)/shard_map/psum | solution.py:199
  86.0 4.9 %copy-start.13 = (bf16[6144,256]{1,0:T(8,128)(2,1)S(1)}, bf16[6144,256]{1,0:T(8,128)(2,1)}, u32[]{:S(2)}) copy-start(bf16[6144,256]{1,0:T(8,128)(2,1)} %copy-done.12) | copy-start | bytes 9437188
  92.6 4.8 %copy-start.2 = (bf16[6144,128]{1,0:T(8,128)(2,1)S(1)}, bf16[6144,128]{1,0:T(8,128)(2,1)}, u32[]{:S(2)}) copy-start(bf16[6144,128]{1,0:T(8,128)(2,1)} %copy-done.1) | copy-start | bytes 4718596
  92.6 4.8 %copy-start.4 = (bf16[6144,128]{1,0:T(8,128)(2,1)S(1)}, bf16[6144,128]{1,0:T(8,128)(2,1)}, u32[]{:S(2)}) copy-start(bf16[6144,128]{1,0:T(8,128)(2,1)} %copy-done.3) | copy-start | bytes 4718596
Sparse Core Ops, SparseCore 0:
  99.3 15.2 all-reduce.3

commit v2 on v1

--- a/solution.py
+++ b/solution.py
@@ -195,14 +195,41 @@
     received = received.reshape(4, slot_count).T
     totals = backward(samples, params, saved, received[:, :3], received[:, 3])
     grad_first, grad_second, grad_head, bias_first, bias_second, bias_head = totals
-    small_sums = lax.psum((grad_head, bias_first, bias_second, bias_head), "ray")
-    whole_first, whole_second = lax.psum((grad_first, grad_second), "ray")
     replicas = lax.axis_size("ray")
-    position = lax.axis_index("ray")
-    rows_first = whole_first.shape[0] // replicas
-    rows_second = whole_second.shape[0] // replicas
-    part_first = lax.dynamic_slice_in_dim(whole_first, position * rows_first, rows_first, 0)
-    part_second = lax.dynamic_slice_in_dim(whole_second, position * rows_second, rows_second, 0)
+    small = jnp.concatenate(
+        [grad_head.reshape(-1), bias_first, bias_second, bias_head], axis=0
+    )
+    if replicas & (replicas - 1) == 0:
+        position = lax.axis_index("ray")
+        part_first, part_second = grad_first, grad_second
+        distance = replicas // 2
+        while distance >= 1:
+            pairs = [(i, i ^ distance) for i in range(replicas)]
+            half = part_first.shape[0] // 2
+            upper = (position // distance) % 2
+            keep_first = lax.dynamic_slice_in_dim(part_first, upper * half, half, 0)
+            send_first = lax.dynamic_slice_in_dim(part_first, (1 - upper) * half, half, 0)
+            keep_second = lax.dynamic_slice_in_dim(part_second, upper * half, half, 0)
+            send_second = lax.dynamic_slice_in_dim(part_second, (1 - upper) * half, half, 0)
+            got_first, got_second, got_small = lax.ppermute(
+                (send_first, send_second, small), "ray", pairs
+            )
+            part_first = keep_first + got_first
+            part_second = keep_second + got_second
+            small = small + got_small
+            distance //= 2
+    else:
+        part_first = lax.psum_scatter(grad_first, "ray", scatter_dimension=0, tiled=True)
+        part_second = lax.psum_scatter(grad_second, "ray", scatter_dimension=0, tiled=True)
+        small = lax.psum(small, "ray")
+    heads = grad_head.size
+    hidden = bias_first.shape[0]
+    small_sums = (
+        small[:heads].reshape(grad_head.shape),
+        small[heads : heads + hidden],
+        small[heads + hidden : heads + 2 * hidden],
+        small[heads + 2 * hidden :],
+    )
     return (
         part_first[None],
         part_second[None],

time: 124 us -> 97.9 us (0.79)
  between operations: 14.4 us -> 1.16 us
  blocking collectives: 13 us -> 0 us
  waiting for transfers between devices: 24.5 us -> 20 us
  starting transfers between devices: 11.9 us -> 16.2 us
  matrix products: 26.2 us -> 23.1 us
  local copies, waits for them, and re-layouts: 15.7 us -> 17.7 us
  other arithmetic: 17.4 us -> 18.7 us
    psum x1 -> x0, waiting for transfers between devices: 11.7 us -> none  [per_device(): whole_first, whole_second = lax.psum((grad_first, grad_second), 'ray')]
    all_to_all x1 -> x0, blocking collectives: 9.98 us -> none  [per_device(): lax.all_to_all(sendback, 'space', split_axis=1, concat_axis=1, tiled=True)]
    all_to_all x0 -> x1, waiting for transfers between devices: none -> 7.17 us  [per_device(): lax.all_to_all(sendback, 'space', split_axis=1, concat_axis=1, tiled=True)]
    all_to_all x0 -> x1, starting transfers between devices: none -> 3.68 us  [per_device(): lax.all_to_all(sendback, 'space', split_axis=1, concat_axis=1, tiled=True)]
    psum x1 -> x0, blocking collectives: 3.05 us -> none  [per_device(): lax.psum((grad_head, bias_first, bias_second, bias_head), 'ray')]
    dot_general x1, matrix products: 4.8 us -> 2.8 us  [backward(): lax.dot_general(delta_second, second_weight, (((1,), (1,)), ((), ())), pr...]
    broadcast_in_dim x0 -> x2, other arithmetic: none -> 1.34 us  [the longest x1 0.67 us: per_device(): part_first[None]]
  transfers between devices with their start and end apart: 3 -> 6, of which waited for: 3 -> 3; matrix products, arithmetic and copies ran while one was open for 2% -> 6% of each run, Pallas kernels for 0% -> 0%
where the time goes in v2:
time: 97.9 us; the launch traced here: 97 us
  matrix products  23.1 us (24%)
  waiting for transfers between devices  20 us (20%)
  other arithmetic  18.7 us (19%)
  local copies, waits for them, and re-layouts  17.7 us (18%)
  starting transfers between devices  16.2 us (17%)
  between operations  1.16 us (1%)
    another operation x2, other arithmetic  12.7 us
    all_to_all x1, starting transfers between devices, per_device(): lax.all_to_all(outgoing, 'space', split_axis=0, concat_axis=0, tiled=True)  8.31 us
    all_to_all x1, waiting for transfers between devices, per_device(): lax.all_to_all(sendback, 'space', split_axis=1, concat_axis=1, tiled=True)  7.17 us
    all_to_all x1, waiting for transfers between devices, per_device(): lax.all_to_all(outgoing, 'space', split_axis=0, concat_axis=0, tiled=True)  7 us
    all_to_all x1, waiting for transfers between devices, per_device(): lax.all_to_all(partials, 'space', split_axis=1, concat_axis=1, tiled=True)  5.86 us
    dot_general x1, matrix products, backward(): jnp.dot(grad_raw, head_weight, preferred_element_type=jnp.float32)  5.17 us
    dot_general x1, matrix products, network(): jnp.dot(encoded, first_weight, preferred_element_type=jnp.float32)  4.73 us
    dot_general x1, matrix products, network(): jnp.dot(act_first, second_weight, preferred_element_type=jnp.float32)  4.38 us
  transfers between devices with their start and end apart: 6, of which 3 were waited for; matrix products, arithmetic and copies ran while one was open for 6% of the time, Pallas kernels for 0%

profile of v2, /device:TPU:0, one launch (start us, length us, event | category | flops | bytes accessed | tf_op | source)
XLA Modules:
  0.0 97.0 jit_solution(459410366137176465)
XLA Ops:
  2.0 0.9 reshape.234
  4.0 0.9 fusion.11
  4.9 8.3 %all-to-all-start = ((f32[16,12,128]{2,1,0:T(8,128)}), f32[16,12,128]{2,1,0:T(8,128)S(1)}, u32[]{:S(2)}, u32[]{:S(2)}) async-start(f32[16,12,128]{2,1,0:T(8,128)} %fusion.11), calls=%async_computation | async-start | bytes 262144 | tf_op jit(solution)/shard_map/all_to_all | solution.py:150
  14.0 7.0 %all-to-all-done = f32[16,12,128]{2,1,0:T(8,128)S(1)} async-done(((f32[16,12,128]{2,1,0:T(8,128)}), f32[16,12,128]{2,1,0:T(8,128)S(1)}, u32[]{:S(2)}, u32[]{:S(2)}) %all-to-all-start) | async-done | bytes 98336 | tf_op jit(solution)/shard_map/all_to_all | solution.py:150
  21.2 0.9 slice_reduce_fusion.2
  22.4 12.6 %sine_convert_fusion = (bf16[6144,128]{1,0:T(8,128)(2,1)S(1)}, bf16[6144,128]{1,0:T(8,128)(2,1)S(1)}) fusion(f32[128]{0:T(128)S(1)} %get-tuple-element.19, f32[6144]{0:T(1024)S(1)} %mul.242, f32[128]{0:T(128)S(1)} %get-tuple-element.20, f32[6144]{0:T(1024)S(1)} %mul.237, f32[128]{0:T(128)S(1)} %get-tuple-element.18, f32[6144]{0:T(1024)S(1)} %mul.232), kind=kLoop, calls=%fused_computation.15 | loop fusion | flops 6291456 | bytes 3220992 | tf_op jit(solution)/shard_map/convert.4
  35.1 4.7 %multiply_convert_fusion.1 = (bf16[6144,256]{1,0:T(8,128)(2,1)S(1)}, f32[6144,256]{1,0:T(8,128)}) fusion(f32[256]{0:T(256)S(1)} %bitcast.134, bf16[1,256,256]{2,1,0:T(8,128)(2,1)} %param.18, bf16[6144,128]{1,0:T(8,128)(2,1)S(1)} %get-tuple-element.13, bf16[6144,128]{1,0:T(8,128)(2,1)S(1)} %get-tuple-element.12), kind=kOutput, calls=%fused_computation.11 | convolution fusion | flops 821035008 | bytes 12715008 | tf_op jit(solution)/shard_map/dot_general | solution.py:32
  39.9 4.4 %multiply_convert_fusion = (bf16[6144,256]{1,0:T(8,128)(2,1)S(1)}, f32[6144,256]{1,0:T(8,128)}) fusion(f32[256]{0:T(256)S(1)} %bitcast.135, bf16[6144,256]{1,0:T(8,128)(2,1)S(1)} %get-tuple-element.21, bf16[1,256,256]{2,1,0:T(8,128)(2,1)S(1)} %copy-done), kind=kOutput, calls=%fused_computation.9 | convolution fusion | flops 814743552 | bytes 12715008 | tf_op jit(solution)/shard_map/dot_general | solution.py:34
  44.3 0.9 convolution_add_fusion.2
  45.2 0.9 reshape.238
  46.2 0.9 slice.77
  47.5 1.2 %multiply_reduce_fusion.1 = f32[192,3]{0,1:T(4,128)S(1)} fusion(f32[192,32]{1,0:T(8,128)S(1)} %copy.60, f32[192,32,4]{1,0,2:T(8,128)} %reshape.238), kind=kLoop, calls=%fused_computation.25 | loop fusion | flops 91584 | bytes 100608 | tf_op jit(solution)/shard_map/reduce_sum | solution.py:50
  49.4 3.5 %all-to-all-start.1 = ((f32[4,16,12]{2,0,1:T(4,128)}), f32[4,16,12]{2,0,1:T(4,128)S(1)}, u32[]{:S(2)}, u32[]{:S(2)}) async-start(f32[4,16,12]{2,0,1:T(4,128)} %copy.61), calls=%async_computation.1 | async-start | bytes 65536 | tf_op jit(solution)/shard_map/all_to_all | solution.py:169
  54.5 5.9 %all-to-all-done.1 = f32[4,16,12]{2,0,1:T(4,128)S(1)} async-done(((f32[4,16,12]{2,0,1:T(4,128)}), f32[4,16,12]{2,0,1:T(4,128)S(1)}, u32[]{:S(2)}, u32[]{:S(2)}) %all-to-all-start.1) | async-done | bytes 3104 | tf_op jit(solution)/shard_map/all_to_all | solution.py:169
  63.5 0.9 fusion.9
  65.1 3.7 %all-to-all-start.2 = ((f32[4,16,12]{2,0,1:T(4,128)}), f32[4,16,12]{2,0,1:T(4,128)S(1)}, u32[]{:S(2)}, u32[]{:S(2)}) async-start(f32[4,16,12]{2,0,1:T(4,128)} %copy.67), calls=%async_computation.2 | async-start | bytes 65536 | tf_op jit(solution)/shard_map/all_to_all | solution.py:194
  68.8 7.2 %all-to-all-done.2 = f32[4,16,12]{2,0,1:T(4,128)S(1)} async-done(((f32[4,16,12]{2,0,1:T(4,128)}), f32[4,16,12]{2,0,1:T(4,128)S(1)}, u32[]{:S(2)}, u32[]{:S(2)}) %all-to-all-start.2) | async-done | bytes 3104 | tf_op jit(solution)/shard_map/all_to_all | solution.py:194
  77.4 2.4 %multiply_reduce_fusion = (f32[192,32]{1,0:T(8,128)}, bf16[192,32,3]{1,0,2:T(8,128)(2,1)}) fusion(f32[192,3]{0,1:T(4,128)S(1)} %bitcast.126, f32[192,32,4]{1,0,2:T(8,128)} %reshape.238, f32[192,32]{1,0:T(8,128)S(1)} %copy.60), kind=kLoop, calls=%fused_computation.24 | loop fusion | flops 178176 | bytes 162048 | tf_op jit(solution)/shard_map/reduce_sum | solution.py:71
  79.9 1.0 copy.69
  81.2 1.1 %concatenate.35 = bf16[6144,3]{0,1:T(4,128)(2,1)S(1)} reshape(bf16[192,32,3]{1,0,2:T(8,128)(2,1)} %get-tuple-element.10) | data formatting | bytes 73728 | tf_op jit(solution)/shard_map/concatenate | solution.py:78
  83.0 5.2 %convert_reduce_fusion = (f32[256]{0:T(256)S(1)}, bf16[6144,256]{1,0:T(8,128)(2,1)S(1)}) fusion(f32[6144,256]{1,0:T(8,128)} %get-tuple-element.24, bf16[1,4,256]{2,1,0:T(4,128)(2,1)S(1)} %copy-done.6, bf16[6144,3]{0,1:T(4,128)(2,1)S(1)} %concatenate.35, bf16[6144,1]{0,1:T(2,128)(2,1)S(1)} %concatenate.34), kind=kOutput, calls=%fused_computation.7 | convolution fusion | flops 29982464 | bytes 9489408 | tf_op jit(solution)/shard_map/dot_general | solution.py:86
  88.2 1.0 %fusion.46 = f32[256,256]{1,0:T(8,128)S(1)} fusion(bf16[6144,256]{1,0:T(8,128)(2,1)S(1)} %copy-done.13, bf16[6144,256]{1,0:T(8,128)(2,1)S(1)} %get-tuple-element.26), kind=kOutput, calls=%fused_computation.103 | convolution fusion | flops 805306368 | bytes 6553600 | tf_op jit(solution)/shard_map/dot_general | solution.py:88
  89.3 2.8 %convert_reduce_fusion.1 = (f32[256]{0:T(256)S(1)}, bf16[6144,256]{1,0:T(8,128)(2,1)S(1)}) fusion(f32[6144,256]{1,0:T(8,128)S(1)} %bitcast.137, bf16[6144,256]{1,0:T(8,128)(2,1)S(1)} %get-tuple-element.26, bf16[1,256,256]{2,1,0:T(8,128)(2,1)S(1)} %copy-done), kind=kOutput, calls=%fused_computation.8 | convolution fusion | flops 822607616 | bytes 12715008 | tf_op jit(solution)/shard_map/dot_general | solution.py:92
  92.8 1.0 %fusion.2 = f32[256,256]{1,0:T(8,128)S(1)} fusion(bf16[6144,256]{1,0:T(8,128)(2,1)S(1)} %get-tuple-element.28, bf16[6144,128]{1,0:T(8,128)(2,1)S(1)} %copy-done.4, bf16[6144,128]{1,0:T(8,128)(2,1)S(1)} %copy-done.2), kind=kOutput, calls=%fused_computation.17 | convolution fusion | flops 811597824 | bytes 6553600 | tf_op jit(solution)/shard_map/dot_general | solution.py:96
  (110 shorter events, 16.6 us)
Async XLA Ops:
  0.6 39.2 %copy-start = (bf16[1,256,256]{2,1,0:T(8,128)(2,1)S(1)}, bf16[1,256,256]{2,1,0:T(8,128)(2,1)}, u32[]{:S(2)}) copy-start(bf16[1,256,256]{2,1,0:T(8,128)(2,1)} %param.20) | copy-start | bytes 393220
  1.8 33.3 %copy-start.10 = (f32[1,256]{1,0:T(1,128)S(1)}, f32[1,256]{1,0:T(1,128)}, u32[]{:S(2)}) copy-start(f32[1,256]{1,0:T(1,128)} %param.19) | copy-start | bytes 3076
  2.0 19.0 %copy-start.9 = (s32[128]{0:T(128)}, s32[128]{0:T(128)S(1)}, u32[]{:S(2)}) copy-start(s32[128]{0:T(128)S(1)} %multiply_add_fusion.1) | copy-start | bytes 1540
  4.9 16.1 %all-to-all-start = ((f32[16,12,128]{2,1,0:T(8,128)}), f32[16,12,128]{2,1,0:T(8,128)S(1)}, u32[]{:S(2)}, u32[]{:S(2)}) async-start(f32[16,12,128]{2,1,0:T(8,128)} %fusion.11), calls=%async_computation | async-start | bytes 262144 | tf_op jit(solution)/shard_map/all_to_all | solution.py:150
  35.1 4.8 %copy-start.1 = (bf16[6144,128]{1,0:T(8,128)(2,1)}, bf16[6144,128]{1,0:T(8,128)(2,1)S(1)}, u32[]{:S(2)}) copy-start(bf16[6144,128]{1,0:T(8,128)(2,1)S(1)} %get-tuple-element.12) | copy-start | bytes 4718596
  35.1 4.8 %copy-start.3 = (bf16[6144,128]{1,0:T(8,128)(2,1)}, bf16[6144,128]{1,0:T(8,128)(2,1)S(1)}, u32[]{:S(2)}) copy-start(bf16[6144,128]{1,0:T(8,128)(2,1)S(1)} %get-tuple-element.13) | copy-start | bytes 4718596
  35.1 4.8 %copy-start.11 = (f32[1,256]{1,0:T(1,128)S(1)}, f32[1,256]{1,0:T(1,128)}, u32[]{:S(2)}) copy-start(f32[1,256]{1,0:T(1,128)} %param.21) | copy-start | bytes 3076
  39.9 4.4 %copy-start.12 = (bf16[6144,256]{1,0:T(8,128)(2,1)}, bf16[6144,256]{1,0:T(8,128)(2,1)S(1)}, u32[]{:S(2)}) copy-start(bf16[6144,256]{1,0:T(8,128)(2,1)S(1)} %get-tuple-element.21) | copy-start | bytes 9437188
  39.9 4.4 %copy-start.6 = (bf16[1,4,256]{2,1,0:T(4,128)(2,1)S(1)}, bf16[1,4,256]{2,1,0:T(4,128)(2,1)}, u32[]{:S(2)}) copy-start(bf16[1,4,256]{2,1,0:T(4,128)(2,1)} %param.22) | copy-start | bytes 6148
  39.9 4.4 %copy-start.7 = (f32[1,4]{1,0:T(1,128)S(1)}, f32[1,4]{1,0:T(1,128)}, u32[]{:S(2)}) copy-start(f32[1,4]{1,0:T(1,128)} %param.23) | copy-start | bytes 52
  44.3 8.7 %copy-start.8 = (f32[3,16]{1,0:T(4,128)S(1)}, f32[3,16]{1,0:T(4,128)}, u32[]{:S(2)}) copy-start(f32[3,16]{1,0:T(4,128)} %param.16) | copy-start | bytes 580
  44.3 18.8 %copy-start.5 = (s32[16,8]{0,1:T(8,128)S(1)}, s32[16,8]{0,1:T(8,128)}, u32[]{:S(2)}) copy-start(s32[16,8]{0,1:T(8,128)} %param.15) | copy-start | bytes 1540
  49.4 10.9 %all-to-all-start.1 = ((f32[4,16,12]{2,0,1:T(4,128)}), f32[4,16,12]{2,0,1:T(4,128)S(1)}, u32[]{:S(2)}, u32[]{:S(2)}) async-start(f32[4,16,12]{2,0,1:T(4,128)} %copy.61), calls=%async_computation.1 | async-start | bytes 65536 | tf_op jit(solution)/shard_map/all_to_all | solution.py:169
  65.1 10.9 %all-to-all-start.2 = ((f32[4,16,12]{2,0,1:T(4,128)}), f32[4,16,12]{2,0,1:T(4,128)S(1)}, u32[]{:S(2)}, u32[]{:S(2)}) async-start(f32[4,16,12]{2,0,1:T(4,128)} %copy.67), calls=%async_computation.2 | async-start | bytes 65536 | tf_op jit(solution)/shard_map/all_to_all | solution.py:194
  82.3 7.0 %slice-start = ((s8[6291456]{0:T(1024)(128)(4,1)}), s8[4194304]{0:T(1024)(128)(4,1)S(1)}, s32[]{:S(2)}) async-start(s8[6291456]{0:T(1024)(128)(4,1)} %bitcast.136), calls=%async_computation.3 | async-start | bytes 8388608
  83.0 5.2 %copy-start.13 = (bf16[6144,256]{1,0:T(8,128)(2,1)S(1)}, bf16[6144,256]{1,0:T(8,128)(2,1)}, u32[]{:S(2)}) copy-start(bf16[6144,256]{1,0:T(8,128)(2,1)} %copy-done.12) | copy-start | bytes 9437188
  83.0 6.2 %slice-start.1 = ((s8[6291456]{0:T(1024)(128)(4,1)}), s8[2097152]{0:T(1024)(128)(4,1)S(1)}, s32[]{:S(2)}) async-start(s8[6291456]{0:T(1024)(128)(4,1)} %bitcast.136), calls=%async_computation.4 | async-start | bytes 4194304
  89.3 3.5 %copy-start.2 = (bf16[6144,128]{1,0:T(8,128)(2,1)S(1)}, bf16[6144,128]{1,0:T(8,128)(2,1)}, u32[]{:S(2)}) copy-start(bf16[6144,128]{1,0:T(8,128)(2,1)} %copy-done.1) | copy-start | bytes 4718596
  89.3 3.5 %copy-start.4 = (bf16[6144,128]{1,0:T(8,128)(2,1)S(1)}, bf16[6144,128]{1,0:T(8,128)(2,1)}, u32[]{:S(2)}) copy-start(bf16[6144,128]{1,0:T(8,128)(2,1)} %copy-done.3) | copy-start | bytes 4718596
  92.1 1.8 %collective-permute-start.2 = (f32[1540]{0:T(1024)S(1)}, f32[1540]{0:T(1024)S(1)}, u32[]{:S(2)}, u32[]{:S(2)}) collective-permute-start(f32[1540]{0:T(1024)S(1)} %pad_maximum_fusion.6), channel_id=1, source_target_pairs={{0,1},{1,0},{2,3},{3,2},{4,5},{5,4},{6,7},{7,6},{8,9},{9,8},{10,11... | collective-permute-start | bytes 18488 | tf_op jit(solution)/shard_map/ppermute | solution.py:214
  92.2 3.4 %collective-permute-start.1 = (f32[128,256]{1,0:T(8,128)S(1)}, f32[128,256]{1,0:T(8,128)S(1)}, u32[]{:S(2)}, u32[]{:S(2)}) collective-permute-start(f32[128,256]{1,0:T(8,128)S(1)} %constant_dynamic-slice_fusion.1), channel_id=1, source_target_pairs={{0,1},{1,0},{2,3},{3,2},{4,5},{5,4},{6,7},{7,6},{8,9},{9,8},{10,11... | collective-permute-start | bytes 393224 | tf_op jit(solution)/shard_map/ppermute | solution.py:214
  93.9 2.5 %collective-permute-start = (f32[128,256]{1,0:T(8,128)S(1)}, f32[128,256]{1,0:T(8,128)S(1)}, u32[]{:S(2)}, u32[]{:S(2)}) collective-permute-start(f32[128,256]{1,0:T(8,128)S(1)} %constant_dynamic-slice_fusion), channel_id=1, source_target_pairs={{0,1},{1,0},{2,3},{3,2},{4,5},{5,4},{6,7},{7,6},{8,9},{9,8},{10,11... | collective-permute-start | bytes 393224 | tf_op jit(solution)/shard_map/ppermute | solution.py:214

commit v3 on v2

--- a/solution.py
+++ b/solution.py
@@ -139,6 +139,17 @@
     seg_pos = jnp.transpose(positions.reshape(3, total, SEG_LEN), (1, 0, 2))
     seg_gap = spacing.reshape(total, 1, SEG_LEN)
     segments = jnp.concatenate([seg_pos, seg_gap], axis=1).reshape(total, 4 * SEG_LEN)
+    place = owner * slot_count + lax.axis_index("space") * capacity + within
+    ray_place = jnp.broadcast_to(
+        place.reshape(ray_count, 1, SEGS), (ray_count, SEGS, SEGS)
+    ).astype(jnp.float32)
+    ray_rank = jnp.broadcast_to(
+        depth_rank.reshape(ray_count, 1, SEGS), (ray_count, SEGS, SEGS)
+    ).astype(jnp.float32)
+    ray_pixel = jnp.broadcast_to(pixel_grad.T[:, None, :], (ray_count, SEGS, 3))
+    own_rank = depth_rank.reshape(ray_count, SEGS, 1).astype(jnp.float32)
+    extra = jnp.concatenate([ray_place, ray_rank, ray_pixel, own_rank], axis=2)
+    segments = jnp.concatenate([segments, extra.reshape(total, 2 * SEGS + 4)], axis=1)
     outgoing = lax.dot_general(
         dispatch,
         segments,
@@ -146,9 +157,11 @@
         precision=lax.Precision.HIGHEST,
         preferred_element_type=jnp.float32,
     )
-    outgoing = outgoing.reshape(groups, capacity, 4 * SEG_LEN)
+    outgoing = outgoing.reshape(groups, capacity, 4 * SEG_LEN + 2 * SEGS + 4)
     arrived = lax.all_to_all(outgoing, "space", split_axis=0, concat_axis=0, tiled=True)
-    samples = arrived.reshape(slot_count, 4, SEG_LEN)
+    arrived = arrived.reshape(slot_count, 4 * SEG_LEN + 2 * SEGS + 4)
+    samples = arrived[:, : 4 * SEG_LEN].reshape(slot_count, 4, SEG_LEN)
+    meta = arrived[:, 4 * SEG_LEN :]
     params = tuple(
         (
             item[0]
@@ -163,37 +176,41 @@
         )
     )
     seg_colour, seg_log, saved = network(samples, fourier, params)
-    partials = jnp.concatenate([seg_colour.T, seg_log[None, :]], axis=0).reshape(
-        4, groups, capacity
-    )
-    returned = lax.all_to_all(partials, "space", split_axis=1, concat_axis=1, tiled=True).reshape(
-        4, slot_count
-    )
-    mine = lax.dot_general(
-        dispatch,
-        returned,
-        (((1,), (1,)), ((), ())),
+    partials = jnp.concatenate([seg_colour, seg_log[:, None]], axis=1)
+    spread = jnp.broadcast_to(partials[None], (groups, slot_count, 4))
+    table = lax.all_to_all(spread, "space", split_axis=0, concat_axis=0, tiled=True)
+    table = jnp.transpose(table.reshape(groups, slot_count, 4), (1, 0, 2)).reshape(
+        slot_count, groups * 4
+    )
+    index = meta[:, :SEGS].astype(jnp.int32)
+    column = index % slot_count
+    holder = index // slot_count
+    pick_column = (column[:, :, None] == jnp.arange(slot_count, dtype=jnp.int32)).astype(
+        jnp.float32
+    )
+    rows = lax.dot_general(
+        pick_column,
+        table,
+        (((2,), (0,)), ((), ())),
         precision=lax.Precision.HIGHEST,
         preferred_element_type=jnp.float32,
-    )
-    up_colour, up_log = composite(
-        mine[:, :3].reshape(ray_count, SEGS, 3),
-        mine[:, 3].reshape(ray_count, SEGS),
-        depth_rank,
-        pixel_grad.T,
-    )
-    upstream = jnp.concatenate([up_colour.reshape(total, 3), up_log.reshape(total, 1)], axis=1)
-    sendback = lax.dot_general(
-        upstream,
-        dispatch,
-        (((0,), (0,)), ((), ())),
-        precision=lax.Precision.HIGHEST,
-        preferred_element_type=jnp.float32,
-    )
-    sendback = sendback.reshape(4, groups, capacity)
-    received = lax.all_to_all(sendback, "space", split_axis=1, concat_axis=1, tiled=True)
-    received = received.reshape(4, slot_count).T
-    totals = backward(samples, params, saved, received[:, :3], received[:, 3])
+    ).reshape(slot_count, SEGS, groups, 4)
+    pick_holder = (holder[:, :, None] == jnp.arange(groups, dtype=jnp.int32)).astype(
+        jnp.float32
+    )
+    values = jnp.sum(rows * pick_holder[..., None], axis=2)
+    ranks = meta[:, SEGS : 2 * SEGS]
+    pixel = meta[:, 2 * SEGS : 2 * SEGS + 3]
+    own = meta[:, 2 * SEGS + 3 :]
+    logs = values[..., 3]
+    before = (ranks[:, None, :] < ranks[:, :, None]).astype(jnp.float32)
+    prefix = jnp.exp(jnp.sum(before * logs[:, None, :], axis=2))
+    shaded = prefix * jnp.sum(values[..., :3] * pixel[:, None, :], axis=2)
+    own_before = (ranks < own).astype(jnp.float32)
+    own_prefix = jnp.exp(jnp.sum(own_before * logs, axis=1))
+    up_colour = own_prefix[:, None] * pixel
+    up_log = jnp.sum((own < ranks).astype(jnp.float32) * shaded, axis=1)
+    totals = backward(samples, params, saved, up_colour, up_log)
     grad_first, grad_second, grad_head, bias_first, bias_second, bias_head = totals
     replicas = lax.axis_size("ray")
     small = jnp.concatenate(

time: 97.9 us -> 113 us (1.15)
  other arithmetic: 18.7 us -> 36 us
  waiting for transfers between devices: 20 us -> 8.47 us
  local copies, waits for them, and re-layouts: 17.7 us -> 28.3 us
  starting transfers between devices: 16.2 us -> 13.3 us
    all_to_all x2 -> x1, waiting for transfers between devices: 13 us -> 1.56 us  [per_device(): lax.all_to_all(spread, 'space', split_axis=0, concat_axis=0, tiled=True)]
    unnamed x36 -> x40, local copies, waits for them, and re-layouts: 1.02 us -> 5.3 us
    all_to_all x2 -> x1, starting transfers between devices: 7.18 us -> 4.32 us  [per_device(): lax.all_to_all(spread, 'space', split_axis=0, concat_axis=0, tiled=True)]
    reduce_sum x3, other arithmetic: 0.06 us -> 2.71 us  [the longest x1 1.98 us: per_device(): shaded = prefix * jnp.sum(values[..., :3] * pixel[:, None, :], axis=2)]
    convert_element_type x0 -> x3, other arithmetic: none -> 2.57 us  [the longest x1 1.18 us: per_device(): (holder[:, :, None] == jnp.arange(groups, dtype=jnp.int32)).astype(jnp.fl...]
    slice x2 -> x8, local copies, waits for them, and re-layouts: 0.08 us -> 2.26 us  [the longest x1 0.95 us: per_device(): ranks = meta[:, SEGS:2 * SEGS]]
    mul x4 -> x0, local copies, waits for them, and re-layouts: 1.67 us -> none  [the longest x2 1.5 us: composite(): up_colour = prefix[..., None] * pixel_rows[:, None, :]]
    dot_general x2 -> x1, matrix products: 1.7 us -> 3.32 us  [per_device(): lax.dot_general(pick_column, table, (((2,), (0,)), ((), ())), precision=l...]
  transfers between devices with their start and end apart: 6 -> 5, of which waited for: 3 -> 2; matrix products, arithmetic and copies ran while one was open for 6% -> 9% of each run, Pallas kernels for 0% -> 0%
where the time goes in v3:
time: 113 us; the launch traced here: 111 us
  other arithmetic  36 us (32%)
  local copies, waits for them, and re-layouts  28.3 us (25%)
  matrix products  23.7 us (21%)
  starting transfers between devices  13.3 us (12%)
  waiting for transfers between devices  8.47 us (7%)
  between operations  1.18 us (1%)
    another operation x2, other arithmetic  13.4 us
    all_to_all x1, starting transfers between devices, per_device(): lax.all_to_all(outgoing, 'space', split_axis=0, concat_axis=0, tiled=True)  8.31 us
    all_to_all x1, waiting for transfers between devices, per_device(): lax.all_to_all(outgoing, 'space', split_axis=0, concat_axis=0, tiled=True)  6.91 us
    unnamed x40, local copies, waits for them, and re-layouts  5.3 us
    dot_general x1, matrix products, backward(): jnp.dot(grad_raw, head_weight, preferred_element_type=jnp.float32)  5.18 us
    dot_general x1, matrix products, network(): jnp.dot(act_first, second_weight, preferred_element_type=jnp.float32)  4.4 us
    all_to_all x1, starting transfers between devices, per_device(): lax.all_to_all(spread, 'space', split_axis=0, concat_axis=0, tiled=True)  4.32 us
    dot_general x1, matrix products, network(): jnp.dot(encoded, first_weight, preferred_element_type=jnp.float32)  3.62 us
  transfers between devices with their start and end apart: 5, of which 2 were waited for; matrix products, arithmetic and copies ran while one was open for 9% of the time, Pallas kernels for 0%

profile of v3, /device:TPU:0, one launch (start us, length us, event | category | flops | bytes accessed | tf_op | source)
XLA Modules:
  0.0 111.0 jit_solution(6764933040528100580)
XLA Ops:
  8.2 8.3 %all-to-all-start = ((f32[16,1,1776]{2,1,0:T(1,128)}), f32[16,1,1776]{2,1,0:T(1,128)S(1)}, u32[]{:S(2)}, u32[]{:S(2)}) async-start(f32[16,1,1776]{2,1,0:T(1,128)} %reshape.227), calls=%async_computation | async-start | bytes 229376 | tf_op jit(solution)/shard_map/all_to_all | solution.py:161
  17.3 6.9 %all-to-all-done = f32[16,1,1776]{2,1,0:T(1,128)S(1)} async-done(((f32[16,1,1776]{2,1,0:T(1,128)}), f32[16,1,1776]{2,1,0:T(1,128)S(1)}, u32[]{:S(2)}, u32[]{:S(2)}) %all-to-all-start) | async-done | bytes 113696 | tf_op jit(solution)/shard_map/all_to_all | solution.py:161
  26.6 12.6 %sine_convert_fusion = (bf16[6144,128]{1,0:T(8,128)(2,1)S(1)}, bf16[6144,128]{1,0:T(8,128)(2,1)S(1)}) fusion(f32[128]{0:T(128)S(1)} %get-tuple-element.20, f32[6144]{0:T(1024)S(1)} %mul.252, f32[128]{0:T(128)S(1)} %get-tuple-element.21, f32[6144]{0:T(1024)S(1)} %mul.247, f32[128]{0:T(128)S(1)} %get-tuple-element.19, f32[6144]{0:T(1024)S(1)} %mul.242), kind=kLoop, calls=%fused_computation.16 | loop fusion | flops 6291456 | bytes 3220992 | tf_op jit(solution)/shard_map/convert.4
  39.3 3.6 %multiply_convert_fusion.1 = (bf16[6144,256]{1,0:T(8,128)(2,1)S(1)}, f32[6144,256]{1,0:T(8,128)}) fusion(f32[256]{0:T(256)S(1)} %bitcast.161, bf16[1,256,256]{2,1,0:T(8,128)(2,1)S(1)} %copy-done.10, bf16[6144,128]{1,0:T(8,128)(2,1)S(1)} %get-tuple-element.16, bf16[6144,128]{1,0:T(8,128)(2,1)S(1)} %get-tuple-element.15), kind=kOutput, calls=%fused_computation.11 | convolution fusion | flops 821035008 | bytes 12715008 | tf_op jit(solution)/shard_map/dot_general | solution.py:32
  43.0 4.4 %multiply_convert_fusion = (bf16[6144,256]{1,0:T(8,128)(2,1)S(1)}, f32[6144,256]{1,0:T(8,128)}) fusion(f32[256]{0:T(256)S(1)} %bitcast.162, bf16[6144,256]{1,0:T(8,128)(2,1)S(1)} %get-tuple-element.22, bf16[1,256,256]{2,1,0:T(8,128)(2,1)S(1)} %copy-done), kind=kOutput, calls=%fused_computation.9 | convolution fusion | flops 814743552 | bytes 12715008 | tf_op jit(solution)/shard_map/dot_general | solution.py:34
  47.4 1.6 %convolution_add_fusion.2 = f32[6144,4]{0,1:T(4,128)} fusion(bf16[6144,256]{1,0:T(8,128)(2,1)S(1)} %get-tuple-element.24, f32[4]{0:T(128)S(1)} %bitcast.157, bf16[1,4,256]{2,1,0:T(4,128)(2,1)S(1)} %copy-done.8), kind=kOutput, calls=%fused_computation.6 | convolution fusion | flops 12607488 | bytes 3246096 | tf_op jit(solution)/shard_map/dot_general | solution.py:37
  49.0 1.8 %reshape.221 = f32[192,32,4]{1,0,2:T(8,128)} reshape(f32[6144,4]{0,1:T(4,128)} %convolution_add_fusion.2) | data formatting | bytes 196608 | tf_op jit(solution)/shard_map/reshape | solution.py:42
  50.8 1.5 %slice.95 = f32[192,32,1]{1,0,2:T(8,128)} slice(f32[192,32,4]{1,0,2:T(8,128)} %reshape.221), slice={[0:192], [0:32], [0:1]} | slice | bytes 49152 | tf_op jit(solution)/shard_map/slice | solution.py:43
  53.3 1.4 %fusion.24 = f32[192,32]{0,1:T(8,128)} fusion(f32[192,32,1]{0,1,2:T(8,128)S(1)} %copy.138, f32[192,4,32]{0,2,1:T(8,128)} %bitcast.145), kind=kLoop, calls=%fused_computation.64 | loop fusion | flops 43008 | bytes 73728 | tf_op jit(solution)/shard_map/mul | solution.py:45
  55.5 1.4 %fusion.45 = f32[192,32]{0,1:T(8,128)} fusion(f32[192,32]{0,1:T(8,128)S(1)} %reduce_window_sum.31, f32[192,4,32]{0,2,1:T(8,128)} %bitcast.146, f32[192,32,1]{0,1,2:T(8,128)S(1)} %copy.138), kind=kLoop, calls=%fused_computation.104 | loop fusion | flops 61440 | bytes 98304 | tf_op jit(solution)/shard_map/mul | solution.py:50
  57.8 1.5 %copy.121 = f32[192,32]{1,0:T(8,128)} copy(f32[192,32]{0,1:T(8,128)} %fusion.45) | data formatting | bytes 49152 | tf_op jit(solution)/shard_map/mul | solution.py:50
  61.2 4.3 %all-to-all-start.1 = ((f32[16,192,4]{1,2,0:T(4,128)}), f32[16,192,4]{1,2,0:T(4,128)}, u32[]{:S(2)}, u32[]{:S(2)}) async-start(f32[16,192,4]{1,2,0:T(4,128)} %broadcast_in_dim.21), calls=%async_computation.1 | async-start | bytes 131072 | tf_op jit(solution)/shard_map/all_to_all | solution.py:181
  69.9 1.4 %copy.131 = pred[192,8]{0,1:T(8,128)(4,1)} copy(pred[192,8]{1,0:T(8,128)(4,1)} %broadcast_compare_fusion) | data formatting | bytes 3072 | tf_op jit(solution)/shard_map/lt | solution.py:212
  71.3 1.6 %all-to-all-done.1 = f32[16,192,4]{1,2,0:T(4,128)} async-done(((f32[16,192,4]{1,2,0:T(4,128)}), f32[16,192,4]{1,2,0:T(4,128)}, u32[]{:S(2)}, u32[]{:S(2)}) %all-to-all-start.1) | async-done | bytes 49184 | tf_op jit(solution)/shard_map/all_to_all | solution.py:181
  72.9 1.5 %reshape.222 = f32[192,64]{0,1:T(8,128)} reshape(f32[192,16,4]{0,2,1:T(4,128)} %bitcast.22) | data formatting | bytes 98304 | tf_op jit(solution)/shard_map/reshape | solution.py:182
  74.4 1.5 %dot_general.39 = f32[16,4,192]{2,1,0:T(4,128)} reshape(f32[64,192]{1,0:T(8,128)} %bitcast.153) | data formatting | bytes 98304 | tf_op jit(solution)/shard_map/dot_general | solution.py:191
  75.8 3.3 %multiply_reduce_fusion = f32[192,8,4]{1,2,0:T(4,128)S(1)} fusion(f32[192,8,16]{2,1,0:T(8,128)} %fusion.6, s32[192,8]{1,0:T(8,128)} %get-tuple-element.6, f32[16,4,192]{2,1,0:T(4,128)} %dot_general.39), kind=kOutput, calls=%fused_computation.14 | convolution fusion | flops 226977792 | bytes 178176 | tf_op jit(solution)/shard_map/dot_general | solution.py:191
  82.9 2.0 %fusion.7 = f32[192,8]{1,0:T(8,128)} fusion(f32[192,8,4]{1,2,0:T(4,128)} %copy-done.7, f32[192,3]{1,0:T(8,128)} %slice.103), kind=kLoop, calls=%fused_computation.26 | loop fusion | flops 7680 | bytes 26880 | tf_op jit(solution)/shard_map/reduce_sum | solution.py:208
  85.6 1.8 %multiply_reduce_fusion.1 = (f32[192,32]{1,0:T(8,128)}, bf16[192,32,3]{1,0,2:T(8,128)(2,1)S(1)}) fusion(f32[192,3]{0,1:T(4,128)S(1)} %broadcast_multiply_fusion, f32[192,32,4]{1,0,2:T(8,128)} %reshape.221, f32[192,32]{1,0:T(8,128)} %copy.121), kind=kLoop, calls=%fused_computation.32 | loop fusion | flops 178176 | bytes 162048 | tf_op jit(solution)/shard_map/reduce_sum | solution.py:71
  88.3 1.4 %multiply_reduce_fusion.3 = f32[192]{0:T(256)} fusion(f32[192,32]{0,1:T(8,128)S(1)} %copy.124, f32[192,32]{0,1:T(8,128)S(1)} %reduce_window_sum.31, f32[192,32]{0,1:T(8,128)} %fusion.24), kind=kLoop, calls=%fused_computation.84 | loop fusion | flops 30528 | bytes 74496 | tf_op jit(solution)/shard_map/reduce_sum | solution.py:73
  89.7 1.4 %bitcast_multiply_fusion = f32[192,32,1]{0,1,2:T(8,128)} fusion(f32[192,32]{0,1:T(8,128)S(1)} %copy.124, f32[192,32]{0,1:T(8,128)S(1)} %reduce_window_sum.31, f32[192,4,32]{0,2,1:T(8,128)} %bitcast.147, f32[192,32,1]{0,1,2:T(8,128)S(1)} %copy.138), kind=kLoop, calls=%fused_computation.69 | loop fusion | flops 67584 | bytes 122880 | tf_op jit(solution)/shard_map/mul | solution.py:72
  93.0 1.4 %reduce_window_sum.33 = f32[192,32,1]{0,1,2:T(8,128)} reduce-window(f32[192,32,1]{0,1,2:T(8,128)} %bitcast_multiply_fusion, f32[]{:T(128)} %constant.77.clone.1), window={size=1x32x1 pad=0_0x31_0x0_0}, to_apply=%region_8.9 | reduce-window | flops 190464 | bytes 49156 | tf_op jit(solution)/shard_map/jit(cumsum)/reduce_window_sum | solution.py:73
  97.1 5.2 %convert_reduce_fusion = (f32[256]{0:T(256)S(1)}, bf16[6144,256]{1,0:T(8,128)(2,1)S(1)}) fusion(f32[6144,256]{1,0:T(8,128)} %get-tuple-element.25, bf16[1,4,256]{2,1,0:T(4,128)(2,1)} %param.22, bf16[6144,3]{0,1:T(4,128)(2,1)S(1)} %concatenate.46, bf16[6144,1]{0,1:T(2,128)(2,1)S(1)} %concatenate.45), kind=kOutput, calls=%fused_computation.7 | convolution fusion | flops 29982464 | bytes 9489408 | tf_op jit(solution)/shard_map/dot_general | solution.py:86
  103.4 2.7 %convert_reduce_fusion.1 = (f32[256]{0:T(256)S(1)}, bf16[6144,256]{1,0:T(8,128)(2,1)S(1)}) fusion(f32[6144,256]{1,0:T(8,128)S(1)} %bitcast.164, bf16[6144,256]{1,0:T(8,128)(2,1)S(1)} %get-tuple-element.27, bf16[1,256,256]{2,1,0:T(8,128)(2,1)S(1)} %copy-done), kind=kOutput, calls=%fused_computation.8 | convolution fusion | flops 822607616 | bytes 12715008 | tf_op jit(solution)/shard_map/dot_general | solution.py:92
  (124 shorter events, 35.3 us)
Async XLA Ops:
  0.6 42.4 %copy-start = (bf16[1,256,256]{2,1,0:T(8,128)(2,1)S(1)}, bf16[1,256,256]{2,1,0:T(8,128)(2,1)}, u32[]{:S(2)}) copy-start(bf16[1,256,256]{2,1,0:T(8,128)(2,1)} %param.20) | copy-start | bytes 393220
  7.2 32.1 %copy-start.10 = (bf16[1,256,256]{2,1,0:T(8,128)(2,1)S(1)}, bf16[1,256,256]{2,1,0:T(8,128)(2,1)}, u32[]{:S(2)}) copy-start(bf16[1,256,256]{2,1,0:T(8,128)(2,1)} %param.18) | copy-start | bytes 393220
  7.2 32.1 %copy-start.11 = (f32[1,256]{1,0:T(1,128)S(1)}, f32[1,256]{1,0:T(1,128)}, u32[]{:S(2)}) copy-start(f32[1,256]{1,0:T(1,128)} %param.19) | copy-start | bytes 3076
  8.2 16.1 %all-to-all-start = ((f32[16,1,1776]{2,1,0:T(1,128)}), f32[16,1,1776]{2,1,0:T(1,128)S(1)}, u32[]{:S(2)}, u32[]{:S(2)}) async-start(f32[16,1,1776]{2,1,0:T(1,128)} %reshape.227), calls=%async_computation | async-start | bytes 229376 | tf_op jit(solution)/shard_map/all_to_all | solution.py:161
  26.0 16.9 %copy-start.5 = (f32[192,128]{0,1:T(8,128)}, f32[192,128]{0,1:T(8,128)S(1)}, u32[]{:S(2)}) copy-start(f32[192,128]{0,1:T(8,128)S(1)} %copy.116) | copy-start | bytes 294916
  39.3 3.7 %copy-start.1 = (bf16[6144,128]{1,0:T(8,128)(2,1)}, bf16[6144,128]{1,0:T(8,128)(2,1)S(1)}, u32[]{:S(2)}) copy-start(bf16[6144,128]{1,0:T(8,128)(2,1)S(1)} %get-tuple-element.15) | copy-start | bytes 4718596
  39.3 3.7 %copy-start.3 = (bf16[6144,128]{1,0:T(8,128)(2,1)}, bf16[6144,128]{1,0:T(8,128)(2,1)S(1)}, u32[]{:S(2)}) copy-start(bf16[6144,128]{1,0:T(8,128)(2,1)S(1)} %get-tuple-element.16) | copy-start | bytes 4718596
  39.3 3.7 %copy-start.12 = (f32[1,256]{1,0:T(1,128)S(1)}, f32[1,256]{1,0:T(1,128)}, u32[]{:S(2)}) copy-start(f32[1,256]{1,0:T(1,128)} %param.21) | copy-start | bytes 3076
  43.0 4.5 %copy-start.13 = (bf16[6144,256]{1,0:T(8,128)(2,1)}, bf16[6144,256]{1,0:T(8,128)(2,1)S(1)}, u32[]{:S(2)}) copy-start(bf16[6144,256]{1,0:T(8,128)(2,1)S(1)} %get-tuple-element.22) | copy-start | bytes 9437188
  43.0 4.4 %copy-start.8 = (bf16[1,4,256]{2,1,0:T(4,128)(2,1)S(1)}, bf16[1,4,256]{2,1,0:T(4,128)(2,1)}, u32[]{:S(2)}) copy-start(bf16[1,4,256]{2,1,0:T(4,128)(2,1)} %param.22) | copy-start | bytes 6148
  43.0 4.4 %copy-start.9 = (f32[1,4]{1,0:T(1,128)S(1)}, f32[1,4]{1,0:T(1,128)}, u32[]{:S(2)}) copy-start(f32[1,4]{1,0:T(1,128)} %param.23) | copy-start | bytes 52
  61.2 11.7 %all-to-all-start.1 = ((f32[16,192,4]{1,2,0:T(4,128)}), f32[16,192,4]{1,2,0:T(4,128)}, u32[]{:S(2)}, u32[]{:S(2)}) async-start(f32[16,192,4]{1,2,0:T(4,128)} %broadcast_in_dim.21), calls=%async_computation.1 | async-start | bytes 131072 | tf_op jit(solution)/shard_map/all_to_all | solution.py:181
  79.2 0.8 copy-start.7
  80.0 0.6 copy-start.6
  96.4 6.9 %slice-start = ((s8[6291456]{0:T(1024)(128)(4,1)}), s8[4194304]{0:T(1024)(128)(4,1)S(1)}, s32[]{:S(2)}) async-start(s8[6291456]{0:T(1024)(128)(4,1)} %bitcast.163), calls=%async_computation.2 | async-start | bytes 8388608
  97.1 5.2 %copy-start.14 = (bf16[6144,256]{1,0:T(8,128)(2,1)S(1)}, bf16[6144,256]{1,0:T(8,128)(2,1)}, u32[]{:S(2)}) copy-start(bf16[6144,256]{1,0:T(8,128)(2,1)} %copy-done.13) | copy-start | bytes 9437188
  97.1 6.2 %slice-start.1 = ((s8[6291456]{0:T(1024)(128)(4,1)}), s8[2097152]{0:T(1024)(128)(4,1)S(1)}, s32[]{:S(2)}) async-start(s8[6291456]{0:T(1024)(128)(4,1)} %bitcast.163), calls=%async_computation.3 | async-start | bytes 4194304
  103.3 3.4 %copy-start.2 = (bf16[6144,128]{1,0:T(8,128)(2,1)S(1)}, bf16[6144,128]{1,0:T(8,128)(2,1)}, u32[]{:S(2)}) copy-start(bf16[6144,128]{1,0:T(8,128)(2,1)} %copy-done.1) | copy-start | bytes 4718596
  103.4 3.4 %copy-start.4 = (bf16[6144,128]{1,0:T(8,128)(2,1)S(1)}, bf16[6144,128]{1,0:T(8,128)(2,1)}, u32[]{:S(2)}) copy-start(bf16[6144,128]{1,0:T(8,128)(2,1)} %copy-done.3) | copy-start | bytes 4718596
  106.1 1.8 %collective-permute-start.2 = (f32[1540]{0:T(1024)S(1)}, f32[1540]{0:T(1024)S(1)}, u32[]{:S(2)}, u32[]{:S(2)}) collective-permute-start(f32[1540]{0:T(1024)S(1)} %pad_maximum_fusion.5), channel_id=1, source_target_pairs={{0,1},{1,0},{2,3},{3,2},{4,5},{5,4},{6,7},{7,6},{8,9},{9,8},{10,11... | collective-permute-start | bytes 18488 | tf_op jit(solution)/shard_map/ppermute | solution.py:231
  106.2 3.4 %collective-permute-start.1 = (f32[128,256]{1,0:T(8,128)S(1)}, f32[128,256]{1,0:T(8,128)S(1)}, u32[]{:S(2)}, u32[]{:S(2)}) collective-permute-start(f32[128,256]{1,0:T(8,128)S(1)} %constant_dynamic-slice_fusion), channel_id=1, source_target_pairs={{0,1},{1,0},{2,3},{3,2},{4,5},{5,4},{6,7},{7,6},{8,9},{9,8},{10,11... | collective-permute-start | bytes 393224 | tf_op jit(solution)/shard_map/ppermute | solution.py:231
  107.8 2.5 %collective-permute-start = (f32[128,256]{1,0:T(8,128)S(1)}, f32[128,256]{1,0:T(8,128)S(1)}, u32[]{:S(2)}, u32[]{:S(2)}) collective-permute-start(f32[128,256]{1,0:T(8,128)S(1)} %constant_dynamic-slice_fusion.1), channel_id=1, source_target_pairs={{0,1},{1,0},{2,3},{3,2},{4,5},{5,4},{6,7},{7,6},{8,9},{9,8},{10,11... | collective-permute-start | bytes 393224 | tf_op jit(solution)/shard_map/ppermute | solution.py:231

commit v4 on v2

--- a/solution.py
+++ b/solution.py
@@ -15,13 +15,44 @@
     return gate * (1.0 + value * (1.0 - gate))
 
 
+def turn_sin_cos(turns):
+    quarter = jnp.round(turns * 4.0)
+    angle = (turns - quarter * 0.25) * two_pi
+    square = angle * angle
+    sine = angle * (
+        1.0
+        + square
+        * (
+            -1.0 / 6.0
+            + square * (1.0 / 120.0 + square * (-1.0 / 5040.0 + square * (1.0 / 362880.0)))
+        )
+    )
+    cosine = 1.0 + square * (
+        -0.5
+        + square
+        * (
+            1.0 / 24.0
+            + square * (-1.0 / 720.0 + square * (1.0 / 40320.0 + square * (-1.0 / 3628800.0)))
+        )
+    )
+    step = quarter - 4.0 * jnp.floor(quarter * 0.25)
+    flip = step >= 2.0
+    odd = (step == 1.0) | (step == 3.0)
+    sin_out = jnp.where(odd, cosine, sine)
+    cos_out = jnp.where(odd, sine, cosine)
+    sin_out = jnp.where(flip, -sin_out, sin_out)
+    cos_out = jnp.where(flip != odd, -cos_out, cos_out)
+    return sin_out, cos_out
+
+
 def encode(samples, fourier):
-    phases = two_pi * (
+    turns = (
         samples[:, 0, :, None] * fourier[0]
         + samples[:, 1, :, None] * fourier[1]
         + samples[:, 2, :, None] * fourier[2]
     )
-    joined = jnp.concatenate([jnp.sin(phases), jnp.cos(phases)], axis=-1)
+    sine, cosine = turn_sin_cos(turns)
+    joined = jnp.concatenate([sine, cosine], axis=-1)
     return joined.astype(jnp.bfloat16).reshape(-1, joined.shape[-1])
 
 

time: 97.9 us -> 90.9 us (0.928)
  other arithmetic: 18.7 us -> 11.7 us
    another operation x2, other arithmetic: 12.7 us -> 5.68 us
where the time goes in v4:
time: 90.9 us; the launch traced here: 90 us
  matrix products  23.1 us (25%)
  waiting for transfers between devices  20 us (22%)
  local copies, waits for them, and re-layouts  17.7 us (19%)
  starting transfers between devices  16.2 us (18%)
  other arithmetic  11.7 us (13%)
  between operations  1.16 us (1%)
    all_to_all x1, starting transfers between devices, per_device(): lax.all_to_all(outgoing, 'space', split_axis=0, concat_axis=0, tiled=True)  8.31 us
    all_to_all x1, waiting for transfers between devices, per_device(): lax.all_to_all(sendback, 'space', split_axis=1, concat_axis=1, tiled=True)  7.17 us
    all_to_all x1, waiting for transfers between devices, per_device(): lax.all_to_all(outgoing, 'space', split_axis=0, concat_axis=0, tiled=True)  7 us
    all_to_all x1, waiting for transfers between devices, per_device(): lax.all_to_all(partials, 'space', split_axis=1, concat_axis=1, tiled=True)  5.86 us
    another operation x2, other arithmetic  5.68 us
    dot_general x1, matrix products, backward(): jnp.dot(grad_raw, head_weight, preferred_element_type=jnp.float32)  5.17 us
    dot_general x1, matrix products, network(): jnp.dot(encoded, first_weight, preferred_element_type=jnp.float32)  4.72 us
    dot_general x1, matrix products, network(): jnp.dot(act_first, second_weight, preferred_element_type=jnp.float32)  4.37 us
  transfers between devices with their start and end apart: 6, of which 3 were waited for; matrix products, arithmetic and copies ran while one was open for 6% of the time, Pallas kernels for 0%

profile of v4, /device:TPU:0, one launch (start us, length us, event | category | flops | bytes accessed | tf_op | source)
XLA Modules:
  0.0 90.0 jit_solution(858286756958283039)
XLA Ops:
  2.0 0.9 reshape.234
  4.0 0.9 fusion.21
  4.9 8.3 %all-to-all-start = ((f32[16,12,128]{2,1,0:T(8,128)}), f32[16,12,128]{2,1,0:T(8,128)S(1)}, u32[]{:S(2)}, u32[]{:S(2)}) async-start(f32[16,12,128]{2,1,0:T(8,128)} %fusion.21), calls=%async_computation | async-start | bytes 262144 | tf_op jit(solution)/shard_map/all_to_all | solution.py:181
  14.0 7.0 %all-to-all-done = f32[16,12,128]{2,1,0:T(8,128)S(1)} async-done(((f32[16,12,128]{2,1,0:T(8,128)}), f32[16,12,128]{2,1,0:T(8,128)S(1)}, u32[]{:S(2)}, u32[]{:S(2)}) %all-to-all-start) | async-done | bytes 98336 | tf_op jit(solution)/shard_map/all_to_all | solution.py:181
  21.2 0.9 %slice_reduce_fusion.2 = (f32[192,32]{1,0:T(8,128)S(1)}, f32[192,32]{1,0:T(8,128)S(1)}, f32[192,32]{1,0:T(8,128)S(1)}, f32[192,1,32]{2,1,0:T(1,128)S(1)}) fusion(f32[192,4,32]{2,1,0:T(4,128)S(1)} %reshape.237), kind=kLoop, calls=%fused_computation.61 | loop fusion | bytes 196608 | tf_op jit(solution)/shard_map/slice | solution.py:50
  22.4 5.6 %fusion.2 = (bf16[6144,128]{1,0:T(8,128)(2,1)S(1)}, bf16[6144,128]{1,0:T(8,128)(2,1)S(1)}) fusion(f32[128]{0:T(128)S(1)} %get-tuple-element.19, f32[6144]{0:T(1024)S(1)} %mul.319, f32[128]{0:T(128)S(1)} %get-tuple-element.20, f32[6144]{0:T(1024)S(1)} %mul.314, f32[128]{0:T(128)S(1)} %get-tuple-element.18, f32[6144]{0:T(1024)S(1)} %mul.309), kind=kLoop, calls=%fused_computation.15 | loop fusion | flops 36175872 | bytes 3220992 | tf_op jit(solution)/shard_map/convert.4
  28.1 4.7 %multiply_convert_fusion.1 = (bf16[6144,256]{1,0:T(8,128)(2,1)S(1)}, f32[6144,256]{1,0:T(8,128)}) fusion(f32[256]{0:T(256)S(1)} %bitcast.134, bf16[1,256,256]{2,1,0:T(8,128)(2,1)} %param.18, bf16[6144,128]{1,0:T(8,128)(2,1)S(1)} %get-tuple-element.13, bf16[6144,128]{1,0:T(8,128)(2,1)S(1)} %get-tuple-element.12), kind=kOutput, calls=%fused_computation.11 | convolution fusion | flops 821035008 | bytes 12715008 | tf_op jit(solution)/shard_map/dot_general | solution.py:63
  32.9 4.4 %multiply_convert_fusion = (bf16[6144,256]{1,0:T(8,128)(2,1)S(1)}, f32[6144,256]{1,0:T(8,128)}) fusion(f32[256]{0:T(256)S(1)} %bitcast.135, bf16[6144,256]{1,0:T(8,128)(2,1)S(1)} %get-tuple-element.21, bf16[1,256,256]{2,1,0:T(8,128)(2,1)S(1)} %copy-done), kind=kOutput, calls=%fused_computation.9 | convolution fusion | flops 814743552 | bytes 12715008 | tf_op jit(solution)/shard_map/dot_general | solution.py:65
  37.3 0.9 %convolution_add_fusion.2 = f32[6144,4]{0,1:T(4,128)S(1)} fusion(bf16[6144,256]{1,0:T(8,128)(2,1)S(1)} %get-tuple-element.23, f32[4]{0:T(128)S(1)} %bitcast.130, bf16[1,4,256]{2,1,0:T(4,128)(2,1)S(1)} %copy-done.6), kind=kOutput, calls=%fused_computation.6 | convolution fusion | flops 12607488 | bytes 3246096 | tf_op jit(solution)/shard_map/dot_general | solution.py:68
  38.2 0.9 %reshape.238 = f32[192,32,4]{1,0,2:T(8,128)} reshape(f32[6144,4]{0,1:T(4,128)S(1)} %convolution_add_fusion.2) | data formatting | bytes 196608 | tf_op jit(solution)/shard_map/reshape | solution.py:73
  39.2 0.9 slice.77
  40.5 1.2 %multiply_reduce_fusion.1 = f32[192,3]{0,1:T(4,128)S(1)} fusion(f32[192,32]{1,0:T(8,128)S(1)} %copy.60, f32[192,32,4]{1,0,2:T(8,128)} %reshape.238), kind=kLoop, calls=%fused_computation.48 | loop fusion | flops 91584 | bytes 100608 | tf_op jit(solution)/shard_map/reduce_sum | solution.py:81
  42.5 3.5 %all-to-all-start.1 = ((f32[4,16,12]{2,0,1:T(4,128)}), f32[4,16,12]{2,0,1:T(4,128)S(1)}, u32[]{:S(2)}, u32[]{:S(2)}) async-start(f32[4,16,12]{2,0,1:T(4,128)} %copy.61), calls=%async_computation.1 | async-start | bytes 65536 | tf_op jit(solution)/shard_map/all_to_all | solution.py:200
  47.5 5.9 %all-to-all-done.1 = f32[4,16,12]{2,0,1:T(4,128)S(1)} async-done(((f32[4,16,12]{2,0,1:T(4,128)}), f32[4,16,12]{2,0,1:T(4,128)S(1)}, u32[]{:S(2)}, u32[]{:S(2)}) %all-to-all-start.1) | async-done | bytes 3104 | tf_op jit(solution)/shard_map/all_to_all | solution.py:200
  56.5 0.9 fusion.19
  58.1 3.7 %all-to-all-start.2 = ((f32[4,16,12]{2,0,1:T(4,128)}), f32[4,16,12]{2,0,1:T(4,128)S(1)}, u32[]{:S(2)}, u32[]{:S(2)}) async-start(f32[4,16,12]{2,0,1:T(4,128)} %copy.67), calls=%async_computation.2 | async-start | bytes 65536 | tf_op jit(solution)/shard_map/all_to_all | solution.py:225
  61.8 7.2 %all-to-all-done.2 = f32[4,16,12]{2,0,1:T(4,128)S(1)} async-done(((f32[4,16,12]{2,0,1:T(4,128)}), f32[4,16,12]{2,0,1:T(4,128)S(1)}, u32[]{:S(2)}, u32[]{:S(2)}) %all-to-all-start.2) | async-done | bytes 3104 | tf_op jit(solution)/shard_map/all_to_all | solution.py:225
  70.4 2.4 %multiply_reduce_fusion = (f32[192,32]{1,0:T(8,128)}, bf16[192,32,3]{1,0,2:T(8,128)(2,1)}) fusion(f32[192,3]{0,1:T(4,128)S(1)} %bitcast.126, f32[192,32,4]{1,0,2:T(8,128)} %reshape.238, f32[192,32]{1,0:T(8,128)S(1)} %copy.60), kind=kLoop, calls=%fused_computation.47 | loop fusion | flops 178176 | bytes 162048 | tf_op jit(solution)/shard_map/reduce_sum | solution.py:102
  72.9 1.0 %copy.69 = f32[192,32]{0,1:T(8,128)S(1)} copy(f32[192,32]{1,0:T(8,128)} %get-tuple-element.9) | data formatting | bytes 49152 | tf_op jit(solution)/shard_map/reduce_sum | solution.py:102
  74.2 1.1 %concatenate.35 = bf16[6144,3]{0,1:T(4,128)(2,1)S(1)} reshape(bf16[192,32,3]{1,0,2:T(8,128)(2,1)} %get-tuple-element.10) | data formatting | bytes 73728 | tf_op jit(solution)/shard_map/concatenate | solution.py:109
  76.1 5.2 %convert_reduce_fusion = (f32[256]{0:T(256)S(1)}, bf16[6144,256]{1,0:T(8,128)(2,1)S(1)}) fusion(f32[6144,256]{1,0:T(8,128)} %get-tuple-element.24, bf16[1,4,256]{2,1,0:T(4,128)(2,1)S(1)} %copy-done.6, bf16[6144,3]{0,1:T(4,128)(2,1)S(1)} %concatenate.35, bf16[6144,1]{0,1:T(2,128)(2,1)S(1)} %concatenate.34), kind=kOutput, calls=%fused_computation.7 | convolution fusion | flops 29982464 | bytes 9489408 | tf_op jit(solution)/shard_map/dot_general | solution.py:117
  81.2 1.0 %fusion.56 = f32[256,256]{1,0:T(8,128)S(1)} fusion(bf16[6144,256]{1,0:T(8,128)(2,1)S(1)} %copy-done.13, bf16[6144,256]{1,0:T(8,128)(2,1)S(1)} %get-tuple-element.26), kind=kOutput, calls=%fused_computation.126 | convolution fusion | flops 805306368 | bytes 6553600 | tf_op jit(solution)/shard_map/dot_general | solution.py:119
  82.3 2.8 %convert_reduce_fusion.1 = (f32[256]{0:T(256)S(1)}, bf16[6144,256]{1,0:T(8,128)(2,1)S(1)}) fusion(f32[6144,256]{1,0:T(8,128)S(1)} %bitcast.137, bf16[6144,256]{1,0:T(8,128)(2,1)S(1)} %get-tuple-element.26, bf16[1,256,256]{2,1,0:T(8,128)(2,1)S(1)} %copy-done), kind=kOutput, calls=%fused_computation.8 | convolution fusion | flops 822607616 | bytes 12715008 | tf_op jit(solution)/shard_map/dot_general | solution.py:123
  85.8 1.0 %fusion.12 = f32[256,256]{1,0:T(8,128)S(1)} fusion(bf16[6144,256]{1,0:T(8,128)(2,1)S(1)} %get-tuple-element.28, bf16[6144,128]{1,0:T(8,128)(2,1)S(1)} %copy-done.4, bf16[6144,128]{1,0:T(8,128)(2,1)S(1)} %copy-done.2), kind=kOutput, calls=%fused_computation.39 | convolution fusion | flops 811597824 | bytes 6553600 | tf_op jit(solution)/shard_map/dot_general | solution.py:127
  (110 shorter events, 16.6 us)
Async XLA Ops:
  0.6 32.2 %copy-start = (bf16[1,256,256]{2,1,0:T(8,128)(2,1)S(1)}, bf16[1,256,256]{2,1,0:T(8,128)(2,1)}, u32[]{:S(2)}) copy-start(bf16[1,256,256]{2,1,0:T(8,128)(2,1)} %param.20) | copy-start | bytes 393220
  1.8 26.3 %copy-start.10 = (f32[1,256]{1,0:T(1,128)S(1)}, f32[1,256]{1,0:T(1,128)}, u32[]{:S(2)}) copy-start(f32[1,256]{1,0:T(1,128)} %param.19) | copy-start | bytes 3076
  2.0 19.0 %copy-start.9 = (s32[128]{0:T(128)}, s32[128]{0:T(128)S(1)}, u32[]{:S(2)}) copy-start(s32[128]{0:T(128)S(1)} %multiply_add_fusion.2) | copy-start | bytes 1540
  4.9 16.1 %all-to-all-start = ((f32[16,12,128]{2,1,0:T(8,128)}), f32[16,12,128]{2,1,0:T(8,128)S(1)}, u32[]{:S(2)}, u32[]{:S(2)}) async-start(f32[16,12,128]{2,1,0:T(8,128)} %fusion.21), calls=%async_computation | async-start | bytes 262144 | tf_op jit(solution)/shard_map/all_to_all | solution.py:181
  28.1 4.8 %copy-start.1 = (bf16[6144,128]{1,0:T(8,128)(2,1)}, bf16[6144,128]{1,0:T(8,128)(2,1)S(1)}, u32[]{:S(2)}) copy-start(bf16[6144,128]{1,0:T(8,128)(2,1)S(1)} %get-tuple-element.12) | copy-start | bytes 4718596
  28.1 4.8 %copy-start.3 = (bf16[6144,128]{1,0:T(8,128)(2,1)}, bf16[6144,128]{1,0:T(8,128)(2,1)S(1)}, u32[]{:S(2)}) copy-start(bf16[6144,128]{1,0:T(8,128)(2,1)S(1)} %get-tuple-element.13) | copy-start | bytes 4718596
  28.1 4.8 %copy-start.11 = (f32[1,256]{1,0:T(1,128)S(1)}, f32[1,256]{1,0:T(1,128)}, u32[]{:S(2)}) copy-start(f32[1,256]{1,0:T(1,128)} %param.21) | copy-start | bytes 3076
  32.9 4.4 %copy-start.12 = (bf16[6144,256]{1,0:T(8,128)(2,1)}, bf16[6144,256]{1,0:T(8,128)(2,1)S(1)}, u32[]{:S(2)}) copy-start(bf16[6144,256]{1,0:T(8,128)(2,1)S(1)} %get-tuple-element.21) | copy-start | bytes 9437188
  32.9 4.4 %copy-start.6 = (bf16[1,4,256]{2,1,0:T(4,128)(2,1)S(1)}, bf16[1,4,256]{2,1,0:T(4,128)(2,1)}, u32[]{:S(2)}) copy-start(bf16[1,4,256]{2,1,0:T(4,128)(2,1)} %param.22) | copy-start | bytes 6148
  32.9 4.4 %copy-start.7 = (f32[1,4]{1,0:T(1,128)S(1)}, f32[1,4]{1,0:T(1,128)}, u32[]{:S(2)}) copy-start(f32[1,4]{1,0:T(1,128)} %param.23) | copy-start | bytes 52
  37.3 8.7 %copy-start.8 = (f32[3,16]{1,0:T(4,128)S(1)}, f32[3,16]{1,0:T(4,128)}, u32[]{:S(2)}) copy-start(f32[3,16]{1,0:T(4,128)} %param.16) | copy-start | bytes 580
  37.3 18.8 %copy-start.5 = (s32[16,8]{0,1:T(8,128)S(1)}, s32[16,8]{0,1:T(8,128)}, u32[]{:S(2)}) copy-start(s32[16,8]{0,1:T(8,128)} %param.15) | copy-start | bytes 1540
  42.5 10.9 %all-to-all-start.1 = ((f32[4,16,12]{2,0,1:T(4,128)}), f32[4,16,12]{2,0,1:T(4,128)S(1)}, u32[]{:S(2)}, u32[]{:S(2)}) async-start(f32[4,16,12]{2,0,1:T(4,128)} %copy.61), calls=%async_computation.1 | async-start | bytes 65536 | tf_op jit(solution)/shard_map/all_to_all | solution.py:200
  58.1 10.9 %all-to-all-start.2 = ((f32[4,16,12]{2,0,1:T(4,128)}), f32[4,16,12]{2,0,1:T(4,128)S(1)}, u32[]{:S(2)}, u32[]{:S(2)}) async-start(f32[4,16,12]{2,0,1:T(4,128)} %copy.67), calls=%async_computation.2 | async-start | bytes 65536 | tf_op jit(solution)/shard_map/all_to_all | solution.py:225
  75.3 7.0 %slice-start = ((s8[6291456]{0:T(1024)(128)(4,1)}), s8[4194304]{0:T(1024)(128)(4,1)S(1)}, s32[]{:S(2)}) async-start(s8[6291456]{0:T(1024)(128)(4,1)} %bitcast.136), calls=%async_computation.3 | async-start | bytes 8388608
  76.0 5.2 %copy-start.13 = (bf16[6144,256]{1,0:T(8,128)(2,1)S(1)}, bf16[6144,256]{1,0:T(8,128)(2,1)}, u32[]{:S(2)}) copy-start(bf16[6144,256]{1,0:T(8,128)(2,1)} %copy-done.12) | copy-start | bytes 9437188
  76.0 6.2 %slice-start.1 = ((s8[6291456]{0:T(1024)(128)(4,1)}), s8[2097152]{0:T(1024)(128)(4,1)S(1)}, s32[]{:S(2)}) async-start(s8[6291456]{0:T(1024)(128)(4,1)} %bitcast.136), calls=%async_computation.4 | async-start | bytes 4194304
  82.3 3.5 %copy-start.2 = (bf16[6144,128]{1,0:T(8,128)(2,1)S(1)}, bf16[6144,128]{1,0:T(8,128)(2,1)}, u32[]{:S(2)}) copy-start(bf16[6144,128]{1,0:T(8,128)(2,1)} %copy-done.1) | copy-start | bytes 4718596
  82.3 3.5 %copy-start.4 = (bf16[6144,128]{1,0:T(8,128)(2,1)S(1)}, bf16[6144,128]{1,0:T(8,128)(2,1)}, u32[]{:S(2)}) copy-start(bf16[6144,128]{1,0:T(8,128)(2,1)} %copy-done.3) | copy-start | bytes 4718596
  85.1 1.8 %collective-permute-start.2 = (f32[1540]{0:T(1024)S(1)}, f32[1540]{0:T(1024)S(1)}, u32[]{:S(2)}, u32[]{:S(2)}) collective-permute-start(f32[1540]{0:T(1024)S(1)} %pad_maximum_fusion.6), channel_id=1, source_target_pairs={{0,1},{1,0},{2,3},{3,2},{4,5},{5,4},{6,7},{7,6},{8,9},{9,8},{10,11... | collective-permute-start | bytes 18488 | tf_op jit(solution)/shard_map/ppermute | solution.py:245
  85.3 3.4 %collective-permute-start.1 = (f32[128,256]{1,0:T(8,128)S(1)}, f32[128,256]{1,0:T(8,128)S(1)}, u32[]{:S(2)}, u32[]{:S(2)}) collective-permute-start(f32[128,256]{1,0:T(8,128)S(1)} %constant_dynamic-slice_fusion.1), channel_id=1, source_target_pairs={{0,1},{1,0},{2,3},{3,2},{4,5},{5,4},{6,7},{7,6},{8,9},{9,8},{10,11... | collective-permute-start | bytes 393224 | tf_op jit(solution)/shard_map/ppermute | solution.py:245
  86.9 2.5 %collective-permute-start = (f32[128,256]{1,0:T(8,128)S(1)}, f32[128,256]{1,0:T(8,128)S(1)}, u32[]{:S(2)}, u32[]{:S(2)}) collective-permute-start(f32[128,256]{1,0:T(8,128)S(1)} %constant_dynamic-slice_fusion), channel_id=1, source_target_pairs={{0,1},{1,0},{2,3},{3,2},{4,5},{5,4},{6,7},{7,6},{8,9},{9,8},{10,11... | collective-permute-start | bytes 393224 | tf_op jit(solution)/shard_map/ppermute | solution.py:245

commit v5 on v4

--- a/solution.py
+++ b/solution.py
@@ -138,6 +138,16 @@
     shaded = prefix * jnp.sum(seg_colour * pixel_rows[:, None, :], axis=2)
     up_log = jnp.sum(before * shaded[:, :, None], axis=1)
     return (up_colour, up_log)
+
+
+def shift_exchange(blocks, axis, direction):
+    count = blocks.shape[axis]
+    parts = [lax.index_in_dim(blocks, 0, axis, keepdims=False)]
+    for shift in range(1, count):
+        pairs = [(i, (i + direction * shift) % count) for i in range(count)]
+        piece = lax.index_in_dim(blocks, shift, axis, keepdims=False)
+        parts.append(lax.ppermute(piece, "space", pairs))
+    return jnp.stack(parts, axis=axis)
 
 
 def per_device(
@@ -163,7 +173,7 @@
     member = (owner[:, None] == jnp.arange(groups, dtype=jnp.int32)[None, :]).astype(jnp.int32)
     earlier = jnp.cumsum(member, axis=0) - member
     within = jnp.sum(earlier * member, axis=1)
-    target = owner * capacity + within
+    target = ((owner - lax.axis_index("space")) % groups) * capacity + within
     dispatch = (target[:, None] == jnp.arange(slot_count, dtype=jnp.int32)[None, :]).astype(
         jnp.float32
     )
@@ -178,7 +188,7 @@
         preferred_element_type=jnp.float32,
     )
     outgoing = outgoing.reshape(groups, capacity, 4 * SEG_LEN)
-    arrived = lax.all_to_all(outgoing, "space", split_axis=0, concat_axis=0, tiled=True)
+    arrived = shift_exchange(outgoing, 0, 1)
     samples = arrived.reshape(slot_count, 4, SEG_LEN)
     params = tuple(
         (
@@ -197,7 +207,7 @@
     partials = jnp.concatenate([seg_colour.T, seg_log[None, :]], axis=0).reshape(
         4, groups, capacity
     )
-    returned = lax.all_to_all(partials, "space", split_axis=1, concat_axis=1, tiled=True).reshape(
+    returned = shift_exchange(partials, 1, -1).reshape(
         4, slot_count
     )
     mine = lax.dot_general(
@@ -222,7 +232,7 @@
         preferred_element_type=jnp.float32,
     )
     sendback = sendback.reshape(4, groups, capacity)
-    received = lax.all_to_all(sendback, "space", split_axis=1, concat_axis=1, tiled=True)
+    received = shift_exchange(sendback, 1, 1)
     received = received.reshape(4, slot_count).T
     totals = backward(samples, params, saved, received[:, :3], received[:, 3])
     grad_first, grad_second, grad_head, bias_first, bias_second, bias_head = totals

time: 90.9 us -> 156 us (1.72)
  starting transfers between devices: 16.2 us -> 83.1 us
  waiting for transfers between devices: 20 us -> 10.5 us
  local copies, waits for them, and re-layouts: 17.7 us -> 22.2 us
  other arithmetic: 11.7 us -> 14 us
    ppermute x0 -> x45, starting transfers between devices: none -> 82.5 us  [shift_exchange(): parts.append(lax.ppermute(piece, 'space', pairs))]
    all_to_all x3 -> x0, waiting for transfers between devices: 20 us -> none  [the longest x1 7.17 us: per_device(): lax.all_to_all(sendback, 'space', split_axis=1, concat_axis=1, tiled=True)]
    all_to_all x3 -> x0, starting transfers between devices: 15.5 us -> none  [the longest x1 8.31 us: per_device(): lax.all_to_all(outgoing, 'space', split_axis=0, concat_axis=0, tiled=True)]
    ppermute x0 -> x45, waiting for transfers between devices: none -> 10.5 us  [shift_exchange(): parts.append(lax.ppermute(piece, 'space', pairs))]
    unnamed x36 -> x108, local copies, waits for them, and re-layouts: 1.02 us -> 4.44 us
    another operation x1 -> x4, local copies, waits for them, and re-layouts: 0.11 us -> 3.16 us  [the longest x3 3.04 us: shift_exchange(): return jnp.stack(parts, axis=axis)]
  transfers between devices with their start and end apart: 6 -> 48, of which waited for: 3 -> 6; matrix products, arithmetic and copies ran while one was open for 6% -> 4% of each run, Pallas kernels for 0% -> 0%
where the time goes in v5:
time: 156 us; the launch traced here: 154 us
  starting transfers between devices  83.1 us (53%)
  matrix products  22.5 us (14%)
  local copies, waits for them, and re-layouts  22.2 us (14%)
  other arithmetic  14 us (9%)
  waiting for transfers between devices  10.5 us (7%)
  between operations  1.56 us (1%)
    ppermute x45, starting transfers between devices, shift_exchange(): parts.append(lax.ppermute(piece, 'space', pairs))  82.5 us
    ppermute x45, waiting for transfers between devices, shift_exchange(): parts.append(lax.ppermute(piece, 'space', pairs))  10.5 us
    another operation x2, other arithmetic  5.68 us
    dot_general x1, matrix products, backward(): jnp.dot(grad_raw, head_weight, preferred_element_type=jnp.float32)  5.18 us
    dot_general x1, matrix products, network(): jnp.dot(encoded, first_weight, preferred_element_type=jnp.float32)  4.71 us
    unnamed x108, local copies, waits for them, and re-layouts  4.44 us
    dot_general x1, matrix products, network(): jnp.dot(act_first, second_weight, preferred_element_type=jnp.float32)  4.41 us
  transfers between devices with their start and end apart: 48, of which 6 were waited for; matrix products, arithmetic and copies ran while one was open for 4% of the time, Pallas kernels for 0%

profile of v5, /device:TPU:0, one launch (start us, length us, event | category | flops | bytes accessed | tf_op | source)
XLA Modules:
  0.0 153.9 jit_solution(5360012754248196150)
XLA Ops:
  4.3 3.0 %collective-permute-start = (f32[12,128]{1,0:T(8,128)S(1)}, f32[12,128]{1,0:T(8,128)S(1)}, u32[]{:S(2)}, u32[]{:S(2)}) collective-permute-start(f32[12,128]{1,0:T(8,128)S(1)} %get-tuple-element.26), channel_id=1, source_target_pairs={{0,2},{2,4},{4,6},{6,8},{8,10},{10,12},{12,14},{14,16},{16,18},{18... | collective-permute-start | bytes 18440 | tf_op jit(solution)/shard_map/ppermute | solution.py:149
  8.8 2.4 %collective-permute-start.2 = (f32[12,128]{1,0:T(8,128)S(1)}, f32[12,128]{1,0:T(8,128)S(1)}, u32[]{:S(2)}, u32[]{:S(2)}) collective-permute-start(f32[12,128]{1,0:T(8,128)S(1)} %get-tuple-element.24), channel_id=1, source_target_pairs={{0,6},{2,8},{4,10},{6,12},{8,14},{10,16},{12,18},{14,20},{16,22},{... | collective-permute-start | bytes 18440 | tf_op jit(solution)/shard_map/ppermute | solution.py:149
  17.3 4.4 %collective-permute-start.6 = (f32[12,128]{1,0:T(8,128)S(1)}, f32[12,128]{1,0:T(8,128)S(1)}, u32[]{:S(2)}, u32[]{:S(2)}) collective-permute-start(f32[12,128]{1,0:T(8,128)S(1)} %get-tuple-element.20), channel_id=1, source_target_pairs={{0,14},{2,16},{4,18},{6,20},{8,22},{10,24},{12,26},{14,28},{16,30}... | collective-permute-start | bytes 18440 | tf_op jit(solution)/shard_map/ppermute | solution.py:149
  25.1 4.0 %collective-permute-start.10 = (f32[12,128]{1,0:T(8,128)S(1)}, f32[12,128]{1,0:T(8,128)S(1)}, u32[]{:S(2)}, u32[]{:S(2)}) collective-permute-start(f32[12,128]{1,0:T(8,128)S(1)} %get-tuple-element.16), channel_id=1, source_target_pairs={{0,22},{2,24},{4,26},{6,28},{8,30},{10,0},{12,2},{14,4},{16,6},{18... | collective-permute-start | bytes 18440 | tf_op jit(solution)/shard_map/ppermute | solution.py:149
  32.4 3.6 %collective-permute-start.14 = (f32[12,128]{1,0:T(8,128)S(1)}, f32[12,128]{1,0:T(8,128)S(1)}, u32[]{:S(2)}, u32[]{:S(2)}) collective-permute-start(f32[12,128]{1,0:T(8,128)S(1)} %get-tuple-element.12), channel_id=1, source_target_pairs={{0,30},{2,0},{4,2},{6,4},{8,6},{10,8},{12,10},{14,12},{16,14},{18,... | collective-permute-start | bytes 18440 | tf_op jit(solution)/shard_map/ppermute | solution.py:149
  38.8 5.6 %fusion.2 = (bf16[6144,128]{1,0:T(8,128)(2,1)S(1)}, bf16[6144,128]{1,0:T(8,128)(2,1)S(1)}) fusion(f32[128]{0:T(128)S(1)} %get-tuple-element.66, f32[6144]{0:T(1024)S(1)} %mul.319, f32[128]{0:T(128)S(1)} %get-tuple-element.67, f32[6144]{0:T(1024)S(1)} %mul.314, f32[128]{0:T(128)S(1)} %get-tuple-element.65, f32[6144]{0:T(1024)S(1)} %mul.309), kind=kLoop, calls=%fused_computation.15 | loop fusion | flops 36175872 | bytes 3220992 | tf_op jit(solution)/shard_map/convert.4
  44.5 4.7 %multiply_convert_fusion.1 = (bf16[6144,256]{1,0:T(8,128)(2,1)S(1)}, f32[6144,256]{1,0:T(8,128)}) fusion(f32[256]{0:T(256)S(1)} %bitcast.346, bf16[1,256,256]{2,1,0:T(8,128)(2,1)} %param.18, bf16[6144,128]{1,0:T(8,128)(2,1)S(1)} %get-tuple-element.28, bf16[6144,128]{1,0:T(8,128)(2,1)S(1)} %get-tuple-element.27), kind=kOutput, calls=%fused_computation.11 | convolution fusion | flops 821035008 | bytes 12715008 | tf_op jit(solution)/shard_map/dot_general | solution.py:63
  49.3 4.4 %multiply_convert_fusion = (bf16[6144,256]{1,0:T(8,128)(2,1)S(1)}, f32[6144,256]{1,0:T(8,128)}) fusion(f32[256]{0:T(256)S(1)} %bitcast.347, bf16[6144,256]{1,0:T(8,128)(2,1)S(1)} %get-tuple-element.68, bf16[1,256,256]{2,1,0:T(8,128)(2,1)S(1)} %copy-done), kind=kOutput, calls=%fused_computation.9 | convolution fusion | flops 814743552 | bytes 12715008 | tf_op jit(solution)/shard_map/dot_general | solution.py:65
  62.3 5.9 %collective-permute-start.15 = (f32[4,12]{1,0:T(4,128)S(1)}, f32[4,12]{1,0:T(4,128)S(1)}, u32[]{:S(2)}, u32[]{:S(2)}) collective-permute-start(f32[4,12]{1,0:T(4,128)S(1)} %bitcast.339), channel_id=1, source_target_pairs={{0,30},{2,0},{4,2},{6,4},{8,6},{10,8},{12,10},{14,12},{16,14},{18,... | collective-permute-start | bytes 584 | tf_op jit(solution)/shard_map/ppermute | solution.py:149
  69.0 2.5 %collective-permute-start.19 = (f32[4,12]{1,0:T(4,128)S(1)}, f32[4,12]{1,0:T(4,128)S(1)}, u32[]{:S(2)}, u32[]{:S(2)}) collective-permute-start(f32[4,12]{1,0:T(4,128)S(1)} %bitcast.323), channel_id=1, source_target_pairs={{0,22},{2,24},{4,26},{6,28},{8,30},{10,0},{12,2},{14,4},{16,6},{18... | collective-permute-start | bytes 584 | tf_op jit(solution)/shard_map/ppermute | solution.py:149
  71.5 3.5 %collective-permute-start.20 = (f32[4,12]{1,0:T(4,128)S(1)}, f32[4,12]{1,0:T(4,128)S(1)}, u32[]{:S(2)}, u32[]{:S(2)}) collective-permute-start(f32[4,12]{1,0:T(4,128)S(1)} %bitcast.319), channel_id=1, source_target_pairs={{0,20},{2,22},{4,24},{6,26},{8,28},{10,30},{12,0},{14,2},{16,4},{1... | collective-permute-start | bytes 584 | tf_op jit(solution)/shard_map/ppermute | solution.py:149
  77.1 3.0 %collective-permute-start.23 = (f32[4,12]{1,0:T(4,128)S(1)}, f32[4,12]{1,0:T(4,128)S(1)}, u32[]{:S(2)}, u32[]{:S(2)}) collective-permute-start(f32[4,12]{1,0:T(4,128)S(1)} %bitcast.307), channel_id=1, source_target_pairs={{0,14},{2,16},{4,18},{6,20},{8,22},{10,24},{12,26},{14,28},{16,30}... | collective-permute-start | bytes 584 | tf_op jit(solution)/shard_map/ppermute | solution.py:149
  84.3 3.3 %collective-permute-start.27 = (f32[4,12]{1,0:T(4,128)S(1)}, f32[4,12]{1,0:T(4,128)S(1)}, u32[]{:S(2)}, u32[]{:S(2)}) collective-permute-start(f32[4,12]{1,0:T(4,128)S(1)} %bitcast.291), channel_id=1, source_target_pairs={{0,6},{2,8},{4,10},{6,12},{8,14},{10,16},{12,18},{14,20},{16,22},{... | collective-permute-start | bytes 584 | tf_op jit(solution)/shard_map/ppermute | solution.py:149
  88.7 3.2 %collective-permute-done.27 = f32[4,12]{1,0:T(4,128)S(1)} collective-permute-done((f32[4,12]{1,0:T(4,128)S(1)}, f32[4,12]{1,0:T(4,128)S(1)}, u32[]{:S(2)}, u32[]{:S(2)}) %collective-permute-start.27) | collective-permute-done | bytes 224 | tf_op jit(solution)/shard_map/ppermute | solution.py:149
  93.8 2.0 %collective-permute-done.29 = f32[4,12]{1,0:T(4,128)S(1)} collective-permute-done((f32[4,12]{1,0:T(4,128)S(1)}, f32[4,12]{1,0:T(4,128)S(1)}, u32[]{:S(2)}, u32[]{:S(2)}) %collective-permute-start.29) | collective-permute-done | bytes 224 | tf_op jit(solution)/shard_map/ppermute | solution.py:149
  103.5 3.1 %collective-permute-start.40 = (f32[4,12]{1,0:T(4,128)S(1)}, f32[4,12]{1,0:T(4,128)S(1)}, u32[]{:S(2)}, u32[]{:S(2)}) collective-permute-start(f32[4,12]{1,0:T(4,128)S(1)} %bitcast.329), channel_id=1, source_target_pairs={{0,22},{2,24},{4,26},{6,28},{8,30},{10,0},{12,2},{14,4},{16,6},{18... | collective-permute-start | bytes 584 | tf_op jit(solution)/shard_map/ppermute | solution.py:149
  106.6 2.4 %collective-permute-start.41 = (f32[4,12]{1,0:T(4,128)S(1)}, f32[4,12]{1,0:T(4,128)S(1)}, u32[]{:S(2)}, u32[]{:S(2)}) collective-permute-start(f32[4,12]{1,0:T(4,128)S(1)} %bitcast.325), channel_id=1, source_target_pairs={{0,24},{2,26},{4,28},{6,30},{8,0},{10,2},{12,4},{14,6},{16,8},{18,... | collective-permute-start | bytes 584 | tf_op jit(solution)/shard_map/ppermute | solution.py:149
  109.0 2.4 %collective-permute-start.43 = (f32[4,12]{1,0:T(4,128)S(1)}, f32[4,12]{1,0:T(4,128)S(1)}, u32[]{:S(2)}, u32[]{:S(2)}) collective-permute-start(f32[4,12]{1,0:T(4,128)S(1)} %bitcast.317), channel_id=1, source_target_pairs={{0,28},{2,30},{4,0},{6,2},{8,4},{10,6},{12,8},{14,10},{16,12},{18,... | collective-permute-start | bytes 584 | tf_op jit(solution)/shard_map/ppermute | solution.py:149
  111.4 2.9 %collective-permute-start.44 = (f32[4,12]{1,0:T(4,128)S(1)}, f32[4,12]{1,0:T(4,128)S(1)}, u32[]{:S(2)}, u32[]{:S(2)}) collective-permute-start(f32[4,12]{1,0:T(4,128)S(1)} %bitcast.313), channel_id=1, source_target_pairs={{0,30},{2,0},{4,2},{6,4},{8,6},{10,8},{12,10},{14,12},{16,14},{18,... | collective-permute-start | bytes 584 | tf_op jit(solution)/shard_map/ppermute | solution.py:149
  115.3 2.9 %collective-permute-start.32 = (f32[4,12]{1,0:T(4,128)S(1)}, f32[4,12]{1,0:T(4,128)S(1)}, u32[]{:S(2)}, u32[]{:S(2)}) collective-permute-start(f32[4,12]{1,0:T(4,128)S(1)} %bitcast.301), channel_id=1, source_target_pairs={{0,6},{2,8},{4,10},{6,12},{8,14},{10,16},{12,18},{14,20},{16,22},{... | collective-permute-start | bytes 584 | tf_op jit(solution)/shard_map/ppermute | solution.py:149
  122.8 5.0 %collective-permute-start.36 = (f32[4,12]{1,0:T(4,128)S(1)}, f32[4,12]{1,0:T(4,128)S(1)}, u32[]{:S(2)}, u32[]{:S(2)}) collective-permute-start(f32[4,12]{1,0:T(4,128)S(1)} %bitcast.285), channel_id=1, source_target_pairs={{0,14},{2,16},{4,18},{6,20},{8,22},{10,24},{12,26},{14,28},{16,30}... | collective-permute-start | bytes 584 | tf_op jit(solution)/shard_map/ppermute | solution.py:149
  131.3 2.4 %multiply_reduce_fusion = (f32[192,32]{1,0:T(8,128)}, bf16[192,32,3]{1,0,2:T(8,128)(2,1)}) fusion(f32[192,3]{0,1:T(4,128)S(1)} %bitcast.278, f32[192,32,4]{1,0,2:T(8,128)} %reshape.264, f32[192,32]{1,0:T(8,128)S(1)} %copy.125), kind=kLoop, calls=%fused_computation.47 | loop fusion | flops 178176 | bytes 162048 | tf_op jit(solution)/shard_map/reduce_sum | solution.py:102
  136.9 5.2 %convert_reduce_fusion = (f32[256]{0:T(256)S(1)}, bf16[6144,256]{1,0:T(8,128)(2,1)S(1)}) fusion(f32[6144,256]{1,0:T(8,128)} %get-tuple-element.71, bf16[1,4,256]{2,1,0:T(4,128)(2,1)} %param.22, bf16[6144,3]{0,1:T(4,128)(2,1)S(1)} %concatenate.35, bf16[6144,1]{0,1:T(2,128)(2,1)S(1)} %concatenate.34), kind=kOutput, calls=%fused_computation.7 | convolution fusion | flops 29982464 | bytes 9489408 | tf_op jit(solution)/shard_map/dot_general | solution.py:117
  143.2 2.7 %convert_reduce_fusion.1 = (f32[256]{0:T(256)S(1)}, bf16[6144,256]{1,0:T(8,128)(2,1)S(1)}) fusion(f32[6144,256]{1,0:T(8,128)S(1)} %bitcast.349, bf16[6144,256]{1,0:T(8,128)(2,1)S(1)} %get-tuple-element.73, bf16[1,256,256]{2,1,0:T(8,128)(2,1)S(1)} %copy-done), kind=kOutput, calls=%fused_computation.8 | convolution fusion | flops 822607616 | bytes 12715008 | tf_op jit(solution)/shard_map/dot_general | solution.py:123
  (266 shorter events, 67.6 us)
Async XLA Ops:
  4.3 11.8 %collective-permute-start = (f32[12,128]{1,0:T(8,128)S(1)}, f32[12,128]{1,0:T(8,128)S(1)}, u32[]{:S(2)}, u32[]{:S(2)}) collective-permute-start(f32[12,128]{1,0:T(8,128)S(1)} %get-tuple-element.26), channel_id=1, source_target_pairs={{0,2},{2,4},{4,6},{6,8},{8,10},{10,12},{12,14},{14,16},{16,18},{18... | collective-permute-start | bytes 18440 | tf_op jit(solution)/shard_map/ppermute | solution.py:149
  7.3 10.1 %collective-permute-start.1 = (f32[12,128]{1,0:T(8,128)S(1)}, f32[12,128]{1,0:T(8,128)S(1)}, u32[]{:S(2)}, u32[]{:S(2)}) collective-permute-start(f32[12,128]{1,0:T(8,128)S(1)} %get-tuple-element.25), channel_id=1, source_target_pairs={{0,4},{2,6},{4,8},{6,10},{8,12},{10,14},{12,16},{14,18},{16,20},{1... | collective-permute-start | bytes 18440 | tf_op jit(solution)/shard_map/ppermute | solution.py:149
  8.8 12.9 %collective-permute-start.2 = (f32[12,128]{1,0:T(8,128)S(1)}, f32[12,128]{1,0:T(8,128)S(1)}, u32[]{:S(2)}, u32[]{:S(2)}) collective-permute-start(f32[12,128]{1,0:T(8,128)S(1)} %get-tuple-element.24), channel_id=1, source_target_pairs={{0,6},{2,8},{4,10},{6,12},{8,14},{10,16},{12,18},{14,20},{16,22},{... | collective-permute-start | bytes 18440 | tf_op jit(solution)/shard_map/ppermute | solution.py:149
  11.2 10.8 %collective-permute-start.3 = (f32[12,128]{1,0:T(8,128)S(1)}, f32[12,128]{1,0:T(8,128)S(1)}, u32[]{:S(2)}, u32[]{:S(2)}) collective-permute-start(f32[12,128]{1,0:T(8,128)S(1)} %get-tuple-element.23), channel_id=1, source_target_pairs={{0,8},{2,10},{4,12},{6,14},{8,16},{10,18},{12,20},{14,22},{16,24},... | collective-permute-start | bytes 18440 | tf_op jit(solution)/shard_map/ppermute | solution.py:149
  12.8 10.9 %collective-permute-start.4 = (f32[12,128]{1,0:T(8,128)S(1)}, f32[12,128]{1,0:T(8,128)S(1)}, u32[]{:S(2)}, u32[]{:S(2)}) collective-permute-start(f32[12,128]{1,0:T(8,128)S(1)} %get-tuple-element.22), channel_id=1, source_target_pairs={{0,10},{2,12},{4,14},{6,16},{8,18},{10,20},{12,22},{14,24},{16,26}... | collective-permute-start | bytes 18440 | tf_op jit(solution)/shard_map/ppermute | solution.py:149
  16.1 9.0 %collective-permute-start.5 = (f32[12,128]{1,0:T(8,128)S(1)}, f32[12,128]{1,0:T(8,128)S(1)}, u32[]{:S(2)}, u32[]{:S(2)}) collective-permute-start(f32[12,128]{1,0:T(8,128)S(1)} %get-tuple-element.21), channel_id=1, source_target_pairs={{0,12},{2,14},{4,16},{6,18},{8,20},{10,22},{12,24},{14,26},{16,28}... | collective-permute-start | bytes 18440 | tf_op jit(solution)/shard_map/ppermute | solution.py:149
  17.3 11.8 %collective-permute-start.6 = (f32[12,128]{1,0:T(8,128)S(1)}, f32[12,128]{1,0:T(8,128)S(1)}, u32[]{:S(2)}, u32[]{:S(2)}) collective-permute-start(f32[12,128]{1,0:T(8,128)S(1)} %get-tuple-element.20), channel_id=1, source_target_pairs={{0,14},{2,16},{4,18},{6,20},{8,22},{10,24},{12,26},{14,28},{16,30}... | collective-permute-start | bytes 18440 | tf_op jit(solution)/shard_map/ppermute | solution.py:149
  21.7 9.2 %collective-permute-start.7 = (f32[12,128]{1,0:T(8,128)S(1)}, f32[12,128]{1,0:T(8,128)S(1)}, u32[]{:S(2)}, u32[]{:S(2)}) collective-permute-start(f32[12,128]{1,0:T(8,128)S(1)} %get-tuple-element.19), channel_id=1, source_target_pairs={{0,16},{2,18},{4,20},{6,22},{8,24},{10,26},{12,28},{14,30},{16,0},... | collective-permute-start | bytes 18440 | tf_op jit(solution)/shard_map/ppermute | solution.py:149
  22.0 8.9 %collective-permute-start.8 = (f32[12,128]{1,0:T(8,128)S(1)}, f32[12,128]{1,0:T(8,128)S(1)}, u32[]{:S(2)}, u32[]{:S(2)}) collective-permute-start(f32[12,128]{1,0:T(8,128)S(1)} %get-tuple-element.18), channel_id=1, source_target_pairs={{0,18},{2,20},{4,22},{6,24},{8,26},{10,28},{12,30},{14,0},{16,2},{... | collective-permute-start | bytes 18440 | tf_op jit(solution)/shard_map/ppermute | solution.py:149
  23.8 8.6 %collective-permute-start.9 = (f32[12,128]{1,0:T(8,128)S(1)}, f32[12,128]{1,0:T(8,128)S(1)}, u32[]{:S(2)}, u32[]{:S(2)}) collective-permute-start(f32[12,128]{1,0:T(8,128)S(1)} %get-tuple-element.17), channel_id=1, source_target_pairs={{0,20},{2,22},{4,24},{6,26},{8,28},{10,30},{12,0},{14,2},{16,4},{1... | collective-permute-start | bytes 18440 | tf_op jit(solution)/shard_map/ppermute | solution.py:149
  25.1 11.0 %collective-permute-start.10 = (f32[12,128]{1,0:T(8,128)S(1)}, f32[12,128]{1,0:T(8,128)S(1)}, u32[]{:S(2)}, u32[]{:S(2)}) collective-permute-start(f32[12,128]{1,0:T(8,128)S(1)} %get-tuple-element.16), channel_id=1, source_target_pairs={{0,22},{2,24},{4,26},{6,28},{8,30},{10,0},{12,2},{14,4},{16,6},{18... | collective-permute-start | bytes 18440 | tf_op jit(solution)/shard_map/ppermute | solution.py:149
  62.3 9.1 %collective-permute-start.15 = (f32[4,12]{1,0:T(4,128)S(1)}, f32[4,12]{1,0:T(4,128)S(1)}, u32[]{:S(2)}, u32[]{:S(2)}) collective-permute-start(f32[4,12]{1,0:T(4,128)S(1)} %bitcast.339), channel_id=1, source_target_pairs={{0,30},{2,0},{4,2},{6,4},{8,6},{10,8},{12,10},{14,12},{16,14},{18,... | collective-permute-start | bytes 584 | tf_op jit(solution)/shard_map/ppermute | solution.py:149
  68.3 8.8 %collective-permute-start.18 = (f32[4,12]{1,0:T(4,128)S(1)}, f32[4,12]{1,0:T(4,128)S(1)}, u32[]{:S(2)}, u32[]{:S(2)}) collective-permute-start(f32[4,12]{1,0:T(4,128)S(1)} %bitcast.327), channel_id=1, source_target_pairs={{0,24},{2,26},{4,28},{6,30},{8,0},{10,2},{12,4},{14,6},{16,8},{18,... | collective-permute-start | bytes 584 | tf_op jit(solution)/shard_map/ppermute | solution.py:149
  69.0 11.1 %collective-permute-start.19 = (f32[4,12]{1,0:T(4,128)S(1)}, f32[4,12]{1,0:T(4,128)S(1)}, u32[]{:S(2)}, u32[]{:S(2)}) collective-permute-start(f32[4,12]{1,0:T(4,128)S(1)} %bitcast.323), channel_id=1, source_target_pairs={{0,22},{2,24},{4,26},{6,28},{8,30},{10,0},{12,2},{14,4},{16,6},{18... | collective-permute-start | bytes 584 | tf_op jit(solution)/shard_map/ppermute | solution.py:149
  71.5 10.4 %collective-permute-start.20 = (f32[4,12]{1,0:T(4,128)S(1)}, f32[4,12]{1,0:T(4,128)S(1)}, u32[]{:S(2)}, u32[]{:S(2)}) collective-permute-start(f32[4,12]{1,0:T(4,128)S(1)} %bitcast.319), channel_id=1, source_target_pairs={{0,20},{2,22},{4,24},{6,26},{8,28},{10,30},{12,0},{14,2},{16,4},{1... | collective-permute-start | bytes 584 | tf_op jit(solution)/shard_map/ppermute | solution.py:149
  75.1 9.2 %collective-permute-start.22 = (f32[4,12]{1,0:T(4,128)S(1)}, f32[4,12]{1,0:T(4,128)S(1)}, u32[]{:S(2)}, u32[]{:S(2)}) collective-permute-start(f32[4,12]{1,0:T(4,128)S(1)} %bitcast.311), channel_id=1, source_target_pairs={{0,16},{2,18},{4,20},{6,22},{8,24},{10,26},{12,28},{14,30},{16,0},... | collective-permute-start | bytes 584 | tf_op jit(solution)/shard_map/ppermute | solution.py:149
  77.1 10.4 %collective-permute-start.23 = (f32[4,12]{1,0:T(4,128)S(1)}, f32[4,12]{1,0:T(4,128)S(1)}, u32[]{:S(2)}, u32[]{:S(2)}) collective-permute-start(f32[4,12]{1,0:T(4,128)S(1)} %bitcast.307), channel_id=1, source_target_pairs={{0,14},{2,16},{4,18},{6,20},{8,22},{10,24},{12,26},{14,28},{16,30}... | collective-permute-start | bytes 584 | tf_op jit(solution)/shard_map/ppermute | solution.py:149
  80.1 8.5 %collective-permute-start.24 = (f32[4,12]{1,0:T(4,128)S(1)}, f32[4,12]{1,0:T(4,128)S(1)}, u32[]{:S(2)}, u32[]{:S(2)}) collective-permute-start(f32[4,12]{1,0:T(4,128)S(1)} %bitcast.303), channel_id=1, source_target_pairs={{0,12},{2,14},{4,16},{6,18},{8,20},{10,22},{12,24},{14,26},{16,28}... | collective-permute-start | bytes 584 | tf_op jit(solution)/shard_map/ppermute | solution.py:149
  102.8 8.7 %collective-permute-start.39 = (f32[4,12]{1,0:T(4,128)S(1)}, f32[4,12]{1,0:T(4,128)S(1)}, u32[]{:S(2)}, u32[]{:S(2)}) collective-permute-start(f32[4,12]{1,0:T(4,128)S(1)} %bitcast.333), channel_id=1, source_target_pairs={{0,20},{2,22},{4,24},{6,26},{8,28},{10,30},{12,0},{14,2},{16,4},{1... | collective-permute-start | bytes 584 | tf_op jit(solution)/shard_map/ppermute | solution.py:149
  103.5 10.8 %collective-permute-start.40 = (f32[4,12]{1,0:T(4,128)S(1)}, f32[4,12]{1,0:T(4,128)S(1)}, u32[]{:S(2)}, u32[]{:S(2)}) collective-permute-start(f32[4,12]{1,0:T(4,128)S(1)} %bitcast.329), channel_id=1, source_target_pairs={{0,22},{2,24},{4,26},{6,28},{8,30},{10,0},{12,2},{14,4},{16,6},{18... | collective-permute-start | bytes 584 | tf_op jit(solution)/shard_map/ppermute | solution.py:149
  109.0 9.2 %collective-permute-start.43 = (f32[4,12]{1,0:T(4,128)S(1)}, f32[4,12]{1,0:T(4,128)S(1)}, u32[]{:S(2)}, u32[]{:S(2)}) collective-permute-start(f32[4,12]{1,0:T(4,128)S(1)} %bitcast.317), channel_id=1, source_target_pairs={{0,28},{2,30},{4,0},{6,2},{8,4},{10,6},{12,8},{14,10},{16,12},{18,... | collective-permute-start | bytes 584 | tf_op jit(solution)/shard_map/ppermute | solution.py:149
  115.3 12.5 %collective-permute-start.32 = (f32[4,12]{1,0:T(4,128)S(1)}, f32[4,12]{1,0:T(4,128)S(1)}, u32[]{:S(2)}, u32[]{:S(2)}) collective-permute-start(f32[4,12]{1,0:T(4,128)S(1)} %bitcast.301), channel_id=1, source_target_pairs={{0,6},{2,8},{4,10},{6,12},{8,14},{10,16},{12,18},{14,20},{16,22},{... | collective-permute-start | bytes 584 | tf_op jit(solution)/shard_map/ppermute | solution.py:149
  118.2 9.6 %collective-permute-start.33 = (f32[4,12]{1,0:T(4,128)S(1)}, f32[4,12]{1,0:T(4,128)S(1)}, u32[]{:S(2)}, u32[]{:S(2)}) collective-permute-start(f32[4,12]{1,0:T(4,128)S(1)} %bitcast.297), channel_id=1, source_target_pairs={{0,8},{2,10},{4,12},{6,14},{8,16},{10,18},{12,20},{14,22},{16,24},... | collective-permute-start | bytes 584 | tf_op jit(solution)/shard_map/ppermute | solution.py:149
  119.3 8.5 %collective-permute-start.34 = (f32[4,12]{1,0:T(4,128)S(1)}, f32[4,12]{1,0:T(4,128)S(1)}, u32[]{:S(2)}, u32[]{:S(2)}) collective-permute-start(f32[4,12]{1,0:T(4,128)S(1)} %bitcast.293), channel_id=1, source_target_pairs={{0,10},{2,12},{4,14},{6,16},{8,18},{10,20},{12,22},{14,24},{16,26}... | collective-permute-start | bytes 584 | tf_op jit(solution)/shard_map/ppermute | solution.py:149
  (68 other events, 615.3 us)

commit v6 on v4

--- a/solution.py
+++ b/solution.py
@@ -10,8 +10,12 @@
 two_pi = 6.283185307179586
 
 
+def gate_of(value):
+    return 0.5 * jnp.tanh(0.5 * value) + 0.5
+
+
 def silu_slope(value):
-    gate = jax.nn.sigmoid(value)
+    gate = gate_of(value)
     return gate * (1.0 + value * (1.0 - gate))
 
 
@@ -61,9 +65,9 @@
     seg_count, length = (samples.shape[0], samples.shape[2])
     encoded = encode(samples, fourier)
     pre_first = jnp.dot(encoded, first_weight, preferred_element_type=jnp.float32) + first_bias
-    act_first = jax.nn.silu(pre_first).astype(jnp.bfloat16)
+    act_first = (pre_first * gate_of(pre_first)).astype(jnp.bfloat16)
     pre_second = jnp.dot(act_first, second_weight, preferred_element_type=jnp.float32) + second_bias
-    act_second = jax.nn.silu(pre_second).astype(jnp.bfloat16)
+    act_second = (pre_second * gate_of(pre_second)).astype(jnp.bfloat16)
     head_raw = (
         lax.dot_general(
             act_second, head_weight, (((1,), (1,)), ((), ())), preferred_element_type=jnp.float32

time: 90.9 us -> 94.5 us (1.040)
  local copies, waits for them, and re-layouts: 17.7 us -> 22.8 us
  matrix products: 23.1 us -> 19.9 us
  other arithmetic: 11.7 us -> 13.5 us
    unnamed x36 -> x30, local copies, waits for them, and re-layouts: 1.02 us -> 5.46 us
    dot_general x1, matrix products: 0.51 us -> 4.22 us  [backward(): lax.dot_general(grad_raw, act_second, (((0,), (0,)), ((), ())), preferred...]
    dot_general x1, matrix products: 4.37 us -> 1.47 us  [network(): jnp.dot(act_first, second_weight, preferred_element_type=jnp.float32)]
    dot_general x1, matrix products: 4.72 us -> 1.89 us  [network(): jnp.dot(encoded, first_weight, preferred_element_type=jnp.float32)]
  transfers between devices with their start and end apart: 6 -> 6, of which waited for: 3 -> 3; matrix products, arithmetic and copies ran while one was open for 6% -> 8% of each run, Pallas kernels for 0% -> 0%
where the time goes in v6:
time: 94.5 us; the launch traced here: 93.6 us
  local copies, waits for them, and re-layouts  22.8 us (24%)
  waiting for transfers between devices  20 us (21%)
  matrix products  19.9 us (21%)
  starting transfers between devices  16.1 us (17%)
  other arithmetic  13.5 us (14%)
  between operations  1.13 us (1%)
    all_to_all x1, starting transfers between devices, per_device(): lax.all_to_all(outgoing, 'space', split_axis=0, concat_axis=0, tiled=True)  8.31 us
    all_to_all x1, waiting for transfers between devices, per_device(): lax.all_to_all(sendback, 'space', split_axis=1, concat_axis=1, tiled=True)  7.17 us
    all_to_all x1, waiting for transfers between devices, per_device(): lax.all_to_all(outgoing, 'space', split_axis=0, concat_axis=0, tiled=True)  7 us
    all_to_all x1, waiting for transfers between devices, per_device(): lax.all_to_all(partials, 'space', split_axis=1, concat_axis=1, tiled=True)  5.86 us
    another operation x2, other arithmetic  5.68 us
    unnamed x30, local copies, waits for them, and re-layouts  5.46 us
    dot_general x1, matrix products, backward(): jnp.dot(grad_raw, head_weight, preferred_element_type=jnp.float32)  4.73 us
    dot_general x1, matrix products, backward(): lax.dot_general(grad_raw, act_second, (((0,), (0,)), ((), ())), preferred...  4.22 us
  transfers between devices with their start and end apart: 6, of which 3 were waited for; matrix products, arithmetic and copies ran while one was open for 8% of the time, Pallas kernels for 0%

profile of v6, /device:TPU:0, one launch (start us, length us, event | category | flops | bytes accessed | tf_op | source)
XLA Modules:
  0.0 93.6 jit_solution(1870629814423336442)
XLA Ops:
  4.9 8.3 %all-to-all-start = ((f32[16,12,128]{2,1,0:T(8,128)}), f32[16,12,128]{2,1,0:T(8,128)S(1)}, u32[]{:S(2)}, u32[]{:S(2)}) async-start(f32[16,12,128]{2,1,0:T(8,128)} %fusion.21), calls=%async_computation | async-start | bytes 262144 | tf_op jit(solution)/shard_map/all_to_all | solution.py:185
  14.0 7.0 %all-to-all-done = f32[16,12,128]{2,1,0:T(8,128)S(1)} async-done(((f32[16,12,128]{2,1,0:T(8,128)}), f32[16,12,128]{2,1,0:T(8,128)S(1)}, u32[]{:S(2)}, u32[]{:S(2)}) %all-to-all-start) | async-done | bytes 98336 | tf_op jit(solution)/shard_map/all_to_all | solution.py:185
  22.4 5.6 %fusion.2 = (bf16[6144,128]{1,0:T(8,128)(2,1)S(1)}, bf16[6144,128]{1,0:T(8,128)(2,1)S(1)}) fusion(f32[128]{0:T(128)S(1)} %get-tuple-element.19, f32[6144]{0:T(1024)S(1)} %mul.334, f32[128]{0:T(128)S(1)} %get-tuple-element.20, f32[6144]{0:T(1024)S(1)} %mul.329, f32[128]{0:T(128)S(1)} %get-tuple-element.18, f32[6144]{0:T(1024)S(1)} %mul.324), kind=kLoop, calls=%fused_computation.15 | loop fusion | flops 36175872 | bytes 3220992 | tf_op jit(solution)/shard_map/convert.4
  28.1 1.9 %convolution_add_fusion.1 = f32[6144,256]{1,0:T(8,128)S(1)} fusion(f32[256]{0:T(256)S(1)} %bitcast.123, bf16[6144,128]{1,0:T(8,128)(2,1)S(1)} %get-tuple-element.13, bf16[6144,128]{1,0:T(8,128)(2,1)S(1)} %get-tuple-element.12, bf16[1,256,256]{2,1,0:T(8,128)(2,1)} %param.18), kind=kOutput, calls=%fused_computation.3 | convolution fusion | flops 813170688 | bytes 9569280 | tf_op jit(solution)/shard_map/dot_general | solution.py:67
  30.1 1.5 %convolution_add_fusion = f32[6144,256]{1,0:T(8,128)S(1)} fusion(f32[256]{0:T(256)S(1)} %bitcast.125, bf16[1,256,256]{2,1,0:T(8,128)(2,1)S(1)} %copy-done, f32[6144,256]{1,0:T(8,128)S(1)} %convolution_add_fusion.1), kind=kOutput, calls=%fused_computation.2 | convolution fusion | flops 814743552 | bytes 12715008 | tf_op jit(solution)/shard_map/dot_general | solution.py:69
  31.5 1.1 %copy-done.1 = f32[6144,256]{1,0:T(8,128)} copy-done((f32[6144,256]{1,0:T(8,128)}, f32[6144,256]{1,0:T(8,128)S(1)}, u32[]{:S(2)}) %copy-start.1) | copy-done | bytes 6291480
  32.7 2.7 %copy-done.2 = f32[6144,256]{1,0:T(8,128)} copy-done((f32[6144,256]{1,0:T(8,128)}, f32[6144,256]{1,0:T(8,128)S(1)}, u32[]{:S(2)}) %copy-start.2) | copy-done | bytes 6291480
  35.3 1.3 %convolution_add_fusion.2 = f32[6144,4]{0,1:T(4,128)S(1)} fusion(f32[4]{0:T(128)S(1)} %bitcast.129, bf16[1,4,256]{2,1,0:T(4,128)(2,1)S(1)} %copy-done.8, f32[6144,256]{1,0:T(8,128)S(1)} %convolution_add_fusion), kind=kOutput, calls=%fused_computation.6 | convolution fusion | flops 20471808 | bytes 6391824 | tf_op jit(solution)/shard_map/dot_general | solution.py:72
  36.6 0.9 reshape.238
  38.8 1.2 %multiply_reduce_fusion.1 = f32[192,3]{0,1:T(4,128)S(1)} fusion(f32[192,32]{1,0:T(8,128)S(1)} %copy.60, f32[192,32,4]{1,0,2:T(8,128)} %reshape.238), kind=kLoop, calls=%fused_computation.48 | loop fusion | flops 91584 | bytes 100608 | tf_op jit(solution)/shard_map/reduce_sum | solution.py:85
  40.8 3.5 %all-to-all-start.1 = ((f32[4,16,12]{2,0,1:T(4,128)}), f32[4,16,12]{2,0,1:T(4,128)S(1)}, u32[]{:S(2)}, u32[]{:S(2)}) async-start(f32[4,16,12]{2,0,1:T(4,128)} %copy.61), calls=%async_computation.1 | async-start | bytes 65536 | tf_op jit(solution)/shard_map/all_to_all | solution.py:204
  45.9 5.9 %all-to-all-done.1 = f32[4,16,12]{2,0,1:T(4,128)S(1)} async-done(((f32[4,16,12]{2,0,1:T(4,128)}), f32[4,16,12]{2,0,1:T(4,128)S(1)}, u32[]{:S(2)}, u32[]{:S(2)}) %all-to-all-start.1) | async-done | bytes 3104 | tf_op jit(solution)/shard_map/all_to_all | solution.py:204
  55.2 3.7 %all-to-all-start.2 = ((f32[4,16,12]{2,0,1:T(4,128)}), f32[4,16,12]{2,0,1:T(4,128)S(1)}, u32[]{:S(2)}, u32[]{:S(2)}) async-start(f32[4,16,12]{2,0,1:T(4,128)} %copy.67), calls=%async_computation.2 | async-start | bytes 65536 | tf_op jit(solution)/shard_map/all_to_all | solution.py:229
  58.9 7.2 %all-to-all-done.2 = f32[4,16,12]{2,0,1:T(4,128)S(1)} async-done(((f32[4,16,12]{2,0,1:T(4,128)}), f32[4,16,12]{2,0,1:T(4,128)S(1)}, u32[]{:S(2)}, u32[]{:S(2)}) %all-to-all-start.2) | async-done | bytes 3104 | tf_op jit(solution)/shard_map/all_to_all | solution.py:229
  67.5 2.4 %multiply_reduce_fusion = (f32[192,32]{1,0:T(8,128)}, bf16[192,32,3]{1,0,2:T(8,128)(2,1)}) fusion(f32[192,3]{0,1:T(4,128)S(1)} %bitcast.120, f32[192,32,4]{1,0,2:T(8,128)} %reshape.238, f32[192,32]{1,0:T(8,128)S(1)} %copy.60), kind=kLoop, calls=%fused_computation.47 | loop fusion | flops 178176 | bytes 162048 | tf_op jit(solution)/shard_map/reduce_sum | solution.py:106
  69.9 1.0 %copy.69 = f32[192,32]{0,1:T(8,128)S(1)} copy(f32[192,32]{1,0:T(8,128)} %get-tuple-element.9) | data formatting | bytes 49152 | tf_op jit(solution)/shard_map/reduce_sum | solution.py:106
  71.3 1.1 %concatenate.35 = bf16[6144,3]{0,1:T(4,128)(2,1)S(1)} reshape(bf16[192,32,3]{1,0,2:T(8,128)(2,1)} %get-tuple-element.10) | data formatting | bytes 73728 | tf_op jit(solution)/shard_map/concatenate | solution.py:113
  72.4 4.2 %convolution_bitcast_fusion = f32[1,2,4,128]{3,2,1,0:T(4,128)S(1)} fusion(bf16[6144,3]{0,1:T(4,128)(2,1)S(1)} %concatenate.35, bf16[6144,1]{0,1:T(2,128)(2,1)S(1)} %concatenate.34, f32[6144,256]{1,0:T(8,128)} %copy-done.2), kind=kOutput, calls=%fused_computation.41 | convolution fusion | flops 20545536 | bytes 6344704 | tf_op jit(solution)/shard_map/dot_general | solution.py:117
  76.8 4.7 %convert_reduce_fusion = (f32[256]{0:T(256)S(1)}, bf16[6144,256]{1,0:T(8,128)(2,1)S(1)}) fusion(f32[6144,256]{1,0:T(8,128)} %copy-done.2, bf16[1,4,256]{2,1,0:T(4,128)(2,1)S(1)} %copy-done.9, bf16[6144,3]{0,1:T(4,128)(2,1)S(1)} %concatenate.35, bf16[6144,1]{0,1:T(2,128)(2,1)S(1)} %concatenate.34), kind=kOutput, calls=%fused_computation.7 | convolution fusion | flops 29982464 | bytes 9489408 | tf_op jit(solution)/shard_map/dot_general | solution.py:121
  81.6 2.6 %convert_reduce_fusion.1 = (f32[256]{0:T(256)S(1)}, bf16[6144,256]{1,0:T(8,128)(2,1)S(1)}) fusion(f32[6144,256]{1,0:T(8,128)S(1)} %bitcast.115, bf16[6144,256]{1,0:T(8,128)(2,1)S(1)} %get-tuple-element.22, bf16[1,256,256]{2,1,0:T(8,128)(2,1)S(1)} %copy-done), kind=kOutput, calls=%fused_computation.8 | convolution fusion | flops 822607616 | bytes 12715008 | tf_op jit(solution)/shard_map/dot_general | solution.py:127
  84.2 1.3 %fusion.54 = f32[256,256]{1,0:T(8,128)S(1)} fusion(bf16[6144,256]{1,0:T(8,128)(2,1)S(1)} %get-tuple-element.22, f32[6144,256]{1,0:T(8,128)S(1)} %bitcast.115), kind=kOutput, calls=%fused_computation.124 | convolution fusion | flops 813170688 | bytes 9699328 | tf_op jit(solution)/shard_map/dot_general | solution.py:123
  86.8 1.0 %fusion.12 = f32[256,256]{1,0:T(8,128)S(1)} fusion(bf16[6144,256]{1,0:T(8,128)(2,1)S(1)} %get-tuple-element.24, bf16[6144,128]{1,0:T(8,128)(2,1)S(1)} %get-tuple-element.13, bf16[6144,128]{1,0:T(8,128)(2,1)S(1)} %get-tuple-element.12), kind=kOutput, calls=%fused_computation.39 | convolution fusion | flops 811597824 | bytes 6553600 | tf_op jit(solution)/shard_map/dot_general | solution.py:131
  90.4 1.6 %add_bitcast_fusion = f32[1,128,256]{2,1,0:T(8,128)} fusion(f32[128,256]{1,0:T(8,128)} %collective-permute-done.1, f32[256,256]{1,0:T(8,128)S(1)} %fusion.54, s32[]{:T(128)S(6)} %select_n.49), kind=kLoop, calls=%fused_computation.52 | loop fusion | flops 32768 | bytes 393220 | tf_op jit(solution)/shard_map/broadcast_in_dim | solution.py:270
  92.0 1.6 %add_bitcast_fusion.1 = f32[1,128,256]{2,1,0:T(8,128)} fusion(f32[128,256]{1,0:T(8,128)S(1)} %collective-permute-done, f32[256,256]{1,0:T(8,128)} %copy-done.3, s32[]{:T(128)S(6)} %select_n.49), kind=kLoop, calls=%fused_computation.53 | loop fusion | flops 32768 | bytes 393220 | tf_op jit(solution)/shard_map/broadcast_in_dim | solution.py:269
  (104 shorter events, 19.2 us)
Async XLA Ops:
  0.6 29.4 %copy-start = (bf16[1,256,256]{2,1,0:T(8,128)(2,1)S(1)}, bf16[1,256,256]{2,1,0:T(8,128)(2,1)}, u32[]{:S(2)}) copy-start(bf16[1,256,256]{2,1,0:T(8,128)(2,1)} %param.20) | copy-start | bytes 393220
  1.8 26.3 %copy-start.5 = (f32[1,256]{1,0:T(1,128)S(1)}, f32[1,256]{1,0:T(1,128)}, u32[]{:S(2)}) copy-start(f32[1,256]{1,0:T(1,128)} %param.19) | copy-start | bytes 3076
  4.9 16.1 %all-to-all-start = ((f32[16,12,128]{2,1,0:T(8,128)}), f32[16,12,128]{2,1,0:T(8,128)S(1)}, u32[]{:S(2)}, u32[]{:S(2)}) async-start(f32[16,12,128]{2,1,0:T(8,128)} %fusion.21), calls=%async_computation | async-start | bytes 262144 | tf_op jit(solution)/shard_map/all_to_all | solution.py:185
  28.1 1.9 %copy-start.6 = (f32[1,256]{1,0:T(1,128)S(1)}, f32[1,256]{1,0:T(1,128)}, u32[]{:S(2)}) copy-start(f32[1,256]{1,0:T(1,128)} %param.21) | copy-start | bytes 3076
  30.0 2.7 %copy-start.1 = (f32[6144,256]{1,0:T(8,128)}, f32[6144,256]{1,0:T(8,128)S(1)}, u32[]{:S(2)}) copy-start(f32[6144,256]{1,0:T(8,128)S(1)} %convolution_add_fusion.1) | copy-start | bytes 18874372
  30.0 5.3 %copy-start.8 = (bf16[1,4,256]{2,1,0:T(4,128)(2,1)S(1)}, bf16[1,4,256]{2,1,0:T(4,128)(2,1)}, u32[]{:S(2)}) copy-start(bf16[1,4,256]{2,1,0:T(4,128)(2,1)} %param.22) | copy-start | bytes 6148
  30.0 5.3 %copy-start.10 = (f32[1,4]{1,0:T(1,128)S(1)}, f32[1,4]{1,0:T(1,128)}, u32[]{:S(2)}) copy-start(f32[1,4]{1,0:T(1,128)} %param.23) | copy-start | bytes 52
  32.7 2.7 %copy-start.2 = (f32[6144,256]{1,0:T(8,128)}, f32[6144,256]{1,0:T(8,128)S(1)}, u32[]{:S(2)}) copy-start(f32[6144,256]{1,0:T(8,128)S(1)} %convolution_add_fusion) | copy-start | bytes 18874372
  35.3 9.0 %copy-start.7 = (f32[3,16]{1,0:T(4,128)S(1)}, f32[3,16]{1,0:T(4,128)}, u32[]{:S(2)}) copy-start(f32[3,16]{1,0:T(4,128)} %param.16) | copy-start | bytes 580
  35.3 18.5 %copy-start.4 = (s32[16,8]{0,1:T(8,128)S(1)}, s32[16,8]{0,1:T(8,128)}, u32[]{:S(2)}) copy-start(s32[16,8]{0,1:T(8,128)} %param.15) | copy-start | bytes 1540
  40.8 10.9 %all-to-all-start.1 = ((f32[4,16,12]{2,0,1:T(4,128)}), f32[4,16,12]{2,0,1:T(4,128)S(1)}, u32[]{:S(2)}, u32[]{:S(2)}) async-start(f32[4,16,12]{2,0,1:T(4,128)} %copy.61), calls=%async_computation.1 | async-start | bytes 65536 | tf_op jit(solution)/shard_map/all_to_all | solution.py:204
  55.2 10.9 %all-to-all-start.2 = ((f32[4,16,12]{2,0,1:T(4,128)}), f32[4,16,12]{2,0,1:T(4,128)S(1)}, u32[]{:S(2)}, u32[]{:S(2)}) async-start(f32[4,16,12]{2,0,1:T(4,128)} %copy.67), calls=%async_computation.2 | async-start | bytes 65536 | tf_op jit(solution)/shard_map/all_to_all | solution.py:229
  72.4 4.4 %copy-start.9 = (bf16[1,4,256]{2,1,0:T(4,128)(2,1)S(1)}, bf16[1,4,256]{2,1,0:T(4,128)(2,1)}, u32[]{:S(2)}) copy-start(bf16[1,4,256]{2,1,0:T(4,128)(2,1)} %param.22) | copy-start | bytes 6148
  72.4 9.2 %slice-start = ((s8[6291456]{0:T(1024)(128)(4,1)}), s8[4194304]{0:T(1024)(128)(4,1)S(1)}, s32[]{:S(2)}) async-start(s8[6291456]{0:T(1024)(128)(4,1)} %bitcast.114), calls=%async_computation.3 | async-start | bytes 8388608
  76.8 4.8 %slice-start.1 = ((s8[6291456]{0:T(1024)(128)(4,1)}), s8[2097152]{0:T(1024)(128)(4,1)S(1)}, s32[]{:S(2)}) async-start(s8[6291456]{0:T(1024)(128)(4,1)} %bitcast.114), calls=%async_computation.4 | async-start | bytes 4194304
  85.6 3.1 %collective-permute-start.2 = (f32[1540]{0:T(1024)S(1)}, f32[1540]{0:T(1024)S(1)}, u32[]{:S(2)}, u32[]{:S(2)}) collective-permute-start(f32[1540]{0:T(1024)S(1)} %pad_maximum_fusion.6), channel_id=1, source_target_pairs={{0,1},{1,0},{2,3},{3,2},{4,5},{5,4},{6,7},{7,6},{8,9},{9,8},{10,11... | collective-permute-start | bytes 18488 | tf_op jit(solution)/shard_map/ppermute | solution.py:249
  86.4 4.0 %collective-permute-start.1 = (f32[128,256]{1,0:T(8,128)}, f32[128,256]{1,0:T(8,128)}, u32[]{:S(2)}, u32[]{:S(2)}) collective-permute-start(f32[128,256]{1,0:T(8,128)} %constant_dynamic-slice_fusion.1), channel_id=1, source_target_pairs={{0,1},{1,0},{2,3},{3,2},{4,5},{5,4},{6,7},{7,6},{8,9},{9,8},{10,11... | collective-permute-start | bytes 393224 | tf_op jit(solution)/shard_map/ppermute | solution.py:249
  87.9 0.7 copy-start.3
  88.6 3.4 %collective-permute-start = (f32[128,256]{1,0:T(8,128)S(1)}, f32[128,256]{1,0:T(8,128)S(1)}, u32[]{:S(2)}, u32[]{:S(2)}) collective-permute-start(f32[128,256]{1,0:T(8,128)S(1)} %constant_dynamic-slice_fusion), channel_id=1, source_target_pairs={{0,1},{1,0},{2,3},{3,2},{4,5},{5,4},{6,7},{7,6},{8,9},{9,8},{10,11... | collective-permute-start | bytes 393224 | tf_op jit(solution)/shard_map/ppermute | solution.py:249

commit v7 on v6

--- a/solution.py
+++ b/solution.py
@@ -198,6 +198,7 @@
         )
     )
     seg_colour, seg_log, saved = network(samples, fourier, params)
+    saved = lax.optimization_barrier(saved)
     partials = jnp.concatenate([seg_colour.T, seg_log[None, :]], axis=0).reshape(
         4, groups, capacity
     )

time: 94.5 us -> 92.1 us (0.975)
  other arithmetic: 13.5 us -> 20.2 us
  local copies, waits for them, and re-layouts: 22.8 us -> 17.3 us
  waiting for transfers between devices: 20 us -> 14.8 us
  matrix products: 19.9 us -> 21.6 us
    concatenate x0 -> x1, other arithmetic: none -> 3.89 us  [encode(): joined = jnp.concatenate([sine, cosine], axis=-1)]
    unnamed x30 -> x42, local copies, waits for them, and re-layouts: 5.46 us -> 1.71 us
    dot_general x1, matrix products: 4.22 us -> 0.51 us  [backward(): lax.dot_general(grad_raw, act_second, (((0,), (0,)), ((), ())), preferred...]
    dot_general x1, matrix products: 1.47 us -> 4.16 us  [network(): jnp.dot(act_first, second_weight, preferred_element_type=jnp.float32)]
    all_to_all x1, waiting for transfers between devices: 7.17 us -> 4.64 us  [per_device(): lax.all_to_all(sendback, 'space', split_axis=1, concat_axis=1, tiled=True)]
    all_to_all x1, waiting for transfers between devices: 5.86 us -> 3.45 us  [per_device(): lax.all_to_all(partials, 'space', split_axis=1, concat_axis=1, tiled=True)]
    dot_general x1, matrix products: 2.64 us -> 4.61 us  [backward(): lax.dot_general(delta_second, second_weight, (((1,), (1,)), ((), ())), pr...]
    optimization_barrier x0 -> x2, local copies, waits for them, and re-layouts: none -> 1.93 us  [per_device(): saved = lax.optimization_barrier(saved)]
  transfers between devices with their start and end apart: 6 -> 6, of which waited for: 3 -> 4; matrix products, arithmetic and copies ran while one was open for 8% -> 14% of each run, Pallas kernels for 0% -> 0%
where the time goes in v7:
time: 92.1 us; the launch traced here: 91.3 us
  matrix products  21.6 us (23%)
  other arithmetic  20.2 us (22%)
  local copies, waits for them, and re-layouts  17.3 us (19%)
  starting transfers between devices  16.1 us (17%)
  waiting for transfers between devices  14.8 us (16%)
  between operations  1.13 us (1%)
    all_to_all x1, starting transfers between devices, per_device(): lax.all_to_all(outgoing, 'space', split_axis=0, concat_axis=0, tiled=True)  8.31 us
    another operation x2, other arithmetic  6.45 us
    all_to_all x1, waiting for transfers between devices, per_device(): lax.all_to_all(outgoing, 'space', split_axis=0, concat_axis=0, tiled=True)  6.12 us
    all_to_all x1, waiting for transfers between devices, per_device(): lax.all_to_all(sendback, 'space', split_axis=1, concat_axis=1, tiled=True)  4.64 us
    dot_general x1, matrix products, backward(): lax.dot_general(delta_second, second_weight, (((1,), (1,)), ((), ())), pr...  4.61 us
    dot_general x1, matrix products, backward(): jnp.dot(grad_raw, head_weight, preferred_element_type=jnp.float32)  4.58 us
    dot_general x1, matrix products, network(): jnp.dot(act_first, second_weight, preferred_element_type=jnp.float32)  4.16 us
    concatenate x1, other arithmetic, encode(): joined = jnp.concatenate([sine, cosine], axis=-1)  3.89 us
  transfers between devices with their start and end apart: 6, of which 4 were waited for; matrix products, arithmetic and copies ran while one was open for 14% of the time, Pallas kernels for 0%

profile of v7, /device:TPU:0, one launch (start us, length us, event | category | flops | bytes accessed | tf_op | source)
XLA Modules:
  0.0 91.3 jit_solution(6972858190646661483)
XLA Ops:
  1.5 0.9 %reshape.159 = f32[3,128,32]{2,1,0:T(8,128)S(1)} reshape(f32[3,16,256]{2,1,0:T(8,128)} %param.12) | data formatting | bytes 98304 | tf_op jit(solution)/shard_map/reshape | solution.py:174
  4.9 8.3 %all-to-all-start = ((f32[16,12,128]{2,1,0:T(8,128)}), f32[16,12,128]{2,1,0:T(8,128)S(1)}, u32[]{:S(2)}, u32[]{:S(2)}) async-start(f32[16,12,128]{2,1,0:T(8,128)} %fusion.20), calls=%async_computation | async-start | bytes 262144 | tf_op jit(solution)/shard_map/all_to_all | solution.py:185
  14.9 6.1 %all-to-all-done = f32[16,12,128]{2,1,0:T(8,128)S(1)} async-done(((f32[16,12,128]{2,1,0:T(8,128)}), f32[16,12,128]{2,1,0:T(8,128)S(1)}, u32[]{:S(2)}, u32[]{:S(2)}) %all-to-all-start) | async-done | bytes 98336 | tf_op jit(solution)/shard_map/all_to_all | solution.py:185
  21.3 0.9 %slice_reduce_fusion.2 = (f32[192,32]{1,0:T(8,128)S(1)}, f32[192,32]{1,0:T(8,128)S(1)}, f32[192,32]{1,0:T(8,128)S(1)}, f32[192,1,32]{2,1,0:T(1,128)S(1)}) fusion(f32[192,4,32]{2,1,0:T(4,128)S(1)} %reshape.162), kind=kLoop, calls=%fused_computation.58 | loop fusion | bytes 196608 | tf_op jit(solution)/shard_map/slice | solution.py:54
  22.5 5.6 %fusion.2 = (bf16[6144,128]{1,0:T(8,128)(2,1)S(1)}, bf16[6144,128]{1,0:T(8,128)(2,1)S(1)}) fusion(f32[128]{0:T(128)S(1)} %get-tuple-element.43, f32[6144]{0:T(1024)S(1)} %mul.325, f32[128]{0:T(128)S(1)} %get-tuple-element.44, f32[6144]{0:T(1024)S(1)} %mul.320, f32[128]{0:T(128)S(1)} %get-tuple-element.42, f32[6144]{0:T(1024)S(1)} %mul.315), kind=kLoop, calls=%fused_computation.13 | loop fusion | flops 36175872 | bytes 3220992 | tf_op jit(solution)/shard_map/convert.4
  28.2 3.5 %multiply_convert_fusion.1 = (bf16[6144,256]{1,0:T(8,128)(2,1)S(1)}, f32[6144,256]{1,0:T(8,128)}) fusion(f32[256]{0:T(256)S(1)} %bitcast.120, bf16[1,256,256]{2,1,0:T(8,128)(2,1)S(1)} %copy-done.14, bf16[6144,128]{1,0:T(8,128)(2,1)S(1)} %get-tuple-element.35, bf16[6144,128]{1,0:T(8,128)(2,1)S(1)} %get-tuple-element.34), kind=kOutput, calls=%fused_computation.10 | convolution fusion | flops 821035008 | bytes 12715008 | tf_op jit(solution)/shard_map/dot_general | solution.py:67
  31.8 4.2 %multiply_convert_fusion = (bf16[6144,256]{1,0:T(8,128)(2,1)S(1)}, f32[6144,256]{1,0:T(8,128)}) fusion(f32[256]{0:T(256)S(1)} %bitcast.121, bf16[6144,256]{1,0:T(8,128)(2,1)S(1)} %get-tuple-element.22, bf16[1,256,256]{2,1,0:T(8,128)(2,1)S(1)} %copy-done), kind=kOutput, calls=%fused_computation.9 | convolution fusion | flops 814743552 | bytes 12715008 | tf_op jit(solution)/shard_map/dot_general | solution.py:69
  35.9 0.9 convolution_add_fusion.2
  36.9 0.9 %reshape.163 = f32[192,32,4]{1,0,2:T(8,128)} reshape(f32[6144,4]{0,1:T(4,128)S(1)} %convolution_add_fusion.2) | data formatting | bytes 196608 | tf_op jit(solution)/shard_map/reshape | solution.py:77
  40.4 1.8 %multiply_reduce_fusion.1 = (f32[192,3]{0,1:T(4,128)S(1)}, f32[192,32,3]{1,0,2:T(8,128)}) fusion(f32[192,32]{1,0:T(8,128)S(1)} %copy.66, f32[192,32,4]{1,0,2:T(8,128)} %reshape.163), kind=kLoop, calls=%fused_computation.45 | loop fusion | flops 91584 | bytes 174336 | tf_op jit(solution)/shard_map/reduce_sum | solution.py:85
  43.0 3.5 %all-to-all-start.1 = ((f32[4,16,12]{2,0,1:T(4,128)}), f32[4,16,12]{2,0,1:T(4,128)S(1)}, u32[]{:S(2)}, u32[]{:S(2)}) async-start(f32[4,16,12]{2,0,1:T(4,128)} %copy.67), calls=%async_computation.1 | async-start | bytes 65536 | tf_op jit(solution)/shard_map/all_to_all | solution.py:205
  46.5 3.9 %pad_maximum_fusion = bf16[6144,256]{1,0:T(8,128)(2,1)} fusion(bf16[6144,128]{1,0:T(8,128)(2,1)} %copy-done.2, bf16[6144,128]{1,0:T(8,128)(2,1)} %copy-done.1), kind=kLoop, calls=%fused_computation.15 | loop fusion | flops 6291456 | bytes 6291456 | tf_op jit(solution)/shard_map/concatenate | solution.py:59
  50.4 3.5 %all-to-all-done.1 = f32[4,16,12]{2,0,1:T(4,128)S(1)} async-done(((f32[4,16,12]{2,0,1:T(4,128)}), f32[4,16,12]{2,0,1:T(4,128)S(1)}, u32[]{:S(2)}, u32[]{:S(2)}) %all-to-all-start.1) | async-done | bytes 3104 | tf_op jit(solution)/shard_map/all_to_all | solution.py:205
  55.9 3.7 %all-to-all-start.2 = ((f32[4,16,12]{2,0,1:T(4,128)}), f32[4,16,12]{2,0,1:T(4,128)S(1)}, u32[]{:S(2)}, u32[]{:S(2)}) async-start(f32[4,16,12]{2,0,1:T(4,128)} %copy.73), calls=%async_computation.2 | async-start | bytes 65536 | tf_op jit(solution)/shard_map/all_to_all | solution.py:230
  60.3 1.8 %copy.77 = f32[192,32,4]{0,1,2:T(8,128)} copy(f32[192,32,4]{1,0,2:T(8,128)} %reshape.163) | data formatting | bytes 196608 | tf_op jit(solution)/shard_map/optimization_barrier | solution.py:201
  62.2 4.6 %all-to-all-done.2 = f32[4,16,12]{2,0,1:T(4,128)S(1)} async-done(((f32[4,16,12]{2,0,1:T(4,128)}), f32[4,16,12]{2,0,1:T(4,128)S(1)}, u32[]{:S(2)}, u32[]{:S(2)}) %all-to-all-start.2) | async-done | bytes 3104 | tf_op jit(solution)/shard_map/all_to_all | solution.py:230
  67.5 1.8 %multiply_reduce_fusion = (f32[192,32]{1,0:T(8,128)}, bf16[192,32,3]{1,0,2:T(8,128)(2,1)S(1)}) fusion(f32[192,32,3]{1,0,2:T(8,128)} %get-tuple-element.17, f32[192,3]{0,1:T(4,128)} %bitcast.113, f32[192,32]{1,0:T(8,128)S(1)} %copy.79), kind=kLoop, calls=%fused_computation.44 | loop fusion | flops 122880 | bytes 162048 | tf_op jit(solution)/shard_map/reduce_sum | solution.py:106
  69.4 1.0 %copy.75 = f32[192,32]{0,1:T(8,128)S(1)} copy(f32[192,32]{1,0:T(8,128)} %get-tuple-element.32) | data formatting | bytes 49152 | tf_op jit(solution)/shard_map/reduce_sum | solution.py:106
  72.4 4.6 %convert_reduce_fusion = (f32[256]{0:T(256)S(1)}, bf16[6144,256]{1,0:T(8,128)(2,1)S(1)}) fusion(f32[6144,256]{1,0:T(8,128)} %get-tuple-element.20, bf16[1,4,256]{2,1,0:T(4,128)(2,1)} %param.22, bf16[6144,3]{0,1:T(4,128)(2,1)S(1)} %concatenate.35, bf16[6144,1]{0,1:T(2,128)(2,1)S(1)} %concatenate.34), kind=kOutput, calls=%fused_computation.7 | convolution fusion | flops 29982464 | bytes 9489408 | tf_op jit(solution)/shard_map/dot_general | solution.py:121
  77.0 4.6 %convert_reduce_fusion.1 = (f32[256]{0:T(256)S(1)}, bf16[6144,256]{1,0:T(8,128)(2,1)S(1)}) fusion(f32[6144,256]{1,0:T(8,128)} %get-tuple-element.21, bf16[6144,256]{1,0:T(8,128)(2,1)S(1)} %get-tuple-element.50, bf16[1,256,256]{2,1,0:T(8,128)(2,1)S(1)} %copy-done), kind=kOutput, calls=%fused_computation.8 | convolution fusion | flops 822607616 | bytes 12715008 | tf_op jit(solution)/shard_map/dot_general | solution.py:127
  81.7 1.0 %fusion.56 = f32[256,256]{1,0:T(8,128)S(1)} fusion(bf16[6144,256]{1,0:T(8,128)(2,1)S(1)} %copy-done.3, bf16[6144,256]{1,0:T(8,128)(2,1)S(1)} %get-tuple-element.52), kind=kOutput, calls=%fused_computation.124 | convolution fusion | flops 805306368 | bytes 6553600 | tf_op jit(solution)/shard_map/dot_general | solution.py:131
  83.6 1.0 %fusion.57 = f32[256,256]{1,0:T(8,128)S(1)} fusion(bf16[6144,256]{1,0:T(8,128)(2,1)S(1)} %copy-done.18, bf16[6144,256]{1,0:T(8,128)(2,1)S(1)} %get-tuple-element.50), kind=kOutput, calls=%fused_computation.125 | convolution fusion | flops 805306368 | bytes 6553600 | tf_op jit(solution)/shard_map/dot_general | solution.py:123
  88.1 1.6 %add_bitcast_fusion.1 = f32[1,128,256]{2,1,0:T(8,128)} fusion(f32[128,256]{1,0:T(8,128)S(1)} %collective-permute-done, f32[256,256]{1,0:T(8,128)} %copy-done.6, s32[]{:T(128)S(6)} %select_n.48), kind=kLoop, calls=%fused_computation.50 | loop fusion | flops 32768 | bytes 393220 | tf_op jit(solution)/shard_map/broadcast_in_dim | solution.py:270
  89.7 1.6 %add_bitcast_fusion = f32[1,128,256]{2,1,0:T(8,128)} fusion(f32[128,256]{1,0:T(8,128)S(1)} %collective-permute-done.1, f32[256,256]{1,0:T(8,128)} %copy-done.7, s32[]{:T(128)S(6)} %select_n.48), kind=kLoop, calls=%fused_computation.49 | loop fusion | flops 32768 | bytes 393220 | tf_op jit(solution)/shard_map/broadcast_in_dim | solution.py:271
  (118 shorter events, 18.8 us)
Async XLA Ops:
  0.6 31.1 %copy-start = (bf16[1,256,256]{2,1,0:T(8,128)(2,1)S(1)}, bf16[1,256,256]{2,1,0:T(8,128)(2,1)}, u32[]{:S(2)}) copy-start(bf16[1,256,256]{2,1,0:T(8,128)(2,1)} %param.20) | copy-start | bytes 393220
  2.5 25.7 %copy-start.14 = (bf16[1,256,256]{2,1,0:T(8,128)(2,1)S(1)}, bf16[1,256,256]{2,1,0:T(8,128)(2,1)}, u32[]{:S(2)}) copy-start(bf16[1,256,256]{2,1,0:T(8,128)(2,1)} %param.18) | copy-start | bytes 393220
  2.5 25.7 %copy-start.15 = (f32[1,256]{1,0:T(1,128)S(1)}, f32[1,256]{1,0:T(1,128)}, u32[]{:S(2)}) copy-start(f32[1,256]{1,0:T(1,128)} %param.19) | copy-start | bytes 3076
  3.9 11.0 %copy-start.12 = (s32[128]{0:T(128)}, s32[128]{0:T(128)S(1)}, u32[]{:S(2)}) copy-start(s32[128]{0:T(128)S(1)} %multiply_add_fusion.2) | copy-start | bytes 1540
  4.9 16.1 %all-to-all-start = ((f32[16,12,128]{2,1,0:T(8,128)}), f32[16,12,128]{2,1,0:T(8,128)S(1)}, u32[]{:S(2)}, u32[]{:S(2)}) async-start(f32[16,12,128]{2,1,0:T(8,128)} %fusion.20), calls=%async_computation | async-start | bytes 262144 | tf_op jit(solution)/shard_map/all_to_all | solution.py:185
  28.1 3.6 %copy-start.1 = (bf16[6144,128]{1,0:T(8,128)(2,1)}, bf16[6144,128]{1,0:T(8,128)(2,1)S(1)}, u32[]{:S(2)}) copy-start(bf16[6144,128]{1,0:T(8,128)(2,1)S(1)} %get-tuple-element.34) | copy-start | bytes 4718596
  28.1 3.6 %copy-start.2 = (bf16[6144,128]{1,0:T(8,128)(2,1)}, bf16[6144,128]{1,0:T(8,128)(2,1)S(1)}, u32[]{:S(2)}) copy-start(bf16[6144,128]{1,0:T(8,128)(2,1)S(1)} %get-tuple-element.35) | copy-start | bytes 4718596
  28.2 3.6 %copy-start.16 = (f32[1,256]{1,0:T(1,128)S(1)}, f32[1,256]{1,0:T(1,128)}, u32[]{:S(2)}) copy-start(f32[1,256]{1,0:T(1,128)} %param.21) | copy-start | bytes 3076
  31.7 4.2 %copy-start.17 = (bf16[6144,256]{1,0:T(8,128)(2,1)}, bf16[6144,256]{1,0:T(8,128)(2,1)S(1)}, u32[]{:S(2)}) copy-start(bf16[6144,256]{1,0:T(8,128)(2,1)S(1)} %get-tuple-element.22) | copy-start | bytes 9437188
  31.7 4.2 %copy-start.10 = (bf16[1,4,256]{2,1,0:T(4,128)(2,1)S(1)}, bf16[1,4,256]{2,1,0:T(4,128)(2,1)}, u32[]{:S(2)}) copy-start(bf16[1,4,256]{2,1,0:T(4,128)(2,1)} %param.22) | copy-start | bytes 6148
  31.8 4.2 %copy-start.11 = (f32[1,4]{1,0:T(1,128)S(1)}, f32[1,4]{1,0:T(1,128)}, u32[]{:S(2)}) copy-start(f32[1,4]{1,0:T(1,128)} %param.23) | copy-start | bytes 52
  38.7 0.6 copy-start.5
  43.0 10.9 %all-to-all-start.1 = ((f32[4,16,12]{2,0,1:T(4,128)}), f32[4,16,12]{2,0,1:T(4,128)S(1)}, u32[]{:S(2)}, u32[]{:S(2)}) async-start(f32[4,16,12]{2,0,1:T(4,128)} %copy.67), calls=%async_computation.1 | async-start | bytes 65536 | tf_op jit(solution)/shard_map/all_to_all | solution.py:205
  46.5 7.5 %copy-start.13 = (s32[128]{0:T(128)S(1)}, s32[128]{0:T(128)}, u32[]{:S(2)}) copy-start(s32[128]{0:T(128)} %copy-done.12) | copy-start | bytes 1540
  46.5 8.1 %copy-start.8 = (s32[16,8]{0,1:T(8,128)S(1)}, s32[16,8]{0,1:T(8,128)}, u32[]{:S(2)}) copy-start(s32[16,8]{0,1:T(8,128)} %param.15) | copy-start | bytes 1540
  55.9 10.9 %all-to-all-start.2 = ((f32[4,16,12]{2,0,1:T(4,128)}), f32[4,16,12]{2,0,1:T(4,128)S(1)}, u32[]{:S(2)}, u32[]{:S(2)}) async-start(f32[4,16,12]{2,0,1:T(4,128)} %copy.73), calls=%async_computation.2 | async-start | bytes 65536 | tf_op jit(solution)/shard_map/all_to_all | solution.py:230
  60.2 7.2 %copy-start.4 = (f32[192,32]{0,1:T(8,128)}, f32[192,32]{0,1:T(8,128)S(1)}, u32[]{:S(2)}) copy-start(f32[192,32]{0,1:T(8,128)S(1)} %get-tuple-element.18) | copy-start | bytes 73732
  77.0 4.6 %copy-start.3 = (bf16[6144,256]{1,0:T(8,128)(2,1)S(1)}, bf16[6144,256]{1,0:T(8,128)(2,1)}, u32[]{:S(2)}) copy-start(bf16[6144,256]{1,0:T(8,128)(2,1)} %pad_maximum_fusion) | copy-start | bytes 9437188
  81.7 1.9 %copy-start.18 = (bf16[6144,256]{1,0:T(8,128)(2,1)S(1)}, bf16[6144,256]{1,0:T(8,128)(2,1)}, u32[]{:S(2)}) copy-start(bf16[6144,256]{1,0:T(8,128)(2,1)} %copy-done.17) | copy-start | bytes 9437188
  82.7 1.9 %copy-start.6 = (f32[256,256]{1,0:T(8,128)}, f32[256,256]{1,0:T(8,128)S(1)}, u32[]{:S(2)}) copy-start(f32[256,256]{1,0:T(8,128)S(1)} %fusion.56) | copy-start | bytes 786436
  83.4 4.7 %collective-permute-start = (f32[128,256]{1,0:T(8,128)}, f32[128,256]{1,0:T(8,128)S(1)}, u32[]{:S(2)}, u32[]{:S(2)}) collective-permute-start(f32[128,256]{1,0:T(8,128)} %constant_dynamic-slice_fusion), channel_id=1, source_target_pairs={{0,1},{1,0},{2,3},{3,2},{4,5},{5,4},{6,7},{7,6},{8,9},{9,8},{10,11... | collective-permute-start | bytes 393224 | tf_op jit(solution)/shard_map/ppermute | solution.py:250
  84.6 1.0 %copy-start.7 = (f32[256,256]{1,0:T(8,128)}, f32[256,256]{1,0:T(8,128)S(1)}, u32[]{:S(2)}) copy-start(f32[256,256]{1,0:T(8,128)S(1)} %fusion.57) | copy-start | bytes 786436
  85.1 1.3 %collective-permute-start.2 = (f32[1540]{0:T(1024)S(1)}, f32[1540]{0:T(1024)S(1)}, u32[]{:S(2)}, u32[]{:S(2)}) collective-permute-start(f32[1540]{0:T(1024)S(1)} %pad_maximum_fusion.4), channel_id=1, source_target_pairs={{0,1},{1,0},{2,3},{3,2},{4,5},{5,4},{6,7},{7,6},{8,9},{9,8},{10,11... | collective-permute-start | bytes 18488 | tf_op jit(solution)/shard_map/ppermute | solution.py:250
  85.6 4.1 %collective-permute-start.1 = (f32[128,256]{1,0:T(8,128)S(1)}, f32[128,256]{1,0:T(8,128)S(1)}, u32[]{:S(2)}, u32[]{:S(2)}) collective-permute-start(f32[128,256]{1,0:T(8,128)S(1)} %constant_dynamic-slice_fusion.1), channel_id=1, source_target_pairs={{0,1},{1,0},{2,3},{3,2},{4,5},{5,4},{6,7},{7,6},{8,9},{9,8},{10,11... | collective-permute-start | bytes 393224 | tf_op jit(solution)/shard_map/ppermute | solution.py:250
  (1 other events, 0.6 us)

commit v8 on v6

--- a/solution.py
+++ b/solution.py
@@ -2,6 +2,8 @@
 import jax.numpy as jnp
 from jax import lax
 from jax.sharding import PartitionSpec as P
+from jax.experimental import pallas as pl
+from jax.experimental.pallas import tpu as pltpu
 
 SEG_LEN = 32
 SEGS = 8
@@ -20,7 +22,7 @@
 
 
 def turn_sin_cos(turns):
-    quarter = jnp.round(turns * 4.0)
+    quarter = jnp.floor(turns * 4.0 + 0.5)
     angle = (turns - quarter * 0.25) * two_pi
     square = angle * angle
     sine = angle * (
@@ -84,25 +86,69 @@
     weight = enter_light - leave_light
     seg_colour = jnp.sum(weight[..., None] * colour, axis=1)
     seg_log = -inclusive[:, -1]
-    saved = (
-        encoded,
-        pre_first,
-        act_first,
-        pre_second,
-        act_second,
-        head_raw,
-        colour,
-        weight,
-        leave_light,
-    )
+    saved = (head_raw, colour, weight, leave_light)
     return (seg_colour, seg_log, saved)
 
 
-def backward(samples, params, saved, up_colour, up_log):
+def backward_kernel(
+    place_ref, fourier_ref, w1_ref, b1_ref, w2_ref, b2_ref, wh_ref, raw_ref,
+    g1_ref, gb1_ref, g2_ref, gb2_ref, gh_ref,
+):
+    @pl.when(pl.program_id(0) == 0)
+    def _():
+        g1_ref[...] = jnp.zeros_like(g1_ref)
+        gb1_ref[...] = jnp.zeros_like(gb1_ref)
+        g2_ref[...] = jnp.zeros_like(g2_ref)
+        gb2_ref[...] = jnp.zeros_like(gb2_ref)
+        gh_ref[...] = jnp.zeros_like(gh_ref)
+
+    place = place_ref[...]
+    fourier = fourier_ref[...]
+    turns = (
+        place[:, 0:1] * fourier[0:1, :]
+        + place[:, 1:2] * fourier[1:2, :]
+        + place[:, 2:3] * fourier[2:3, :]
+    )
+    sine, cosine = turn_sin_cos(turns)
+    encoded = jnp.concatenate([sine, cosine], axis=1).astype(jnp.bfloat16)
+    pre_first = jnp.dot(encoded, w1_ref[...], preferred_element_type=jnp.float32) + b1_ref[...]
+    gate_first = gate_of(pre_first)
+    act_first = (pre_first * gate_first).astype(jnp.bfloat16)
+    pre_second = jnp.dot(act_first, w2_ref[...], preferred_element_type=jnp.float32) + b2_ref[...]
+    gate_second = gate_of(pre_second)
+    act_second = (pre_second * gate_second).astype(jnp.bfloat16).astype(jnp.float32)
+    raw = raw_ref[...].astype(jnp.float32)
+    head = wh_ref[...].astype(jnp.float32)
+    back_second = (
+        raw[:, 0:1] * head[0:1, :]
+        + raw[:, 1:2] * head[1:2, :]
+        + raw[:, 2:3] * head[2:3, :]
+        + raw[:, 3:4] * head[3:4, :]
+    )
+    slope_second = gate_second * (1.0 + pre_second * (1.0 - gate_second))
+    delta_second = (back_second * slope_second).astype(jnp.bfloat16)
+    g2_ref[...] += lax.dot_general(
+        act_first, delta_second, (((0,), (0,)), ((), ())), preferred_element_type=jnp.float32
+    )
+    gb2_ref[...] += jnp.sum(delta_second.astype(jnp.float32), axis=0, keepdims=True)
+    back_first = lax.dot_general(
+        delta_second, w2_ref[...], (((1,), (1,)), ((), ())), preferred_element_type=jnp.float32
+    )
+    slope_first = gate_first * (1.0 + pre_first * (1.0 - gate_first))
+    delta_first = (back_first * slope_first).astype(jnp.bfloat16)
+    g1_ref[...] += lax.dot_general(
+        encoded, delta_first, (((0,), (0,)), ((), ())), preferred_element_type=jnp.float32
+    )
+    gb1_ref[...] += jnp.sum(delta_first.astype(jnp.float32), axis=0, keepdims=True)
+    gh_ref[...] += jnp.concatenate(
+        [jnp.sum(raw[:, c : c + 1] * act_second, axis=0, keepdims=True) for c in range(4)],
+        axis=0,
+    )
+
+
+def backward(samples, fourier, params, saved, up_colour, up_log):
     first_weight, first_bias, second_weight, second_bias, head_weight, head_bias = params
-    encoded, pre_first, act_first, pre_second, act_second, head_raw, colour, weight, leave_light = (
-        saved
-    )
+    head_raw, colour, weight, leave_light = saved
     energy = jnp.sum(colour * up_colour[:, None, :], axis=-1)
     spent = weight * energy
     remaining = jnp.sum(spent, axis=1, keepdims=True) - jnp.cumsum(spent, axis=1)
@@ -114,25 +160,53 @@
         .reshape(-1, 4)
         .astype(jnp.bfloat16)
     )
-    grad_head = lax.dot_general(
-        grad_raw, act_second, (((0,), (0,)), ((), ())), preferred_element_type=jnp.float32
-    )
     grad_head_bias = jnp.sum(grad_raw.astype(jnp.float32), axis=0)
-    back_second = jnp.dot(grad_raw, head_weight, preferred_element_type=jnp.float32)
-    delta_second = (back_second * silu_slope(pre_second)).astype(jnp.bfloat16)
-    grad_second = lax.dot_general(
-        act_first, delta_second, (((0,), (0,)), ((), ())), preferred_element_type=jnp.float32
-    )
-    grad_second_bias = jnp.sum(delta_second.astype(jnp.float32), axis=0)
-    back_first = lax.dot_general(
-        delta_second, second_weight, (((1,), (1,)), ((), ())), preferred_element_type=jnp.float32
-    )
-    delta_first = (back_first * silu_slope(pre_first)).astype(jnp.bfloat16)
-    grad_first = lax.dot_general(
-        encoded, delta_first, (((0,), (0,)), ((), ())), preferred_element_type=jnp.float32
-    )
-    grad_first_bias = jnp.sum(delta_first.astype(jnp.float32), axis=0)
-    return (grad_first, grad_second, grad_head, grad_first_bias, grad_second_bias, grad_head_bias)
+    rows = grad_raw.shape[0]
+    block = 512
+    place = jnp.transpose(samples[:, :3, :], (0, 2, 1)).reshape(rows, 3)
+    features = first_weight.shape[0]
+    hidden = first_weight.shape[1]
+    whole = lambda i: (0, 0)
+    outs = pl.pallas_call(
+        backward_kernel,
+        grid=(rows // block,),
+        in_specs=[
+            pl.BlockSpec((block, 3), lambda i: (i, 0)),
+            pl.BlockSpec(fourier.shape, whole),
+            pl.BlockSpec(first_weight.shape, whole),
+            pl.BlockSpec((1, hidden), whole),
+            pl.BlockSpec(second_weight.shape, whole),
+            pl.BlockSpec((1, hidden), whole),
+            pl.BlockSpec(head_weight.shape, whole),
+            pl.BlockSpec((block, 4), lambda i: (i, 0)),
+        ],
+        out_specs=[
+            pl.BlockSpec((features, hidden), whole),
+            pl.BlockSpec((1, hidden), whole),
+            pl.BlockSpec((hidden, hidden), whole),
+            pl.BlockSpec((1, hidden), whole),
+            pl.BlockSpec((4, hidden), whole),
+        ],
+        out_shape=[
+            jax.ShapeDtypeStruct((features, hidden), jnp.float32),
+            jax.ShapeDtypeStruct((1, hidden), jnp.float32),
+            jax.ShapeDtypeStruct((hidden, hidden), jnp.float32),
+            jax.ShapeDtypeStruct((1, hidden), jnp.float32),
+            jax.ShapeDtypeStruct((4, hidden), jnp.float32),
+        ],
+        compiler_params=pltpu.CompilerParams(dimension_semantics=("arbitrary",)),
+    )(
+        place,
+        fourier,
+        first_weight,
+        first_bias.reshape(1, hidden),
+        second_weight,
+        second_bias.reshape(1, hidden),
+        head_weight,
+        grad_raw,
+    )
+    grad_first, bias_first, grad_second, bias_second, grad_head = outs
+    return (grad_first, grad_second, grad_head, bias_first[0], bias_second[0], grad_head_bias)
 
 
 def composite(seg_colour, seg_log, depth_rank, pixel_rows):
@@ -228,7 +302,7 @@
     sendback = sendback.reshape(4, groups, capacity)
     received = lax.all_to_all(sendback, "space", split_axis=1, concat_axis=1, tiled=True)
     received = received.reshape(4, slot_count).T
-    totals = backward(samples, params, saved, received[:, :3], received[:, 3])
+    totals = backward(samples, fourier, params, saved, received[:, :3], received[:, 3])
     grad_first, grad_second, grad_head, bias_first, bias_second, bias_head = totals
     replicas = lax.axis_size("ray")
     small = jnp.concatenate(

time: 94.5 us -> 94.9 us (level)
  Pallas kernels: 0 us -> 21.6 us
  matrix products: 19.9 us -> 7.97 us
  local copies, waits for them, and re-layouts: 22.8 us -> 16.7 us
  other arithmetic: 13.5 us -> 11.8 us
  waiting for transfers between devices: 20 us -> 19 us
    pallas_call x0 -> x1, Pallas kernels: none -> 21.6 us  [backward(): pl.pallas_call(backward_kernel, grid=(rows // block,), in_specs=[pl.Block...]
    dot_general x6 -> x0, matrix products: 15.4 us -> none  [the longest x1 4.73 us: backward(): jnp.dot(grad_raw, head_weight, preferred_element_type=jnp.float32)]
    unnamed x30 -> x20, local copies, waits for them, and re-layouts: 5.46 us -> 1.64 us
    dot_general x1, matrix products: 1.28 us -> 3.81 us  [network(): lax.dot_general(act_second, head_weight, (((1,), (1,)), ((), ())), prefer...]
    transpose x0 -> x2, local copies, waits for them, and re-layouts: none -> 2.5 us  [backward(): place = jnp.transpose(samples[:, :3, :], (0, 2, 1)).reshape(rows, 3)]
    all_to_all x1, waiting for transfers between devices: 7.17 us -> 4.86 us  [per_device(): lax.all_to_all(sendback, 'space', split_axis=1, concat_axis=1, tiled=True)]
    reduce_sum x1, other arithmetic: 2.43 us -> 0.16 us  [backward(): energy = jnp.sum(colour * up_colour[:, None, :], axis=-1)]
    mul x2, local copies, waits for them, and re-layouts: 1.5 us -> 0.16 us  [composite(): up_colour = prefix[..., None] * pixel_rows[:, None, :]]
  transfers between devices with their start and end apart: 6 -> 6, of which waited for: 3 -> 3; matrix products, arithmetic and copies ran while one was open for 8% -> 10% of each run, Pallas kernels for 0% -> 0%
where the time goes in v8:
time: 94.9 us; the launch traced here: 94.2 us
  Pallas kernels  21.6 us (23%)
  waiting for transfers between devices  19 us (20%)
  local copies, waits for them, and re-layouts  16.7 us (18%)
  starting transfers between devices  16 us (17%)
  other arithmetic  11.8 us (12%)
  matrix products  7.97 us (8%)
  between operations  1.05 us (1%)
    pallas_call x1, Pallas kernels, backward(): pl.pallas_call(backward_kernel, grid=(rows // block,), in_specs=[pl.Block...  21.6 us
    all_to_all x1, starting transfers between devices, per_device(): lax.all_to_all(outgoing, 'space', split_axis=0, concat_axis=0, tiled=True)  8.31 us
    all_to_all x1, waiting for transfers between devices, per_device(): lax.all_to_all(partials, 'space', split_axis=1, concat_axis=1, tiled=True)  7.17 us
    all_to_all x1, waiting for transfers between devices, per_device(): lax.all_to_all(outgoing, 'space', split_axis=0, concat_axis=0, tiled=True)  7 us
    another operation x2, other arithmetic  5.79 us
    all_to_all x1, waiting for transfers between devices, per_device(): lax.all_to_all(sendback, 'space', split_axis=1, concat_axis=1, tiled=True)  4.86 us
    dot_general x1, matrix products, network(): lax.dot_general(act_second, head_weight, (((1,), (1,)), ((), ())), prefer...  3.81 us
    all_to_all x1, starting transfers between devices, per_device(): lax.all_to_all(partials, 'space', split_axis=1, concat_axis=1, tiled=True)  3.5 us
  transfers between devices with their start and end apart: 6, of which 3 were waited for; matrix products, arithmetic and copies ran while one was open for 10% of the time, Pallas kernels for 0%

profile of v8, /device:TPU:0, one launch (start us, length us, event | category | flops | bytes accessed | tf_op | source)
XLA Modules:
  0.0 94.2 jit_solution(7181730095076006759)
XLA Ops:
  0.6 0.8 copy.81
  2.0 0.9 reshape.237
  3.0 0.8 reshape.238
  4.0 0.9 fusion.18
  4.9 8.3 %all-to-all-start = ((f32[16,12,128]{2,1,0:T(8,128)}), f32[16,12,128]{2,1,0:T(8,128)S(1)}, u32[]{:S(2)}, u32[]{:S(2)}) async-start(f32[16,12,128]{2,1,0:T(8,128)} %fusion.18), calls=%async_computation | async-start | bytes 262144 | tf_op jit(solution)/shard_map/all_to_all | solution.py:259
  13.2 0.8 slice_bitcast_fusion.4
  14.0 7.0 %all-to-all-done = f32[16,12,128]{2,1,0:T(8,128)S(1)} async-done(((f32[16,12,128]{2,1,0:T(8,128)}), f32[16,12,128]{2,1,0:T(8,128)S(1)}, u32[]{:S(2)}, u32[]{:S(2)}) %all-to-all-start) | async-done | bytes 98336 | tf_op jit(solution)/shard_map/all_to_all | solution.py:259
  21.2 0.9 %slice_reduce_fusion.2 = (f32[192,32]{1,0:T(8,128)S(1)}, f32[192,32]{1,0:T(8,128)S(1)}, f32[192,32]{1,0:T(8,128)S(1)}, f32[192,1,32]{2,1,0:T(1,128)S(1)}) fusion(f32[192,4,32]{2,1,0:T(4,128)S(1)} %reshape.240), kind=kLoop, calls=%fused_computation.51 | loop fusion | bytes 196608 | tf_op jit(solution)/shard_map/slice | solution.py:56
  22.4 5.8 %fusion = (bf16[6144,128]{1,0:T(8,128)(2,1)S(1)}, bf16[6144,128]{1,0:T(8,128)(2,1)S(1)}) fusion(f32[128]{0:T(128)S(1)} %get-tuple-element.32, f32[6144]{0:T(1024)S(1)} %mul.312, f32[128]{0:T(128)S(1)} %get-tuple-element.31, f32[6144]{0:T(1024)S(1)} %mul.307, f32[128]{0:T(128)S(1)} %get-tuple-element.30, f32[6144]{0:T(1024)S(1)} %mul.302), kind=kLoop, calls=%fused_computation.7 | loop fusion | flops 36962304 | bytes 3220992 | tf_op jit(solution)/shard_map/convert.4
  28.2 2.9 %multiply_convert_fusion.1 = bf16[6144,256]{1,0:T(8,128)(2,1)} fusion(bf16[6144,128]{1,0:T(8,128)(2,1)S(1)} %get-tuple-element.25, bf16[6144,128]{1,0:T(8,128)(2,1)S(1)} %get-tuple-element.24, f32[256]{0:T(256)S(1)} %bitcast.129, bf16[1,256,256]{2,1,0:T(8,128)(2,1)S(1)} %copy-done), kind=kOutput, calls=%fused_computation.4 | convolution fusion | flops 821035008 | bytes 6423552 | tf_op jit(solution)/shard_map/dot_general | solution.py:69
  31.2 3.8 %convolution_add_fusion.2 = f32[6144,4]{0,1:T(4,128)S(1)} fusion(bf16[6144,256]{1,0:T(8,128)(2,1)} %multiply_convert_fusion.1, f32[256]{0:T(256)S(1)} %bitcast.130, f32[4]{0:T(128)S(1)} %bitcast.131, bf16[1,4,256]{2,1,0:T(4,128)(2,1)S(1)} %copy-done.3, bf16[1,256,256]{2,1,0:T(8,128)(2,1)S(1)} %copy-done.1), kind=kOutput, calls=%fused_computation.2 | convolution fusion | flops 827351040 | bytes 3378192 | tf_op jit(solution)/shard_map/dot_general | solution.py:74
  36.6 3.5 %all-to-all-start.1 = ((f32[4,16,12]{2,0,1:T(4,128)}), f32[4,16,12]{2,0,1:T(4,128)S(1)}, u32[]{:S(2)}, u32[]{:S(2)}) async-start(f32[4,16,12]{2,0,1:T(4,128)} %copy.90), calls=%async_computation.1 | async-start | bytes 65536 | tf_op jit(solution)/shard_map/all_to_all | solution.py:278
  40.3 7.2 %all-to-all-done.1 = f32[4,16,12]{2,0,1:T(4,128)S(1)} async-done(((f32[4,16,12]{2,0,1:T(4,128)}), f32[4,16,12]{2,0,1:T(4,128)S(1)}, u32[]{:S(2)}, u32[]{:S(2)}) %all-to-all-start.1) | async-done | bytes 3104 | tf_op jit(solution)/shard_map/all_to_all | solution.py:278
  49.5 3.5 %all-to-all-start.2 = ((f32[4,16,12]{2,0,1:T(4,128)}), f32[4,16,12]{2,0,1:T(4,128)S(1)}, u32[]{:S(2)}, u32[]{:S(2)}) async-start(f32[4,16,12]{2,0,1:T(4,128)} %copy.96), calls=%async_computation.2 | async-start | bytes 65536 | tf_op jit(solution)/shard_map/all_to_all | solution.py:303
  53.1 2.5 %copy.86 = f32[192,32,3]{2,1,0:T(8,128)} copy(f32[192,32,3]{1,2,0:T(4,128)S(1)} %slice_bitcast_fusion) | data formatting | bytes 147456 | tf_op jit(solution)/shard_map/transpose | solution.py:166
  55.6 4.9 %all-to-all-done.2 = f32[4,16,12]{2,0,1:T(4,128)S(1)} async-done(((f32[4,16,12]{2,0,1:T(4,128)}), f32[4,16,12]{2,0,1:T(4,128)S(1)}, u32[]{:S(2)}, u32[]{:S(2)}) %all-to-all-start.2) | async-done | bytes 3104 | tf_op jit(solution)/shard_map/all_to_all | solution.py:303
  61.5 1.6 %copy.101.raw_ref = bf16[6144,4]{1,0:T(8,128)(2,1)} copy(bf16[6144,4]{0,1:T(4,128)(2,1)S(1)} %get-tuple-element.20) | data formatting | bytes 98304 | tf_op jit(solution)/shard_map/concatenate | solution.py:159
  63.1 21.6 %shard_map.163 = (f32[256,256]{1,0:T(8,128)}, f32[1,256]{1,0:T(1,128)}, f32[256,256]{1,0:T(8,128)}, f32[1,256]{1,0:T(1,128)}, f32[4,256]{1,0:T(4,128)}) custom-call(f32[6144,3]{1,0:T(8,128)} %bitcast.109, f32[3,128]{1,0:T(4,128)} %fourier_ref.1, bf16[256,256]{1,0:T(8,128)(2,1)} %bitcast.112, f32[1,256]{1,0:T(1,128)} %b1_ref.1, bf16[256,256]{1,0:T(8,128)(2,1)} %bitcast.113, ...), custom_call_target="tpu_custom_call" | custom-call | tf_op jit(solution)/shard_map/pallas_call | solution.py:170
  85.5 0.7 pad_maximum_fusion.3
  86.2 0.9 constant_dynamic-slice_fusion.1
  87.6 0.9 constant_dynamic-slice_fusion
  88.7 0.7 fusion.51
  91.1 1.6 %add_bitcast_fusion = f32[1,128,256]{2,1,0:T(8,128)} fusion(f32[128,256]{1,0:T(8,128)S(1)} %collective-permute-done.1, f32[256,256]{1,0:T(8,128)} %get-tuple-element.12, s32[]{:T(128)S(6)} %select_n.49), kind=kLoop, calls=%fused_computation.42 | loop fusion | flops 32768 | bytes 393220 | tf_op jit(solution)/shard_map/broadcast_in_dim | solution.py:344
  92.6 1.6 %add_bitcast_fusion.1 = f32[1,128,256]{2,1,0:T(8,128)} fusion(f32[128,256]{1,0:T(8,128)S(1)} %collective-permute-done, f32[256,256]{1,0:T(8,128)} %get-tuple-element.11, s32[]{:T(128)S(6)} %select_n.49), kind=kLoop, calls=%fused_computation.43 | loop fusion | flops 32768 | bytes 393220 | tf_op jit(solution)/shard_map/broadcast_in_dim | solution.py:343
  (91 shorter events, 9.2 us)
Async XLA Ops:
  1.8 26.4 %copy-start = (bf16[1,256,256]{2,1,0:T(8,128)(2,1)S(1)}, bf16[1,256,256]{2,1,0:T(8,128)(2,1)}, u32[]{:S(2)}) copy-start(bf16[1,256,256]{2,1,0:T(8,128)(2,1)} %param.18) | copy-start | bytes 393220
  1.8 26.4 %copy-start.5 = (f32[1,256]{1,0:T(1,128)S(1)}, f32[1,256]{1,0:T(1,128)}, u32[]{:S(2)}) copy-start(f32[1,256]{1,0:T(1,128)} %b1_ref.1) | copy-start | bytes 3076
  4.9 16.1 %all-to-all-start = ((f32[16,12,128]{2,1,0:T(8,128)}), f32[16,12,128]{2,1,0:T(8,128)S(1)}, u32[]{:S(2)}, u32[]{:S(2)}) async-start(f32[16,12,128]{2,1,0:T(8,128)} %fusion.18), calls=%async_computation | async-start | bytes 262144 | tf_op jit(solution)/shard_map/all_to_all | solution.py:259
  28.2 2.9 %copy-start.1 = (bf16[1,256,256]{2,1,0:T(8,128)(2,1)S(1)}, bf16[1,256,256]{2,1,0:T(8,128)(2,1)}, u32[]{:S(2)}) copy-start(bf16[1,256,256]{2,1,0:T(8,128)(2,1)} %param.20) | copy-start | bytes 393220
  28.2 2.9 %copy-start.3 = (bf16[1,4,256]{2,1,0:T(4,128)(2,1)S(1)}, bf16[1,4,256]{2,1,0:T(4,128)(2,1)}, u32[]{:S(2)}) copy-start(bf16[1,4,256]{2,1,0:T(4,128)(2,1)} %param.22) | copy-start | bytes 6148
  28.2 2.9 %copy-start.6 = (f32[1,256]{1,0:T(1,128)S(1)}, f32[1,256]{1,0:T(1,128)}, u32[]{:S(2)}) copy-start(f32[1,256]{1,0:T(1,128)} %b2_ref.1) | copy-start | bytes 3076
  28.2 2.9 %copy-start.7 = (f32[1,4]{1,0:T(1,128)S(1)}, f32[1,4]{1,0:T(1,128)}, u32[]{:S(2)}) copy-start(f32[1,4]{1,0:T(1,128)} %param.23) | copy-start | bytes 52
  31.1 9.0 %copy-start.4 = (f32[3,16]{1,0:T(4,128)S(1)}, f32[3,16]{1,0:T(4,128)}, u32[]{:S(2)}) copy-start(f32[3,16]{1,0:T(4,128)} %param.16) | copy-start | bytes 580
  31.1 17.0 %copy-start.2 = (s32[16,8]{0,1:T(8,128)S(1)}, s32[16,8]{0,1:T(8,128)}, u32[]{:S(2)}) copy-start(s32[16,8]{0,1:T(8,128)} %param.15) | copy-start | bytes 1540
  36.6 10.9 %all-to-all-start.1 = ((f32[4,16,12]{2,0,1:T(4,128)}), f32[4,16,12]{2,0,1:T(4,128)S(1)}, u32[]{:S(2)}, u32[]{:S(2)}) async-start(f32[4,16,12]{2,0,1:T(4,128)} %copy.90), calls=%async_computation.1 | async-start | bytes 65536 | tf_op jit(solution)/shard_map/all_to_all | solution.py:278
  49.5 10.9 %all-to-all-start.2 = ((f32[4,16,12]{2,0,1:T(4,128)}), f32[4,16,12]{2,0,1:T(4,128)S(1)}, u32[]{:S(2)}, u32[]{:S(2)}) async-start(f32[4,16,12]{2,0,1:T(4,128)} %copy.96), calls=%async_computation.2 | async-start | bytes 65536 | tf_op jit(solution)/shard_map/all_to_all | solution.py:303
  86.2 2.5 %collective-permute-start.2 = (f32[1540]{0:T(1024)S(1)}, f32[1540]{0:T(1024)S(1)}, u32[]{:S(2)}, u32[]{:S(2)}) collective-permute-start(f32[1540]{0:T(1024)S(1)} %pad_maximum_fusion.3), channel_id=1, source_target_pairs={{0,1},{1,0},{2,3},{3,2},{4,5},{5,4},{6,7},{7,6},{8,9},{9,8},{10,11... | collective-permute-start | bytes 18488 | tf_op jit(solution)/shard_map/ppermute | solution.py:323
  87.1 4.0 %collective-permute-start.1 = (f32[128,256]{1,0:T(8,128)S(1)}, f32[128,256]{1,0:T(8,128)S(1)}, u32[]{:S(2)}, u32[]{:S(2)}) collective-permute-start(f32[128,256]{1,0:T(8,128)S(1)} %constant_dynamic-slice_fusion.1), channel_id=1, source_target_pairs={{0,1},{1,0},{2,3},{3,2},{4,5},{5,4},{6,7},{7,6},{8,9},{9,8},{10,11... | collective-permute-start | bytes 393224 | tf_op jit(solution)/shard_map/ppermute | solution.py:323
  88.6 4.1 %collective-permute-start = (f32[128,256]{1,0:T(8,128)S(1)}, f32[128,256]{1,0:T(8,128)S(1)}, u32[]{:S(2)}, u32[]{:S(2)}) collective-permute-start(f32[128,256]{1,0:T(8,128)S(1)} %constant_dynamic-slice_fusion), channel_id=1, source_target_pairs={{0,1},{1,0},{2,3},{3,2},{4,5},{5,4},{6,7},{7,6},{8,9},{9,8},{10,11... | collective-permute-start | bytes 393224 | tf_op jit(solution)/shard_map/ppermute | solution.py:323

commit v9 on v8

--- a/solution.py
+++ b/solution.py
@@ -116,15 +116,9 @@
     act_first = (pre_first * gate_first).astype(jnp.bfloat16)
     pre_second = jnp.dot(act_first, w2_ref[...], preferred_element_type=jnp.float32) + b2_ref[...]
     gate_second = gate_of(pre_second)
-    act_second = (pre_second * gate_second).astype(jnp.bfloat16).astype(jnp.float32)
-    raw = raw_ref[...].astype(jnp.float32)
-    head = wh_ref[...].astype(jnp.float32)
-    back_second = (
-        raw[:, 0:1] * head[0:1, :]
-        + raw[:, 1:2] * head[1:2, :]
-        + raw[:, 2:3] * head[2:3, :]
-        + raw[:, 3:4] * head[3:4, :]
-    )
+    act_second = (pre_second * gate_second).astype(jnp.bfloat16)
+    raw = raw_ref[...]
+    back_second = jnp.dot(raw, wh_ref[...], preferred_element_type=jnp.float32)
     slope_second = gate_second * (1.0 + pre_second * (1.0 - gate_second))
     delta_second = (back_second * slope_second).astype(jnp.bfloat16)
     g2_ref[...] += lax.dot_general(
@@ -140,9 +134,8 @@
         encoded, delta_first, (((0,), (0,)), ((), ())), preferred_element_type=jnp.float32
     )
     gb1_ref[...] += jnp.sum(delta_first.astype(jnp.float32), axis=0, keepdims=True)
-    gh_ref[...] += jnp.concatenate(
-        [jnp.sum(raw[:, c : c + 1] * act_second, axis=0, keepdims=True) for c in range(4)],
-        axis=0,
+    gh_ref[...] += lax.dot_general(
+        raw, act_second, (((0,), (0,)), ((), ())), preferred_element_type=jnp.float32
     )
 
 
@@ -162,7 +155,7 @@
     )
     grad_head_bias = jnp.sum(grad_raw.astype(jnp.float32), axis=0)
     rows = grad_raw.shape[0]
-    block = 512
+    block = 1024
     place = jnp.transpose(samples[:, :3, :], (0, 2, 1)).reshape(rows, 3)
     features = first_weight.shape[0]
     hidden = first_weight.shape[1]

time: 94.9 us -> 88.1 us (0.928)
  Pallas kernels: 21.6 us -> 14.8 us
    pallas_call x1, Pallas kernels: 21.6 us -> 14.8 us  [backward(): pl.pallas_call(backward_kernel, grid=(rows // block,), in_specs=[pl.Block...]
  transfers between devices with their start and end apart: 6 -> 6, of which waited for: 3 -> 3; matrix products, arithmetic and copies ran while one was open for 10% -> 11% of each run, Pallas kernels for 0% -> 0%
where the time goes in v9:
time: 88.1 us; the launch traced here: 87.4 us
  waiting for transfers between devices  19 us (22%)
  local copies, waits for them, and re-layouts  16.7 us (19%)
  starting transfers between devices  16 us (18%)
  Pallas kernels  14.8 us (17%)
  other arithmetic  11.8 us (13%)
  matrix products  7.97 us (9%)
  between operations  1.05 us (1%)
    pallas_call x1, Pallas kernels, backward(): pl.pallas_call(backward_kernel, grid=(rows // block,), in_specs=[pl.Block...  14.8 us
    all_to_all x1, starting transfers between devices, per_device(): lax.all_to_all(outgoing, 'space', split_axis=0, concat_axis=0, tiled=True)  8.31 us
    all_to_all x1, waiting for transfers between devices, per_device(): lax.all_to_all(partials, 'space', split_axis=1, concat_axis=1, tiled=True)  7.17 us
    all_to_all x1, waiting for transfers between devices, per_device(): lax.all_to_all(outgoing, 'space', split_axis=0, concat_axis=0, tiled=True)  7 us
    another operation x2, other arithmetic  5.79 us
    all_to_all x1, waiting for transfers between devices, per_device(): lax.all_to_all(sendback, 'space', split_axis=1, concat_axis=1, tiled=True)  4.86 us
    dot_general x1, matrix products, network(): lax.dot_general(act_second, head_weight, (((1,), (1,)), ((), ())), prefer...  3.81 us
    all_to_all x1, starting transfers between devices, per_device(): lax.all_to_all(partials, 'space', split_axis=1, concat_axis=1, tiled=True)  3.5 us
  transfers between devices with their start and end apart: 6, of which 3 were waited for; matrix products, arithmetic and copies ran while one was open for 11% of the time, Pallas kernels for 0%

profile of v9, /device:TPU:0, one launch (start us, length us, event | category | flops | bytes accessed | tf_op | source)
XLA Modules:
  0.0 87.4 jit_solution(177364142583693841)
XLA Ops:
  0.6 0.8 copy.81
  2.0 0.9 %reshape.237 = f32[3,128,32]{2,1,0:T(8,128)S(1)} reshape(f32[3,16,256]{2,1,0:T(8,128)} %param.12) | data formatting | bytes 98304 | tf_op jit(solution)/shard_map/reshape | solution.py:241
  3.0 0.8 reshape.238
  4.0 0.9 %fusion.18 = f32[16,12,128]{2,1,0:T(8,128)} fusion(f32[128,128,1]{0,1,2:T(8,128)S(1)} %bitcast.111, pred[16,12,128]{2,0,1:T(8,128)(4,1)S(1)} %broadcast_compare_fusion.1), kind=kOutput, calls=%fused_computation.47 | convolution fusion | flops 37748736 | bytes 188416 | tf_op jit(solution)/shard_map/dot_general | solution.py:244
  4.9 8.3 %all-to-all-start = ((f32[16,12,128]{2,1,0:T(8,128)}), f32[16,12,128]{2,1,0:T(8,128)S(1)}, u32[]{:S(2)}, u32[]{:S(2)}) async-start(f32[16,12,128]{2,1,0:T(8,128)} %fusion.18), calls=%async_computation | async-start | bytes 262144 | tf_op jit(solution)/shard_map/all_to_all | solution.py:252
  13.2 0.8 slice_bitcast_fusion.4
  14.0 7.0 %all-to-all-done = f32[16,12,128]{2,1,0:T(8,128)S(1)} async-done(((f32[16,12,128]{2,1,0:T(8,128)}), f32[16,12,128]{2,1,0:T(8,128)S(1)}, u32[]{:S(2)}, u32[]{:S(2)}) %all-to-all-start) | async-done | bytes 98336 | tf_op jit(solution)/shard_map/all_to_all | solution.py:252
  21.2 0.9 %slice_reduce_fusion.2 = (f32[192,32]{1,0:T(8,128)S(1)}, f32[192,32]{1,0:T(8,128)S(1)}, f32[192,32]{1,0:T(8,128)S(1)}, f32[192,1,32]{2,1,0:T(1,128)S(1)}) fusion(f32[192,4,32]{2,1,0:T(4,128)S(1)} %reshape.240), kind=kLoop, calls=%fused_computation.51 | loop fusion | bytes 196608 | tf_op jit(solution)/shard_map/slice | solution.py:56
  22.4 5.8 %fusion = (bf16[6144,128]{1,0:T(8,128)(2,1)S(1)}, bf16[6144,128]{1,0:T(8,128)(2,1)S(1)}) fusion(f32[128]{0:T(128)S(1)} %get-tuple-element.32, f32[6144]{0:T(1024)S(1)} %mul.312, f32[128]{0:T(128)S(1)} %get-tuple-element.31, f32[6144]{0:T(1024)S(1)} %mul.307, f32[128]{0:T(128)S(1)} %get-tuple-element.30, f32[6144]{0:T(1024)S(1)} %mul.302), kind=kLoop, calls=%fused_computation.7 | loop fusion | flops 36962304 | bytes 3220992 | tf_op jit(solution)/shard_map/convert.4
  28.2 2.9 %multiply_convert_fusion.1 = bf16[6144,256]{1,0:T(8,128)(2,1)} fusion(bf16[6144,128]{1,0:T(8,128)(2,1)S(1)} %get-tuple-element.25, bf16[6144,128]{1,0:T(8,128)(2,1)S(1)} %get-tuple-element.24, f32[256]{0:T(256)S(1)} %bitcast.129, bf16[1,256,256]{2,1,0:T(8,128)(2,1)S(1)} %copy-done), kind=kOutput, calls=%fused_computation.4 | convolution fusion | flops 821035008 | bytes 6423552 | tf_op jit(solution)/shard_map/dot_general | solution.py:69
  31.2 3.8 %convolution_add_fusion.2 = f32[6144,4]{0,1:T(4,128)S(1)} fusion(bf16[6144,256]{1,0:T(8,128)(2,1)} %multiply_convert_fusion.1, f32[256]{0:T(256)S(1)} %bitcast.130, f32[4]{0:T(128)S(1)} %bitcast.131, bf16[1,4,256]{2,1,0:T(4,128)(2,1)S(1)} %copy-done.3, bf16[1,256,256]{2,1,0:T(8,128)(2,1)S(1)} %copy-done.1), kind=kOutput, calls=%fused_computation.2 | convolution fusion | flops 827351040 | bytes 3378192 | tf_op jit(solution)/shard_map/dot_general | solution.py:74
  36.6 3.5 %all-to-all-start.1 = ((f32[4,16,12]{2,0,1:T(4,128)}), f32[4,16,12]{2,0,1:T(4,128)S(1)}, u32[]{:S(2)}, u32[]{:S(2)}) async-start(f32[4,16,12]{2,0,1:T(4,128)} %copy.90), calls=%async_computation.1 | async-start | bytes 65536 | tf_op jit(solution)/shard_map/all_to_all | solution.py:271
  40.3 7.2 %all-to-all-done.1 = f32[4,16,12]{2,0,1:T(4,128)S(1)} async-done(((f32[4,16,12]{2,0,1:T(4,128)}), f32[4,16,12]{2,0,1:T(4,128)S(1)}, u32[]{:S(2)}, u32[]{:S(2)}) %all-to-all-start.1) | async-done | bytes 3104 | tf_op jit(solution)/shard_map/all_to_all | solution.py:271
  49.5 3.5 %all-to-all-start.2 = ((f32[4,16,12]{2,0,1:T(4,128)}), f32[4,16,12]{2,0,1:T(4,128)S(1)}, u32[]{:S(2)}, u32[]{:S(2)}) async-start(f32[4,16,12]{2,0,1:T(4,128)} %copy.96), calls=%async_computation.2 | async-start | bytes 65536 | tf_op jit(solution)/shard_map/all_to_all | solution.py:296
  53.1 2.5 %copy.86 = f32[192,32,3]{2,1,0:T(8,128)} copy(f32[192,32,3]{1,2,0:T(4,128)S(1)} %slice_bitcast_fusion) | data formatting | bytes 147456 | tf_op jit(solution)/shard_map/transpose | solution.py:159
  55.6 4.9 %all-to-all-done.2 = f32[4,16,12]{2,0,1:T(4,128)S(1)} async-done(((f32[4,16,12]{2,0,1:T(4,128)}), f32[4,16,12]{2,0,1:T(4,128)S(1)}, u32[]{:S(2)}, u32[]{:S(2)}) %all-to-all-start.2) | async-done | bytes 3104 | tf_op jit(solution)/shard_map/all_to_all | solution.py:296
  61.5 1.6 %copy.101.raw_ref = bf16[6144,4]{1,0:T(8,128)(2,1)} copy(bf16[6144,4]{0,1:T(4,128)(2,1)S(1)} %get-tuple-element.20) | data formatting | bytes 98304 | tf_op jit(solution)/shard_map/concatenate | solution.py:152
  63.1 14.8 %shard_map.163 = (f32[256,256]{1,0:T(8,128)}, f32[1,256]{1,0:T(1,128)}, f32[256,256]{1,0:T(8,128)}, f32[1,256]{1,0:T(1,128)}, f32[4,256]{1,0:T(4,128)}) custom-call(f32[6144,3]{1,0:T(8,128)} %bitcast.109, f32[3,128]{1,0:T(4,128)} %fourier_ref.1, bf16[256,256]{1,0:T(8,128)(2,1)} %bitcast.112, f32[1,256]{1,0:T(1,128)} %b1_ref.1, bf16[256,256]{1,0:T(8,128)(2,1)} %bitcast.113, ...), custom_call_target="tpu_custom_call" | custom-call | tf_op jit(solution)/shard_map/pallas_call | solution.py:163
  78.6 0.7 pad_maximum_fusion.3
  79.4 0.9 %constant_dynamic-slice_fusion.1 = f32[128,256]{1,0:T(8,128)S(1)} fusion(f32[256,256]{1,0:T(8,128)} %get-tuple-element.12, s32[]{:T(128)S(6)} %select_n.50), kind=kLoop, calls=%fused_computation.99 | loop fusion | bytes 262148 | tf_op jit(solution)/shard_map/dynamic_slice | solution.py:315
  80.8 0.9 %constant_dynamic-slice_fusion = f32[128,256]{1,0:T(8,128)S(1)} fusion(f32[256,256]{1,0:T(8,128)} %get-tuple-element.11, s32[]{:T(128)S(6)} %select_n.50), kind=kLoop, calls=%fused_computation.98 | loop fusion | bytes 262148 | tf_op jit(solution)/shard_map/dynamic_slice | solution.py:313
  81.8 0.7 fusion.51
  84.2 1.6 %add_bitcast_fusion = f32[1,128,256]{2,1,0:T(8,128)} fusion(f32[128,256]{1,0:T(8,128)S(1)} %collective-permute-done.1, f32[256,256]{1,0:T(8,128)} %get-tuple-element.12, s32[]{:T(128)S(6)} %select_n.49), kind=kLoop, calls=%fused_computation.42 | loop fusion | flops 32768 | bytes 393220 | tf_op jit(solution)/shard_map/broadcast_in_dim | solution.py:337
  85.8 1.6 %add_bitcast_fusion.1 = f32[1,128,256]{2,1,0:T(8,128)} fusion(f32[128,256]{1,0:T(8,128)S(1)} %collective-permute-done, f32[256,256]{1,0:T(8,128)} %get-tuple-element.11, s32[]{:T(128)S(6)} %select_n.49), kind=kLoop, calls=%fused_computation.43 | loop fusion | flops 32768 | bytes 393220 | tf_op jit(solution)/shard_map/broadcast_in_dim | solution.py:336
  (91 shorter events, 9.2 us)
Async XLA Ops:
  1.8 26.4 %copy-start = (bf16[1,256,256]{2,1,0:T(8,128)(2,1)S(1)}, bf16[1,256,256]{2,1,0:T(8,128)(2,1)}, u32[]{:S(2)}) copy-start(bf16[1,256,256]{2,1,0:T(8,128)(2,1)} %param.18) | copy-start | bytes 393220
  1.8 26.4 %copy-start.5 = (f32[1,256]{1,0:T(1,128)S(1)}, f32[1,256]{1,0:T(1,128)}, u32[]{:S(2)}) copy-start(f32[1,256]{1,0:T(1,128)} %b1_ref.1) | copy-start | bytes 3076
  4.9 16.1 %all-to-all-start = ((f32[16,12,128]{2,1,0:T(8,128)}), f32[16,12,128]{2,1,0:T(8,128)S(1)}, u32[]{:S(2)}, u32[]{:S(2)}) async-start(f32[16,12,128]{2,1,0:T(8,128)} %fusion.18), calls=%async_computation | async-start | bytes 262144 | tf_op jit(solution)/shard_map/all_to_all | solution.py:252
  28.2 2.9 %copy-start.1 = (bf16[1,256,256]{2,1,0:T(8,128)(2,1)S(1)}, bf16[1,256,256]{2,1,0:T(8,128)(2,1)}, u32[]{:S(2)}) copy-start(bf16[1,256,256]{2,1,0:T(8,128)(2,1)} %param.20) | copy-start | bytes 393220
  28.2 2.9 %copy-start.3 = (bf16[1,4,256]{2,1,0:T(4,128)(2,1)S(1)}, bf16[1,4,256]{2,1,0:T(4,128)(2,1)}, u32[]{:S(2)}) copy-start(bf16[1,4,256]{2,1,0:T(4,128)(2,1)} %param.22) | copy-start | bytes 6148
  28.2 2.9 %copy-start.6 = (f32[1,256]{1,0:T(1,128)S(1)}, f32[1,256]{1,0:T(1,128)}, u32[]{:S(2)}) copy-start(f32[1,256]{1,0:T(1,128)} %b2_ref.1) | copy-start | bytes 3076
  28.2 2.9 %copy-start.7 = (f32[1,4]{1,0:T(1,128)S(1)}, f32[1,4]{1,0:T(1,128)}, u32[]{:S(2)}) copy-start(f32[1,4]{1,0:T(1,128)} %param.23) | copy-start | bytes 52
  31.1 9.0 %copy-start.4 = (f32[3,16]{1,0:T(4,128)S(1)}, f32[3,16]{1,0:T(4,128)}, u32[]{:S(2)}) copy-start(f32[3,16]{1,0:T(4,128)} %param.16) | copy-start | bytes 580
  31.1 17.0 %copy-start.2 = (s32[16,8]{0,1:T(8,128)S(1)}, s32[16,8]{0,1:T(8,128)}, u32[]{:S(2)}) copy-start(s32[16,8]{0,1:T(8,128)} %param.15) | copy-start | bytes 1540
  36.6 10.9 %all-to-all-start.1 = ((f32[4,16,12]{2,0,1:T(4,128)}), f32[4,16,12]{2,0,1:T(4,128)S(1)}, u32[]{:S(2)}, u32[]{:S(2)}) async-start(f32[4,16,12]{2,0,1:T(4,128)} %copy.90), calls=%async_computation.1 | async-start | bytes 65536 | tf_op jit(solution)/shard_map/all_to_all | solution.py:271
  49.5 10.9 %all-to-all-start.2 = ((f32[4,16,12]{2,0,1:T(4,128)}), f32[4,16,12]{2,0,1:T(4,128)S(1)}, u32[]{:S(2)}, u32[]{:S(2)}) async-start(f32[4,16,12]{2,0,1:T(4,128)} %copy.96), calls=%async_computation.2 | async-start | bytes 65536 | tf_op jit(solution)/shard_map/all_to_all | solution.py:296
  79.3 2.5 %collective-permute-start.2 = (f32[1540]{0:T(1024)S(1)}, f32[1540]{0:T(1024)S(1)}, u32[]{:S(2)}, u32[]{:S(2)}) collective-permute-start(f32[1540]{0:T(1024)S(1)} %pad_maximum_fusion.3), channel_id=1, source_target_pairs={{0,1},{1,0},{2,3},{3,2},{4,5},{5,4},{6,7},{7,6},{8,9},{9,8},{10,11... | collective-permute-start | bytes 18488 | tf_op jit(solution)/shard_map/ppermute | solution.py:316
  80.3 4.0 %collective-permute-start.1 = (f32[128,256]{1,0:T(8,128)S(1)}, f32[128,256]{1,0:T(8,128)S(1)}, u32[]{:S(2)}, u32[]{:S(2)}) collective-permute-start(f32[128,256]{1,0:T(8,128)S(1)} %constant_dynamic-slice_fusion.1), channel_id=1, source_target_pairs={{0,1},{1,0},{2,3},{3,2},{4,5},{5,4},{6,7},{7,6},{8,9},{9,8},{10,11... | collective-permute-start | bytes 393224 | tf_op jit(solution)/shard_map/ppermute | solution.py:316
  81.8 4.1 %collective-permute-start = (f32[128,256]{1,0:T(8,128)S(1)}, f32[128,256]{1,0:T(8,128)S(1)}, u32[]{:S(2)}, u32[]{:S(2)}) collective-permute-start(f32[128,256]{1,0:T(8,128)S(1)} %constant_dynamic-slice_fusion), channel_id=1, source_target_pairs={{0,1},{1,0},{2,3},{3,2},{4,5},{5,4},{6,7},{7,6},{8,9},{9,8},{10,11... | collective-permute-start | bytes 393224 | tf_op jit(solution)/shard_map/ppermute | solution.py:316

commit v10 on v9

--- a/solution.py
+++ b/solution.py
@@ -301,7 +301,21 @@
     small = jnp.concatenate(
         [grad_head.reshape(-1), bias_first, bias_second, bias_head], axis=0
     )
-    if replicas & (replicas - 1) == 0:
+    if replicas == 2:
+        position = lax.axis_index("ray")
+        got_first, got_second, got_small = lax.ppermute(
+            (grad_first, grad_second, small), "ray", [(0, 1), (1, 0)]
+        )
+        rows_first = grad_first.shape[0] // 2
+        rows_second = grad_second.shape[0] // 2
+        part_first = lax.dynamic_slice_in_dim(
+            grad_first + got_first, position * rows_first, rows_first, 0
+        )
+        part_second = lax.dynamic_slice_in_dim(
+            grad_second + got_second, position * rows_second, rows_second, 0
+        )
+        small = small + got_small
+    elif replicas & (replicas - 1) == 0:
         position = lax.axis_index("ray")
         part_first, part_second = grad_first, grad_second
         distance = replicas // 2

time: 88.1 us -> 86.7 us (0.984)
  local copies, waits for them, and re-layouts: 16.7 us -> 14.9 us
    dynamic_slice x2 -> x0, local copies, waits for them, and re-layouts: 1.83 us -> none  [the longest x1 0.92 us: per_device(): lax.dynamic_slice_in_dim(part_second, (1 - upper) * half, half, 0)]
  transfers between devices with their start and end apart: 6 -> 6, of which waited for: 3 -> 4; matrix products, arithmetic and copies ran while one was open for 11% -> 9% of each run, Pallas kernels for 0% -> 0%
where the time goes in v10:
time: 86.7 us; the launch traced here: 86.1 us
  waiting for transfers between devices  19.6 us (23%)
  starting transfers between devices  15.9 us (18%)
  local copies, waits for them, and re-layouts  14.9 us (17%)
  Pallas kernels  14.8 us (17%)
  other arithmetic  11.8 us (14%)
  matrix products  7.95 us (9%)
  between operations  1.02 us (1%)
    pallas_call x1, Pallas kernels, backward(): pl.pallas_call(backward_kernel, grid=(rows // block,), in_specs=[pl.Block...  14.8 us
    all_to_all x1, starting transfers between devices, per_device(): lax.all_to_all(outgoing, 'space', split_axis=0, concat_axis=0, tiled=True)  8.31 us
    all_to_all x1, waiting for transfers between devices, per_device(): lax.all_to_all(partials, 'space', split_axis=1, concat_axis=1, tiled=True)  7.19 us
    all_to_all x1, waiting for transfers between devices, per_device(): lax.all_to_all(outgoing, 'space', split_axis=0, concat_axis=0, tiled=True)  7 us
    another operation x2, other arithmetic  5.79 us
    all_to_all x1, waiting for transfers between devices, per_device(): lax.all_to_all(sendback, 'space', split_axis=1, concat_axis=1, tiled=True)  4.86 us
    dot_general x1, matrix products, network(): lax.dot_general(act_second, head_weight, (((1,), (1,)), ((), ())), prefer...  3.81 us
    all_to_all x1, starting transfers between devices, per_device(): lax.all_to_all(partials, 'space', split_axis=1, concat_axis=1, tiled=True)  3.5 us
  transfers between devices with their start and end apart: 6, of which 4 were waited for; matrix products, arithmetic and copies ran while one was open for 9% of the time, Pallas kernels for 0%

profile of v10, /device:TPU:0, one launch (start us, length us, event | category | flops | bytes accessed | tf_op | source)
XLA Modules:
  0.0 86.1 jit_solution(7428861959197240079)
XLA Ops:
  0.6 0.8 copy.81
  2.0 0.9 %reshape.237 = f32[3,128,32]{2,1,0:T(8,128)S(1)} reshape(f32[3,16,256]{2,1,0:T(8,128)} %param.12) | data formatting | bytes 98304 | tf_op jit(solution)/shard_map/reshape | solution.py:241
  3.0 0.8 reshape.238
  4.0 0.9 %fusion.20 = f32[16,12,128]{2,1,0:T(8,128)} fusion(f32[128,128,1]{0,1,2:T(8,128)S(1)} %bitcast.111, pred[16,12,128]{2,0,1:T(8,128)(4,1)S(1)} %broadcast_compare_fusion.1), kind=kOutput, calls=%fused_computation.49 | convolution fusion | flops 37748736 | bytes 188416 | tf_op jit(solution)/shard_map/dot_general | solution.py:244
  4.9 8.3 %all-to-all-start = ((f32[16,12,128]{2,1,0:T(8,128)}), f32[16,12,128]{2,1,0:T(8,128)S(1)}, u32[]{:S(2)}, u32[]{:S(2)}) async-start(f32[16,12,128]{2,1,0:T(8,128)} %fusion.20), calls=%async_computation | async-start | bytes 262144 | tf_op jit(solution)/shard_map/all_to_all | solution.py:252
  13.2 0.8 slice_bitcast_fusion.4
  14.0 7.0 %all-to-all-done = f32[16,12,128]{2,1,0:T(8,128)S(1)} async-done(((f32[16,12,128]{2,1,0:T(8,128)}), f32[16,12,128]{2,1,0:T(8,128)S(1)}, u32[]{:S(2)}, u32[]{:S(2)}) %all-to-all-start) | async-done | bytes 98336 | tf_op jit(solution)/shard_map/all_to_all | solution.py:252
  21.2 0.9 %slice_reduce_fusion.2 = (f32[192,32]{1,0:T(8,128)S(1)}, f32[192,32]{1,0:T(8,128)S(1)}, f32[192,32]{1,0:T(8,128)S(1)}, f32[192,1,32]{2,1,0:T(1,128)S(1)}) fusion(f32[192,4,32]{2,1,0:T(4,128)S(1)} %reshape.240), kind=kLoop, calls=%fused_computation.53 | loop fusion | bytes 196608 | tf_op jit(solution)/shard_map/slice | solution.py:56
  22.4 5.8 %fusion = (bf16[6144,128]{1,0:T(8,128)(2,1)S(1)}, bf16[6144,128]{1,0:T(8,128)(2,1)S(1)}) fusion(f32[128]{0:T(128)S(1)} %get-tuple-element.32, f32[6144]{0:T(1024)S(1)} %mul.308, f32[128]{0:T(128)S(1)} %get-tuple-element.31, f32[6144]{0:T(1024)S(1)} %mul.303, f32[128]{0:T(128)S(1)} %get-tuple-element.30, f32[6144]{0:T(1024)S(1)} %mul.298), kind=kLoop, calls=%fused_computation.7 | loop fusion | flops 36962304 | bytes 3220992 | tf_op jit(solution)/shard_map/convert.4
  28.2 2.8 %multiply_convert_fusion.1 = bf16[6144,256]{1,0:T(8,128)(2,1)} fusion(bf16[6144,128]{1,0:T(8,128)(2,1)S(1)} %get-tuple-element.25, bf16[6144,128]{1,0:T(8,128)(2,1)S(1)} %get-tuple-element.24, f32[256]{0:T(256)S(1)} %bitcast.129, bf16[1,256,256]{2,1,0:T(8,128)(2,1)S(1)} %copy-done), kind=kOutput, calls=%fused_computation.4 | convolution fusion | flops 821035008 | bytes 6423552 | tf_op jit(solution)/shard_map/dot_general | solution.py:69
  31.1 3.8 %convolution_add_fusion.2 = f32[6144,4]{0,1:T(4,128)S(1)} fusion(bf16[6144,256]{1,0:T(8,128)(2,1)} %multiply_convert_fusion.1, f32[256]{0:T(256)S(1)} %bitcast.130, f32[4]{0:T(128)S(1)} %bitcast.131, bf16[1,4,256]{2,1,0:T(4,128)(2,1)S(1)} %copy-done.3, bf16[1,256,256]{2,1,0:T(8,128)(2,1)S(1)} %copy-done.1), kind=kOutput, calls=%fused_computation.2 | convolution fusion | flops 827351040 | bytes 3378192 | tf_op jit(solution)/shard_map/dot_general | solution.py:74
  35.9 0.6 copy.90
  36.6 3.5 %all-to-all-start.1 = ((f32[4,16,12]{2,0,1:T(4,128)}), f32[4,16,12]{2,0,1:T(4,128)S(1)}, u32[]{:S(2)}, u32[]{:S(2)}) async-start(f32[4,16,12]{2,0,1:T(4,128)} %copy.90), calls=%async_computation.1 | async-start | bytes 65536 | tf_op jit(solution)/shard_map/all_to_all | solution.py:271
  40.2 7.2 %all-to-all-done.1 = f32[4,16,12]{2,0,1:T(4,128)S(1)} async-done(((f32[4,16,12]{2,0,1:T(4,128)}), f32[4,16,12]{2,0,1:T(4,128)S(1)}, u32[]{:S(2)}, u32[]{:S(2)}) %all-to-all-start.1) | async-done | bytes 3104 | tf_op jit(solution)/shard_map/all_to_all | solution.py:271
  49.5 3.5 %all-to-all-start.2 = ((f32[4,16,12]{2,0,1:T(4,128)}), f32[4,16,12]{2,0,1:T(4,128)S(1)}, u32[]{:S(2)}, u32[]{:S(2)}) async-start(f32[4,16,12]{2,0,1:T(4,128)} %copy.96), calls=%async_computation.2 | async-start | bytes 65536 | tf_op jit(solution)/shard_map/all_to_all | solution.py:296
  53.1 2.5 %copy.86 = f32[192,32,3]{2,1,0:T(8,128)} copy(f32[192,32,3]{1,2,0:T(4,128)S(1)} %slice_bitcast_fusion) | data formatting | bytes 147456 | tf_op jit(solution)/shard_map/transpose | solution.py:159
  55.5 4.9 %all-to-all-done.2 = f32[4,16,12]{2,0,1:T(4,128)S(1)} async-done(((f32[4,16,12]{2,0,1:T(4,128)}), f32[4,16,12]{2,0,1:T(4,128)S(1)}, u32[]{:S(2)}, u32[]{:S(2)}) %all-to-all-start.2) | async-done | bytes 3104 | tf_op jit(solution)/shard_map/all_to_all | solution.py:296
  61.5 1.6 %copy.101.raw_ref = bf16[6144,4]{1,0:T(8,128)(2,1)} copy(bf16[6144,4]{0,1:T(4,128)(2,1)S(1)} %get-tuple-element.20) | data formatting | bytes 98304 | tf_op jit(solution)/shard_map/concatenate | solution.py:152
  63.1 14.8 %shard_map.163 = (f32[256,256]{1,0:T(8,128)}, f32[1,256]{1,0:T(1,128)}, f32[256,256]{1,0:T(8,128)}, f32[1,256]{1,0:T(1,128)}, f32[4,256]{1,0:T(4,128)}) custom-call(f32[6144,3]{1,0:T(8,128)} %bitcast.109, f32[3,128]{1,0:T(4,128)} %fourier_ref.1, bf16[256,256]{1,0:T(8,128)(2,1)} %bitcast.112, f32[1,256]{1,0:T(1,128)} %b1_ref.1, bf16[256,256]{1,0:T(8,128)(2,1)} %bitcast.113, ...), custom_call_target="tpu_custom_call" | custom-call | tf_op jit(solution)/shard_map/pallas_call | solution.py:163
  77.9 0.7 copy.108
  78.6 0.7 pad_maximum_fusion.3
  80.5 0.7 fusion.53
  82.9 1.6 %fusion.16 = f32[1,128,256]{2,1,0:T(8,128)} fusion(f32[256,256]{1,0:T(8,128)S(1)} %collective-permute-done.1, s32[]{:T(128)S(6)} %select_n.35, f32[256,256]{1,0:T(8,128)} %get-tuple-element.12), kind=kLoop, calls=%fused_computation.43 | loop fusion | flops 32768 | bytes 393220 | tf_op jit(solution)/shard_map/broadcast_in_dim | solution.py:351
  84.5 1.6 %fusion.17 = f32[1,128,256]{2,1,0:T(8,128)} fusion(f32[256,256]{1,0:T(8,128)S(1)} %collective-permute-done, s32[]{:T(128)S(6)} %select_n.35, f32[256,256]{1,0:T(8,128)} %get-tuple-element.11), kind=kLoop, calls=%fused_computation.45 | loop fusion | flops 32768 | bytes 393220 | tf_op jit(solution)/shard_map/broadcast_in_dim | solution.py:350
  (89 shorter events, 8.4 us)
Async XLA Ops:
  1.8 26.4 %copy-start = (bf16[1,256,256]{2,1,0:T(8,128)(2,1)S(1)}, bf16[1,256,256]{2,1,0:T(8,128)(2,1)}, u32[]{:S(2)}) copy-start(bf16[1,256,256]{2,1,0:T(8,128)(2,1)} %param.18) | copy-start | bytes 393220
  1.8 26.4 %copy-start.5 = (f32[1,256]{1,0:T(1,128)S(1)}, f32[1,256]{1,0:T(1,128)}, u32[]{:S(2)}) copy-start(f32[1,256]{1,0:T(1,128)} %b1_ref.1) | copy-start | bytes 3076
  4.9 16.1 %all-to-all-start = ((f32[16,12,128]{2,1,0:T(8,128)}), f32[16,12,128]{2,1,0:T(8,128)S(1)}, u32[]{:S(2)}, u32[]{:S(2)}) async-start(f32[16,12,128]{2,1,0:T(8,128)} %fusion.20), calls=%async_computation | async-start | bytes 262144 | tf_op jit(solution)/shard_map/all_to_all | solution.py:252
  28.2 2.9 %copy-start.1 = (bf16[1,256,256]{2,1,0:T(8,128)(2,1)S(1)}, bf16[1,256,256]{2,1,0:T(8,128)(2,1)}, u32[]{:S(2)}) copy-start(bf16[1,256,256]{2,1,0:T(8,128)(2,1)} %param.20) | copy-start | bytes 393220
  28.2 2.9 %copy-start.3 = (bf16[1,4,256]{2,1,0:T(4,128)(2,1)S(1)}, bf16[1,4,256]{2,1,0:T(4,128)(2,1)}, u32[]{:S(2)}) copy-start(bf16[1,4,256]{2,1,0:T(4,128)(2,1)} %param.22) | copy-start | bytes 6148
  28.2 2.9 %copy-start.6 = (f32[1,256]{1,0:T(1,128)S(1)}, f32[1,256]{1,0:T(1,128)}, u32[]{:S(2)}) copy-start(f32[1,256]{1,0:T(1,128)} %b2_ref.1) | copy-start | bytes 3076
  28.2 2.9 %copy-start.7 = (f32[1,4]{1,0:T(1,128)S(1)}, f32[1,4]{1,0:T(1,128)}, u32[]{:S(2)}) copy-start(f32[1,4]{1,0:T(1,128)} %param.23) | copy-start | bytes 52
  31.1 9.0 %copy-start.4 = (f32[3,16]{1,0:T(4,128)S(1)}, f32[3,16]{1,0:T(4,128)}, u32[]{:S(2)}) copy-start(f32[3,16]{1,0:T(4,128)} %param.16) | copy-start | bytes 580
  31.1 17.0 %copy-start.2 = (s32[16,8]{0,1:T(8,128)S(1)}, s32[16,8]{0,1:T(8,128)}, u32[]{:S(2)}) copy-start(s32[16,8]{0,1:T(8,128)} %param.15) | copy-start | bytes 1540
  36.6 10.9 %all-to-all-start.1 = ((f32[4,16,12]{2,0,1:T(4,128)}), f32[4,16,12]{2,0,1:T(4,128)S(1)}, u32[]{:S(2)}, u32[]{:S(2)}) async-start(f32[4,16,12]{2,0,1:T(4,128)} %copy.90), calls=%async_computation.1 | async-start | bytes 65536 | tf_op jit(solution)/shard_map/all_to_all | solution.py:271
  49.5 10.9 %all-to-all-start.2 = ((f32[4,16,12]{2,0,1:T(4,128)}), f32[4,16,12]{2,0,1:T(4,128)S(1)}, u32[]{:S(2)}, u32[]{:S(2)}) async-start(f32[4,16,12]{2,0,1:T(4,128)} %copy.96), calls=%async_computation.2 | async-start | bytes 65536 | tf_op jit(solution)/shard_map/all_to_all | solution.py:296
  79.3 1.2 %collective-permute-start.2 = (f32[1540]{0:T(1024)S(1)}, f32[1540]{0:T(1024)S(1)}, u32[]{:S(2)}, u32[]{:S(2)}) collective-permute-start(f32[1540]{0:T(1024)S(1)} %pad_maximum_fusion.3), channel_id=1, source_target_pairs={{0,1},{1,0},{2,3},{3,2},{4,5},{5,4},{6,7},{7,6},{8,9},{9,8},{10,11... | collective-permute-start | bytes 18488 | tf_op jit(solution)/shard_map/ppermute | solution.py:306
  79.3 3.6 %collective-permute-start.1 = (f32[256,256]{1,0:T(8,128)}, f32[256,256]{1,0:T(8,128)S(1)}, u32[]{:S(2)}, u32[]{:S(2)}) collective-permute-start(f32[256,256]{1,0:T(8,128)} %get-tuple-element.12), channel_id=1, source_target_pairs={{0,1},{1,0},{2,3},{3,2},{4,5},{5,4},{6,7},{7,6},{8,9},{9,8},{10,11... | collective-permute-start | bytes 786440 | tf_op jit(solution)/shard_map/ppermute | solution.py:306
  79.8 4.6 %collective-permute-start = (f32[256,256]{1,0:T(8,128)}, f32[256,256]{1,0:T(8,128)S(1)}, u32[]{:S(2)}, u32[]{:S(2)}) collective-permute-start(f32[256,256]{1,0:T(8,128)} %get-tuple-element.11), channel_id=1, source_target_pairs={{0,1},{1,0},{2,3},{3,2},{4,5},{5,4},{6,7},{7,6},{8,9},{9,8},{10,11... | collective-permute-start | bytes 786440 | tf_op jit(solution)/shard_map/ppermute | solution.py:306

commit v11 on v10

--- a/solution.py
+++ b/solution.py
@@ -62,19 +62,127 @@
     return joined.astype(jnp.bfloat16).reshape(-1, joined.shape[-1])
 
 
+def forward_kernel(
+    place_ref, fourier_ref, w1_ref, b1_ref, w2_ref, b2_ref, wh_ref, bh_ref,
+    enc_ref, a1_ref, a2_ref, s1_ref, s2_ref, head_ref,
+):
+    place = place_ref[...]
+    fourier = fourier_ref[...]
+    turns = (
+        place[:, 0:1] * fourier[0:1, :]
+        + place[:, 1:2] * fourier[1:2, :]
+        + place[:, 2:3] * fourier[2:3, :]
+    )
+    sine, cosine = turn_sin_cos(turns)
+    encoded = jnp.concatenate([sine, cosine], axis=1).astype(jnp.bfloat16)
+    enc_ref[...] = encoded
+    pre_first = jnp.dot(encoded, w1_ref[...], preferred_element_type=jnp.float32) + b1_ref[...]
+    gate_first = gate_of(pre_first)
+    act_first = (pre_first * gate_first).astype(jnp.bfloat16)
+    a1_ref[...] = act_first
+    s1_ref[...] = gate_first * (1.0 + pre_first * (1.0 - gate_first))
+    pre_second = jnp.dot(act_first, w2_ref[...], preferred_element_type=jnp.float32) + b2_ref[...]
+    gate_second = gate_of(pre_second)
+    act_second = (pre_second * gate_second).astype(jnp.bfloat16)
+    a2_ref[...] = act_second
+    s2_ref[...] = gate_second * (1.0 + pre_second * (1.0 - gate_second))
+    head_ref[...] = (
+        lax.dot_general(
+            act_second, wh_ref[...], (((1,), (1,)), ((), ())), preferred_element_type=jnp.float32
+        )
+        + bh_ref[...]
+    )
+
+
+def backward_kernel(
+    enc_ref, a1_ref, a2_ref, s1_ref, s2_ref, raw_ref, w2_ref, wh_ref,
+    g1_ref, gb1_ref, g2_ref, gb2_ref, gh_ref,
+):
+    @pl.when(pl.program_id(0) == 0)
+    def _():
+        g1_ref[...] = jnp.zeros_like(g1_ref)
+        gb1_ref[...] = jnp.zeros_like(gb1_ref)
+        g2_ref[...] = jnp.zeros_like(g2_ref)
+        gb2_ref[...] = jnp.zeros_like(gb2_ref)
+        gh_ref[...] = jnp.zeros_like(gh_ref)
+
+    raw = raw_ref[...]
+    back_second = jnp.dot(raw, wh_ref[...], preferred_element_type=jnp.float32)
+    delta_second = (back_second * s2_ref[...]).astype(jnp.bfloat16)
+    g2_ref[...] += lax.dot_general(
+        a1_ref[...], delta_second, (((0,), (0,)), ((), ())), preferred_element_type=jnp.float32
+    )
+    gb2_ref[...] += jnp.sum(delta_second.astype(jnp.float32), axis=0, keepdims=True)
+    back_first = lax.dot_general(
+        delta_second, w2_ref[...], (((1,), (1,)), ((), ())), preferred_element_type=jnp.float32
+    )
+    delta_first = (back_first * s1_ref[...]).astype(jnp.bfloat16)
+    g1_ref[...] += lax.dot_general(
+        enc_ref[...], delta_first, (((0,), (0,)), ((), ())), preferred_element_type=jnp.float32
+    )
+    gb1_ref[...] += jnp.sum(delta_first.astype(jnp.float32), axis=0, keepdims=True)
+    gh_ref[...] += lax.dot_general(
+        raw, a2_ref[...], (((0,), (0,)), ((), ())), preferred_element_type=jnp.float32
+    )
+
+
+BLOCK = 1024
+
+
+def forward_layers(samples, fourier, params):
+    first_weight, first_bias, second_weight, second_bias, head_weight, head_bias = params
+    rows = samples.shape[0] * samples.shape[2]
+    place = jnp.transpose(samples[:, :3, :], (0, 2, 1)).reshape(rows, 3)
+    features, hidden = first_weight.shape
+    heads = head_weight.shape[0]
+    whole = lambda i: (0, 0)
+    by_row = lambda i: (i, 0)
+    return pl.pallas_call(
+        forward_kernel,
+        grid=(rows // BLOCK,),
+        in_specs=[
+            pl.BlockSpec((BLOCK, 3), by_row),
+            pl.BlockSpec(fourier.shape, whole),
+            pl.BlockSpec(first_weight.shape, whole),
+            pl.BlockSpec((1, hidden), whole),
+            pl.BlockSpec(second_weight.shape, whole),
+            pl.BlockSpec((1, hidden), whole),
+            pl.BlockSpec(head_weight.shape, whole),
+            pl.BlockSpec((1, heads), whole),
+        ],
+        out_specs=[
+            pl.BlockSpec((BLOCK, features), by_row),
+            pl.BlockSpec((BLOCK, hidden), by_row),
+            pl.BlockSpec((BLOCK, hidden), by_row),
+            pl.BlockSpec((BLOCK, hidden), by_row),
+            pl.BlockSpec((BLOCK, hidden), by_row),
+            pl.BlockSpec((BLOCK, heads), by_row),
+        ],
+        out_shape=[
+            jax.ShapeDtypeStruct((rows, features), jnp.bfloat16),
+            jax.ShapeDtypeStruct((rows, hidden), jnp.bfloat16),
+            jax.ShapeDtypeStruct((rows, hidden), jnp.bfloat16),
+            jax.ShapeDtypeStruct((rows, hidden), jnp.float32),
+            jax.ShapeDtypeStruct((rows, hidden), jnp.float32),
+            jax.ShapeDtypeStruct((rows, heads), jnp.float32),
+        ],
+        compiler_params=pltpu.CompilerParams(dimension_semantics=("arbitrary",)),
+    )(
+        place,
+        fourier,
+        first_weight,
+        first_bias.reshape(1, hidden),
+        second_weight,
+        second_bias.reshape(1, hidden),
+        head_weight,
+        head_bias.reshape(1, heads),
+    )
+
+
 def network(samples, fourier, params):
-    first_weight, first_bias, second_weight, second_bias, head_weight, head_bias = params
     seg_count, length = (samples.shape[0], samples.shape[2])
-    encoded = encode(samples, fourier)
-    pre_first = jnp.dot(encoded, first_weight, preferred_element_type=jnp.float32) + first_bias
-    act_first = (pre_first * gate_of(pre_first)).astype(jnp.bfloat16)
-    pre_second = jnp.dot(act_first, second_weight, preferred_element_type=jnp.float32) + second_bias
-    act_second = (pre_second * gate_of(pre_second)).astype(jnp.bfloat16)
-    head_raw = (
-        lax.dot_general(
-            act_second, head_weight, (((1,), (1,)), ((), ())), preferred_element_type=jnp.float32
-        )
-        + head_bias
+    encoded, act_first, act_second, slope_first, slope_second, head_raw = forward_layers(
+        samples, fourier, params
     )
     head_raw = head_raw.reshape(seg_count, length, 4)
     density = jax.nn.softplus(head_raw[..., 0])
@@ -86,62 +194,17 @@
     weight = enter_light - leave_light
     seg_colour = jnp.sum(weight[..., None] * colour, axis=1)
     seg_log = -inclusive[:, -1]
-    saved = (head_raw, colour, weight, leave_light)
+    saved = (
+        encoded, act_first, act_second, slope_first, slope_second,
+        head_raw, colour, weight, leave_light,
+    )
     return (seg_colour, seg_log, saved)
-
-
-def backward_kernel(
-    place_ref, fourier_ref, w1_ref, b1_ref, w2_ref, b2_ref, wh_ref, raw_ref,
-    g1_ref, gb1_ref, g2_ref, gb2_ref, gh_ref,
-):
-    @pl.when(pl.program_id(0) == 0)
-    def _():
-        g1_ref[...] = jnp.zeros_like(g1_ref)
-        gb1_ref[...] = jnp.zeros_like(gb1_ref)
-        g2_ref[...] = jnp.zeros_like(g2_ref)
-        gb2_ref[...] = jnp.zeros_like(gb2_ref)
-        gh_ref[...] = jnp.zeros_like(gh_ref)
-
-    place = place_ref[...]
-    fourier = fourier_ref[...]
-    turns = (
-        place[:, 0:1] * fourier[0:1, :]
-        + place[:, 1:2] * fourier[1:2, :]
-        + place[:, 2:3] * fourier[2:3, :]
-    )
-    sine, cosine = turn_sin_cos(turns)
-    encoded = jnp.concatenate([sine, cosine], axis=1).astype(jnp.bfloat16)
-    pre_first = jnp.dot(encoded, w1_ref[...], preferred_element_type=jnp.float32) + b1_ref[...]
-    gate_first = gate_of(pre_first)
-    act_first = (pre_first * gate_first).astype(jnp.bfloat16)
-    pre_second = jnp.dot(act_first, w2_ref[...], preferred_element_type=jnp.float32) + b2_ref[...]
-    gate_second = gate_of(pre_second)
-    act_second = (pre_second * gate_second).astype(jnp.bfloat16)
-    raw = raw_ref[...]
-    back_second = jnp.dot(raw, wh_ref[...], preferred_element_type=jnp.float32)
-    slope_second = gate_second * (1.0 + pre_second * (1.0 - gate_second))
-    delta_second = (back_second * slope_second).astype(jnp.bfloat16)
-    g2_ref[...] += lax.dot_general(
-        act_first, delta_second, (((0,), (0,)), ((), ())), preferred_element_type=jnp.float32
-    )
-    gb2_ref[...] += jnp.sum(delta_second.astype(jnp.float32), axis=0, keepdims=True)
-    back_first = lax.dot_general(
-        delta_second, w2_ref[...], (((1,), (1,)), ((), ())), preferred_element_type=jnp.float32
-    )
-    slope_first = gate_first * (1.0 + pre_first * (1.0 - gate_first))
-    delta_first = (back_first * slope_first).astype(jnp.bfloat16)
-    g1_ref[...] += lax.dot_general(
-        encoded, delta_first, (((0,), (0,)), ((), ())), preferred_element_type=jnp.float32
-    )
-    gb1_ref[...] += jnp.sum(delta_first.astype(jnp.float32), axis=0, keepdims=True)
-    gh_ref[...] += lax.dot_general(
-        raw, act_second, (((0,), (0,)), ((), ())), preferred_element_type=jnp.float32
-    )
 
 
 def backward(samples, fourier, params, saved, up_colour, up_log):
     first_weight, first_bias, second_weight, second_bias, head_weight, head_bias = params
-    head_raw, colour, weight, leave_light = saved
+    encoded, act_first, act_second, slope_first, slope_second = saved[:5]
+    head_raw, colour, weight, leave_light = saved[5:]
     energy = jnp.sum(colour * up_colour[:, None, :], axis=-1)
     spent = weight * energy
     remaining = jnp.sum(spent, axis=1, keepdims=True) - jnp.cumsum(spent, axis=1)
@@ -155,23 +218,21 @@
     )
     grad_head_bias = jnp.sum(grad_raw.astype(jnp.float32), axis=0)
     rows = grad_raw.shape[0]
-    block = 1024
-    place = jnp.transpose(samples[:, :3, :], (0, 2, 1)).reshape(rows, 3)
-    features = first_weight.shape[0]
-    hidden = first_weight.shape[1]
+    features, hidden = first_weight.shape
     whole = lambda i: (0, 0)
+    by_row = lambda i: (i, 0)
     outs = pl.pallas_call(
         backward_kernel,
-        grid=(rows // block,),
+        grid=(rows // BLOCK,),
         in_specs=[
-            pl.BlockSpec((block, 3), lambda i: (i, 0)),
-            pl.BlockSpec(fourier.shape, whole),
-            pl.BlockSpec(first_weight.shape, whole),
-            pl.BlockSpec((1, hidden), whole),
+            pl.BlockSpec((BLOCK, features), by_row),
+            pl.BlockSpec((BLOCK, hidden), by_row),
+            pl.BlockSpec((BLOCK, hidden), by_row),
+            pl.BlockSpec((BLOCK, hidden), by_row),
+            pl.BlockSpec((BLOCK, hidden), by_row),
+            pl.BlockSpec((BLOCK, 4), by_row),
             pl.BlockSpec(second_weight.shape, whole),
-            pl.BlockSpec((1, hidden), whole),
             pl.BlockSpec(head_weight.shape, whole),
-            pl.BlockSpec((block, 4), lambda i: (i, 0)),
         ],
         out_specs=[
             pl.BlockSpec((features, hidden), whole),
@@ -189,14 +250,8 @@
         ],
         compiler_params=pltpu.CompilerParams(dimension_semantics=("arbitrary",)),
     )(
-        place,
-        fourier,
-        first_weight,
-        first_bias.reshape(1, hidden),
-        second_weight,
-        second_bias.reshape(1, hidden),
-        head_weight,
-        grad_raw,
+        encoded, act_first, act_second, slope_first, slope_second, grad_raw,
+        second_weight, head_weight,
     )
     grad_first, bias_first, grad_second, bias_second, grad_head = outs
     return (grad_first, grad_second, grad_head, bias_first[0], bias_second[0], grad_head_bias)

time: 86.7 us -> 92.1 us (1.062)
  blocking collectives: 0 us -> 25.9 us
  starting transfers between devices: 15.9 us -> 4.08 us
  waiting for transfers between devices: 19.6 us -> 7.79 us
  Pallas kernels: 14.8 us -> 25.5 us
  matrix products: 7.95 us -> 0.63 us
  other arithmetic: 11.8 us -> 5.78 us
  local copies, waits for them, and re-layouts: 14.9 us -> 20.9 us
    all_to_all x0 -> x2, blocking collectives: none -> 25.9 us  [the longest x1 15.9 us: per_device(): lax.all_to_all(outgoing, 'space', split_axis=0, concat_axis=0, tiled=True)]
    all_to_all x2 -> x0, waiting for transfers between devices: 11.9 us -> none  [the longest x1 7 us: per_device(): lax.all_to_all(outgoing, 'space', split_axis=0, concat_axis=0, tiled=True)]
    all_to_all x2 -> x0, starting transfers between devices: 11.8 us -> none  [the longest x1 8.31 us: per_device(): lax.all_to_all(outgoing, 'space', split_axis=0, concat_axis=0, tiled=True)]
    pallas_call x1 -> x2, Pallas kernels: 14.8 us -> 25.5 us  [the longest x1 13.9 us: forward_layers(): pl.pallas_call(forward_kernel, grid=(rows // BLOCK,), in_specs=[pl.BlockS...]
    dot_general x2 -> x0, matrix products: 6.65 us -> none  [the longest x1 3.81 us: network(): lax.dot_general(act_second, head_weight, (((1,), (1,)), ((), ())), prefer...]
    unnamed x20 -> x12, local copies, waits for them, and re-layouts: 1.64 us -> 7.68 us
    another operation x2 -> x1, other arithmetic: 5.79 us -> 0.03 us
    slice x2, local copies, waits for them, and re-layouts: 0.96 us -> 2.64 us  [the longest x1 2.53 us: network(): colour = jax.nn.sigmoid(head_raw[..., 1:])]
  transfers between devices with their start and end apart: 6 -> 4, of which waited for: 4 -> 2; matrix products, arithmetic and copies ran while one was open for 9% -> 5% of each run, Pallas kernels for 0% -> 0%
where the time goes in v11:
time: 92.1 us; the launch traced here: 91.5 us
  blocking collectives  25.9 us (28%)
  Pallas kernels  25.5 us (28%)
  local copies, waits for them, and re-layouts  20.9 us (23%)
  waiting for transfers between devices  7.79 us (8%)
  other arithmetic  5.78 us (6%)
  starting transfers between devices  4.08 us (4%)
    all_to_all x1, blocking collectives, per_device(): lax.all_to_all(outgoing, 'space', split_axis=0, concat_axis=0, tiled=True)  15.9 us
    pallas_call x1, Pallas kernels, forward_layers(): pl.pallas_call(forward_kernel, grid=(rows // BLOCK,), in_specs=[pl.BlockS...  13.9 us
    pallas_call x1, Pallas kernels, backward(): pl.pallas_call(backward_kernel, grid=(rows // BLOCK,), in_specs=[pl.Block...  11.6 us
    all_to_all x1, blocking collectives, per_device(): lax.all_to_all(sendback, 'space', split_axis=1, concat_axis=1, tiled=True)  9.98 us
    unnamed x12, local copies, waits for them, and re-layouts  7.68 us
    all_to_all x1, waiting for transfers between devices, per_device(): lax.all_to_all(partials, 'space', split_axis=1, concat_axis=1, tiled=True)  7.19 us
    all_to_all x1, starting transfers between devices, per_device(): lax.all_to_all(partials, 'space', split_axis=1, concat_axis=1, tiled=True)  3.5 us
    slice x1, local copies, waits for them, and re-layouts, network(): colour = jax.nn.sigmoid(head_raw[..., 1:])  2.53 us
  transfers between devices with their start and end apart: 4, of which 2 were waited for; matrix products, arithmetic and copies ran while one was open for 5% of the time, Pallas kernels for 0%

profile of v11, /device:TPU:0, one launch (start us, length us, event | category | flops | bytes accessed | tf_op | source)
XLA Modules:
  0.0 91.5 jit_solution(12850437559461028873)
XLA Ops:
  0.6 0.8 copy.112
  1.9 0.8 reshape.217
  2.8 0.9 %reshape.216 = f32[3,128,32]{2,1,0:T(8,128)S(1)} reshape(f32[3,16,256]{2,1,0:T(8,128)} %param.12) | data formatting | bytes 98304 | tf_op jit(solution)/shard_map/reshape | solution.py:296
  4.2 15.9 %all_to_all.15 = f32[16,12,128]{2,1,0:T(8,128)S(1)} all-to-all(f32[16,12,128]{2,1,0:T(8,128)S(1)} %fusion.4), channel_id=1, replica_groups=mesh['space'=16,'ray'=2] {'space'}, dimensions={0} | all-to-all | bytes 196608 | tf_op jit(solution)/shard_map/all_to_all | solution.py:307
  20.5 2.5 %copy.117 = f32[192,32,3]{2,1,0:T(8,128)} copy(f32[192,32,3]{1,2,0:T(4,128)S(1)} %slice_bitcast_fusion) | data formatting | bytes 147456 | tf_op jit(solution)/shard_map/transpose | solution.py:135
  23.0 13.9 %shard_map.163 = (bf16[6144,256]{1,0:T(8,128)(2,1)}, bf16[6144,256]{1,0:T(8,128)(2,1)}, bf16[6144,256]{1,0:T(8,128)(2,1)}, f32[6144,256]{1,0:T(8,128)}, f32[6144,256]{1,0:T(8,128)}, /*index=5*/f32[6144,4]{1,0:T(8,128)}) custom-call(f32[6144,3]{1,0:T(8,128)} %bitcast.94, f32[3,128]{1,0:T(4,128)} %fourier_ref.1, bf16[256,256]{1,0:T(8,128)(2,1)} %bitcast.100, ...), custom_call_target="tpu_custom_call" | custom-call | tf_op jit(solution)/shard_map/pallas_call | solution.py:140
  36.9 3.1 %copy.143 = f32[192,32,1]{0,1,2:T(8,128)S(1)} copy(f32[192,32,1]{2,1,0:T(8,128)} %bitcast.92) | data formatting | bytes 49152
  40.2 2.5 %slice.57 = f32[192,32,3]{2,1,0:T(8,128)} slice(f32[192,32,4]{2,1,0:T(8,128)S(1)} %bitcast.93), slice={[0:192], [0:32], [1:4]} | slice | bytes 147456 | tf_op jit(solution)/shard_map/slice | solution.py:189
  42.8 3.0 %copy.145 = f32[192,32,3]{0,1,2:T(8,128)S(1)} copy(f32[192,32,3]{2,1,0:T(8,128)} %slice.57) | data formatting | bytes 147456
  46.1 0.6 copy.123
  46.8 3.5 %all-to-all-start.1 = ((f32[4,16,12]{2,0,1:T(4,128)}), f32[4,16,12]{2,0,1:T(4,128)S(1)}, u32[]{:S(2)}, u32[]{:S(2)}) async-start(f32[4,16,12]{2,0,1:T(4,128)} %copy.123), calls=%async_computation.1 | async-start | bytes 65536 | tf_op jit(solution)/shard_map/all_to_all | solution.py:326
  50.5 7.2 %all-to-all-done.1 = f32[4,16,12]{2,0,1:T(4,128)S(1)} async-done(((f32[4,16,12]{2,0,1:T(4,128)}), f32[4,16,12]{2,0,1:T(4,128)S(1)}, u32[]{:S(2)}, u32[]{:S(2)}) %all-to-all-start.1) | async-done | bytes 3104 | tf_op jit(solution)/shard_map/all_to_all | solution.py:326
  59.1 10.0 %all_to_all.16 = f32[4,16,12]{2,0,1:T(4,128)S(1)} all-to-all(f32[4,16,12]{2,0,1:T(4,128)S(1)} %copy.129), channel_id=1, replica_groups=mesh['space'=16,'ray'=2] {'space'}, dimensions={1} | all-to-all | bytes 6144 | tf_op jit(solution)/shard_map/all_to_all | solution.py:351
  70.2 1.6 %copy.136.raw_ref = bf16[6144,4]{1,0:T(8,128)(2,1)} copy(bf16[6144,4]{0,1:T(4,128)(2,1)S(1)} %get-tuple-element.29) | data formatting | bytes 98304 | tf_op jit(solution)/shard_map/concatenate | solution.py:215
  71.8 11.6 %shard_map.164 = (f32[256,256]{1,0:T(8,128)}, f32[1,256]{1,0:T(1,128)}, f32[256,256]{1,0:T(8,128)}, f32[1,256]{1,0:T(1,128)}, f32[4,256]{1,0:T(4,128)}) custom-call(bf16[6144,256]{1,0:T(8,128)(2,1)} %get-tuple-element.17.enc_ref, bf16[6144,256]{1,0:T(8,128)(2,1)} %get-tuple-element.18.a1_ref, bf16[6144,256]{1,0:T(8,128)(2,1)} %get-tuple-element.19.a2_ref, ...), custom_call_target="tpu_custom_call" | custom-call | tf_op jit(solution)/shard_map/pallas_call | solution.py:224
  83.4 0.7 copy.146
  84.1 0.7 pad_maximum_fusion.3
  85.4 0.6 collective-permute-done.2
  86.0 0.7 fusion.31
  86.7 0.6 fusion.33
  87.3 0.6 broadcast_in_dim_reshape.4
  87.9 0.5 slice_bitcast_fusion.1
  88.4 1.6 %fusion.1 = f32[1,128,256]{2,1,0:T(8,128)} fusion(f32[256,256]{1,0:T(8,128)S(1)} %collective-permute-done, s32[]{:T(128)S(6)} %select_n.14, f32[256,256]{1,0:T(8,128)} %get-tuple-element.23), kind=kLoop, calls=%fused_computation.4 | loop fusion | flops 32768 | bytes 393220 | tf_op jit(solution)/shard_map/broadcast_in_dim | solution.py:405
  90.0 1.6 %fusion = f32[1,128,256]{2,1,0:T(8,128)} fusion(f32[256,256]{1,0:T(8,128)S(1)} %collective-permute-done.1, s32[]{:T(128)S(6)} %select_n.14, f32[256,256]{1,0:T(8,128)} %get-tuple-element.24), kind=kLoop, calls=%fused_computation.2 | loop fusion | flops 32768 | bytes 393220 | tf_op jit(solution)/shard_map/broadcast_in_dim | solution.py:406
  (72 shorter events, 5.2 us)
Async XLA Ops:
  36.9 3.3 %copy-start = (f32[6144,4]{1,0:T(8,128)S(1)}, f32[6144,4]{1,0:T(8,128)}, u32[]{:S(2)}) copy-start(f32[6144,4]{1,0:T(8,128)} %get-tuple-element.22) | copy-start | bytes 294916
  42.7 7.6 %copy-start.2 = (f32[3,16]{1,0:T(4,128)S(1)}, f32[3,16]{1,0:T(4,128)}, u32[]{:S(2)}) copy-start(f32[3,16]{1,0:T(4,128)} %param.16) | copy-start | bytes 580
  42.7 15.6 %copy-start.1 = (s32[16,8]{0,1:T(8,128)S(1)}, s32[16,8]{0,1:T(8,128)}, u32[]{:S(2)}) copy-start(s32[16,8]{0,1:T(8,128)} %param.15) | copy-start | bytes 1540
  46.8 10.9 %all-to-all-start.1 = ((f32[4,16,12]{2,0,1:T(4,128)}), f32[4,16,12]{2,0,1:T(4,128)S(1)}, u32[]{:S(2)}, u32[]{:S(2)}) async-start(f32[4,16,12]{2,0,1:T(4,128)} %copy.123), calls=%async_computation.1 | async-start | bytes 65536 | tf_op jit(solution)/shard_map/all_to_all | solution.py:326
  84.8 1.2 %collective-permute-start.2 = (f32[1540]{0:T(1024)S(1)}, f32[1540]{0:T(1024)S(1)}, u32[]{:S(2)}, u32[]{:S(2)}) collective-permute-start(f32[1540]{0:T(1024)S(1)} %pad_maximum_fusion.3), channel_id=1, source_target_pairs={{0,1},{1,0},{2,3},{3,2},{4,5},{5,4},{6,7},{7,6},{8,9},{9,8},{10,11... | collective-permute-start | bytes 18488 | tf_op jit(solution)/shard_map/ppermute | solution.py:361
  84.8 3.6 %collective-permute-start = (f32[256,256]{1,0:T(8,128)}, f32[256,256]{1,0:T(8,128)S(1)}, u32[]{:S(2)}, u32[]{:S(2)}) collective-permute-start(f32[256,256]{1,0:T(8,128)} %get-tuple-element.23), channel_id=1, source_target_pairs={{0,1},{1,0},{2,3},{3,2},{4,5},{5,4},{6,7},{7,6},{8,9},{9,8},{10,11... | collective-permute-start | bytes 786440 | tf_op jit(solution)/shard_map/ppermute | solution.py:361
  85.3 4.6 %collective-permute-start.1 = (f32[256,256]{1,0:T(8,128)}, f32[256,256]{1,0:T(8,128)S(1)}, u32[]{:S(2)}, u32[]{:S(2)}) collective-permute-start(f32[256,256]{1,0:T(8,128)} %get-tuple-element.24), channel_id=1, source_target_pairs={{0,1},{1,0},{2,3},{3,2},{4,5},{5,4},{6,7},{7,6},{8,9},{9,8},{10,11... | collective-permute-start | bytes 786440 | tf_op jit(solution)/shard_map/ppermute | solution.py:361

commit v12 on v11

--- a/solution.py
+++ b/solution.py
@@ -69,14 +69,19 @@
     place = place_ref[...]
     fourier = fourier_ref[...]
     turns = (
-        place[:, 0:1] * fourier[0:1, :]
-        + place[:, 1:2] * fourier[1:2, :]
-        + place[:, 2:3] * fourier[2:3, :]
+        fourier[:, 0:1] * place[0:1, :]
+        + fourier[:, 1:2] * place[1:2, :]
+        + fourier[:, 2:3] * place[2:3, :]
     )
     sine, cosine = turn_sin_cos(turns)
-    encoded = jnp.concatenate([sine, cosine], axis=1).astype(jnp.bfloat16)
+    encoded = jnp.concatenate([sine, cosine], axis=0).astype(jnp.bfloat16)
     enc_ref[...] = encoded
-    pre_first = jnp.dot(encoded, w1_ref[...], preferred_element_type=jnp.float32) + b1_ref[...]
+    pre_first = (
+        lax.dot_general(
+            encoded, w1_ref[...], (((0,), (0,)), ((), ())), preferred_element_type=jnp.float32
+        )
+        + b1_ref[...]
+    )
     gate_first = gate_of(pre_first)
     act_first = (pre_first * gate_first).astype(jnp.bfloat16)
     a1_ref[...] = act_first
@@ -88,7 +93,7 @@
     s2_ref[...] = gate_second * (1.0 + pre_second * (1.0 - gate_second))
     head_ref[...] = (
         lax.dot_general(
-            act_second, wh_ref[...], (((1,), (1,)), ((), ())), preferred_element_type=jnp.float32
+            wh_ref[...], act_second, (((1,), (1,)), ((), ())), preferred_element_type=jnp.float32
         )
         + bh_ref[...]
     )
@@ -117,9 +122,7 @@
         delta_second, w2_ref[...], (((1,), (1,)), ((), ())), preferred_element_type=jnp.float32
     )
     delta_first = (back_first * s1_ref[...]).astype(jnp.bfloat16)
-    g1_ref[...] += lax.dot_general(
-        enc_ref[...], delta_first, (((0,), (0,)), ((), ())), preferred_element_type=jnp.float32
-    )
+    g1_ref[...] += jnp.dot(enc_ref[...], delta_first, preferred_element_type=jnp.float32)
     gb1_ref[...] += jnp.sum(delta_first.astype(jnp.float32), axis=0, keepdims=True)
     gh_ref[...] += lax.dot_general(
         raw, a2_ref[...], (((0,), (0,)), ((), ())), preferred_element_type=jnp.float32
@@ -132,50 +135,51 @@
 def forward_layers(samples, fourier, params):
     first_weight, first_bias, second_weight, second_bias, head_weight, head_bias = params
     rows = samples.shape[0] * samples.shape[2]
-    place = jnp.transpose(samples[:, :3, :], (0, 2, 1)).reshape(rows, 3)
+    place = jnp.transpose(samples, (1, 0, 2)).reshape(4, rows)
     features, hidden = first_weight.shape
     heads = head_weight.shape[0]
     whole = lambda i: (0, 0)
     by_row = lambda i: (i, 0)
+    by_column = lambda i: (0, i)
     return pl.pallas_call(
         forward_kernel,
         grid=(rows // BLOCK,),
         in_specs=[
-            pl.BlockSpec((BLOCK, 3), by_row),
-            pl.BlockSpec(fourier.shape, whole),
+            pl.BlockSpec((4, BLOCK), by_column),
+            pl.BlockSpec((fourier.shape[1], fourier.shape[0]), whole),
             pl.BlockSpec(first_weight.shape, whole),
             pl.BlockSpec((1, hidden), whole),
             pl.BlockSpec(second_weight.shape, whole),
             pl.BlockSpec((1, hidden), whole),
             pl.BlockSpec(head_weight.shape, whole),
-            pl.BlockSpec((1, heads), whole),
+            pl.BlockSpec((heads, 1), whole),
         ],
         out_specs=[
-            pl.BlockSpec((BLOCK, features), by_row),
-            pl.BlockSpec((BLOCK, hidden), by_row),
-            pl.BlockSpec((BLOCK, hidden), by_row),
-            pl.BlockSpec((BLOCK, hidden), by_row),
-            pl.BlockSpec((BLOCK, hidden), by_row),
-            pl.BlockSpec((BLOCK, heads), by_row),
+            pl.BlockSpec((features, BLOCK), by_column),
+            pl.BlockSpec((BLOCK, hidden), by_row),
+            pl.BlockSpec((BLOCK, hidden), by_row),
+            pl.BlockSpec((BLOCK, hidden), by_row),
+            pl.BlockSpec((BLOCK, hidden), by_row),
+            pl.BlockSpec((heads, BLOCK), by_column),
         ],
         out_shape=[
-            jax.ShapeDtypeStruct((rows, features), jnp.bfloat16),
+            jax.ShapeDtypeStruct((features, rows), jnp.bfloat16),
             jax.ShapeDtypeStruct((rows, hidden), jnp.bfloat16),
             jax.ShapeDtypeStruct((rows, hidden), jnp.bfloat16),
             jax.ShapeDtypeStruct((rows, hidden), jnp.float32),
             jax.ShapeDtypeStruct((rows, hidden), jnp.float32),
-            jax.ShapeDtypeStruct((rows, heads), jnp.float32),
+            jax.ShapeDtypeStruct((heads, rows), jnp.float32),
         ],
         compiler_params=pltpu.CompilerParams(dimension_semantics=("arbitrary",)),
     )(
         place,
-        fourier,
+        fourier.T,
         first_weight,
         first_bias.reshape(1, hidden),
         second_weight,
         second_bias.reshape(1, hidden),
         head_weight,
-        head_bias.reshape(1, heads),
+        head_bias.reshape(heads, 1),
     )
 
 
@@ -184,15 +188,15 @@
     encoded, act_first, act_second, slope_first, slope_second, head_raw = forward_layers(
         samples, fourier, params
     )
-    head_raw = head_raw.reshape(seg_count, length, 4)
-    density = jax.nn.softplus(head_raw[..., 0])
-    colour = jax.nn.sigmoid(head_raw[..., 1:])
+    head_raw = head_raw.reshape(4, seg_count, length)
+    density = jax.nn.softplus(head_raw[0])
+    colour = jax.nn.sigmoid(head_raw[1:])
     optical = density * samples[:, 3, :]
     inclusive = jnp.cumsum(optical, axis=1)
     enter_light = jnp.exp(optical - inclusive)
     leave_light = jnp.exp(-inclusive)
     weight = enter_light - leave_light
-    seg_colour = jnp.sum(weight[..., None] * colour, axis=1)
+    seg_colour = jnp.sum(weight[None] * colour, axis=2)
     seg_log = -inclusive[:, -1]
     saved = (
         encoded, act_first, act_second, slope_first, slope_second,
@@ -205,16 +209,17 @@
     first_weight, first_bias, second_weight, second_bias, head_weight, head_bias = params
     encoded, act_first, act_second, slope_first, slope_second = saved[:5]
     head_raw, colour, weight, leave_light = saved[5:]
-    energy = jnp.sum(colour * up_colour[:, None, :], axis=-1)
+    up_rows = up_colour.T[:, :, None]
+    energy = jnp.sum(colour * up_rows, axis=0)
     spent = weight * energy
     remaining = jnp.sum(spent, axis=1, keepdims=True) - jnp.cumsum(spent, axis=1)
     grad_optical = leave_light * energy - remaining - up_log[:, None]
-    grad_density = grad_optical * samples[:, 3, :] * jax.nn.sigmoid(head_raw[..., 0])
-    grad_tint = weight[..., None] * up_colour[:, None, :] * colour * (1.0 - colour)
+    grad_density = grad_optical * samples[:, 3, :] * jax.nn.sigmoid(head_raw[0])
+    grad_tint = weight[None] * up_rows * colour * (1.0 - colour)
     grad_raw = (
-        jnp.concatenate([grad_density[..., None], grad_tint], axis=-1)
-        .reshape(-1, 4)
-        .astype(jnp.bfloat16)
+        jnp.concatenate([grad_density[None], grad_tint], axis=0)
+        .reshape(4, -1)
+        .T.astype(jnp.bfloat16)
     )
     grad_head_bias = jnp.sum(grad_raw.astype(jnp.float32), axis=0)
     rows = grad_raw.shape[0]
@@ -225,7 +230,7 @@
         backward_kernel,
         grid=(rows // BLOCK,),
         in_specs=[
-            pl.BlockSpec((BLOCK, features), by_row),
+            pl.BlockSpec((features, BLOCK), lambda i: (0, i)),
             pl.BlockSpec((BLOCK, hidden), by_row),
             pl.BlockSpec((BLOCK, hidden), by_row),
             pl.BlockSpec((BLOCK, hidden), by_row),
@@ -320,7 +325,7 @@
         )
     )
     seg_colour, seg_log, saved = network(samples, fourier, params)
-    partials = jnp.concatenate([seg_colour.T, seg_log[None, :]], axis=0).reshape(
+    partials = jnp.concatenate([seg_colour, seg_log[None, :]], axis=0).reshape(
         4, groups, capacity
     )
     returned = lax.all_to_all(partials, "space", split_axis=1, concat_axis=1, tiled=True).reshape(

time: 92.1 us -> 86.8 us (0.942)
  blocking collectives: 25.9 us -> 0 us
  starting transfers between devices: 4.08 us -> 15.9 us
  waiting for transfers between devices: 7.79 us -> 19.6 us
  local copies, waits for them, and re-layouts: 20.9 us -> 16 us
  other arithmetic: 5.78 us -> 7.73 us
    all_to_all x2 -> x0, blocking collectives: 25.9 us -> none  [the longest x1 15.9 us: per_device(): lax.all_to_all(outgoing, 'space', split_axis=0, concat_axis=0, tiled=True)]
    all_to_all x0 -> x2, waiting for transfers between devices: none -> 12.1 us  [the longest x1 7 us: per_device(): lax.all_to_all(sendback, 'space', split_axis=1, concat_axis=1, tiled=True)]
    all_to_all x0 -> x2, starting transfers between devices: none -> 11.8 us  [the longest x1 8.31 us: per_device(): lax.all_to_all(outgoing, 'space', split_axis=0, concat_axis=0, tiled=True)]
    unnamed x12, local copies, waits for them, and re-layouts: 7.68 us -> 3.33 us
    transpose x3 -> x2, local copies, waits for them, and re-layouts: 2.59 us -> 0.03 us  [the longest x1 0.03 us: forward_layers(): place = jnp.transpose(samples, (1, 0, 2)).reshape(4, rows)]
    slice x1, local copies, waits for them, and re-layouts: 2.53 us -> 1.03 us  [network(): density = jax.nn.softplus(head_raw[0])]
    another operation x2 -> x5, local copies, waits for them, and re-layouts: 0.28 us -> 1.71 us  [the longest x1 1.31 us: forward_layers(): head_bias.reshape(heads, 1)]
    concatenate x5 -> x3, local copies, waits for them, and re-layouts: 2.64 us -> 1.6 us  [the longest x1 0.88 us: backward(): jnp.concatenate([grad_density[None], grad_tint], axis=0).reshape(4, -1)]
  transfers between devices with their start and end apart: 4 -> 6, of which waited for: 2 -> 4; matrix products, arithmetic and copies ran while one was open for 5% -> 9% of each run, Pallas kernels for 0% -> 0%
where the time goes in v12:
time: 86.8 us; the launch traced here: 86.2 us
  Pallas kernels  24.6 us (28%)
  waiting for transfers between devices  19.6 us (23%)
  local copies, waits for them, and re-layouts  16 us (18%)
  starting transfers between devices  15.9 us (18%)
  other arithmetic  7.73 us (9%)
  matrix products  1.29 us (1%)
  between operations  1.04 us (1%)
    pallas_call x1, Pallas kernels, forward_layers(): pl.pallas_call(forward_kernel, grid=(rows // BLOCK,), in_specs=[pl.BlockS...  13 us
    pallas_call x1, Pallas kernels, backward(): pl.pallas_call(backward_kernel, grid=(rows // BLOCK,), in_specs=[pl.Block...  11.6 us
    all_to_all x1, starting transfers between devices, per_device(): lax.all_to_all(outgoing, 'space', split_axis=0, concat_axis=0, tiled=True)  8.31 us
    all_to_all x1, waiting for transfers between devices, per_device(): lax.all_to_all(sendback, 'space', split_axis=1, concat_axis=1, tiled=True)  7 us
    all_to_all x1, waiting for transfers between devices, per_device(): lax.all_to_all(partials, 'space', split_axis=1, concat_axis=1, tiled=True)  6.91 us
    all_to_all x1, waiting for transfers between devices, per_device(): lax.all_to_all(outgoing, 'space', split_axis=0, concat_axis=0, tiled=True)  5.07 us
    all_to_all x1, starting transfers between devices, per_device(): lax.all_to_all(partials, 'space', split_axis=1, concat_axis=1, tiled=True)  3.5 us
    all_to_all x1, starting transfers between devices, per_device(): lax.all_to_all(sendback, 'space', split_axis=1, concat_axis=1, tiled=True)  3.5 us
  transfers between devices with their start and end apart: 6, of which 4 were waited for; matrix products, arithmetic and copies ran while one was open for 9% of the time, Pallas kernels for 0%

profile of v12, /device:TPU:0, one launch (start us, length us, event | category | flops | bytes accessed | tf_op | source)
XLA Modules:
  0.0 86.2 jit_solution(2328942610239711507)
XLA Ops:
  0.7 0.8 copy.129
  2.0 0.9 %reshape.252 = f32[3,128,32]{2,1,0:T(8,128)S(1)} reshape(f32[3,16,256]{2,1,0:T(8,128)} %param.12) | data formatting | bytes 98304 | tf_op jit(solution)/shard_map/reshape | solution.py:301
  3.0 0.8 reshape.253
  4.0 0.9 %fusion.4 = f32[16,12,128]{2,1,0:T(8,128)} fusion(f32[128,128,1]{0,1,2:T(8,128)S(1)} %bitcast.55, pred[16,12,128]{2,0,1:T(8,128)(4,1)S(1)} %broadcast_compare_fusion), kind=kOutput, calls=%fused_computation.9 | convolution fusion | flops 37748736 | bytes 188416 | tf_op jit(solution)/shard_map/dot_general | solution.py:304
  4.9 8.3 %all-to-all-start = ((f32[16,12,128]{2,1,0:T(8,128)}), f32[16,12,128]{2,1,0:T(8,128)S(1)}, u32[]{:S(2)}, u32[]{:S(2)}) async-start(f32[16,12,128]{2,1,0:T(8,128)} %fusion.4), calls=%async_computation | async-start | bytes 262144 | tf_op jit(solution)/shard_map/all_to_all | solution.py:312
  13.2 1.4 %copy.135 = f32[3,128]{0,1:T(8,128)} copy(f32[3,128]{1,0:T(4,128)} %param.17) | data formatting | bytes 3072 | tf_op args[5]
  14.6 1.3 %copy.136.bh_ref = f32[4,1]{1,0:T(4,128)} copy(f32[4,1]{0,1:T(1,128)} %bitcast.75) | data formatting | bytes 32 | tf_op jit(solution)/shard_map/reshape;squeeze | solution.py:182
  15.9 5.1 %all-to-all-done = f32[16,12,128]{2,1,0:T(8,128)S(1)} async-done(((f32[16,12,128]{2,1,0:T(8,128)}), f32[16,12,128]{2,1,0:T(8,128)S(1)}, u32[]{:S(2)}, u32[]{:S(2)}) %all-to-all-start) | async-done | bytes 98336 | tf_op jit(solution)/shard_map/all_to_all | solution.py:312
  21.4 0.8 reshape.256.place_ref
  22.2 13.0 %shard_map.163 = (bf16[256,6144]{1,0:T(8,128)(2,1)}, bf16[6144,256]{1,0:T(8,128)(2,1)}, bf16[6144,256]{1,0:T(8,128)(2,1)}, f32[6144,256]{1,0:T(8,128)}, f32[6144,256]{1,0:T(8,128)}, /*index=5*/f32[4,6144]{1,0:T(4,128)}) custom-call(f32[4,6144]{1,0:T(4,128)} %reshape.256.place_ref, f32[128,3]{1,0:T(8,128)} %bitcast.56, bf16[256,256]{1,0:T(8,128)(2,1)} %bitcast.58, ...), custom_call_target="tpu_custom_call" | custom-call | tf_op jit(solution)/shard_map/pallas_call | solution.py:144
  35.2 1.0 %fusion.24 = (f32[1,6144]{1,0:T(1,128)S(1)}, f32[6144]{0:T(1024)S(1)}) fusion(f32[4,6144]{1,0:T(4,128)} %get-tuple-element.22), kind=kLoop, calls=%fused_computation.56 | loop fusion | bytes 73728 | tf_op jit(solution)/shard_map/slice | solution.py:192
  36.3 1.0 %add_divide_fusion = f32[3,6144]{1,0:T(4,128)S(1)} fusion(f32[4,6144]{1,0:T(4,128)} %get-tuple-element.22), kind=kLoop, calls=%fused_computation.13 | loop fusion | flops 55296 | bytes 147456 | tf_op jit(solution)/shard_map/div | solution.py:193
  38.9 3.5 %all-to-all-start.1 = ((f32[4,16,12]{2,0,1:T(4,128)}), f32[4,16,12]{2,0,1:T(4,128)S(1)}, u32[]{:S(2)}, u32[]{:S(2)}) async-start(f32[4,16,12]{2,0,1:T(4,128)} %copy.147), calls=%async_computation.1 | async-start | bytes 65536 | tf_op jit(solution)/shard_map/all_to_all | solution.py:331
  42.8 6.9 %all-to-all-done.1 = f32[4,16,12]{2,0,1:T(4,128)S(1)} async-done(((f32[4,16,12]{2,0,1:T(4,128)}), f32[4,16,12]{2,0,1:T(4,128)S(1)}, u32[]{:S(2)}, u32[]{:S(2)}) %all-to-all-start.1) | async-done | bytes 3104 | tf_op jit(solution)/shard_map/all_to_all | solution.py:331
  51.8 3.5 %all-to-all-start.2 = ((f32[4,16,12]{2,0,1:T(4,128)}), f32[4,16,12]{2,0,1:T(4,128)S(1)}, u32[]{:S(2)}, u32[]{:S(2)}) async-start(f32[4,16,12]{2,0,1:T(4,128)} %copy.153), calls=%async_computation.2 | async-start | bytes 65536 | tf_op jit(solution)/shard_map/all_to_all | solution.py:356
  55.7 7.0 %all-to-all-done.2 = f32[4,16,12]{2,0,1:T(4,128)S(1)} async-done(((f32[4,16,12]{2,0,1:T(4,128)}), f32[4,16,12]{2,0,1:T(4,128)S(1)}, u32[]{:S(2)}, u32[]{:S(2)}) %all-to-all-start.2) | async-done | bytes 3104 | tf_op jit(solution)/shard_map/all_to_all | solution.py:356
  64.3 0.9 %copy.160 = bf16[4,6144]{0,1:T(8,128)(2,1)S(1)} copy(bf16[4,6144]{1,0:T(4,128)(2,1)S(1)} %pad_maximum_fusion.1) | data formatting | bytes 98304 | tf_op jit(solution)/shard_map/concatenate | solution.py:220
  65.2 0.8 convert_reduce_fusion
  66.4 11.6 %shard_map.164 = (f32[256,256]{1,0:T(8,128)}, f32[1,256]{1,0:T(1,128)}, f32[256,256]{1,0:T(8,128)}, f32[1,256]{1,0:T(1,128)}, f32[4,256]{1,0:T(4,128)}) custom-call(bf16[256,6144]{1,0:T(8,128)(2,1)} %get-tuple-element.17.enc_ref, bf16[6144,256]{1,0:T(8,128)(2,1)} %get-tuple-element.18.a1_ref, bf16[6144,256]{1,0:T(8,128)(2,1)} %get-tuple-element.19.a2_ref, ...), custom_call_target="tpu_custom_call" | custom-call | tf_op jit(solution)/shard_map/pallas_call | solution.py:229
  78.0 0.7 copy.168
  78.7 0.7 pad_maximum_fusion.3
  80.6 0.7 fusion.22
  83.0 1.6 %fusion = f32[1,128,256]{2,1,0:T(8,128)} fusion(f32[256,256]{1,0:T(8,128)S(1)} %collective-permute-done.1, s32[]{:T(128)S(6)} %select_n.17, f32[256,256]{1,0:T(8,128)} %get-tuple-element.24), kind=kLoop, calls=%fused_computation.3 | loop fusion | flops 32768 | bytes 393220 | tf_op jit(solution)/shard_map/broadcast_in_dim | solution.py:411
  84.6 1.6 %fusion.1 = f32[1,128,256]{2,1,0:T(8,128)} fusion(f32[256,256]{1,0:T(8,128)S(1)} %collective-permute-done, s32[]{:T(128)S(6)} %select_n.17, f32[256,256]{1,0:T(8,128)} %get-tuple-element.23), kind=kLoop, calls=%fused_computation.5 | loop fusion | flops 32768 | bytes 393220 | tf_op jit(solution)/shard_map/broadcast_in_dim | solution.py:410
  (93 shorter events, 10.3 us)
Async XLA Ops:
  0.6 41.7 %copy-start.3 = (f32[3,16]{1,0:T(4,128)S(1)}, f32[3,16]{1,0:T(4,128)}, u32[]{:S(2)}) copy-start(f32[3,16]{1,0:T(4,128)} %param.16) | copy-start | bytes 580
  2.9 47.6 %copy-start.2 = (s32[16,8]{0,1:T(8,128)S(1)}, s32[16,8]{0,1:T(8,128)}, u32[]{:S(2)}) copy-start(s32[16,8]{0,1:T(8,128)} %param.15) | copy-start | bytes 1540
  4.9 16.1 %all-to-all-start = ((f32[16,12,128]{2,1,0:T(8,128)}), f32[16,12,128]{2,1,0:T(8,128)S(1)}, u32[]{:S(2)}, u32[]{:S(2)}) async-start(f32[16,12,128]{2,1,0:T(8,128)} %fusion.4), calls=%async_computation | async-start | bytes 262144 | tf_op jit(solution)/shard_map/all_to_all | solution.py:312
  35.2 27.9 %copy-start.1 = (f32[4,6144]{1,0:T(4,128)S(1)}, f32[4,6144]{1,0:T(4,128)}, u32[]{:S(2)}) copy-start(f32[4,6144]{1,0:T(4,128)} %get-tuple-element.22) | copy-start | bytes 294916
  38.9 10.9 %all-to-all-start.1 = ((f32[4,16,12]{2,0,1:T(4,128)}), f32[4,16,12]{2,0,1:T(4,128)S(1)}, u32[]{:S(2)}, u32[]{:S(2)}) async-start(f32[4,16,12]{2,0,1:T(4,128)} %copy.147), calls=%async_computation.1 | async-start | bytes 65536 | tf_op jit(solution)/shard_map/all_to_all | solution.py:331
  51.8 10.9 %all-to-all-start.2 = ((f32[4,16,12]{2,0,1:T(4,128)}), f32[4,16,12]{2,0,1:T(4,128)S(1)}, u32[]{:S(2)}, u32[]{:S(2)}) async-start(f32[4,16,12]{2,0,1:T(4,128)} %copy.153), calls=%async_computation.2 | async-start | bytes 65536 | tf_op jit(solution)/shard_map/all_to_all | solution.py:356
  65.2 1.2 %copy-start = (bf16[4,6144]{0,1:T(8,128)(2,1)}, bf16[4,6144]{0,1:T(8,128)(2,1)S(1)}, u32[]{:S(2)}) copy-start(bf16[4,6144]{0,1:T(8,128)(2,1)S(1)} %copy.160) | copy-start | bytes 147460
  79.4 1.2 %collective-permute-start.2 = (f32[1540]{0:T(1024)S(1)}, f32[1540]{0:T(1024)S(1)}, u32[]{:S(2)}, u32[]{:S(2)}) collective-permute-start(f32[1540]{0:T(1024)S(1)} %pad_maximum_fusion.3), channel_id=1, source_target_pairs={{0,1},{1,0},{2,3},{3,2},{4,5},{5,4},{6,7},{7,6},{8,9},{9,8},{10,11... | collective-permute-start | bytes 18488 | tf_op jit(solution)/shard_map/ppermute | solution.py:366
  79.4 3.6 %collective-permute-start.1 = (f32[256,256]{1,0:T(8,128)}, f32[256,256]{1,0:T(8,128)S(1)}, u32[]{:S(2)}, u32[]{:S(2)}) collective-permute-start(f32[256,256]{1,0:T(8,128)} %get-tuple-element.24), channel_id=1, source_target_pairs={{0,1},{1,0},{2,3},{3,2},{4,5},{5,4},{6,7},{7,6},{8,9},{9,8},{10,11... | collective-permute-start | bytes 786440 | tf_op jit(solution)/shard_map/ppermute | solution.py:366
  79.9 4.6 %collective-permute-start = (f32[256,256]{1,0:T(8,128)}, f32[256,256]{1,0:T(8,128)S(1)}, u32[]{:S(2)}, u32[]{:S(2)}) collective-permute-start(f32[256,256]{1,0:T(8,128)} %get-tuple-element.23), channel_id=1, source_target_pairs={{0,1},{1,0},{2,3},{3,2},{4,5},{5,4},{6,7},{7,6},{8,9},{9,8},{10,11... | collective-permute-start | bytes 786440 | tf_op jit(solution)/shard_map/ppermute | solution.py:366

commit v13 on v12

--- a/solution.py
+++ b/solution.py
@@ -76,26 +76,18 @@
     sine, cosine = turn_sin_cos(turns)
     encoded = jnp.concatenate([sine, cosine], axis=0).astype(jnp.bfloat16)
     enc_ref[...] = encoded
-    pre_first = (
-        lax.dot_general(
-            encoded, w1_ref[...], (((0,), (0,)), ((), ())), preferred_element_type=jnp.float32
-        )
-        + b1_ref[...]
-    )
+    pre_first = jnp.dot(w1_ref[...], encoded, preferred_element_type=jnp.float32) + b1_ref[...]
     gate_first = gate_of(pre_first)
     act_first = (pre_first * gate_first).astype(jnp.bfloat16)
     a1_ref[...] = act_first
-    s1_ref[...] = gate_first * (1.0 + pre_first * (1.0 - gate_first))
-    pre_second = jnp.dot(act_first, w2_ref[...], preferred_element_type=jnp.float32) + b2_ref[...]
+    s1_ref[...] = (gate_first * (1.0 + pre_first * (1.0 - gate_first))).astype(s1_ref.dtype)
+    pre_second = jnp.dot(w2_ref[...], act_first, preferred_element_type=jnp.float32) + b2_ref[...]
     gate_second = gate_of(pre_second)
     act_second = (pre_second * gate_second).astype(jnp.bfloat16)
     a2_ref[...] = act_second
-    s2_ref[...] = gate_second * (1.0 + pre_second * (1.0 - gate_second))
+    s2_ref[...] = (gate_second * (1.0 + pre_second * (1.0 - gate_second))).astype(s2_ref.dtype)
     head_ref[...] = (
-        lax.dot_general(
-            wh_ref[...], act_second, (((1,), (1,)), ((), ())), preferred_element_type=jnp.float32
-        )
-        + bh_ref[...]
+        jnp.dot(wh_ref[...], act_second, preferred_element_type=jnp.float32) + bh_ref[...]
     )
 
 
@@ -111,24 +103,24 @@
         gb2_ref[...] = jnp.zeros_like(gb2_ref)
         gh_ref[...] = jnp.zeros_like(gh_ref)
 
+    across = (((1,), (1,)), ((), ()))
     raw = raw_ref[...]
-    back_second = jnp.dot(raw, wh_ref[...], preferred_element_type=jnp.float32)
-    delta_second = (back_second * s2_ref[...]).astype(jnp.bfloat16)
+    back_second = jnp.dot(wh_ref[...], raw, preferred_element_type=jnp.float32)
+    delta_second = (back_second * s2_ref[...].astype(jnp.float32)).astype(jnp.bfloat16)
     g2_ref[...] += lax.dot_general(
-        a1_ref[...], delta_second, (((0,), (0,)), ((), ())), preferred_element_type=jnp.float32
-    )
-    gb2_ref[...] += jnp.sum(delta_second.astype(jnp.float32), axis=0, keepdims=True)
-    back_first = lax.dot_general(
-        delta_second, w2_ref[...], (((1,), (1,)), ((), ())), preferred_element_type=jnp.float32
-    )
-    delta_first = (back_first * s1_ref[...]).astype(jnp.bfloat16)
-    g1_ref[...] += jnp.dot(enc_ref[...], delta_first, preferred_element_type=jnp.float32)
-    gb1_ref[...] += jnp.sum(delta_first.astype(jnp.float32), axis=0, keepdims=True)
-    gh_ref[...] += lax.dot_general(
-        raw, a2_ref[...], (((0,), (0,)), ((), ())), preferred_element_type=jnp.float32
-    )
-
-
+        a1_ref[...], delta_second, across, preferred_element_type=jnp.float32
+    )
+    gb2_ref[...] += jnp.sum(delta_second.astype(jnp.float32), axis=1, keepdims=True)
+    back_first = jnp.dot(w2_ref[...], delta_second, preferred_element_type=jnp.float32)
+    delta_first = (back_first * s1_ref[...].astype(jnp.float32)).astype(jnp.bfloat16)
+    g1_ref[...] += lax.dot_general(
+        enc_ref[...], delta_first, across, preferred_element_type=jnp.float32
+    )
+    gb1_ref[...] += jnp.sum(delta_first.astype(jnp.float32), axis=1, keepdims=True)
+    gh_ref[...] += lax.dot_general(raw, a2_ref[...], across, preferred_element_type=jnp.float32)
+
+
+SLOPE_TYPE = jnp.float32
 BLOCK = 1024
 
 
@@ -139,7 +131,6 @@
     features, hidden = first_weight.shape
     heads = head_weight.shape[0]
     whole = lambda i: (0, 0)
-    by_row = lambda i: (i, 0)
     by_column = lambda i: (0, i)
     return pl.pallas_call(
         forward_kernel,
@@ -147,37 +138,37 @@
         in_specs=[
             pl.BlockSpec((4, BLOCK), by_column),
             pl.BlockSpec((fourier.shape[1], fourier.shape[0]), whole),
-            pl.BlockSpec(first_weight.shape, whole),
-            pl.BlockSpec((1, hidden), whole),
-            pl.BlockSpec(second_weight.shape, whole),
-            pl.BlockSpec((1, hidden), whole),
+            pl.BlockSpec((hidden, features), whole),
+            pl.BlockSpec((hidden, 1), whole),
+            pl.BlockSpec((hidden, hidden), whole),
+            pl.BlockSpec((hidden, 1), whole),
             pl.BlockSpec(head_weight.shape, whole),
             pl.BlockSpec((heads, 1), whole),
         ],
         out_specs=[
             pl.BlockSpec((features, BLOCK), by_column),
-            pl.BlockSpec((BLOCK, hidden), by_row),
-            pl.BlockSpec((BLOCK, hidden), by_row),
-            pl.BlockSpec((BLOCK, hidden), by_row),
-            pl.BlockSpec((BLOCK, hidden), by_row),
+            pl.BlockSpec((hidden, BLOCK), by_column),
+            pl.BlockSpec((hidden, BLOCK), by_column),
+            pl.BlockSpec((hidden, BLOCK), by_column),
+            pl.BlockSpec((hidden, BLOCK), by_column),
             pl.BlockSpec((heads, BLOCK), by_column),
         ],
         out_shape=[
             jax.ShapeDtypeStruct((features, rows), jnp.bfloat16),
-            jax.ShapeDtypeStruct((rows, hidden), jnp.bfloat16),
-            jax.ShapeDtypeStruct((rows, hidden), jnp.bfloat16),
-            jax.ShapeDtypeStruct((rows, hidden), jnp.float32),
-            jax.ShapeDtypeStruct((rows, hidden), jnp.float32),
+            jax.ShapeDtypeStruct((hidden, rows), jnp.bfloat16),
+            jax.ShapeDtypeStruct((hidden, rows), jnp.bfloat16),
+            jax.ShapeDtypeStruct((hidden, rows), SLOPE_TYPE),
+            jax.ShapeDtypeStruct((hidden, rows), SLOPE_TYPE),
             jax.ShapeDtypeStruct((heads, rows), jnp.float32),
         ],
         compiler_params=pltpu.CompilerParams(dimension_semantics=("arbitrary",)),
     )(
         place,
         fourier.T,
-        first_weight,
-        first_bias.reshape(1, hidden),
-        second_weight,
-        second_bias.reshape(1, hidden),
+        first_weight.T,
+        first_bias.reshape(hidden, 1),
+        second_weight.T,
+        second_bias.reshape(hidden, 1),
         head_weight,
         head_bias.reshape(heads, 1),
     )
@@ -219,47 +210,47 @@
     grad_raw = (
         jnp.concatenate([grad_density[None], grad_tint], axis=0)
         .reshape(4, -1)
-        .T.astype(jnp.bfloat16)
-    )
-    grad_head_bias = jnp.sum(grad_raw.astype(jnp.float32), axis=0)
-    rows = grad_raw.shape[0]
+        .astype(jnp.bfloat16)
+    )
+    grad_head_bias = jnp.sum(grad_raw.astype(jnp.float32), axis=1)
+    rows = grad_raw.shape[1]
     features, hidden = first_weight.shape
     whole = lambda i: (0, 0)
-    by_row = lambda i: (i, 0)
+    by_column = lambda i: (0, i)
     outs = pl.pallas_call(
         backward_kernel,
         grid=(rows // BLOCK,),
         in_specs=[
-            pl.BlockSpec((features, BLOCK), lambda i: (0, i)),
-            pl.BlockSpec((BLOCK, hidden), by_row),
-            pl.BlockSpec((BLOCK, hidden), by_row),
-            pl.BlockSpec((BLOCK, hidden), by_row),
-            pl.BlockSpec((BLOCK, hidden), by_row),
-            pl.BlockSpec((BLOCK, 4), by_row),
+            pl.BlockSpec((features, BLOCK), by_column),
+            pl.BlockSpec((hidden, BLOCK), by_column),
+            pl.BlockSpec((hidden, BLOCK), by_column),
+            pl.BlockSpec((hidden, BLOCK), by_column),
+            pl.BlockSpec((hidden, BLOCK), by_column),
+            pl.BlockSpec((4, BLOCK), by_column),
             pl.BlockSpec(second_weight.shape, whole),
-            pl.BlockSpec(head_weight.shape, whole),
+            pl.BlockSpec((hidden, 4), whole),
         ],
         out_specs=[
             pl.BlockSpec((features, hidden), whole),
-            pl.BlockSpec((1, hidden), whole),
+            pl.BlockSpec((hidden, 1), whole),
             pl.BlockSpec((hidden, hidden), whole),
-            pl.BlockSpec((1, hidden), whole),
+            pl.BlockSpec((hidden, 1), whole),
             pl.BlockSpec((4, hidden), whole),
         ],
         out_shape=[
             jax.ShapeDtypeStruct((features, hidden), jnp.float32),
-            jax.ShapeDtypeStruct((1, hidden), jnp.float32),
+            jax.ShapeDtypeStruct((hidden, 1), jnp.float32),
             jax.ShapeDtypeStruct((hidden, hidden), jnp.float32),
-            jax.ShapeDtypeStruct((1, hidden), jnp.float32),
+            jax.ShapeDtypeStruct((hidden, 1), jnp.float32),
             jax.ShapeDtypeStruct((4, hidden), jnp.float32),
         ],
         compiler_params=pltpu.CompilerParams(dimension_semantics=("arbitrary",)),
     )(
         encoded, act_first, act_second, slope_first, slope_second, grad_raw,
-        second_weight, head_weight,
+        second_weight, head_weight.T,
     )
     grad_first, bias_first, grad_second, bias_second, grad_head = outs
-    return (grad_first, grad_second, grad_head, bias_first[0], bias_second[0], grad_head_bias)
+    return (grad_first, grad_second, grad_head, bias_first[:, 0], bias_second[:, 0], grad_head_bias)
 
 
 def composite(seg_colour, seg_log, depth_rank, pixel_rows):

time: 86.8 us -> 93.4 us (1.076)
  local copies, waits for them, and re-layouts: 16 us -> 22.5 us
  waiting for transfers between devices: 19.6 us -> 14.5 us
  starting transfers between devices: 15.9 us -> 19.4 us
  Pallas kernels: 24.6 us -> 25.6 us
    all_to_all x1, waiting for transfers between devices: 5.07 us -> 0.01 us  [per_device(): lax.all_to_all(outgoing, 'space', split_axis=0, concat_axis=0, tiled=True)]
    all_to_all x1, starting transfers between devices: 3.5 us -> 6.91 us  [per_device(): lax.all_to_all(partials, 'space', split_axis=1, concat_axis=1, tiled=True)]
    another operation x0 -> x2, local copies, waits for them, and re-layouts: none -> 2.94 us  [the longest x1 1.48 us: forward_layers(): second_bias.reshape(hidden, 1)]
    unnamed x12 -> x14, local copies, waits for them, and re-layouts: 3.33 us -> 5.45 us
    pallas_call x0 -> x2, other arithmetic: none -> 2.02 us  [backward(): pl.pallas_call(backward_kernel, grid=(rows // BLOCK,), in_specs=[pl.Block...]
    transpose x0 -> x1, local copies, waits for them, and re-layouts: none -> 1.65 us  [forward_layers(): return pl.pallas_call(forward_kernel, grid=(rows // BLOCK,), in_specs=[pl...]
    pallas_call x1, Pallas kernels: 13 us -> 14.1 us  [forward_layers(): pl.pallas_call(forward_kernel, grid=(rows // BLOCK,), in_specs=[pl.BlockS...]
  transfers between devices with their start and end apart: 6 -> 6, of which waited for: 4 -> 3; matrix products, arithmetic and copies ran while one was open for 9% -> 16% of each run, Pallas kernels for 0% -> 0%
where the time goes in v13:
time: 93.4 us; the launch traced here: 92.6 us
  Pallas kernels  25.6 us (27%)
  local copies, waits for them, and re-layouts  22.5 us (24%)
  starting transfers between devices  19.4 us (21%)
  waiting for transfers between devices  14.5 us (16%)
  other arithmetic  8.26 us (9%)
  matrix products  1.29 us (1%)
  between operations  1.04 us (1%)
    pallas_call x1, Pallas kernels, forward_layers(): pl.pallas_call(forward_kernel, grid=(rows // BLOCK,), in_specs=[pl.BlockS...  14.1 us
    pallas_call x1, Pallas kernels, backward(): pl.pallas_call(backward_kernel, grid=(rows // BLOCK,), in_specs=[pl.Block...  11.5 us
    all_to_all x1, starting transfers between devices, per_device(): lax.all_to_all(outgoing, 'space', split_axis=0, concat_axis=0, tiled=True)  8.31 us
    all_to_all x1, waiting for transfers between devices, per_device(): lax.all_to_all(sendback, 'space', split_axis=1, concat_axis=1, tiled=True)  7 us
    all_to_all x1, waiting for transfers between devices, per_device(): lax.all_to_all(partials, 'space', split_axis=1, concat_axis=1, tiled=True)  6.95 us
    all_to_all x1, starting transfers between devices, per_device(): lax.all_to_all(partials, 'space', split_axis=1, concat_axis=1, tiled=True)  6.91 us
    unnamed x14, local copies, waits for them, and re-layouts  5.45 us
    all_to_all x1, starting transfers between devices, per_device(): lax.all_to_all(sendback, 'space', split_axis=1, concat_axis=1, tiled=True)  3.5 us
  transfers between devices with their start and end apart: 6, of which 3 were waited for; matrix products, arithmetic and copies ran while one was open for 16% of the time, Pallas kernels for 0%

profile of v13, /device:TPU:0, one launch (start us, length us, event | category | flops | bytes accessed | tf_op | source)
XLA Modules:
  0.0 92.6 jit_solution(7354175774543387559)
XLA Ops:
  1.9 0.8 reshape.253
  2.8 0.9 reshape.252
  4.0 0.9 fusion.4
  4.9 8.3 %all-to-all-start = ((f32[16,12,128]{2,1,0:T(8,128)}), f32[16,12,128]{2,1,0:T(8,128)S(1)}, u32[]{:S(2)}, u32[]{:S(2)}) async-start(f32[16,12,128]{2,1,0:T(8,128)} %fusion.4), calls=%async_computation | async-start | bytes 262144 | tf_op jit(solution)/shard_map/all_to_all | solution.py:303
  13.2 1.3 %copy.146.bh_ref = f32[4,1]{1,0:T(4,128)} copy(f32[4,1]{0,1:T(1,128)} %bitcast.76) | data formatting | bytes 32 | tf_op jit(solution)/shard_map/reshape;squeeze | solution.py:173
  14.5 0.8 copy.141
  16.0 1.4 %copy.139 = f32[3,128]{0,1:T(8,128)} copy(f32[3,128]{1,0:T(4,128)} %param.17) | data formatting | bytes 3072 | tf_op args[5]
  17.4 1.7 %copy.140 = bf16[1,256,256]{1,2,0:T(8,128)(2,1)} copy(bf16[1,256,256]{2,1,0:T(8,128)(2,1)} %param.18) | data formatting | bytes 262144 | tf_op args[6]
  19.1 1.5 %copy.142.b1_ref = f32[256,1]{1,0:T(8,128)} copy(f32[256,1]{0,1:T(1,128)} %bitcast.72) | data formatting | bytes 2048 | tf_op jit(solution)/shard_map/reshape;squeeze | solution.py:169
  20.6 1.5 %copy.144.b2_ref = f32[256,1]{1,0:T(8,128)} copy(f32[256,1]{0,1:T(1,128)} %bitcast.73) | data formatting | bytes 2048 | tf_op jit(solution)/shard_map/reshape;squeeze | solution.py:171
  22.0 1.7 %copy.143.w2_ref = bf16[256,256]{1,0:T(8,128)(2,1)} copy(bf16[256,256]{0,1:T(8,128)(2,1)} %bitcast.58) | data formatting | bytes 262144 | tf_op jit(solution)/shard_map/transpose | solution.py:170
  24.1 0.8 reshape.256.place_ref
  25.0 14.1 %shard_map.163 = (bf16[256,6144]{1,0:T(8,128)(2,1)}, bf16[256,6144]{1,0:T(8,128)(2,1)}, bf16[256,6144]{1,0:T(8,128)(2,1)}, f32[256,6144]{1,0:T(8,128)}, f32[256,6144]{1,0:T(8,128)}, /*index=5*/f32[4,6144]{1,0:T(4,128)}) custom-call(f32[4,6144]{1,0:T(4,128)} %reshape.256.place_ref, f32[128,3]{1,0:T(8,128)} %bitcast.62, bf16[256,256]{1,0:T(8,128)(2,1)} %bitcast.60, ...), custom_call_target="tpu_custom_call" | custom-call | tf_op jit(solution)/shard_map/pallas_call | solution.py:135
  39.0 1.0 %fusion.24 = (f32[1,6144]{1,0:T(1,128)S(1)}, f32[6144]{0:T(1024)S(1)}) fusion(f32[4,6144]{1,0:T(4,128)} %get-tuple-element.22), kind=kLoop, calls=%fused_computation.56 | loop fusion | bytes 73728 | tf_op jit(solution)/shard_map/slice | solution.py:183
  40.4 1.0 %add_divide_fusion = f32[3,6144]{1,0:T(4,128)S(1)} fusion(f32[4,6144]{1,0:T(4,128)} %get-tuple-element.22), kind=kLoop, calls=%fused_computation.13 | loop fusion | flops 55296 | bytes 147456 | tf_op jit(solution)/shard_map/div | solution.py:184
  42.6 6.9 %all-to-all-start.1 = ((f32[4,16,12]{2,0,1:T(4,128)}), f32[4,16,12]{2,0,1:T(4,128)S(1)}, u32[]{:S(2)}, u32[]{:S(2)}) async-start(f32[4,16,12]{2,0,1:T(4,128)} %copy.155), calls=%async_computation.1 | async-start | bytes 65536 | tf_op jit(solution)/shard_map/all_to_all | solution.py:322
  50.0 6.9 %all-to-all-done.1 = f32[4,16,12]{2,0,1:T(4,128)S(1)} async-done(((f32[4,16,12]{2,0,1:T(4,128)}), f32[4,16,12]{2,0,1:T(4,128)S(1)}, u32[]{:S(2)}, u32[]{:S(2)}) %all-to-all-start.1) | async-done | bytes 3104 | tf_op jit(solution)/shard_map/all_to_all | solution.py:322
  59.0 3.5 %all-to-all-start.2 = ((f32[4,16,12]{2,0,1:T(4,128)}), f32[4,16,12]{2,0,1:T(4,128)S(1)}, u32[]{:S(2)}, u32[]{:S(2)}) async-start(f32[4,16,12]{2,0,1:T(4,128)} %copy.161), calls=%async_computation.2 | async-start | bytes 65536 | tf_op jit(solution)/shard_map/all_to_all | solution.py:347
  62.9 7.0 %all-to-all-done.2 = f32[4,16,12]{2,0,1:T(4,128)S(1)} async-done(((f32[4,16,12]{2,0,1:T(4,128)}), f32[4,16,12]{2,0,1:T(4,128)S(1)}, u32[]{:S(2)}, u32[]{:S(2)}) %all-to-all-start.2) | async-done | bytes 3104 | tf_op jit(solution)/shard_map/all_to_all | solution.py:347
  72.2 11.5 %shard_map.164 = (f32[256,256]{1,0:T(8,128)}, f32[256,1]{1,0:T(8,128)}, f32[256,256]{1,0:T(8,128)}, f32[256,1]{1,0:T(8,128)}, f32[4,256]{1,0:T(4,128)}) custom-call(bf16[256,6144]{1,0:T(8,128)(2,1)} %get-tuple-element.17.enc_ref, bf16[256,6144]{1,0:T(8,128)(2,1)} %get-tuple-element.18.a1_ref, bf16[256,6144]{1,0:T(8,128)(2,1)} %get-tuple-element.19.a2_ref, ...), custom_call_target="tpu_custom_call" | custom-call | tf_op jit(solution)/shard_map/pallas_call | solution.py:220
  84.4 1.0 %reduce.5 = f32[256]{0:T(256)S(1)} reduce(f32[256,1]{1,0:T(8,128)} %get-tuple-element.26, f32[]{:T(128)} %constant.44), dimensions={1}, to_apply=%get-tuple-element.26.reduce_sub_computation | reduce | bytes 2052 | tf_op jit(solution)/shard_map/pallas_call | solution.py:220
  85.5 1.0 %reduce.6 = f32[256]{0:T(256)S(1)} reduce(f32[256,1]{1,0:T(8,128)} %get-tuple-element.27, f32[]{:T(128)} %constant.44), dimensions={1}, to_apply=%get-tuple-element.27.reduce_sub_computation | reduce | bytes 2052 | tf_op jit(solution)/shard_map/pallas_call | solution.py:220
  89.4 1.6 %fusion.1 = f32[1,128,256]{2,1,0:T(8,128)} fusion(f32[256,256]{1,0:T(8,128)S(1)} %collective-permute-done, s32[]{:T(128)S(6)} %select_n.17, f32[256,256]{1,0:T(8,128)} %get-tuple-element.23), kind=kLoop, calls=%fused_computation.4 | loop fusion | flops 32768 | bytes 393220 | tf_op jit(solution)/shard_map/broadcast_in_dim | solution.py:401
  91.0 1.6 %fusion = f32[1,128,256]{2,1,0:T(8,128)} fusion(f32[256,256]{1,0:T(8,128)S(1)} %collective-permute-done.1, s32[]{:T(128)S(6)} %select_n.17, f32[256,256]{1,0:T(8,128)} %get-tuple-element.24), kind=kLoop, calls=%fused_computation.2 | loop fusion | flops 32768 | bytes 393220 | tf_op jit(solution)/shard_map/broadcast_in_dim | solution.py:402
  (99 shorter events, 12.9 us)
Async XLA Ops:
  4.0 45.6 %copy-start.3 = (f32[3,16]{1,0:T(4,128)S(1)}, f32[3,16]{1,0:T(4,128)}, u32[]{:S(2)}) copy-start(f32[3,16]{1,0:T(4,128)} %param.16) | copy-start | bytes 580
  4.9 18.8 %all-to-all-start = ((f32[16,12,128]{2,1,0:T(8,128)}), f32[16,12,128]{2,1,0:T(8,128)S(1)}, u32[]{:S(2)}, u32[]{:S(2)}) async-start(f32[16,12,128]{2,1,0:T(8,128)} %fusion.4), calls=%async_computation | async-start | bytes 262144 | tf_op jit(solution)/shard_map/all_to_all | solution.py:303
  15.3 41.9 %copy-start.1 = (bf16[1,4,256]{1,2,0:T(8,128)(2,1)}, bf16[1,4,256]{1,2,0:T(8,128)(2,1)S(1)}, u32[]{:S(2)}) copy-start(bf16[1,4,256]{1,2,0:T(8,128)(2,1)S(1)} %copy.141) | copy-start | bytes 6148
  16.0 41.6 %copy-start.2 = (s32[16,8]{0,1:T(8,128)S(1)}, s32[16,8]{0,1:T(8,128)}, u32[]{:S(2)}) copy-start(s32[16,8]{0,1:T(8,128)} %param.15) | copy-start | bytes 1540
  39.0 31.5 %copy-start = (f32[4,6144]{1,0:T(4,128)S(1)}, f32[4,6144]{1,0:T(4,128)}, u32[]{:S(2)}) copy-start(f32[4,6144]{1,0:T(4,128)} %get-tuple-element.22) | copy-start | bytes 294916
  42.6 14.3 %all-to-all-start.1 = ((f32[4,16,12]{2,0,1:T(4,128)}), f32[4,16,12]{2,0,1:T(4,128)S(1)}, u32[]{:S(2)}, u32[]{:S(2)}) async-start(f32[4,16,12]{2,0,1:T(4,128)} %copy.155), calls=%async_computation.1 | async-start | bytes 65536 | tf_op jit(solution)/shard_map/all_to_all | solution.py:322
  59.0 10.9 %all-to-all-start.2 = ((f32[4,16,12]{2,0,1:T(4,128)}), f32[4,16,12]{2,0,1:T(4,128)S(1)}, u32[]{:S(2)}, u32[]{:S(2)}) async-start(f32[4,16,12]{2,0,1:T(4,128)} %copy.161), calls=%async_computation.2 | async-start | bytes 65536 | tf_op jit(solution)/shard_map/all_to_all | solution.py:347
  86.5 1.2 %collective-permute-start.2 = (f32[1540]{0:T(1024)S(1)}, f32[1540]{0:T(1024)S(1)}, u32[]{:S(2)}, u32[]{:S(2)}) collective-permute-start(f32[1540]{0:T(1024)S(1)} %pad_maximum_fusion.3), channel_id=1, source_target_pairs={{0,1},{1,0},{2,3},{3,2},{4,5},{5,4},{6,7},{7,6},{8,9},{9,8},{10,11... | collective-permute-start | bytes 18488 | tf_op jit(solution)/shard_map/ppermute | solution.py:357
  86.6 2.9 %collective-permute-start = (f32[256,256]{1,0:T(8,128)}, f32[256,256]{1,0:T(8,128)S(1)}, u32[]{:S(2)}, u32[]{:S(2)}) collective-permute-start(f32[256,256]{1,0:T(8,128)} %get-tuple-element.23), channel_id=1, source_target_pairs={{0,1},{1,0},{2,3},{3,2},{4,5},{5,4},{6,7},{7,6},{8,9},{9,8},{10,11... | collective-permute-start | bytes 786440 | tf_op jit(solution)/shard_map/ppermute | solution.py:357
  87.1 3.9 %collective-permute-start.1 = (f32[256,256]{1,0:T(8,128)}, f32[256,256]{1,0:T(8,128)S(1)}, u32[]{:S(2)}, u32[]{:S(2)}) collective-permute-start(f32[256,256]{1,0:T(8,128)} %get-tuple-element.24), channel_id=1, source_target_pairs={{0,1},{1,0},{2,3},{3,2},{4,5},{5,4},{6,7},{7,6},{8,9},{9,8},{10,11... | collective-permute-start | bytes 786440 | tf_op jit(solution)/shard_map/ppermute | solution.py:357

commit v14 on v12

--- a/solution.py
+++ b/solution.py
@@ -358,8 +358,16 @@
     totals = backward(samples, fourier, params, saved, received[:, :3], received[:, 3])
     grad_first, grad_second, grad_head, bias_first, bias_second, bias_head = totals
     replicas = lax.axis_size("ray")
+    hidden = bias_first.shape[0]
+    heads = grad_head.shape[0]
     small = jnp.concatenate(
-        [grad_head.reshape(-1), bias_first, bias_second, bias_head], axis=0
+        [
+            grad_head,
+            bias_first[None],
+            bias_second[None],
+            jnp.pad(bias_head, (0, hidden - heads))[None],
+        ],
+        axis=0,
     )
     if replicas == 2:
         position = lax.axis_index("ray")
@@ -398,14 +406,7 @@
         part_first = lax.psum_scatter(grad_first, "ray", scatter_dimension=0, tiled=True)
         part_second = lax.psum_scatter(grad_second, "ray", scatter_dimension=0, tiled=True)
         small = lax.psum(small, "ray")
-    heads = grad_head.size
-    hidden = bias_first.shape[0]
-    small_sums = (
-        small[:heads].reshape(grad_head.shape),
-        small[heads : heads + hidden],
-        small[heads + hidden : heads + 2 * hidden],
-        small[heads + 2 * hidden :],
-    )
+    small_sums = (small[:heads], small[heads], small[heads + 1], small[heads + 2, :heads])
     return (
         part_first[None],
         part_second[None],

time: 86.8 us -> 86.3 us (level)
    unnamed x12 -> x11, local copies, waits for them, and re-layouts: 3.33 us -> 2.63 us
where the time goes in v14:
time: 86.3 us; the launch traced here: 85.6 us
  Pallas kernels  24.6 us (29%)
  waiting for transfers between devices  19.6 us (23%)
  starting transfers between devices  16 us (19%)
  local copies, waits for them, and re-layouts  15.3 us (18%)
  other arithmetic  7.78 us (9%)
  matrix products  1.29 us (1%)
  between operations  1.06 us (1%)
    pallas_call x1, Pallas kernels, forward_layers(): pl.pallas_call(forward_kernel, grid=(rows // BLOCK,), in_specs=[pl.BlockS...  13 us
    pallas_call x1, Pallas kernels, backward(): pl.pallas_call(backward_kernel, grid=(rows // BLOCK,), in_specs=[pl.Block...  11.6 us
    all_to_all x1, starting transfers between devices, per_device(): lax.all_to_all(outgoing, 'space', split_axis=0, concat_axis=0, tiled=True)  8.31 us
    all_to_all x1, waiting for transfers between devices, per_device(): lax.all_to_all(sendback, 'space', split_axis=1, concat_axis=1, tiled=True)  7 us
    all_to_all x1, waiting for transfers between devices, per_device(): lax.all_to_all(partials, 'space', split_axis=1, concat_axis=1, tiled=True)  6.91 us
    all_to_all x1, waiting for transfers between devices, per_device(): lax.all_to_all(outgoing, 'space', split_axis=0, concat_axis=0, tiled=True)  5.07 us
    all_to_all x1, starting transfers between devices, per_device(): lax.all_to_all(partials, 'space', split_axis=1, concat_axis=1, tiled=True)  3.5 us
    all_to_all x1, starting transfers between devices, per_device(): lax.all_to_all(sendback, 'space', split_axis=1, concat_axis=1, tiled=True)  3.5 us
  transfers between devices with their start and end apart: 6, of which 4 were waited for; matrix products, arithmetic and copies ran while one was open for 9% of the time, Pallas kernels for 0%

profile of v14, /device:TPU:0, one launch (start us, length us, event | category | flops | bytes accessed | tf_op | source)
XLA Modules:
  0.0 85.6 jit_solution(13234579497036984048)
XLA Ops:
  0.7 0.8 copy.129
  2.0 0.9 %reshape.249 = f32[3,128,32]{2,1,0:T(8,128)S(1)} reshape(f32[3,16,256]{2,1,0:T(8,128)} %param.12) | data formatting | bytes 98304 | tf_op jit(solution)/shard_map/reshape | solution.py:301
  3.0 0.8 reshape.250
  4.0 0.9 %fusion.4 = f32[16,12,128]{2,1,0:T(8,128)} fusion(f32[128,128,1]{0,1,2:T(8,128)S(1)} %bitcast.50, pred[16,12,128]{2,0,1:T(8,128)(4,1)S(1)} %broadcast_compare_fusion), kind=kOutput, calls=%fused_computation.9 | convolution fusion | flops 37748736 | bytes 188416 | tf_op jit(solution)/shard_map/dot_general | solution.py:304
  4.9 8.3 %all-to-all-start = ((f32[16,12,128]{2,1,0:T(8,128)}), f32[16,12,128]{2,1,0:T(8,128)S(1)}, u32[]{:S(2)}, u32[]{:S(2)}) async-start(f32[16,12,128]{2,1,0:T(8,128)} %fusion.4), calls=%async_computation | async-start | bytes 262144 | tf_op jit(solution)/shard_map/all_to_all | solution.py:312
  13.2 1.4 %copy.135 = f32[3,128]{0,1:T(8,128)} copy(f32[3,128]{1,0:T(4,128)} %param.17) | data formatting | bytes 3072 | tf_op args[5]
  14.6 1.3 %copy.136.bh_ref = f32[4,1]{1,0:T(4,128)} copy(f32[4,1]{0,1:T(1,128)} %bitcast.63) | data formatting | bytes 32 | tf_op jit(solution)/shard_map/reshape;squeeze | solution.py:182
  15.9 5.1 %all-to-all-done = f32[16,12,128]{2,1,0:T(8,128)S(1)} async-done(((f32[16,12,128]{2,1,0:T(8,128)}), f32[16,12,128]{2,1,0:T(8,128)S(1)}, u32[]{:S(2)}, u32[]{:S(2)}) %all-to-all-start) | async-done | bytes 98336 | tf_op jit(solution)/shard_map/all_to_all | solution.py:312
  21.4 0.8 reshape.253.place_ref
  22.2 13.0 %shard_map.163 = (bf16[256,6144]{1,0:T(8,128)(2,1)}, bf16[6144,256]{1,0:T(8,128)(2,1)}, bf16[6144,256]{1,0:T(8,128)(2,1)}, f32[6144,256]{1,0:T(8,128)}, f32[6144,256]{1,0:T(8,128)}, /*index=5*/f32[4,6144]{1,0:T(4,128)}) custom-call(f32[4,6144]{1,0:T(4,128)} %reshape.253.place_ref, f32[128,3]{1,0:T(8,128)} %bitcast.51, bf16[256,256]{1,0:T(8,128)(2,1)} %bitcast.53, ...), custom_call_target="tpu_custom_call" | custom-call | tf_op jit(solution)/shard_map/pallas_call | solution.py:144
  35.2 1.0 %fusion.24 = (f32[1,6144]{1,0:T(1,128)S(1)}, f32[6144]{0:T(1024)S(1)}) fusion(f32[4,6144]{1,0:T(4,128)} %get-tuple-element.22), kind=kLoop, calls=%fused_computation.56 | loop fusion | bytes 73728 | tf_op jit(solution)/shard_map/slice | solution.py:192
  36.3 1.0 %add_divide_fusion = f32[3,6144]{1,0:T(4,128)S(1)} fusion(f32[4,6144]{1,0:T(4,128)} %get-tuple-element.22), kind=kLoop, calls=%fused_computation.13 | loop fusion | flops 55296 | bytes 147456 | tf_op jit(solution)/shard_map/div | solution.py:193
  38.2 0.6 copy.147
  38.9 3.5 %all-to-all-start.1 = ((f32[4,16,12]{2,0,1:T(4,128)}), f32[4,16,12]{2,0,1:T(4,128)S(1)}, u32[]{:S(2)}, u32[]{:S(2)}) async-start(f32[4,16,12]{2,0,1:T(4,128)} %copy.147), calls=%async_computation.1 | async-start | bytes 65536 | tf_op jit(solution)/shard_map/all_to_all | solution.py:331
  42.8 6.9 %all-to-all-done.1 = f32[4,16,12]{2,0,1:T(4,128)S(1)} async-done(((f32[4,16,12]{2,0,1:T(4,128)}), f32[4,16,12]{2,0,1:T(4,128)S(1)}, u32[]{:S(2)}, u32[]{:S(2)}) %all-to-all-start.1) | async-done | bytes 3104 | tf_op jit(solution)/shard_map/all_to_all | solution.py:331
  51.8 3.5 %all-to-all-start.2 = ((f32[4,16,12]{2,0,1:T(4,128)}), f32[4,16,12]{2,0,1:T(4,128)S(1)}, u32[]{:S(2)}, u32[]{:S(2)}) async-start(f32[4,16,12]{2,0,1:T(4,128)} %copy.153), calls=%async_computation.2 | async-start | bytes 65536 | tf_op jit(solution)/shard_map/all_to_all | solution.py:356
  55.7 7.0 %all-to-all-done.2 = f32[4,16,12]{2,0,1:T(4,128)S(1)} async-done(((f32[4,16,12]{2,0,1:T(4,128)}), f32[4,16,12]{2,0,1:T(4,128)S(1)}, u32[]{:S(2)}, u32[]{:S(2)}) %all-to-all-start.2) | async-done | bytes 3104 | tf_op jit(solution)/shard_map/all_to_all | solution.py:356
  64.3 0.9 %copy.160 = bf16[4,6144]{0,1:T(8,128)(2,1)S(1)} copy(bf16[4,6144]{1,0:T(4,128)(2,1)S(1)} %pad_maximum_fusion.1) | data formatting | bytes 98304 | tf_op jit(solution)/shard_map/concatenate | solution.py:220
  65.2 0.8 convert_reduce_fusion
  66.4 11.6 %shard_map.164 = (f32[256,256]{1,0:T(8,128)}, f32[1,256]{1,0:T(1,128)}, f32[256,256]{1,0:T(8,128)}, f32[1,256]{1,0:T(1,128)}, f32[4,256]{1,0:T(4,128)}) custom-call(bf16[256,6144]{1,0:T(8,128)(2,1)} %get-tuple-element.17.enc_ref, bf16[6144,256]{1,0:T(8,128)(2,1)} %get-tuple-element.18.a1_ref, bf16[6144,256]{1,0:T(8,128)(2,1)} %get-tuple-element.19.a2_ref, ...), custom_call_target="tpu_custom_call" | custom-call | tf_op jit(solution)/shard_map/pallas_call | solution.py:229
  78.0 0.7 pad_maximum_fusion.3
  80.0 0.7 fusion.22
  82.4 1.6 %fusion = f32[1,128,256]{2,1,0:T(8,128)} fusion(f32[256,256]{1,0:T(8,128)S(1)} %collective-permute-done.1, s32[]{:T(128)S(6)} %select_n.17, f32[256,256]{1,0:T(8,128)} %get-tuple-element.24), kind=kLoop, calls=%fused_computation.3 | loop fusion | flops 32768 | bytes 393220 | tf_op jit(solution)/shard_map/broadcast_in_dim | solution.py:412
  84.0 1.6 %fusion.1 = f32[1,128,256]{2,1,0:T(8,128)} fusion(f32[256,256]{1,0:T(8,128)S(1)} %collective-permute-done, s32[]{:T(128)S(6)} %select_n.17, f32[256,256]{1,0:T(8,128)} %get-tuple-element.23), kind=kLoop, calls=%fused_computation.5 | loop fusion | flops 32768 | bytes 393220 | tf_op jit(solution)/shard_map/broadcast_in_dim | solution.py:411
  (92 shorter events, 9.7 us)
Async XLA Ops:
  0.6 41.7 %copy-start.3 = (f32[3,16]{1,0:T(4,128)S(1)}, f32[3,16]{1,0:T(4,128)}, u32[]{:S(2)}) copy-start(f32[3,16]{1,0:T(4,128)} %param.16) | copy-start | bytes 580
  2.9 47.6 %copy-start.2 = (s32[16,8]{0,1:T(8,128)S(1)}, s32[16,8]{0,1:T(8,128)}, u32[]{:S(2)}) copy-start(s32[16,8]{0,1:T(8,128)} %param.15) | copy-start | bytes 1540
  4.9 16.1 %all-to-all-start = ((f32[16,12,128]{2,1,0:T(8,128)}), f32[16,12,128]{2,1,0:T(8,128)S(1)}, u32[]{:S(2)}, u32[]{:S(2)}) async-start(f32[16,12,128]{2,1,0:T(8,128)} %fusion.4), calls=%async_computation | async-start | bytes 262144 | tf_op jit(solution)/shard_map/all_to_all | solution.py:312
  35.2 27.9 %copy-start.1 = (f32[4,6144]{1,0:T(4,128)S(1)}, f32[4,6144]{1,0:T(4,128)}, u32[]{:S(2)}) copy-start(f32[4,6144]{1,0:T(4,128)} %get-tuple-element.22) | copy-start | bytes 294916
  38.9 10.9 %all-to-all-start.1 = ((f32[4,16,12]{2,0,1:T(4,128)}), f32[4,16,12]{2,0,1:T(4,128)S(1)}, u32[]{:S(2)}, u32[]{:S(2)}) async-start(f32[4,16,12]{2,0,1:T(4,128)} %copy.147), calls=%async_computation.1 | async-start | bytes 65536 | tf_op jit(solution)/shard_map/all_to_all | solution.py:331
  51.8 10.9 %all-to-all-start.2 = ((f32[4,16,12]{2,0,1:T(4,128)}), f32[4,16,12]{2,0,1:T(4,128)S(1)}, u32[]{:S(2)}, u32[]{:S(2)}) async-start(f32[4,16,12]{2,0,1:T(4,128)} %copy.153), calls=%async_computation.2 | async-start | bytes 65536 | tf_op jit(solution)/shard_map/all_to_all | solution.py:356
  65.2 1.2 %copy-start = (bf16[4,6144]{0,1:T(8,128)(2,1)}, bf16[4,6144]{0,1:T(8,128)(2,1)S(1)}, u32[]{:S(2)}) copy-start(bf16[4,6144]{0,1:T(8,128)(2,1)S(1)} %copy.160) | copy-start | bytes 147460
  78.8 1.2 %collective-permute-start.2 = (f32[7,256]{1,0:T(8,128)S(1)}, f32[7,256]{1,0:T(8,128)S(1)}, u32[]{:S(2)}, u32[]{:S(2)}) collective-permute-start(f32[7,256]{1,0:T(8,128)S(1)} %pad_maximum_fusion.3), channel_id=1, source_target_pairs={{0,1},{1,0},{2,3},{3,2},{4,5},{5,4},{6,7},{7,6},{8,9},{9,8},{10,11... | collective-permute-start | bytes 21512 | tf_op jit(solution)/shard_map/ppermute | solution.py:374
  78.9 3.6 %collective-permute-start.1 = (f32[256,256]{1,0:T(8,128)}, f32[256,256]{1,0:T(8,128)S(1)}, u32[]{:S(2)}, u32[]{:S(2)}) collective-permute-start(f32[256,256]{1,0:T(8,128)} %get-tuple-element.24), channel_id=1, source_target_pairs={{0,1},{1,0},{2,3},{3,2},{4,5},{5,4},{6,7},{7,6},{8,9},{9,8},{10,11... | collective-permute-start | bytes 786440 | tf_op jit(solution)/shard_map/ppermute | solution.py:374
  79.4 4.7 %collective-permute-start = (f32[256,256]{1,0:T(8,128)}, f32[256,256]{1,0:T(8,128)S(1)}, u32[]{:S(2)}, u32[]{:S(2)}) collective-permute-start(f32[256,256]{1,0:T(8,128)} %get-tuple-element.23), channel_id=1, source_target_pairs={{0,1},{1,0},{2,3},{3,2},{4,5},{5,4},{6,7},{7,6},{8,9},{9,8},{10,11... | collective-permute-start | bytes 786440 | tf_op jit(solution)/shard_map/ppermute | solution.py:374

commit v15 on v14

--- a/solution.py
+++ b/solution.py
@@ -129,7 +129,7 @@
     )
 
 
-BLOCK = 1024
+BLOCK = 2048
 
 
 def forward_layers(samples, fourier, params):

time: 86.3 us -> 85.8 us (level)
  no operation moved by 1% of the time
where the time goes in v15:
time: 85.8 us; the launch traced here: 85.2 us
  Pallas kernels  24.2 us (28%)
  waiting for transfers between devices  19.6 us (23%)
  starting transfers between devices  16 us (19%)
  local copies, waits for them, and re-layouts  15.3 us (18%)
  other arithmetic  7.78 us (9%)
  matrix products  1.29 us (2%)
  between operations  1.05 us (1%)
    pallas_call x1, Pallas kernels, forward_layers(): pl.pallas_call(forward_kernel, grid=(rows // BLOCK,), in_specs=[pl.BlockS...  13.3 us
    pallas_call x1, Pallas kernels, backward(): pl.pallas_call(backward_kernel, grid=(rows // BLOCK,), in_specs=[pl.Block...  10.9 us
    all_to_all x1, starting transfers between devices, per_device(): lax.all_to_all(outgoing, 'space', split_axis=0, concat_axis=0, tiled=True)  8.31 us
    all_to_all x1, waiting for transfers between devices, per_device(): lax.all_to_all(sendback, 'space', split_axis=1, concat_axis=1, tiled=True)  7 us
    all_to_all x1, waiting for transfers between devices, per_device(): lax.all_to_all(partials, 'space', split_axis=1, concat_axis=1, tiled=True)  6.91 us
    all_to_all x1, waiting for transfers between devices, per_device(): lax.all_to_all(outgoing, 'space', split_axis=0, concat_axis=0, tiled=True)  5.07 us
    all_to_all x1, starting transfers between devices, per_device(): lax.all_to_all(partials, 'space', split_axis=1, concat_axis=1, tiled=True)  3.5 us
    all_to_all x1, starting transfers between devices, per_device(): lax.all_to_all(sendback, 'space', split_axis=1, concat_axis=1, tiled=True)  3.5 us
  transfers between devices with their start and end apart: 6, of which 4 were waited for; matrix products, arithmetic and copies ran while one was open for 9% of the time, Pallas kernels for 0%

profile of v15, /device:TPU:0, one launch (start us, length us, event | category | flops | bytes accessed | tf_op | source)
XLA Modules:
  0.0 85.2 jit_solution(17771843605268088821)
XLA Ops:
  0.7 0.8 copy.129
  2.0 0.9 %reshape.249 = f32[3,128,32]{2,1,0:T(8,128)S(1)} reshape(f32[3,16,256]{2,1,0:T(8,128)} %param.12) | data formatting | bytes 98304 | tf_op jit(solution)/shard_map/reshape | solution.py:301
  3.0 0.8 reshape.250
  4.0 0.9 %fusion.4 = f32[16,12,128]{2,1,0:T(8,128)} fusion(f32[128,128,1]{0,1,2:T(8,128)S(1)} %bitcast.50, pred[16,12,128]{2,0,1:T(8,128)(4,1)S(1)} %broadcast_compare_fusion), kind=kOutput, calls=%fused_computation.9 | convolution fusion | flops 37748736 | bytes 188416 | tf_op jit(solution)/shard_map/dot_general | solution.py:304
  4.9 8.3 %all-to-all-start = ((f32[16,12,128]{2,1,0:T(8,128)}), f32[16,12,128]{2,1,0:T(8,128)S(1)}, u32[]{:S(2)}, u32[]{:S(2)}) async-start(f32[16,12,128]{2,1,0:T(8,128)} %fusion.4), calls=%async_computation | async-start | bytes 262144 | tf_op jit(solution)/shard_map/all_to_all | solution.py:312
  13.2 1.4 %copy.135 = f32[3,128]{0,1:T(8,128)} copy(f32[3,128]{1,0:T(4,128)} %param.17) | data formatting | bytes 3072 | tf_op args[5]
  14.6 1.3 %copy.136.bh_ref = f32[4,1]{1,0:T(4,128)} copy(f32[4,1]{0,1:T(1,128)} %bitcast.63) | data formatting | bytes 32 | tf_op jit(solution)/shard_map/reshape;squeeze | solution.py:182
  15.9 5.1 %all-to-all-done = f32[16,12,128]{2,1,0:T(8,128)S(1)} async-done(((f32[16,12,128]{2,1,0:T(8,128)}), f32[16,12,128]{2,1,0:T(8,128)S(1)}, u32[]{:S(2)}, u32[]{:S(2)}) %all-to-all-start) | async-done | bytes 98336 | tf_op jit(solution)/shard_map/all_to_all | solution.py:312
  21.4 0.8 reshape.253.place_ref
  22.2 13.3 %shard_map.163 = (bf16[256,6144]{1,0:T(8,128)(2,1)}, bf16[6144,256]{1,0:T(8,128)(2,1)}, bf16[6144,256]{1,0:T(8,128)(2,1)}, f32[6144,256]{1,0:T(8,128)}, f32[6144,256]{1,0:T(8,128)}, /*index=5*/f32[4,6144]{1,0:T(4,128)}) custom-call(f32[4,6144]{1,0:T(4,128)} %reshape.253.place_ref, f32[128,3]{1,0:T(8,128)} %bitcast.51, bf16[256,256]{1,0:T(8,128)(2,1)} %bitcast.53, ...), custom_call_target="tpu_custom_call" | custom-call | tf_op jit(solution)/shard_map/pallas_call | solution.py:144
  35.5 1.0 %fusion.24 = (f32[1,6144]{1,0:T(1,128)S(1)}, f32[6144]{0:T(1024)S(1)}) fusion(f32[4,6144]{1,0:T(4,128)} %get-tuple-element.22), kind=kLoop, calls=%fused_computation.56 | loop fusion | bytes 73728 | tf_op jit(solution)/shard_map/slice | solution.py:192
  36.5 1.0 %add_divide_fusion = f32[3,6144]{1,0:T(4,128)S(1)} fusion(f32[4,6144]{1,0:T(4,128)} %get-tuple-element.22), kind=kLoop, calls=%fused_computation.13 | loop fusion | flops 55296 | bytes 147456 | tf_op jit(solution)/shard_map/div | solution.py:193
  38.5 0.6 copy.147
  39.1 3.5 %all-to-all-start.1 = ((f32[4,16,12]{2,0,1:T(4,128)}), f32[4,16,12]{2,0,1:T(4,128)S(1)}, u32[]{:S(2)}, u32[]{:S(2)}) async-start(f32[4,16,12]{2,0,1:T(4,128)} %copy.147), calls=%async_computation.1 | async-start | bytes 65536 | tf_op jit(solution)/shard_map/all_to_all | solution.py:331
  43.1 6.9 %all-to-all-done.1 = f32[4,16,12]{2,0,1:T(4,128)S(1)} async-done(((f32[4,16,12]{2,0,1:T(4,128)}), f32[4,16,12]{2,0,1:T(4,128)S(1)}, u32[]{:S(2)}, u32[]{:S(2)}) %all-to-all-start.1) | async-done | bytes 3104 | tf_op jit(solution)/shard_map/all_to_all | solution.py:331
  52.1 3.5 %all-to-all-start.2 = ((f32[4,16,12]{2,0,1:T(4,128)}), f32[4,16,12]{2,0,1:T(4,128)S(1)}, u32[]{:S(2)}, u32[]{:S(2)}) async-start(f32[4,16,12]{2,0,1:T(4,128)} %copy.153), calls=%async_computation.2 | async-start | bytes 65536 | tf_op jit(solution)/shard_map/all_to_all | solution.py:356
  56.0 7.0 %all-to-all-done.2 = f32[4,16,12]{2,0,1:T(4,128)S(1)} async-done(((f32[4,16,12]{2,0,1:T(4,128)}), f32[4,16,12]{2,0,1:T(4,128)S(1)}, u32[]{:S(2)}, u32[]{:S(2)}) %all-to-all-start.2) | async-done | bytes 3104 | tf_op jit(solution)/shard_map/all_to_all | solution.py:356
  64.6 0.9 %copy.160 = bf16[4,6144]{0,1:T(8,128)(2,1)S(1)} copy(bf16[4,6144]{1,0:T(4,128)(2,1)S(1)} %pad_maximum_fusion.1) | data formatting | bytes 98304 | tf_op jit(solution)/shard_map/concatenate | solution.py:220
  65.5 0.8 convert_reduce_fusion
  66.7 10.9 %shard_map.164 = (f32[256,256]{1,0:T(8,128)}, f32[1,256]{1,0:T(1,128)}, f32[256,256]{1,0:T(8,128)}, f32[1,256]{1,0:T(1,128)}, f32[4,256]{1,0:T(4,128)}) custom-call(bf16[256,6144]{1,0:T(8,128)(2,1)} %get-tuple-element.17.enc_ref, bf16[6144,256]{1,0:T(8,128)(2,1)} %get-tuple-element.18.a1_ref, bf16[6144,256]{1,0:T(8,128)(2,1)} %get-tuple-element.19.a2_ref, ...), custom_call_target="tpu_custom_call" | custom-call | tf_op jit(solution)/shard_map/pallas_call | solution.py:229
  77.6 0.7 pad_maximum_fusion.3
  79.6 0.7 fusion.22
  82.0 1.6 %fusion = f32[1,128,256]{2,1,0:T(8,128)} fusion(f32[256,256]{1,0:T(8,128)S(1)} %collective-permute-done.1, s32[]{:T(128)S(6)} %select_n.17, f32[256,256]{1,0:T(8,128)} %get-tuple-element.24), kind=kLoop, calls=%fused_computation.3 | loop fusion | flops 32768 | bytes 393220 | tf_op jit(solution)/shard_map/broadcast_in_dim | solution.py:412
  83.6 1.6 %fusion.1 = f32[1,128,256]{2,1,0:T(8,128)} fusion(f32[256,256]{1,0:T(8,128)S(1)} %collective-permute-done, s32[]{:T(128)S(6)} %select_n.17, f32[256,256]{1,0:T(8,128)} %get-tuple-element.23), kind=kLoop, calls=%fused_computation.5 | loop fusion | flops 32768 | bytes 393220 | tf_op jit(solution)/shard_map/broadcast_in_dim | solution.py:411
  (92 shorter events, 9.7 us)
Async XLA Ops:
  0.6 42.0 %copy-start.3 = (f32[3,16]{1,0:T(4,128)S(1)}, f32[3,16]{1,0:T(4,128)}, u32[]{:S(2)}) copy-start(f32[3,16]{1,0:T(4,128)} %param.16) | copy-start | bytes 580
  2.9 47.9 %copy-start.2 = (s32[16,8]{0,1:T(8,128)S(1)}, s32[16,8]{0,1:T(8,128)}, u32[]{:S(2)}) copy-start(s32[16,8]{0,1:T(8,128)} %param.15) | copy-start | bytes 1540
  4.9 16.1 %all-to-all-start = ((f32[16,12,128]{2,1,0:T(8,128)}), f32[16,12,128]{2,1,0:T(8,128)S(1)}, u32[]{:S(2)}, u32[]{:S(2)}) async-start(f32[16,12,128]{2,1,0:T(8,128)} %fusion.4), calls=%async_computation | async-start | bytes 262144 | tf_op jit(solution)/shard_map/all_to_all | solution.py:312
  35.5 27.9 %copy-start.1 = (f32[4,6144]{1,0:T(4,128)S(1)}, f32[4,6144]{1,0:T(4,128)}, u32[]{:S(2)}) copy-start(f32[4,6144]{1,0:T(4,128)} %get-tuple-element.22) | copy-start | bytes 294916
  39.1 10.9 %all-to-all-start.1 = ((f32[4,16,12]{2,0,1:T(4,128)}), f32[4,16,12]{2,0,1:T(4,128)S(1)}, u32[]{:S(2)}, u32[]{:S(2)}) async-start(f32[4,16,12]{2,0,1:T(4,128)} %copy.147), calls=%async_computation.1 | async-start | bytes 65536 | tf_op jit(solution)/shard_map/all_to_all | solution.py:331
  52.1 10.9 %all-to-all-start.2 = ((f32[4,16,12]{2,0,1:T(4,128)}), f32[4,16,12]{2,0,1:T(4,128)S(1)}, u32[]{:S(2)}, u32[]{:S(2)}) async-start(f32[4,16,12]{2,0,1:T(4,128)} %copy.153), calls=%async_computation.2 | async-start | bytes 65536 | tf_op jit(solution)/shard_map/all_to_all | solution.py:356
  65.5 1.2 %copy-start = (bf16[4,6144]{0,1:T(8,128)(2,1)}, bf16[4,6144]{0,1:T(8,128)(2,1)S(1)}, u32[]{:S(2)}) copy-start(bf16[4,6144]{0,1:T(8,128)(2,1)S(1)} %copy.160) | copy-start | bytes 147460
  78.4 1.2 %collective-permute-start.2 = (f32[7,256]{1,0:T(8,128)S(1)}, f32[7,256]{1,0:T(8,128)S(1)}, u32[]{:S(2)}, u32[]{:S(2)}) collective-permute-start(f32[7,256]{1,0:T(8,128)S(1)} %pad_maximum_fusion.3), channel_id=1, source_target_pairs={{0,1},{1,0},{2,3},{3,2},{4,5},{5,4},{6,7},{7,6},{8,9},{9,8},{10,11... | collective-permute-start | bytes 21512 | tf_op jit(solution)/shard_map/ppermute | solution.py:374
  78.4 3.6 %collective-permute-start.1 = (f32[256,256]{1,0:T(8,128)}, f32[256,256]{1,0:T(8,128)S(1)}, u32[]{:S(2)}, u32[]{:S(2)}) collective-permute-start(f32[256,256]{1,0:T(8,128)} %get-tuple-element.24), channel_id=1, source_target_pairs={{0,1},{1,0},{2,3},{3,2},{4,5},{5,4},{6,7},{7,6},{8,9},{9,8},{10,11... | collective-permute-start | bytes 786440 | tf_op jit(solution)/shard_map/ppermute | solution.py:374
  78.9 4.7 %collective-permute-start = (f32[256,256]{1,0:T(8,128)}, f32[256,256]{1,0:T(8,128)S(1)}, u32[]{:S(2)}, u32[]{:S(2)}) collective-permute-start(f32[256,256]{1,0:T(8,128)} %get-tuple-element.23), channel_id=1, source_target_pairs={{0,1},{1,0},{2,3},{3,2},{4,5},{5,4},{6,7},{7,6},{8,9},{9,8},{10,11... | collective-permute-start | bytes 786440 | tf_op jit(solution)/shard_map/ppermute | solution.py:374

commit v16 on v15

--- a/solution.py
+++ b/solution.py
@@ -26,20 +26,10 @@
     angle = (turns - quarter * 0.25) * two_pi
     square = angle * angle
     sine = angle * (
-        1.0
-        + square
-        * (
-            -1.0 / 6.0
-            + square * (1.0 / 120.0 + square * (-1.0 / 5040.0 + square * (1.0 / 362880.0)))
-        )
+        1.0 + square * (-1.0 / 6.0 + square * (1.0 / 120.0 + square * (-1.0 / 5040.0)))
     )
     cosine = 1.0 + square * (
-        -0.5
-        + square
-        * (
-            1.0 / 24.0
-            + square * (-1.0 / 720.0 + square * (1.0 / 40320.0 + square * (-1.0 / 3628800.0)))
-        )
+        -0.5 + square * (1.0 / 24.0 + square * (-1.0 / 720.0 + square * (1.0 / 40320.0)))
     )
     step = quarter - 4.0 * jnp.floor(quarter * 0.25)
     flip = step >= 2.0
@@ -129,7 +119,7 @@
     )
 
 
-BLOCK = 2048
+BLOCK = 3072
 
 
 def forward_layers(samples, fourier, params):

time: 85.8 us -> 85.8 us (level)
  no operation moved by 1% of the time
where the time goes in v16:
time: 85.8 us; the launch traced here: 85.2 us
  Pallas kernels  24.2 us (28%)
  waiting for transfers between devices  19.4 us (23%)
  starting transfers between devices  16.1 us (19%)
  local copies, waits for them, and re-layouts  15.3 us (18%)
  other arithmetic  7.78 us (9%)
  matrix products  1.29 us (2%)
  between operations  1.06 us (1%)
    pallas_call x1, Pallas kernels, forward_layers(): pl.pallas_call(forward_kernel, grid=(rows // BLOCK,), in_specs=[pl.BlockS...  13.8 us
    pallas_call x1, Pallas kernels, backward(): pl.pallas_call(backward_kernel, grid=(rows // BLOCK,), in_specs=[pl.Block...  10.4 us
    all_to_all x1, starting transfers between devices, per_device(): lax.all_to_all(outgoing, 'space', split_axis=0, concat_axis=0, tiled=True)  8.31 us
    all_to_all x1, waiting for transfers between devices, per_device(): lax.all_to_all(partials, 'space', split_axis=1, concat_axis=1, tiled=True)  6.91 us
    all_to_all x1, waiting for transfers between devices, per_device(): lax.all_to_all(sendback, 'space', split_axis=1, concat_axis=1, tiled=True)  6.82 us
    all_to_all x1, waiting for transfers between devices, per_device(): lax.all_to_all(outgoing, 'space', split_axis=0, concat_axis=0, tiled=True)  5.07 us
    all_to_all x1, starting transfers between devices, per_device(): lax.all_to_all(sendback, 'space', split_axis=1, concat_axis=1, tiled=True)  3.68 us
    all_to_all x1, starting transfers between devices, per_device(): lax.all_to_all(partials, 'space', split_axis=1, concat_axis=1, tiled=True)  3.5 us
  transfers between devices with their start and end apart: 6, of which 4 were waited for; matrix products, arithmetic and copies ran while one was open for 9% of the time, Pallas kernels for 0%

profile of v16, /device:TPU:0, one launch (start us, length us, event | category | flops | bytes accessed | tf_op | source)
XLA Modules:
  0.0 85.2 jit_solution(15200983038571442278)
XLA Ops:
  0.7 0.8 copy.129
  2.0 0.9 %reshape.249 = f32[3,128,32]{2,1,0:T(8,128)S(1)} reshape(f32[3,16,256]{2,1,0:T(8,128)} %param.12) | data formatting | bytes 98304 | tf_op jit(solution)/shard_map/reshape | solution.py:291
  3.0 0.8 reshape.250
  4.0 0.9 %fusion.4 = f32[16,12,128]{2,1,0:T(8,128)} fusion(f32[128,128,1]{0,1,2:T(8,128)S(1)} %bitcast.50, pred[16,12,128]{2,0,1:T(8,128)(4,1)S(1)} %broadcast_compare_fusion), kind=kOutput, calls=%fused_computation.9 | convolution fusion | flops 37748736 | bytes 188416 | tf_op jit(solution)/shard_map/dot_general | solution.py:294
  4.9 8.3 %all-to-all-start = ((f32[16,12,128]{2,1,0:T(8,128)}), f32[16,12,128]{2,1,0:T(8,128)S(1)}, u32[]{:S(2)}, u32[]{:S(2)}) async-start(f32[16,12,128]{2,1,0:T(8,128)} %fusion.4), calls=%async_computation | async-start | bytes 262144 | tf_op jit(solution)/shard_map/all_to_all | solution.py:302
  13.2 1.4 %copy.135 = f32[3,128]{0,1:T(8,128)} copy(f32[3,128]{1,0:T(4,128)} %param.17) | data formatting | bytes 3072 | tf_op args[5]
  14.6 1.3 %copy.136.bh_ref = f32[4,1]{1,0:T(4,128)} copy(f32[4,1]{0,1:T(1,128)} %bitcast.63) | data formatting | bytes 32 | tf_op jit(solution)/shard_map/reshape;squeeze | solution.py:172
  15.9 5.1 %all-to-all-done = f32[16,12,128]{2,1,0:T(8,128)S(1)} async-done(((f32[16,12,128]{2,1,0:T(8,128)}), f32[16,12,128]{2,1,0:T(8,128)S(1)}, u32[]{:S(2)}, u32[]{:S(2)}) %all-to-all-start) | async-done | bytes 98336 | tf_op jit(solution)/shard_map/all_to_all | solution.py:302
  21.4 0.8 reshape.253.place_ref
  22.2 13.8 %shard_map.163 = (bf16[256,6144]{1,0:T(8,128)(2,1)}, bf16[6144,256]{1,0:T(8,128)(2,1)}, bf16[6144,256]{1,0:T(8,128)(2,1)}, f32[6144,256]{1,0:T(8,128)}, f32[6144,256]{1,0:T(8,128)}, /*index=5*/f32[4,6144]{1,0:T(4,128)}) custom-call(f32[4,6144]{1,0:T(4,128)} %reshape.253.place_ref, f32[128,3]{1,0:T(8,128)} %bitcast.51, bf16[256,256]{1,0:T(8,128)(2,1)} %bitcast.53, ...), custom_call_target="tpu_custom_call" | custom-call | tf_op jit(solution)/shard_map/pallas_call | solution.py:134
  36.0 1.0 %fusion.24 = (f32[1,6144]{1,0:T(1,128)S(1)}, f32[6144]{0:T(1024)S(1)}) fusion(f32[4,6144]{1,0:T(4,128)} %get-tuple-element.22), kind=kLoop, calls=%fused_computation.56 | loop fusion | bytes 73728 | tf_op jit(solution)/shard_map/slice | solution.py:182
  37.0 1.0 %add_divide_fusion = f32[3,6144]{1,0:T(4,128)S(1)} fusion(f32[4,6144]{1,0:T(4,128)} %get-tuple-element.22), kind=kLoop, calls=%fused_computation.13 | loop fusion | flops 55296 | bytes 147456 | tf_op jit(solution)/shard_map/div | solution.py:183
  39.0 0.6 copy.147
  39.6 3.5 %all-to-all-start.1 = ((f32[4,16,12]{2,0,1:T(4,128)}), f32[4,16,12]{2,0,1:T(4,128)S(1)}, u32[]{:S(2)}, u32[]{:S(2)}) async-start(f32[4,16,12]{2,0,1:T(4,128)} %copy.147), calls=%async_computation.1 | async-start | bytes 65536 | tf_op jit(solution)/shard_map/all_to_all | solution.py:321
  43.6 6.9 %all-to-all-done.1 = f32[4,16,12]{2,0,1:T(4,128)S(1)} async-done(((f32[4,16,12]{2,0,1:T(4,128)}), f32[4,16,12]{2,0,1:T(4,128)S(1)}, u32[]{:S(2)}, u32[]{:S(2)}) %all-to-all-start.1) | async-done | bytes 3104 | tf_op jit(solution)/shard_map/all_to_all | solution.py:321
  52.6 3.7 %all-to-all-start.2 = ((f32[4,16,12]{2,0,1:T(4,128)}), f32[4,16,12]{2,0,1:T(4,128)S(1)}, u32[]{:S(2)}, u32[]{:S(2)}) async-start(f32[4,16,12]{2,0,1:T(4,128)} %copy.153), calls=%async_computation.2 | async-start | bytes 65536 | tf_op jit(solution)/shard_map/all_to_all | solution.py:346
  56.6 6.8 %all-to-all-done.2 = f32[4,16,12]{2,0,1:T(4,128)S(1)} async-done(((f32[4,16,12]{2,0,1:T(4,128)}), f32[4,16,12]{2,0,1:T(4,128)S(1)}, u32[]{:S(2)}, u32[]{:S(2)}) %all-to-all-start.2) | async-done | bytes 3104 | tf_op jit(solution)/shard_map/all_to_all | solution.py:346
  65.1 0.9 %copy.160 = bf16[4,6144]{0,1:T(8,128)(2,1)S(1)} copy(bf16[4,6144]{1,0:T(4,128)(2,1)S(1)} %pad_maximum_fusion.1) | data formatting | bytes 98304 | tf_op jit(solution)/shard_map/concatenate | solution.py:210
  66.0 0.8 convert_reduce_fusion
  67.2 10.4 %shard_map.164 = (f32[256,256]{1,0:T(8,128)}, f32[1,256]{1,0:T(1,128)}, f32[256,256]{1,0:T(8,128)}, f32[1,256]{1,0:T(1,128)}, f32[4,256]{1,0:T(4,128)}) custom-call(bf16[256,6144]{1,0:T(8,128)(2,1)} %get-tuple-element.17.enc_ref, bf16[6144,256]{1,0:T(8,128)(2,1)} %get-tuple-element.18.a1_ref, bf16[6144,256]{1,0:T(8,128)(2,1)} %get-tuple-element.19.a2_ref, ...), custom_call_target="tpu_custom_call" | custom-call | tf_op jit(solution)/shard_map/pallas_call | solution.py:219
  77.6 0.7 pad_maximum_fusion.3
  79.6 0.7 fusion.22
  82.0 1.6 %fusion = f32[1,128,256]{2,1,0:T(8,128)} fusion(f32[256,256]{1,0:T(8,128)S(1)} %collective-permute-done.1, s32[]{:T(128)S(6)} %select_n.17, f32[256,256]{1,0:T(8,128)} %get-tuple-element.24), kind=kLoop, calls=%fused_computation.3 | loop fusion | flops 32768 | bytes 393220 | tf_op jit(solution)/shard_map/broadcast_in_dim | solution.py:402
  83.6 1.6 %fusion.1 = f32[1,128,256]{2,1,0:T(8,128)} fusion(f32[256,256]{1,0:T(8,128)S(1)} %collective-permute-done, s32[]{:T(128)S(6)} %select_n.17, f32[256,256]{1,0:T(8,128)} %get-tuple-element.23), kind=kLoop, calls=%fused_computation.5 | loop fusion | flops 32768 | bytes 393220 | tf_op jit(solution)/shard_map/broadcast_in_dim | solution.py:401
  (92 shorter events, 9.7 us)
Async XLA Ops:
  0.6 42.5 %copy-start.3 = (f32[3,16]{1,0:T(4,128)S(1)}, f32[3,16]{1,0:T(4,128)}, u32[]{:S(2)}) copy-start(f32[3,16]{1,0:T(4,128)} %param.16) | copy-start | bytes 580
  2.9 48.3 %copy-start.2 = (s32[16,8]{0,1:T(8,128)S(1)}, s32[16,8]{0,1:T(8,128)}, u32[]{:S(2)}) copy-start(s32[16,8]{0,1:T(8,128)} %param.15) | copy-start | bytes 1540
  4.9 16.1 %all-to-all-start = ((f32[16,12,128]{2,1,0:T(8,128)}), f32[16,12,128]{2,1,0:T(8,128)S(1)}, u32[]{:S(2)}, u32[]{:S(2)}) async-start(f32[16,12,128]{2,1,0:T(8,128)} %fusion.4), calls=%async_computation | async-start | bytes 262144 | tf_op jit(solution)/shard_map/all_to_all | solution.py:302
  36.0 27.9 %copy-start.1 = (f32[4,6144]{1,0:T(4,128)S(1)}, f32[4,6144]{1,0:T(4,128)}, u32[]{:S(2)}) copy-start(f32[4,6144]{1,0:T(4,128)} %get-tuple-element.22) | copy-start | bytes 294916
  39.6 10.9 %all-to-all-start.1 = ((f32[4,16,12]{2,0,1:T(4,128)}), f32[4,16,12]{2,0,1:T(4,128)S(1)}, u32[]{:S(2)}, u32[]{:S(2)}) async-start(f32[4,16,12]{2,0,1:T(4,128)} %copy.147), calls=%async_computation.1 | async-start | bytes 65536 | tf_op jit(solution)/shard_map/all_to_all | solution.py:321
  52.6 10.9 %all-to-all-start.2 = ((f32[4,16,12]{2,0,1:T(4,128)}), f32[4,16,12]{2,0,1:T(4,128)S(1)}, u32[]{:S(2)}, u32[]{:S(2)}) async-start(f32[4,16,12]{2,0,1:T(4,128)} %copy.153), calls=%async_computation.2 | async-start | bytes 65536 | tf_op jit(solution)/shard_map/all_to_all | solution.py:346
  66.0 1.2 %copy-start = (bf16[4,6144]{0,1:T(8,128)(2,1)}, bf16[4,6144]{0,1:T(8,128)(2,1)S(1)}, u32[]{:S(2)}) copy-start(bf16[4,6144]{0,1:T(8,128)(2,1)S(1)} %copy.160) | copy-start | bytes 147460
  78.4 1.2 %collective-permute-start.2 = (f32[7,256]{1,0:T(8,128)S(1)}, f32[7,256]{1,0:T(8,128)S(1)}, u32[]{:S(2)}, u32[]{:S(2)}) collective-permute-start(f32[7,256]{1,0:T(8,128)S(1)} %pad_maximum_fusion.3), channel_id=1, source_target_pairs={{0,1},{1,0},{2,3},{3,2},{4,5},{5,4},{6,7},{7,6},{8,9},{9,8},{10,11... | collective-permute-start | bytes 21512 | tf_op jit(solution)/shard_map/ppermute | solution.py:364
  78.4 3.6 %collective-permute-start.1 = (f32[256,256]{1,0:T(8,128)}, f32[256,256]{1,0:T(8,128)S(1)}, u32[]{:S(2)}, u32[]{:S(2)}) collective-permute-start(f32[256,256]{1,0:T(8,128)} %get-tuple-element.24), channel_id=1, source_target_pairs={{0,1},{1,0},{2,3},{3,2},{4,5},{5,4},{6,7},{7,6},{8,9},{9,8},{10,11... | collective-permute-start | bytes 786440 | tf_op jit(solution)/shard_map/ppermute | solution.py:364
  78.9 4.7 %collective-permute-start = (f32[256,256]{1,0:T(8,128)}, f32[256,256]{1,0:T(8,128)S(1)}, u32[]{:S(2)}, u32[]{:S(2)}) collective-permute-start(f32[256,256]{1,0:T(8,128)} %get-tuple-element.23), channel_id=1, source_target_pairs={{0,1},{1,0},{2,3},{3,2},{4,5},{5,4},{6,7},{7,6},{8,9},{9,8},{10,11... | collective-permute-start | bytes 786440 | tf_op jit(solution)/shard_map/ppermute | solution.py:364

commit v17 on v16

--- a/solution.py
+++ b/solution.py
@@ -120,6 +120,7 @@
 
 
 BLOCK = 3072
+FORWARD_BLOCK = 1024
 
 
 def forward_layers(samples, fourier, params):
@@ -133,9 +134,9 @@
     by_column = lambda i: (0, i)
     return pl.pallas_call(
         forward_kernel,
-        grid=(rows // BLOCK,),
+        grid=(rows // FORWARD_BLOCK,),
         in_specs=[
-            pl.BlockSpec((4, BLOCK), by_column),
+            pl.BlockSpec((4, FORWARD_BLOCK), by_column),
             pl.BlockSpec((fourier.shape[1], fourier.shape[0]), whole),
             pl.BlockSpec(first_weight.shape, whole),
             pl.BlockSpec((1, hidden), whole),
@@ -145,12 +146,12 @@
             pl.BlockSpec((heads, 1), whole),
         ],
         out_specs=[
-            pl.BlockSpec((features, BLOCK), by_column),
-            pl.BlockSpec((BLOCK, hidden), by_row),
-            pl.BlockSpec((BLOCK, hidden), by_row),
-            pl.BlockSpec((BLOCK, hidden), by_row),
-            pl.BlockSpec((BLOCK, hidden), by_row),
-            pl.BlockSpec((heads, BLOCK), by_column),
+            pl.BlockSpec((features, FORWARD_BLOCK), by_column),
+            pl.BlockSpec((FORWARD_BLOCK, hidden), by_row),
+            pl.BlockSpec((FORWARD_BLOCK, hidden), by_row),
+            pl.BlockSpec((FORWARD_BLOCK, hidden), by_row),
+            pl.BlockSpec((FORWARD_BLOCK, hidden), by_row),
+            pl.BlockSpec((heads, FORWARD_BLOCK), by_column),
         ],
         out_shape=[
             jax.ShapeDtypeStruct((features, rows), jnp.bfloat16),

time: 85.8 us -> 84.7 us (0.987)
  Pallas kernels: 24.2 us -> 23 us
    pallas_call x1, Pallas kernels: 13.8 us -> 12.6 us  [forward_layers(): pl.pallas_call(forward_kernel, grid=(rows // FORWARD_BLOCK,), in_specs=[p...]
where the time goes in v17:
time: 84.7 us; the launch traced here: 84 us
  Pallas kernels  23 us (27%)
  waiting for transfers between devices  19.6 us (23%)
  starting transfers between devices  16 us (19%)
  local copies, waits for them, and re-layouts  15.3 us (18%)
  other arithmetic  7.78 us (9%)
  matrix products  1.29 us (2%)
  between operations  1.06 us (1%)
    pallas_call x1, Pallas kernels, forward_layers(): pl.pallas_call(forward_kernel, grid=(rows // FORWARD_BLOCK,), in_specs=[p...  12.6 us
    pallas_call x1, Pallas kernels, backward(): pl.pallas_call(backward_kernel, grid=(rows // BLOCK,), in_specs=[pl.Block...  10.4 us
    all_to_all x1, starting transfers between devices, per_device(): lax.all_to_all(outgoing, 'space', split_axis=0, concat_axis=0, tiled=True)  8.31 us
    all_to_all x1, waiting for transfers between devices, per_device(): lax.all_to_all(sendback, 'space', split_axis=1, concat_axis=1, tiled=True)  7 us
    all_to_all x1, waiting for transfers between devices, per_device(): lax.all_to_all(partials, 'space', split_axis=1, concat_axis=1, tiled=True)  6.91 us
    all_to_all x1, waiting for transfers between devices, per_device(): lax.all_to_all(outgoing, 'space', split_axis=0, concat_axis=0, tiled=True)  5.07 us
    all_to_all x1, starting transfers between devices, per_device(): lax.all_to_all(partials, 'space', split_axis=1, concat_axis=1, tiled=True)  3.5 us
    all_to_all x1, starting transfers between devices, per_device(): lax.all_to_all(sendback, 'space', split_axis=1, concat_axis=1, tiled=True)  3.5 us
  transfers between devices with their start and end apart: 6, of which 4 were waited for; matrix products, arithmetic and copies ran while one was open for 9% of the time, Pallas kernels for 0%

profile of v17, /device:TPU:0, one launch (start us, length us, event | category | flops | bytes accessed | tf_op | source)
XLA Modules:
  0.0 84.0 jit_solution(2439099774521185425)
XLA Ops:
  0.7 0.8 copy.129
  2.0 0.9 %reshape.249 = f32[3,128,32]{2,1,0:T(8,128)S(1)} reshape(f32[3,16,256]{2,1,0:T(8,128)} %param.12) | data formatting | bytes 98304 | tf_op jit(solution)/shard_map/reshape | solution.py:292
  3.0 0.8 reshape.250
  4.0 0.9 %fusion.4 = f32[16,12,128]{2,1,0:T(8,128)} fusion(f32[128,128,1]{0,1,2:T(8,128)S(1)} %bitcast.50, pred[16,12,128]{2,0,1:T(8,128)(4,1)S(1)} %broadcast_compare_fusion), kind=kOutput, calls=%fused_computation.9 | convolution fusion | flops 37748736 | bytes 188416 | tf_op jit(solution)/shard_map/dot_general | solution.py:295
  4.9 8.3 %all-to-all-start = ((f32[16,12,128]{2,1,0:T(8,128)}), f32[16,12,128]{2,1,0:T(8,128)S(1)}, u32[]{:S(2)}, u32[]{:S(2)}) async-start(f32[16,12,128]{2,1,0:T(8,128)} %fusion.4), calls=%async_computation | async-start | bytes 262144 | tf_op jit(solution)/shard_map/all_to_all | solution.py:303
  13.2 1.4 %copy.135 = f32[3,128]{0,1:T(8,128)} copy(f32[3,128]{1,0:T(4,128)} %param.17) | data formatting | bytes 3072 | tf_op args[5]
  14.6 1.3 %copy.136.bh_ref = f32[4,1]{1,0:T(4,128)} copy(f32[4,1]{0,1:T(1,128)} %bitcast.63) | data formatting | bytes 32 | tf_op jit(solution)/shard_map/reshape;squeeze | solution.py:173
  15.9 5.1 %all-to-all-done = f32[16,12,128]{2,1,0:T(8,128)S(1)} async-done(((f32[16,12,128]{2,1,0:T(8,128)}), f32[16,12,128]{2,1,0:T(8,128)S(1)}, u32[]{:S(2)}, u32[]{:S(2)}) %all-to-all-start) | async-done | bytes 98336 | tf_op jit(solution)/shard_map/all_to_all | solution.py:303
  21.4 0.8 %reshape.253.place_ref = f32[4,6144]{1,0:T(4,128)} reshape(f32[4,192,32]{2,1,0:T(8,128)S(1)} %copy.134) | data formatting | bytes 196608 | tf_op jit(solution)/shard_map/reshape | solution.py:129
  22.2 12.6 %shard_map.163 = (bf16[256,6144]{1,0:T(8,128)(2,1)}, bf16[6144,256]{1,0:T(8,128)(2,1)}, bf16[6144,256]{1,0:T(8,128)(2,1)}, f32[6144,256]{1,0:T(8,128)}, f32[6144,256]{1,0:T(8,128)}, /*index=5*/f32[4,6144]{1,0:T(4,128)}) custom-call(f32[4,6144]{1,0:T(4,128)} %reshape.253.place_ref, f32[128,3]{1,0:T(8,128)} %bitcast.51, bf16[256,256]{1,0:T(8,128)(2,1)} %bitcast.53, ...), custom_call_target="tpu_custom_call" | custom-call | tf_op jit(solution)/shard_map/pallas_call | solution.py:135
  34.8 1.0 %fusion.24 = (f32[1,6144]{1,0:T(1,128)S(1)}, f32[6144]{0:T(1024)S(1)}) fusion(f32[4,6144]{1,0:T(4,128)} %get-tuple-element.22), kind=kLoop, calls=%fused_computation.56 | loop fusion | bytes 73728 | tf_op jit(solution)/shard_map/slice | solution.py:183
  35.8 1.0 %add_divide_fusion = f32[3,6144]{1,0:T(4,128)S(1)} fusion(f32[4,6144]{1,0:T(4,128)} %get-tuple-element.22), kind=kLoop, calls=%fused_computation.13 | loop fusion | flops 55296 | bytes 147456 | tf_op jit(solution)/shard_map/div | solution.py:184
  37.8 0.6 copy.147
  38.4 3.5 %all-to-all-start.1 = ((f32[4,16,12]{2,0,1:T(4,128)}), f32[4,16,12]{2,0,1:T(4,128)S(1)}, u32[]{:S(2)}, u32[]{:S(2)}) async-start(f32[4,16,12]{2,0,1:T(4,128)} %copy.147), calls=%async_computation.1 | async-start | bytes 65536 | tf_op jit(solution)/shard_map/all_to_all | solution.py:322
  42.4 6.9 %all-to-all-done.1 = f32[4,16,12]{2,0,1:T(4,128)S(1)} async-done(((f32[4,16,12]{2,0,1:T(4,128)}), f32[4,16,12]{2,0,1:T(4,128)S(1)}, u32[]{:S(2)}, u32[]{:S(2)}) %all-to-all-start.1) | async-done | bytes 3104 | tf_op jit(solution)/shard_map/all_to_all | solution.py:322
  51.4 3.5 %all-to-all-start.2 = ((f32[4,16,12]{2,0,1:T(4,128)}), f32[4,16,12]{2,0,1:T(4,128)S(1)}, u32[]{:S(2)}, u32[]{:S(2)}) async-start(f32[4,16,12]{2,0,1:T(4,128)} %copy.153), calls=%async_computation.2 | async-start | bytes 65536 | tf_op jit(solution)/shard_map/all_to_all | solution.py:347
  55.3 7.0 %all-to-all-done.2 = f32[4,16,12]{2,0,1:T(4,128)S(1)} async-done(((f32[4,16,12]{2,0,1:T(4,128)}), f32[4,16,12]{2,0,1:T(4,128)S(1)}, u32[]{:S(2)}, u32[]{:S(2)}) %all-to-all-start.2) | async-done | bytes 3104 | tf_op jit(solution)/shard_map/all_to_all | solution.py:347
  63.9 0.9 %copy.160 = bf16[4,6144]{0,1:T(8,128)(2,1)S(1)} copy(bf16[4,6144]{1,0:T(4,128)(2,1)S(1)} %pad_maximum_fusion.1) | data formatting | bytes 98304 | tf_op jit(solution)/shard_map/concatenate | solution.py:211
  64.8 0.8 convert_reduce_fusion
  66.0 10.4 %shard_map.164 = (f32[256,256]{1,0:T(8,128)}, f32[1,256]{1,0:T(1,128)}, f32[256,256]{1,0:T(8,128)}, f32[1,256]{1,0:T(1,128)}, f32[4,256]{1,0:T(4,128)}) custom-call(bf16[256,6144]{1,0:T(8,128)(2,1)} %get-tuple-element.17.enc_ref, bf16[6144,256]{1,0:T(8,128)(2,1)} %get-tuple-element.18.a1_ref, bf16[6144,256]{1,0:T(8,128)(2,1)} %get-tuple-element.19.a2_ref, ...), custom_call_target="tpu_custom_call" | custom-call | tf_op jit(solution)/shard_map/pallas_call | solution.py:220
  76.4 0.7 pad_maximum_fusion.3
  78.4 0.7 fusion.22
  80.8 1.6 %fusion = f32[1,128,256]{2,1,0:T(8,128)} fusion(f32[256,256]{1,0:T(8,128)S(1)} %collective-permute-done.1, s32[]{:T(128)S(6)} %select_n.17, f32[256,256]{1,0:T(8,128)} %get-tuple-element.24), kind=kLoop, calls=%fused_computation.3 | loop fusion | flops 32768 | bytes 393220 | tf_op jit(solution)/shard_map/broadcast_in_dim | solution.py:403
  82.4 1.6 %fusion.1 = f32[1,128,256]{2,1,0:T(8,128)} fusion(f32[256,256]{1,0:T(8,128)S(1)} %collective-permute-done, s32[]{:T(128)S(6)} %select_n.17, f32[256,256]{1,0:T(8,128)} %get-tuple-element.23), kind=kLoop, calls=%fused_computation.5 | loop fusion | flops 32768 | bytes 393220 | tf_op jit(solution)/shard_map/broadcast_in_dim | solution.py:402
  (92 shorter events, 9.7 us)
Async XLA Ops:
  0.6 41.3 %copy-start.3 = (f32[3,16]{1,0:T(4,128)S(1)}, f32[3,16]{1,0:T(4,128)}, u32[]{:S(2)}) copy-start(f32[3,16]{1,0:T(4,128)} %param.16) | copy-start | bytes 580
  2.9 47.2 %copy-start.2 = (s32[16,8]{0,1:T(8,128)S(1)}, s32[16,8]{0,1:T(8,128)}, u32[]{:S(2)}) copy-start(s32[16,8]{0,1:T(8,128)} %param.15) | copy-start | bytes 1540
  4.9 16.1 %all-to-all-start = ((f32[16,12,128]{2,1,0:T(8,128)}), f32[16,12,128]{2,1,0:T(8,128)S(1)}, u32[]{:S(2)}, u32[]{:S(2)}) async-start(f32[16,12,128]{2,1,0:T(8,128)} %fusion.4), calls=%async_computation | async-start | bytes 262144 | tf_op jit(solution)/shard_map/all_to_all | solution.py:303
  34.8 27.9 %copy-start.1 = (f32[4,6144]{1,0:T(4,128)S(1)}, f32[4,6144]{1,0:T(4,128)}, u32[]{:S(2)}) copy-start(f32[4,6144]{1,0:T(4,128)} %get-tuple-element.22) | copy-start | bytes 294916
  38.4 10.9 %all-to-all-start.1 = ((f32[4,16,12]{2,0,1:T(4,128)}), f32[4,16,12]{2,0,1:T(4,128)S(1)}, u32[]{:S(2)}, u32[]{:S(2)}) async-start(f32[4,16,12]{2,0,1:T(4,128)} %copy.147), calls=%async_computation.1 | async-start | bytes 65536 | tf_op jit(solution)/shard_map/all_to_all | solution.py:322
  51.4 10.9 %all-to-all-start.2 = ((f32[4,16,12]{2,0,1:T(4,128)}), f32[4,16,12]{2,0,1:T(4,128)S(1)}, u32[]{:S(2)}, u32[]{:S(2)}) async-start(f32[4,16,12]{2,0,1:T(4,128)} %copy.153), calls=%async_computation.2 | async-start | bytes 65536 | tf_op jit(solution)/shard_map/all_to_all | solution.py:347
  64.8 1.2 %copy-start = (bf16[4,6144]{0,1:T(8,128)(2,1)}, bf16[4,6144]{0,1:T(8,128)(2,1)S(1)}, u32[]{:S(2)}) copy-start(bf16[4,6144]{0,1:T(8,128)(2,1)S(1)} %copy.160) | copy-start | bytes 147460
  77.2 1.2 %collective-permute-start.2 = (f32[7,256]{1,0:T(8,128)S(1)}, f32[7,256]{1,0:T(8,128)S(1)}, u32[]{:S(2)}, u32[]{:S(2)}) collective-permute-start(f32[7,256]{1,0:T(8,128)S(1)} %pad_maximum_fusion.3), channel_id=1, source_target_pairs={{0,1},{1,0},{2,3},{3,2},{4,5},{5,4},{6,7},{7,6},{8,9},{9,8},{10,11... | collective-permute-start | bytes 21512 | tf_op jit(solution)/shard_map/ppermute | solution.py:365
  77.3 3.6 %collective-permute-start.1 = (f32[256,256]{1,0:T(8,128)}, f32[256,256]{1,0:T(8,128)S(1)}, u32[]{:S(2)}, u32[]{:S(2)}) collective-permute-start(f32[256,256]{1,0:T(8,128)} %get-tuple-element.24), channel_id=1, source_target_pairs={{0,1},{1,0},{2,3},{3,2},{4,5},{5,4},{6,7},{7,6},{8,9},{9,8},{10,11... | collective-permute-start | bytes 786440 | tf_op jit(solution)/shard_map/ppermute | solution.py:365
  77.7 4.7 %collective-permute-start = (f32[256,256]{1,0:T(8,128)}, f32[256,256]{1,0:T(8,128)S(1)}, u32[]{:S(2)}, u32[]{:S(2)}) collective-permute-start(f32[256,256]{1,0:T(8,128)} %get-tuple-element.23), channel_id=1, source_target_pairs={{0,1},{1,0},{2,3},{3,2},{4,5},{5,4},{6,7},{7,6},{8,9},{9,8},{10,11... | collective-permute-start | bytes 786440 | tf_op jit(solution)/shard_map/ppermute | solution.py:365

commit v18 on v17

--- a/solution.py
+++ b/solution.py
@@ -120,7 +120,7 @@
 
 
 BLOCK = 3072
-FORWARD_BLOCK = 1024
+FORWARD_BLOCK = 512
 
 
 def forward_layers(samples, fourier, params):

time: 84.7 us -> 86.1 us (1.017)
  Pallas kernels: 23 us -> 24.5 us
    pallas_call x1, Pallas kernels: 12.6 us -> 14.1 us  [forward_layers(): pl.pallas_call(forward_kernel, grid=(rows // FORWARD_BLOCK,), in_specs=[p...]
where the time goes in v18:
time: 86.1 us; the launch traced here: 85.4 us
  Pallas kernels  24.5 us (28%)
  waiting for transfers between devices  19.6 us (23%)
  starting transfers between devices  16 us (19%)
  local copies, waits for them, and re-layouts  15.3 us (18%)
  other arithmetic  7.78 us (9%)
  matrix products  1.29 us (1%)
  between operations  1.06 us (1%)
    pallas_call x1, Pallas kernels, forward_layers(): pl.pallas_call(forward_kernel, grid=(rows // FORWARD_BLOCK,), in_specs=[p...  14.1 us
    pallas_call x1, Pallas kernels, backward(): pl.pallas_call(backward_kernel, grid=(rows // BLOCK,), in_specs=[pl.Block...  10.4 us
    all_to_all x1, starting transfers between devices, per_device(): lax.all_to_all(outgoing, 'space', split_axis=0, concat_axis=0, tiled=True)  8.31 us
    all_to_all x1, waiting for transfers between devices, per_device(): lax.all_to_all(sendback, 'space', split_axis=1, concat_axis=1, tiled=True)  7 us
    all_to_all x1, waiting for transfers between devices, per_device(): lax.all_to_all(partials, 'space', split_axis=1, concat_axis=1, tiled=True)  6.91 us
    all_to_all x1, waiting for transfers between devices, per_device(): lax.all_to_all(outgoing, 'space', split_axis=0, concat_axis=0, tiled=True)  5.07 us
    all_to_all x1, starting transfers between devices, per_device(): lax.all_to_all(partials, 'space', split_axis=1, concat_axis=1, tiled=True)  3.5 us
    all_to_all x1, starting transfers between devices, per_device(): lax.all_to_all(sendback, 'space', split_axis=1, concat_axis=1, tiled=True)  3.5 us
  transfers between devices with their start and end apart: 6, of which 4 were waited for; matrix products, arithmetic and copies ran while one was open for 9% of the time, Pallas kernels for 0%

profile of v18, /device:TPU:0, one launch (start us, length us, event | category | flops | bytes accessed | tf_op | source)
XLA Modules:
  0.0 85.4 jit_solution(9152117395577892243)
XLA Ops:
  0.7 0.8 copy.129
  2.0 0.9 %reshape.249 = f32[3,128,32]{2,1,0:T(8,128)S(1)} reshape(f32[3,16,256]{2,1,0:T(8,128)} %param.12) | data formatting | bytes 98304 | tf_op jit(solution)/shard_map/reshape | solution.py:292
  3.0 0.8 reshape.250
  4.0 0.9 %fusion.4 = f32[16,12,128]{2,1,0:T(8,128)} fusion(f32[128,128,1]{0,1,2:T(8,128)S(1)} %bitcast.50, pred[16,12,128]{2,0,1:T(8,128)(4,1)S(1)} %broadcast_compare_fusion), kind=kOutput, calls=%fused_computation.9 | convolution fusion | flops 37748736 | bytes 188416 | tf_op jit(solution)/shard_map/dot_general | solution.py:295
  4.9 8.3 %all-to-all-start = ((f32[16,12,128]{2,1,0:T(8,128)}), f32[16,12,128]{2,1,0:T(8,128)S(1)}, u32[]{:S(2)}, u32[]{:S(2)}) async-start(f32[16,12,128]{2,1,0:T(8,128)} %fusion.4), calls=%async_computation | async-start | bytes 262144 | tf_op jit(solution)/shard_map/all_to_all | solution.py:303
  13.2 1.4 %copy.135 = f32[3,128]{0,1:T(8,128)} copy(f32[3,128]{1,0:T(4,128)} %param.17) | data formatting | bytes 3072 | tf_op args[5]
  14.6 1.3 %copy.136.bh_ref = f32[4,1]{1,0:T(4,128)} copy(f32[4,1]{0,1:T(1,128)} %bitcast.63) | data formatting | bytes 32 | tf_op jit(solution)/shard_map/reshape;squeeze | solution.py:173
  15.9 5.1 %all-to-all-done = f32[16,12,128]{2,1,0:T(8,128)S(1)} async-done(((f32[16,12,128]{2,1,0:T(8,128)}), f32[16,12,128]{2,1,0:T(8,128)S(1)}, u32[]{:S(2)}, u32[]{:S(2)}) %all-to-all-start) | async-done | bytes 98336 | tf_op jit(solution)/shard_map/all_to_all | solution.py:303
  21.4 0.8 reshape.253.place_ref
  22.2 14.1 %shard_map.163 = (bf16[256,6144]{1,0:T(8,128)(2,1)}, bf16[6144,256]{1,0:T(8,128)(2,1)}, bf16[6144,256]{1,0:T(8,128)(2,1)}, f32[6144,256]{1,0:T(8,128)}, f32[6144,256]{1,0:T(8,128)}, /*index=5*/f32[4,6144]{1,0:T(4,128)}) custom-call(f32[4,6144]{1,0:T(4,128)} %reshape.253.place_ref, f32[128,3]{1,0:T(8,128)} %bitcast.51, bf16[256,256]{1,0:T(8,128)(2,1)} %bitcast.53, ...), custom_call_target="tpu_custom_call" | custom-call | tf_op jit(solution)/shard_map/pallas_call | solution.py:135
  36.3 1.0 %fusion.24 = (f32[1,6144]{1,0:T(1,128)S(1)}, f32[6144]{0:T(1024)S(1)}) fusion(f32[4,6144]{1,0:T(4,128)} %get-tuple-element.22), kind=kLoop, calls=%fused_computation.56 | loop fusion | bytes 73728 | tf_op jit(solution)/shard_map/slice | solution.py:183
  37.3 1.0 %add_divide_fusion = f32[3,6144]{1,0:T(4,128)S(1)} fusion(f32[4,6144]{1,0:T(4,128)} %get-tuple-element.22), kind=kLoop, calls=%fused_computation.13 | loop fusion | flops 55296 | bytes 147456 | tf_op jit(solution)/shard_map/div | solution.py:184
  39.3 0.6 copy.147
  39.9 3.5 %all-to-all-start.1 = ((f32[4,16,12]{2,0,1:T(4,128)}), f32[4,16,12]{2,0,1:T(4,128)S(1)}, u32[]{:S(2)}, u32[]{:S(2)}) async-start(f32[4,16,12]{2,0,1:T(4,128)} %copy.147), calls=%async_computation.1 | async-start | bytes 65536 | tf_op jit(solution)/shard_map/all_to_all | solution.py:322
  43.9 6.9 %all-to-all-done.1 = f32[4,16,12]{2,0,1:T(4,128)S(1)} async-done(((f32[4,16,12]{2,0,1:T(4,128)}), f32[4,16,12]{2,0,1:T(4,128)S(1)}, u32[]{:S(2)}, u32[]{:S(2)}) %all-to-all-start.1) | async-done | bytes 3104 | tf_op jit(solution)/shard_map/all_to_all | solution.py:322
  52.9 3.5 %all-to-all-start.2 = ((f32[4,16,12]{2,0,1:T(4,128)}), f32[4,16,12]{2,0,1:T(4,128)S(1)}, u32[]{:S(2)}, u32[]{:S(2)}) async-start(f32[4,16,12]{2,0,1:T(4,128)} %copy.153), calls=%async_computation.2 | async-start | bytes 65536 | tf_op jit(solution)/shard_map/all_to_all | solution.py:347
  56.7 7.0 %all-to-all-done.2 = f32[4,16,12]{2,0,1:T(4,128)S(1)} async-done(((f32[4,16,12]{2,0,1:T(4,128)}), f32[4,16,12]{2,0,1:T(4,128)S(1)}, u32[]{:S(2)}, u32[]{:S(2)}) %all-to-all-start.2) | async-done | bytes 3104 | tf_op jit(solution)/shard_map/all_to_all | solution.py:347
  65.4 0.9 %copy.160 = bf16[4,6144]{0,1:T(8,128)(2,1)S(1)} copy(bf16[4,6144]{1,0:T(4,128)(2,1)S(1)} %pad_maximum_fusion.1) | data formatting | bytes 98304 | tf_op jit(solution)/shard_map/concatenate | solution.py:211
  66.3 0.8 convert_reduce_fusion
  67.5 10.4 %shard_map.164 = (f32[256,256]{1,0:T(8,128)}, f32[1,256]{1,0:T(1,128)}, f32[256,256]{1,0:T(8,128)}, f32[1,256]{1,0:T(1,128)}, f32[4,256]{1,0:T(4,128)}) custom-call(bf16[256,6144]{1,0:T(8,128)(2,1)} %get-tuple-element.17.enc_ref, bf16[6144,256]{1,0:T(8,128)(2,1)} %get-tuple-element.18.a1_ref, bf16[6144,256]{1,0:T(8,128)(2,1)} %get-tuple-element.19.a2_ref, ...), custom_call_target="tpu_custom_call" | custom-call | tf_op jit(solution)/shard_map/pallas_call | solution.py:220
  77.9 0.7 pad_maximum_fusion.3
  79.9 0.7 fusion.22
  82.3 1.6 %fusion = f32[1,128,256]{2,1,0:T(8,128)} fusion(f32[256,256]{1,0:T(8,128)S(1)} %collective-permute-done.1, s32[]{:T(128)S(6)} %select_n.17, f32[256,256]{1,0:T(8,128)} %get-tuple-element.24), kind=kLoop, calls=%fused_computation.3 | loop fusion | flops 32768 | bytes 393220 | tf_op jit(solution)/shard_map/broadcast_in_dim | solution.py:403
  83.9 1.6 %fusion.1 = f32[1,128,256]{2,1,0:T(8,128)} fusion(f32[256,256]{1,0:T(8,128)S(1)} %collective-permute-done, s32[]{:T(128)S(6)} %select_n.17, f32[256,256]{1,0:T(8,128)} %get-tuple-element.23), kind=kLoop, calls=%fused_computation.5 | loop fusion | flops 32768 | bytes 393220 | tf_op jit(solution)/shard_map/broadcast_in_dim | solution.py:402
  (92 shorter events, 9.7 us)
Async XLA Ops:
  0.6 42.8 %copy-start.3 = (f32[3,16]{1,0:T(4,128)S(1)}, f32[3,16]{1,0:T(4,128)}, u32[]{:S(2)}) copy-start(f32[3,16]{1,0:T(4,128)} %param.16) | copy-start | bytes 580
  2.9 48.6 %copy-start.2 = (s32[16,8]{0,1:T(8,128)S(1)}, s32[16,8]{0,1:T(8,128)}, u32[]{:S(2)}) copy-start(s32[16,8]{0,1:T(8,128)} %param.15) | copy-start | bytes 1540
  4.9 16.1 %all-to-all-start = ((f32[16,12,128]{2,1,0:T(8,128)}), f32[16,12,128]{2,1,0:T(8,128)S(1)}, u32[]{:S(2)}, u32[]{:S(2)}) async-start(f32[16,12,128]{2,1,0:T(8,128)} %fusion.4), calls=%async_computation | async-start | bytes 262144 | tf_op jit(solution)/shard_map/all_to_all | solution.py:303
  36.3 27.9 %copy-start.1 = (f32[4,6144]{1,0:T(4,128)S(1)}, f32[4,6144]{1,0:T(4,128)}, u32[]{:S(2)}) copy-start(f32[4,6144]{1,0:T(4,128)} %get-tuple-element.22) | copy-start | bytes 294916
  39.9 10.9 %all-to-all-start.1 = ((f32[4,16,12]{2,0,1:T(4,128)}), f32[4,16,12]{2,0,1:T(4,128)S(1)}, u32[]{:S(2)}, u32[]{:S(2)}) async-start(f32[4,16,12]{2,0,1:T(4,128)} %copy.147), calls=%async_computation.1 | async-start | bytes 65536 | tf_op jit(solution)/shard_map/all_to_all | solution.py:322
  52.9 10.9 %all-to-all-start.2 = ((f32[4,16,12]{2,0,1:T(4,128)}), f32[4,16,12]{2,0,1:T(4,128)S(1)}, u32[]{:S(2)}, u32[]{:S(2)}) async-start(f32[4,16,12]{2,0,1:T(4,128)} %copy.153), calls=%async_computation.2 | async-start | bytes 65536 | tf_op jit(solution)/shard_map/all_to_all | solution.py:347
  66.3 1.2 %copy-start = (bf16[4,6144]{0,1:T(8,128)(2,1)}, bf16[4,6144]{0,1:T(8,128)(2,1)S(1)}, u32[]{:S(2)}) copy-start(bf16[4,6144]{0,1:T(8,128)(2,1)S(1)} %copy.160) | copy-start | bytes 147460
  78.6 1.2 %collective-permute-start.2 = (f32[7,256]{1,0:T(8,128)S(1)}, f32[7,256]{1,0:T(8,128)S(1)}, u32[]{:S(2)}, u32[]{:S(2)}) collective-permute-start(f32[7,256]{1,0:T(8,128)S(1)} %pad_maximum_fusion.3), channel_id=1, source_target_pairs={{0,1},{1,0},{2,3},{3,2},{4,5},{5,4},{6,7},{7,6},{8,9},{9,8},{10,11... | collective-permute-start | bytes 21512 | tf_op jit(solution)/shard_map/ppermute | solution.py:365
  78.7 3.6 %collective-permute-start.1 = (f32[256,256]{1,0:T(8,128)}, f32[256,256]{1,0:T(8,128)S(1)}, u32[]{:S(2)}, u32[]{:S(2)}) collective-permute-start(f32[256,256]{1,0:T(8,128)} %get-tuple-element.24), channel_id=1, source_target_pairs={{0,1},{1,0},{2,3},{3,2},{4,5},{5,4},{6,7},{7,6},{8,9},{9,8},{10,11... | collective-permute-start | bytes 786440 | tf_op jit(solution)/shard_map/ppermute | solution.py:365
  79.2 4.7 %collective-permute-start = (f32[256,256]{1,0:T(8,128)}, f32[256,256]{1,0:T(8,128)S(1)}, u32[]{:S(2)}, u32[]{:S(2)}) collective-permute-start(f32[256,256]{1,0:T(8,128)} %get-tuple-element.23), channel_id=1, source_target_pairs={{0,1},{1,0},{2,3},{3,2},{4,5},{5,4},{6,7},{7,6},{8,9},{9,8},{10,11... | collective-permute-start | bytes 786440 | tf_op jit(solution)/shard_map/ppermute | solution.py:365

commit v19 on v18

--- a/solution.py
+++ b/solution.py
@@ -120,7 +120,7 @@
 
 
 BLOCK = 3072
-FORWARD_BLOCK = 512
+FORWARD_BLOCK = 1536
 
 
 def forward_layers(samples, fourier, params):

time: 86.1 us -> 84.8 us (0.985)
  Pallas kernels: 24.5 us -> 23.2 us
    pallas_call x1, Pallas kernels: 14.1 us -> 12.7 us  [forward_layers(): pl.pallas_call(forward_kernel, grid=(rows // FORWARD_BLOCK,), in_specs=[p...]
where the time goes in v19:
time: 84.8 us; the launch traced here: 84.1 us
  Pallas kernels  23.2 us (27%)
  waiting for transfers between devices  19.6 us (23%)
  starting transfers between devices  16 us (19%)
  local copies, waits for them, and re-layouts  15.3 us (18%)
  other arithmetic  7.78 us (9%)
  matrix products  1.29 us (2%)
  between operations  1.05 us (1%)
    pallas_call x1, Pallas kernels, forward_layers(): pl.pallas_call(forward_kernel, grid=(rows // FORWARD_BLOCK,), in_specs=[p...  12.7 us
    pallas_call x1, Pallas kernels, backward(): pl.pallas_call(backward_kernel, grid=(rows // BLOCK,), in_specs=[pl.Block...  10.4 us
    all_to_all x1, starting transfers between devices, per_device(): lax.all_to_all(outgoing, 'space', split_axis=0, concat_axis=0, tiled=True)  8.31 us
    all_to_all x1, waiting for transfers between devices, per_device(): lax.all_to_all(sendback, 'space', split_axis=1, concat_axis=1, tiled=True)  7 us
    all_to_all x1, waiting for transfers between devices, per_device(): lax.all_to_all(partials, 'space', split_axis=1, concat_axis=1, tiled=True)  6.91 us
    all_to_all x1, waiting for transfers between devices, per_device(): lax.all_to_all(outgoing, 'space', split_axis=0, concat_axis=0, tiled=True)  5.07 us
    all_to_all x1, starting transfers between devices, per_device(): lax.all_to_all(partials, 'space', split_axis=1, concat_axis=1, tiled=True)  3.5 us
    all_to_all x1, starting transfers between devices, per_device(): lax.all_to_all(sendback, 'space', split_axis=1, concat_axis=1, tiled=True)  3.5 us
  transfers between devices with their start and end apart: 6, of which 4 were waited for; matrix products, arithmetic and copies ran while one was open for 9% of the time, Pallas kernels for 0%

profile of v19, /device:TPU:0, one launch (start us, length us, event | category | flops | bytes accessed | tf_op | source)
XLA Modules:
  0.0 84.1 jit_solution(15201645231301640628)
XLA Ops:
  0.7 0.8 copy.129
  2.0 0.9 %reshape.249 = f32[3,128,32]{2,1,0:T(8,128)S(1)} reshape(f32[3,16,256]{2,1,0:T(8,128)} %param.12) | data formatting | bytes 98304 | tf_op jit(solution)/shard_map/reshape | solution.py:292
  3.0 0.8 reshape.250
  4.0 0.9 %fusion.4 = f32[16,12,128]{2,1,0:T(8,128)} fusion(f32[128,128,1]{0,1,2:T(8,128)S(1)} %bitcast.50, pred[16,12,128]{2,0,1:T(8,128)(4,1)S(1)} %broadcast_compare_fusion), kind=kOutput, calls=%fused_computation.9 | convolution fusion | flops 37748736 | bytes 188416 | tf_op jit(solution)/shard_map/dot_general | solution.py:295
  4.9 8.3 %all-to-all-start = ((f32[16,12,128]{2,1,0:T(8,128)}), f32[16,12,128]{2,1,0:T(8,128)S(1)}, u32[]{:S(2)}, u32[]{:S(2)}) async-start(f32[16,12,128]{2,1,0:T(8,128)} %fusion.4), calls=%async_computation | async-start | bytes 262144 | tf_op jit(solution)/shard_map/all_to_all | solution.py:303
  13.2 1.4 %copy.135 = f32[3,128]{0,1:T(8,128)} copy(f32[3,128]{1,0:T(4,128)} %param.17) | data formatting | bytes 3072 | tf_op args[5]
  14.6 1.3 %copy.136.bh_ref = f32[4,1]{1,0:T(4,128)} copy(f32[4,1]{0,1:T(1,128)} %bitcast.63) | data formatting | bytes 32 | tf_op jit(solution)/shard_map/reshape;squeeze | solution.py:173
  15.9 5.1 %all-to-all-done = f32[16,12,128]{2,1,0:T(8,128)S(1)} async-done(((f32[16,12,128]{2,1,0:T(8,128)}), f32[16,12,128]{2,1,0:T(8,128)S(1)}, u32[]{:S(2)}, u32[]{:S(2)}) %all-to-all-start) | async-done | bytes 98336 | tf_op jit(solution)/shard_map/all_to_all | solution.py:303
  21.4 0.8 %reshape.253.place_ref = f32[4,6144]{1,0:T(4,128)} reshape(f32[4,192,32]{2,1,0:T(8,128)S(1)} %copy.134) | data formatting | bytes 196608 | tf_op jit(solution)/shard_map/reshape | solution.py:129
  22.2 12.7 %shard_map.163 = (bf16[256,6144]{1,0:T(8,128)(2,1)}, bf16[6144,256]{1,0:T(8,128)(2,1)}, bf16[6144,256]{1,0:T(8,128)(2,1)}, f32[6144,256]{1,0:T(8,128)}, f32[6144,256]{1,0:T(8,128)}, /*index=5*/f32[4,6144]{1,0:T(4,128)}) custom-call(f32[4,6144]{1,0:T(4,128)} %reshape.253.place_ref, f32[128,3]{1,0:T(8,128)} %bitcast.51, bf16[256,256]{1,0:T(8,128)(2,1)} %bitcast.53, ...), custom_call_target="tpu_custom_call" | custom-call | tf_op jit(solution)/shard_map/pallas_call | solution.py:135
  34.9 1.0 %fusion.24 = (f32[1,6144]{1,0:T(1,128)S(1)}, f32[6144]{0:T(1024)S(1)}) fusion(f32[4,6144]{1,0:T(4,128)} %get-tuple-element.22), kind=kLoop, calls=%fused_computation.56 | loop fusion | bytes 73728 | tf_op jit(solution)/shard_map/slice | solution.py:183
  36.0 1.0 %add_divide_fusion = f32[3,6144]{1,0:T(4,128)S(1)} fusion(f32[4,6144]{1,0:T(4,128)} %get-tuple-element.22), kind=kLoop, calls=%fused_computation.13 | loop fusion | flops 55296 | bytes 147456 | tf_op jit(solution)/shard_map/div | solution.py:184
  37.9 0.6 copy.147
  38.6 3.5 %all-to-all-start.1 = ((f32[4,16,12]{2,0,1:T(4,128)}), f32[4,16,12]{2,0,1:T(4,128)S(1)}, u32[]{:S(2)}, u32[]{:S(2)}) async-start(f32[4,16,12]{2,0,1:T(4,128)} %copy.147), calls=%async_computation.1 | async-start | bytes 65536 | tf_op jit(solution)/shard_map/all_to_all | solution.py:322
  42.5 6.9 %all-to-all-done.1 = f32[4,16,12]{2,0,1:T(4,128)S(1)} async-done(((f32[4,16,12]{2,0,1:T(4,128)}), f32[4,16,12]{2,0,1:T(4,128)S(1)}, u32[]{:S(2)}, u32[]{:S(2)}) %all-to-all-start.1) | async-done | bytes 3104 | tf_op jit(solution)/shard_map/all_to_all | solution.py:322
  51.5 3.5 %all-to-all-start.2 = ((f32[4,16,12]{2,0,1:T(4,128)}), f32[4,16,12]{2,0,1:T(4,128)S(1)}, u32[]{:S(2)}, u32[]{:S(2)}) async-start(f32[4,16,12]{2,0,1:T(4,128)} %copy.153), calls=%async_computation.2 | async-start | bytes 65536 | tf_op jit(solution)/shard_map/all_to_all | solution.py:347
  55.4 7.0 %all-to-all-done.2 = f32[4,16,12]{2,0,1:T(4,128)S(1)} async-done(((f32[4,16,12]{2,0,1:T(4,128)}), f32[4,16,12]{2,0,1:T(4,128)S(1)}, u32[]{:S(2)}, u32[]{:S(2)}) %all-to-all-start.2) | async-done | bytes 3104 | tf_op jit(solution)/shard_map/all_to_all | solution.py:347
  64.0 0.9 %copy.160 = bf16[4,6144]{0,1:T(8,128)(2,1)S(1)} copy(bf16[4,6144]{1,0:T(4,128)(2,1)S(1)} %pad_maximum_fusion.1) | data formatting | bytes 98304 | tf_op jit(solution)/shard_map/concatenate | solution.py:211
  64.9 0.8 convert_reduce_fusion
  66.1 10.4 %shard_map.164 = (f32[256,256]{1,0:T(8,128)}, f32[1,256]{1,0:T(1,128)}, f32[256,256]{1,0:T(8,128)}, f32[1,256]{1,0:T(1,128)}, f32[4,256]{1,0:T(4,128)}) custom-call(bf16[256,6144]{1,0:T(8,128)(2,1)} %get-tuple-element.17.enc_ref, bf16[6144,256]{1,0:T(8,128)(2,1)} %get-tuple-element.18.a1_ref, bf16[6144,256]{1,0:T(8,128)(2,1)} %get-tuple-element.19.a2_ref, ...), custom_call_target="tpu_custom_call" | custom-call | tf_op jit(solution)/shard_map/pallas_call | solution.py:220
  76.6 0.7 pad_maximum_fusion.3
  78.5 0.7 fusion.22
  81.0 1.6 %fusion = f32[1,128,256]{2,1,0:T(8,128)} fusion(f32[256,256]{1,0:T(8,128)S(1)} %collective-permute-done.1, s32[]{:T(128)S(6)} %select_n.17, f32[256,256]{1,0:T(8,128)} %get-tuple-element.24), kind=kLoop, calls=%fused_computation.3 | loop fusion | flops 32768 | bytes 393220 | tf_op jit(solution)/shard_map/broadcast_in_dim | solution.py:403
  82.5 1.6 %fusion.1 = f32[1,128,256]{2,1,0:T(8,128)} fusion(f32[256,256]{1,0:T(8,128)S(1)} %collective-permute-done, s32[]{:T(128)S(6)} %select_n.17, f32[256,256]{1,0:T(8,128)} %get-tuple-element.23), kind=kLoop, calls=%fused_computation.5 | loop fusion | flops 32768 | bytes 393220 | tf_op jit(solution)/shard_map/broadcast_in_dim | solution.py:402
  (92 shorter events, 9.7 us)
Async XLA Ops:
  0.6 41.4 %copy-start.3 = (f32[3,16]{1,0:T(4,128)S(1)}, f32[3,16]{1,0:T(4,128)}, u32[]{:S(2)}) copy-start(f32[3,16]{1,0:T(4,128)} %param.16) | copy-start | bytes 580
  2.9 47.3 %copy-start.2 = (s32[16,8]{0,1:T(8,128)S(1)}, s32[16,8]{0,1:T(8,128)}, u32[]{:S(2)}) copy-start(s32[16,8]{0,1:T(8,128)} %param.15) | copy-start | bytes 1540
  4.9 16.1 %all-to-all-start = ((f32[16,12,128]{2,1,0:T(8,128)}), f32[16,12,128]{2,1,0:T(8,128)S(1)}, u32[]{:S(2)}, u32[]{:S(2)}) async-start(f32[16,12,128]{2,1,0:T(8,128)} %fusion.4), calls=%async_computation | async-start | bytes 262144 | tf_op jit(solution)/shard_map/all_to_all | solution.py:303
  34.9 27.9 %copy-start.1 = (f32[4,6144]{1,0:T(4,128)S(1)}, f32[4,6144]{1,0:T(4,128)}, u32[]{:S(2)}) copy-start(f32[4,6144]{1,0:T(4,128)} %get-tuple-element.22) | copy-start | bytes 294916
  38.6 10.9 %all-to-all-start.1 = ((f32[4,16,12]{2,0,1:T(4,128)}), f32[4,16,12]{2,0,1:T(4,128)S(1)}, u32[]{:S(2)}, u32[]{:S(2)}) async-start(f32[4,16,12]{2,0,1:T(4,128)} %copy.147), calls=%async_computation.1 | async-start | bytes 65536 | tf_op jit(solution)/shard_map/all_to_all | solution.py:322
  51.5 10.9 %all-to-all-start.2 = ((f32[4,16,12]{2,0,1:T(4,128)}), f32[4,16,12]{2,0,1:T(4,128)S(1)}, u32[]{:S(2)}, u32[]{:S(2)}) async-start(f32[4,16,12]{2,0,1:T(4,128)} %copy.153), calls=%async_computation.2 | async-start | bytes 65536 | tf_op jit(solution)/shard_map/all_to_all | solution.py:347
  64.9 1.2 %copy-start = (bf16[4,6144]{0,1:T(8,128)(2,1)}, bf16[4,6144]{0,1:T(8,128)(2,1)S(1)}, u32[]{:S(2)}) copy-start(bf16[4,6144]{0,1:T(8,128)(2,1)S(1)} %copy.160) | copy-start | bytes 147460
  77.3 1.2 %collective-permute-start.2 = (f32[7,256]{1,0:T(8,128)S(1)}, f32[7,256]{1,0:T(8,128)S(1)}, u32[]{:S(2)}, u32[]{:S(2)}) collective-permute-start(f32[7,256]{1,0:T(8,128)S(1)} %pad_maximum_fusion.3), channel_id=1, source_target_pairs={{0,1},{1,0},{2,3},{3,2},{4,5},{5,4},{6,7},{7,6},{8,9},{9,8},{10,11... | collective-permute-start | bytes 21512 | tf_op jit(solution)/shard_map/ppermute | solution.py:365
  77.4 3.6 %collective-permute-start.1 = (f32[256,256]{1,0:T(8,128)}, f32[256,256]{1,0:T(8,128)S(1)}, u32[]{:S(2)}, u32[]{:S(2)}) collective-permute-start(f32[256,256]{1,0:T(8,128)} %get-tuple-element.24), channel_id=1, source_target_pairs={{0,1},{1,0},{2,3},{3,2},{4,5},{5,4},{6,7},{7,6},{8,9},{9,8},{10,11... | collective-permute-start | bytes 786440 | tf_op jit(solution)/shard_map/ppermute | solution.py:365
  77.9 4.7 %collective-permute-start = (f32[256,256]{1,0:T(8,128)}, f32[256,256]{1,0:T(8,128)S(1)}, u32[]{:S(2)}, u32[]{:S(2)}) collective-permute-start(f32[256,256]{1,0:T(8,128)} %get-tuple-element.23), channel_id=1, source_target_pairs={{0,1},{1,0},{2,3},{3,2},{4,5},{5,4},{6,7},{7,6},{8,9},{9,8},{10,11... | collective-permute-start | bytes 786440 | tf_op jit(solution)/shard_map/ppermute | solution.py:365

commit v20 on v17

--- a/solution.py
+++ b/solution.py
@@ -119,7 +119,7 @@
     )
 
 
-BLOCK = 3072
+BLOCK = 6144
 FORWARD_BLOCK = 1024
 
 

time: 84.7 us -> 86.5 us (1.021)
  Pallas kernels: 23 us -> 24.9 us
    pallas_call x1, Pallas kernels: 10.4 us -> 12.3 us  [backward(): pl.pallas_call(backward_kernel, grid=(rows // BLOCK,), in_specs=[pl.Block...]
where the time goes in v20:
time: 86.5 us; the launch traced here: 85.8 us
  Pallas kernels  24.9 us (29%)
  waiting for transfers between devices  19.6 us (23%)
  starting transfers between devices  16 us (18%)
  local copies, waits for them, and re-layouts  15.3 us (18%)
  other arithmetic  7.78 us (9%)
  matrix products  1.29 us (1%)
  between operations  1.05 us (1%)
    pallas_call x1, Pallas kernels, forward_layers(): pl.pallas_call(forward_kernel, grid=(rows // FORWARD_BLOCK,), in_specs=[p...  12.6 us
    pallas_call x1, Pallas kernels, backward(): pl.pallas_call(backward_kernel, grid=(rows // BLOCK,), in_specs=[pl.Block...  12.3 us
    all_to_all x1, starting transfers between devices, per_device(): lax.all_to_all(outgoing, 'space', split_axis=0, concat_axis=0, tiled=True)  8.31 us
    all_to_all x1, waiting for transfers between devices, per_device(): lax.all_to_all(sendback, 'space', split_axis=1, concat_axis=1, tiled=True)  7 us
    all_to_all x1, waiting for transfers between devices, per_device(): lax.all_to_all(partials, 'space', split_axis=1, concat_axis=1, tiled=True)  6.91 us
    all_to_all x1, waiting for transfers between devices, per_device(): lax.all_to_all(outgoing, 'space', split_axis=0, concat_axis=0, tiled=True)  5.07 us
    all_to_all x1, starting transfers between devices, per_device(): lax.all_to_all(partials, 'space', split_axis=1, concat_axis=1, tiled=True)  3.5 us
    all_to_all x1, starting transfers between devices, per_device(): lax.all_to_all(sendback, 'space', split_axis=1, concat_axis=1, tiled=True)  3.5 us
  transfers between devices with their start and end apart: 6, of which 4 were waited for; matrix products, arithmetic and copies ran while one was open for 9% of the time, Pallas kernels for 0%

profile of v20, /device:TPU:0, one launch (start us, length us, event | category | flops | bytes accessed | tf_op | source)
XLA Modules:
  0.0 85.8 jit_solution(13995873740617306699)
XLA Ops:
  0.7 0.8 copy.129
  2.0 0.9 %reshape.249 = f32[3,128,32]{2,1,0:T(8,128)S(1)} reshape(f32[3,16,256]{2,1,0:T(8,128)} %param.12) | data formatting | bytes 98304 | tf_op jit(solution)/shard_map/reshape | solution.py:292
  3.0 0.8 reshape.250
  4.0 0.9 %fusion.4 = f32[16,12,128]{2,1,0:T(8,128)} fusion(f32[128,128,1]{0,1,2:T(8,128)S(1)} %bitcast.50, pred[16,12,128]{2,0,1:T(8,128)(4,1)S(1)} %broadcast_compare_fusion), kind=kOutput, calls=%fused_computation.9 | convolution fusion | flops 37748736 | bytes 188416 | tf_op jit(solution)/shard_map/dot_general | solution.py:295
  4.9 8.3 %all-to-all-start = ((f32[16,12,128]{2,1,0:T(8,128)}), f32[16,12,128]{2,1,0:T(8,128)S(1)}, u32[]{:S(2)}, u32[]{:S(2)}) async-start(f32[16,12,128]{2,1,0:T(8,128)} %fusion.4), calls=%async_computation | async-start | bytes 262144 | tf_op jit(solution)/shard_map/all_to_all | solution.py:303
  13.2 1.4 %copy.135 = f32[3,128]{0,1:T(8,128)} copy(f32[3,128]{1,0:T(4,128)} %param.17) | data formatting | bytes 3072 | tf_op args[5]
  14.6 1.3 %copy.136.bh_ref = f32[4,1]{1,0:T(4,128)} copy(f32[4,1]{0,1:T(1,128)} %bitcast.63) | data formatting | bytes 32 | tf_op jit(solution)/shard_map/reshape;squeeze | solution.py:173
  15.9 5.1 %all-to-all-done = f32[16,12,128]{2,1,0:T(8,128)S(1)} async-done(((f32[16,12,128]{2,1,0:T(8,128)}), f32[16,12,128]{2,1,0:T(8,128)S(1)}, u32[]{:S(2)}, u32[]{:S(2)}) %all-to-all-start) | async-done | bytes 98336 | tf_op jit(solution)/shard_map/all_to_all | solution.py:303
  21.4 0.8 reshape.253.place_ref
  22.2 12.6 %shard_map.163 = (bf16[256,6144]{1,0:T(8,128)(2,1)}, bf16[6144,256]{1,0:T(8,128)(2,1)}, bf16[6144,256]{1,0:T(8,128)(2,1)}, f32[6144,256]{1,0:T(8,128)}, f32[6144,256]{1,0:T(8,128)}, /*index=5*/f32[4,6144]{1,0:T(4,128)}) custom-call(f32[4,6144]{1,0:T(4,128)} %reshape.253.place_ref, f32[128,3]{1,0:T(8,128)} %bitcast.51, bf16[256,256]{1,0:T(8,128)(2,1)} %bitcast.53, ...), custom_call_target="tpu_custom_call" | custom-call | tf_op jit(solution)/shard_map/pallas_call | solution.py:135
  34.8 1.0 %fusion.24 = (f32[1,6144]{1,0:T(1,128)S(1)}, f32[6144]{0:T(1024)S(1)}) fusion(f32[4,6144]{1,0:T(4,128)} %get-tuple-element.22), kind=kLoop, calls=%fused_computation.56 | loop fusion | bytes 73728 | tf_op jit(solution)/shard_map/slice | solution.py:183
  35.8 1.0 %add_divide_fusion = f32[3,6144]{1,0:T(4,128)S(1)} fusion(f32[4,6144]{1,0:T(4,128)} %get-tuple-element.22), kind=kLoop, calls=%fused_computation.13 | loop fusion | flops 55296 | bytes 147456 | tf_op jit(solution)/shard_map/div | solution.py:184
  37.8 0.6 copy.147
  38.4 3.5 %all-to-all-start.1 = ((f32[4,16,12]{2,0,1:T(4,128)}), f32[4,16,12]{2,0,1:T(4,128)S(1)}, u32[]{:S(2)}, u32[]{:S(2)}) async-start(f32[4,16,12]{2,0,1:T(4,128)} %copy.147), calls=%async_computation.1 | async-start | bytes 65536 | tf_op jit(solution)/shard_map/all_to_all | solution.py:322
  42.4 6.9 %all-to-all-done.1 = f32[4,16,12]{2,0,1:T(4,128)S(1)} async-done(((f32[4,16,12]{2,0,1:T(4,128)}), f32[4,16,12]{2,0,1:T(4,128)S(1)}, u32[]{:S(2)}, u32[]{:S(2)}) %all-to-all-start.1) | async-done | bytes 3104 | tf_op jit(solution)/shard_map/all_to_all | solution.py:322
  51.4 3.5 %all-to-all-start.2 = ((f32[4,16,12]{2,0,1:T(4,128)}), f32[4,16,12]{2,0,1:T(4,128)S(1)}, u32[]{:S(2)}, u32[]{:S(2)}) async-start(f32[4,16,12]{2,0,1:T(4,128)} %copy.153), calls=%async_computation.2 | async-start | bytes 65536 | tf_op jit(solution)/shard_map/all_to_all | solution.py:347
  55.3 7.0 %all-to-all-done.2 = f32[4,16,12]{2,0,1:T(4,128)S(1)} async-done(((f32[4,16,12]{2,0,1:T(4,128)}), f32[4,16,12]{2,0,1:T(4,128)S(1)}, u32[]{:S(2)}, u32[]{:S(2)}) %all-to-all-start.2) | async-done | bytes 3104 | tf_op jit(solution)/shard_map/all_to_all | solution.py:347
  63.9 0.9 %copy.160 = bf16[4,6144]{0,1:T(8,128)(2,1)S(1)} copy(bf16[4,6144]{1,0:T(4,128)(2,1)S(1)} %pad_maximum_fusion.1) | data formatting | bytes 98304 | tf_op jit(solution)/shard_map/concatenate | solution.py:211
  64.8 0.8 convert_reduce_fusion
  66.0 12.3 %shard_map.164 = (f32[256,256]{1,0:T(8,128)}, f32[1,256]{1,0:T(1,128)}, f32[256,256]{1,0:T(8,128)}, f32[1,256]{1,0:T(1,128)}, f32[4,256]{1,0:T(4,128)}) custom-call(bf16[256,6144]{1,0:T(8,128)(2,1)} %get-tuple-element.17.enc_ref, bf16[6144,256]{1,0:T(8,128)(2,1)} %get-tuple-element.18.a1_ref, bf16[6144,256]{1,0:T(8,128)(2,1)} %get-tuple-element.19.a2_ref, ...), custom_call_target="tpu_custom_call" | custom-call | tf_op jit(solution)/shard_map/pallas_call | solution.py:220
  78.3 0.7 pad_maximum_fusion.3
  80.3 0.7 fusion.22
  82.7 1.6 %fusion = f32[1,128,256]{2,1,0:T(8,128)} fusion(f32[256,256]{1,0:T(8,128)S(1)} %collective-permute-done.1, s32[]{:T(128)S(6)} %select_n.17, f32[256,256]{1,0:T(8,128)} %get-tuple-element.24), kind=kLoop, calls=%fused_computation.3 | loop fusion | flops 32768 | bytes 393220 | tf_op jit(solution)/shard_map/broadcast_in_dim | solution.py:403
  84.3 1.6 %fusion.1 = f32[1,128,256]{2,1,0:T(8,128)} fusion(f32[256,256]{1,0:T(8,128)S(1)} %collective-permute-done, s32[]{:T(128)S(6)} %select_n.17, f32[256,256]{1,0:T(8,128)} %get-tuple-element.23), kind=kLoop, calls=%fused_computation.5 | loop fusion | flops 32768 | bytes 393220 | tf_op jit(solution)/shard_map/broadcast_in_dim | solution.py:402
  (92 shorter events, 9.7 us)
Async XLA Ops:
  0.6 41.3 %copy-start.3 = (f32[3,16]{1,0:T(4,128)S(1)}, f32[3,16]{1,0:T(4,128)}, u32[]{:S(2)}) copy-start(f32[3,16]{1,0:T(4,128)} %param.16) | copy-start | bytes 580
  2.9 47.2 %copy-start.2 = (s32[16,8]{0,1:T(8,128)S(1)}, s32[16,8]{0,1:T(8,128)}, u32[]{:S(2)}) copy-start(s32[16,8]{0,1:T(8,128)} %param.15) | copy-start | bytes 1540
  4.9 16.1 %all-to-all-start = ((f32[16,12,128]{2,1,0:T(8,128)}), f32[16,12,128]{2,1,0:T(8,128)S(1)}, u32[]{:S(2)}, u32[]{:S(2)}) async-start(f32[16,12,128]{2,1,0:T(8,128)} %fusion.4), calls=%async_computation | async-start | bytes 262144 | tf_op jit(solution)/shard_map/all_to_all | solution.py:303
  34.8 27.9 %copy-start.1 = (f32[4,6144]{1,0:T(4,128)S(1)}, f32[4,6144]{1,0:T(4,128)}, u32[]{:S(2)}) copy-start(f32[4,6144]{1,0:T(4,128)} %get-tuple-element.22) | copy-start | bytes 294916
  38.4 10.9 %all-to-all-start.1 = ((f32[4,16,12]{2,0,1:T(4,128)}), f32[4,16,12]{2,0,1:T(4,128)S(1)}, u32[]{:S(2)}, u32[]{:S(2)}) async-start(f32[4,16,12]{2,0,1:T(4,128)} %copy.147), calls=%async_computation.1 | async-start | bytes 65536 | tf_op jit(solution)/shard_map/all_to_all | solution.py:322
  51.4 10.9 %all-to-all-start.2 = ((f32[4,16,12]{2,0,1:T(4,128)}), f32[4,16,12]{2,0,1:T(4,128)S(1)}, u32[]{:S(2)}, u32[]{:S(2)}) async-start(f32[4,16,12]{2,0,1:T(4,128)} %copy.153), calls=%async_computation.2 | async-start | bytes 65536 | tf_op jit(solution)/shard_map/all_to_all | solution.py:347
  64.8 1.2 %copy-start = (bf16[4,6144]{0,1:T(8,128)(2,1)}, bf16[4,6144]{0,1:T(8,128)(2,1)S(1)}, u32[]{:S(2)}) copy-start(bf16[4,6144]{0,1:T(8,128)(2,1)S(1)} %copy.160) | copy-start | bytes 147460
  79.0 1.2 %collective-permute-start.2 = (f32[7,256]{1,0:T(8,128)S(1)}, f32[7,256]{1,0:T(8,128)S(1)}, u32[]{:S(2)}, u32[]{:S(2)}) collective-permute-start(f32[7,256]{1,0:T(8,128)S(1)} %pad_maximum_fusion.3), channel_id=1, source_target_pairs={{0,1},{1,0},{2,3},{3,2},{4,5},{5,4},{6,7},{7,6},{8,9},{9,8},{10,11... | collective-permute-start | bytes 21512 | tf_op jit(solution)/shard_map/ppermute | solution.py:365
  79.1 3.6 %collective-permute-start.1 = (f32[256,256]{1,0:T(8,128)}, f32[256,256]{1,0:T(8,128)S(1)}, u32[]{:S(2)}, u32[]{:S(2)}) collective-permute-start(f32[256,256]{1,0:T(8,128)} %get-tuple-element.24), channel_id=1, source_target_pairs={{0,1},{1,0},{2,3},{3,2},{4,5},{5,4},{6,7},{7,6},{8,9},{9,8},{10,11... | collective-permute-start | bytes 786440 | tf_op jit(solution)/shard_map/ppermute | solution.py:365
  79.6 4.7 %collective-permute-start = (f32[256,256]{1,0:T(8,128)}, f32[256,256]{1,0:T(8,128)S(1)}, u32[]{:S(2)}, u32[]{:S(2)}) collective-permute-start(f32[256,256]{1,0:T(8,128)} %get-tuple-element.23), channel_id=1, source_target_pairs={{0,1},{1,0},{2,3},{3,2},{4,5},{5,4},{6,7},{7,6},{8,9},{9,8},{10,11... | collective-permute-start | bytes 786440 | tf_op jit(solution)/shard_map/ppermute | solution.py:365
